TPU v7x, 128 devices: a whole 4x4x4 slice. The times are simulated.
128 devices in a mesh: runs: 32 (over x, z, y_hi), chan: 4 (over y_lo, core).
Axes of the slice: x: 4, y: 4 (y_hi: 2, y_lo: 2; y = y_hi * 2 + y_lo), z: 4, core: 2. Of those that a mesh axis runs over, the one named last changes fastest.
Arguments:
- slices: bfloat16 [256, 512, 8192], P('runs', None, 'chan'), may hold values from -6 to 6
- spectra: bfloat16 [2, 48, 8192], P(None, None, 'chan'), may hold values from -0.0625 to 0.0625
- loadings: float32 [256, 48], replicated, may hold values from 0.5 to 2
- mixing: float32 [2, 48, 48], replicated, may hold values from -1 to 3.5
- halves: int32 [256], replicated, may hold values from 0 to 1, as said below
- partner: int32 [256], replicated, may hold values from 0 to 255, as said below
Outputs:
- new_spectra: float32 [2, 48, 8192], P(None, None, 'chan')
- held_residual: float32 [256, 48, 8192], P('runs', None, 'chan')
Inputs may be any that keep to these rules, and one draw needn't show every extreme that they name: `halves`: exactly half of the 256 runs are in each half. partner pairs every run with a run of the other half, and the partner of a run's partner is the run itself.
All inputs are finite; a program needn't handle non-finite values.
Results may differ from a plain program's by a relative error of at most 0.0045.
Values may be sent and summed in bfloat16 or wider, within the bound.
No kernel may reach another device: no remote copies, remote signals or barrier semaphores. Data moves between devices by JAX's collectives and lax.ppermute only.
A program may use at most 64 MiB of HBM per device.

v0:
```python
import jax
import jax.numpy as jnp
from jax import lax
from jax.sharding import PartitionSpec as P

NS_STEPS = 10


def polar_scale(gram):
    eye_rank = jnp.eye(gram.shape[-1], dtype=jnp.float32)
    traces = jnp.trace(gram, axis1=1, axis2=2)
    start = eye_rank[None] / jnp.sqrt(traces + 1e-06)[:, None, None]

    def advance(step, factor):
        left = jnp.einsum("nrs,nrt->nst", factor, gram, precision=lax.Precision.HIGHEST)
        inner = jnp.einsum("nst,ntu->nsu", left, factor, precision=lax.Precision.HIGHEST)
        return 0.5 * jnp.einsum(
            "nrs,nsu->nru", factor, 3.0 * eye_rank[None] - inner, precision=lax.Precision.HIGHEST
        )

    return lax.fori_loop(0, NS_STEPS, advance, start)


def project(slices, rows_low, mixed):
    partial_basis = jnp.einsum("nrj,nij->nri", rows_low, slices, preferred_element_type=jnp.float32)
    basis = lax.psum(partial_basis, "chan")
    scaled = jnp.einsum("nrs,nsi->nri", mixed, basis, precision=lax.Precision.HIGHEST)
    gram = jnp.einsum("nri,nsi->nrs", scaled, scaled, precision=lax.Precision.HIGHEST)
    factor = polar_scale(gram)
    rotated = jnp.einsum("nrs,nri->nsi", factor, scaled, precision=lax.Precision.HIGHEST).astype(
        jnp.bfloat16
    )
    result = jnp.einsum("nsi,nij->nsj", rotated, slices, preferred_element_type=jnp.float32)
    return result


def solve_one(lower, target):
    return jax.scipy.linalg.cho_solve((lower, True), target)


def solve_halves(system, moments):
    lower = jnp.linalg.cholesky(system)
    return jax.vmap(solve_one)(lower, moments)


def body(slices, spectra, loadings, mixing, halves, partner):
    run_count = slices.shape[0]
    total_runs = loadings.shape[0]
    first_run = lax.axis_index("runs") * run_count
    mine = first_run + jnp.arange(run_count, dtype=jnp.int32)
    all_runs = jnp.arange(total_runs, dtype=jnp.int32)
    matches = all_runs[None, :] == mine[:, None]
    my_halves = jnp.sum(jnp.where(matches, halves[None, :], 0), axis=1)
    my_mates = jnp.sum(jnp.where(matches, partner[None, :], 0), axis=1)
    my_loads = jnp.dot(matches.astype(jnp.float32), loadings, precision=lax.Precision.HIGHEST)
    mate_match = (all_runs[None, :] == my_mates[:, None]).astype(jnp.float32)
    mate_loads = jnp.dot(mate_match, loadings, precision=lax.Precision.HIGHEST)
    first_half = (my_halves == 0)[:, None, None]
    own_rows = jnp.where(first_half, spectra[0][None], spectra[1][None])
    own_mix = jnp.where(first_half, mixing[0][None], mixing[1][None]) * my_loads[:, None, :]
    projected = project(slices, own_rows, own_mix)
    terms = jnp.einsum("nsr,nsj->nrj", own_mix, projected, precision=lax.Precision.HIGHEST)
    mine_member = (my_halves[:, None] == jnp.arange(2, dtype=jnp.int32)[None, :]).astype(
        jnp.float32
    )
    partial_moments = jnp.einsum("nh,nrj->hrj", mine_member, terms, precision=lax.Precision.HIGHEST)
    member = (halves[:, None] == jnp.arange(2, dtype=jnp.int32)[None, :]).astype(jnp.float32)
    cross = jnp.einsum("kh,kr,ks->hrs", member, loadings, loadings, precision=lax.Precision.HIGHEST)
    inner_mix = jnp.einsum("hsr,hst->hrt", mixing, mixing, precision=lax.Precision.HIGHEST)
    system = inner_mix * cross
    moments = lax.psum(partial_moments, "runs")
    new_spectra = solve_halves(system, moments)
    held_rows = jnp.where(first_half, new_spectra[1][None], new_spectra[0][None])
    held_mix = jnp.where(first_half, mixing[1][None], mixing[0][None]) * mate_loads[:, None, :]
    held_projected = project(slices, held_rows.astype(jnp.bfloat16), held_mix)
    model_part = jnp.einsum("nrs,nsj->nrj", held_mix, held_rows, precision=lax.Precision.HIGHEST)
    return (new_spectra, held_projected - model_part)


def solution(mesh):
    placed = (P("runs", None, "chan"), P(None, None, "chan"), P(), P(), P(), P())
    return jax.shard_map(
        body,
        mesh=mesh,
        in_specs=placed,
        out_specs=(P(None, None, "chan"), P("runs", None, "chan")),
        check_vma=False,
    )
```

profile of v0, /device:TPU:1, one launch (start us, length us, event | category | flops | bytes accessed | tf_op | source)
XLA Modules:
  0.0 539.7 jit_solution(11662439572653921339)
XLA Ops:
  7.2 0.9 select_reduce_fusion.3
  8.1 1.1 slice_bitcast_fusion.3
  9.2 11.9 %fusion.17 = f32[8,48,512]{2,1,0:T(8,128)} fusion(bf16[8,512,2048]{2,1,0:T(8,128)(2,1)} %param.10, pred[8]{0:T(512)(128)(4,1)S(1)} %broadcast_compare_fusion, bf16[48,2048]{1,0:T(8,128)(2,1)S(1)} %get-tuple-element.81, bf16[48,2048]{1,0:T(8,128)(2,1)S(1)} %get-tuple-element.80), kind=kOutput, calls=%fused_computation.23 | convolution fusion | flops 806092800 | bytes 17956872 | tf_op jit(solution)/shard_map/nrj,nij->nri/dot_general | solution.py:25
  22.1 42.1 %all-reduce.4.cloned.1.call-done = f32[8,48,512]{2,1,0:T(8,128)} async-done(((f32[8,48,512]{2,1,0:T(8,128)}), f32[8,48,512]{2,1,0:T(8,128)}) %all-reduce.4.cloned.1.call-update) | async-done | bytes 786448 | tf_op jit(solution)/shard_map/psum | solution.py:26
  64.3 2.0 fusion.26
  66.2 0.9 select_reduce_fusion.1
  67.3 11.6 %while.22 = (s32[]{:T(128)}, f32[8,48,48]{1,2,0:T(8,128)S(1)}, f32[8,48,48]{2,1,0:T(8,128)S(1)}, s32[]{:T(128)}) while((s32[]{:T(128)}, f32[8,48,48]{1,2,0:T(8,128)S(1)}, f32[8,48,48]{2,1,0:T(8,128)S(1)}, s32[]{:T(128)}) %tuple.47), condition=%wide.region_6.7_spmd.clone, body=%wide.region_5.6_spmd.clone.sunk | while | flops 31891968 | bytes 829493 | solution.py:21
  67.5 0.3 fusion.126
  67.8 0.4 convolution_subtract_fusion.5
  68.6 0.3 fusion.126
  69.0 0.4 convolution_subtract_fusion.5
  69.8 0.3 fusion.126
  70.1 0.4 convolution_subtract_fusion.5
  71.3 0.4 convolution_subtract_fusion.5
  72.4 0.4 convolution_subtract_fusion.5
  73.6 0.4 convolution_subtract_fusion.5
  74.7 0.4 convolution_subtract_fusion.5
  75.8 0.4 convolution_subtract_fusion.5
  77.0 0.4 convolution_subtract_fusion.5
  78.1 0.4 convolution_subtract_fusion.5
  78.9 0.8 convolution_convert_fusion.1
  79.7 8.8 %fusion.66 = f32[8,48,2048]{2,1,0:T(8,128)S(1)} fusion(bf16[8,48,512]{2,1,0:T(8,128)(2,1)S(1)} %convolution_convert_fusion.1, bf16[8,512,2048]{2,1,0:T(8,128)(2,1)} %param.10), kind=kOutput, calls=%fused_computation.102 | convolution fusion | flops 805306368 | bytes 20316160 | tf_op jit(solution)/shard_map/nsi,nij->nsj/dot_general | solution.py:33
  88.5 3.1 fusion.25
  91.6 3.3 fusion.10
  94.9 1.3 copy.24
  96.4 9.0 %custom-call.11 = f32[2,48,48]{2,1,0:T(8,128)S(1)} custom-call(f32[2,48,48]{2,1,0:T(8,128)S(1)} %fusion.51), custom_call_target="Cholesky" | custom-call | tf_op jit(solution)/shard_map/jit(cholesky)/cholesky | solution.py:42
  105.6 7.4 %custom-call.12 = f32[2,1,48,48]{2,3,1,0:T(8,128)S(1)} custom-call(f32[2,1,48,48]{3,2,1,0:T(8,128)S(1)} %select_bitcast_fusion), custom_call_target="InvertDiagBlocksLowerTriangular" | custom-call | tf_op jit(solution)/shard_map/vmap(jit(_cho_solve))/triangular_solve | solution.py:38
  113.0 315.1 %all-reduce.6.cloned.1.call-done = f32[2,48,2048]{2,1,0:T(8,128)} async-done(((f32[2,48,2048]{2,1,0:T(8,128)}), f32[2,48,2048]{2,1,0:T(8,128)}) %all-reduce.6.cloned.1.call-update) | async-done | bytes 786448 | tf_op jit(solution)/shard_map/psum | solution.py:71
  428.1 2.0 fusion.48
  430.1 0.8 fusion.46
  431.0 12.1 %fusion.12 = f32[8,48,512]{2,1,0:T(8,128)} fusion(bf16[8,512,2048]{2,1,0:T(8,128)(2,1)} %param.10, f32[48,2048]{1,0:T(8,128)S(1)} %get-tuple-element.79, f32[48,2048]{1,0:T(8,128)S(1)} %get-tuple-element.78, pred[8]{0:T(512)(128)(4,1)S(1)} %broadcast_compare_fusion), kind=kOutput, calls=%fused_computation.18 | convolution fusion | flops 806092800 | bytes 18350088 | tf_op jit(solution)/shard_map/nrj,nij->nri/dot_general | solution.py:25
  443.2 4.5 fusion.8
  447.7 58.4 %all-reduce.8.cloned.1.call-done = f32[8,48,512]{2,1,0:T(8,128)} async-done(((f32[8,48,512]{2,1,0:T(8,128)}), f32[8,48,512]{2,1,0:T(8,128)}) %all-reduce.8.cloned.1.call-update) | async-done | bytes 786448 | tf_op jit(solution)/shard_map/psum | solution.py:26
  506.1 2.0 fusion.24
  508.1 0.9 select_reduce_fusion
  509.2 11.7 %while.23 = (s32[]{:T(128)}, f32[8,48,48]{1,2,0:T(8,128)S(1)}, f32[8,48,48]{2,1,0:T(8,128)S(1)}, s32[]{:T(128)}) while((s32[]{:T(128)}, f32[8,48,48]{1,2,0:T(8,128)S(1)}, f32[8,48,48]{2,1,0:T(8,128)S(1)}, s32[]{:T(128)}) %tuple.50), condition=%wide.region_12.13_spmd.clone, body=%wide.region_11.12_spmd.clone.sunk | while | flops 31891968 | bytes 829493 | solution.py:21
  509.5 0.4 convolution_subtract_fusion.6
  510.7 0.4 convolution_subtract_fusion.6
  511.8 0.4 convolution_subtract_fusion.6
  513.0 0.4 convolution_subtract_fusion.6
  514.1 0.4 convolution_subtract_fusion.6
  515.3 0.4 convolution_subtract_fusion.6
  516.4 0.4 convolution_subtract_fusion.6
  517.6 0.4 convolution_subtract_fusion.6
  518.7 0.4 convolution_subtract_fusion.6
  519.8 0.4 convolution_subtract_fusion.6
  520.9 0.8 convolution_convert_fusion
  521.7 11.5 %convolution_subtract_fusion.2 = f32[8,48,2048]{2,1,0:T(8,128)} fusion(f32[8,48,2048]{2,1,0:T(8,128)} %fusion.8, bf16[8,48,512]{2,1,0:T(8,128)(2,1)S(1)} %convolution_convert_fusion, bf16[8,512,2048]{2,1,0:T(8,128)(2,1)} %param.10), kind=kOutput, calls=%fused_computation.17 | convolution fusion | flops 806092800 | bytes 23461888 | tf_op jit(solution)/shard_map/nsi,nij->nsj/dot_general | solution.py:33
  (114 shorter events, 14.0 us)
Async XLA Ops:
  7.2 57.1 %all-reduce.4.cloned.1.call-start = ((), (), s32[]{:S(2)}) async-start(), calls=%async_computation | async-start | bytes 1572864 | tf_op jit(solution)/shard_map/psum | solution.py:26
  9.2 12.0 %copy-start.3 = (s32[256]{0:T(256)S(1)}, s32[256]{0:T(256)}, u32[]{:S(2)}) copy-start(s32[256]{0:T(256)} %param.14) | copy-start | bytes 3076
  9.2 12.1 %copy-start.2 = (f32[256,48]{0,1:T(8,128)S(1)}, f32[256,48]{0,1:T(8,128)}, u32[]{:S(2)}) copy-start(f32[256,48]{0,1:T(8,128)} %param.12) | copy-start | bytes 147460
  9.2 12.4 %copy-start.1 = (f32[2,48,48]{2,1,0:T(8,128)S(1)}, f32[2,48,48]{2,1,0:T(8,128)}, u32[]{:S(2)}) copy-start(f32[2,48,48]{2,1,0:T(8,128)} %param.13) | copy-start | bytes 55300
  21.1 407.0 %all-reduce.6.cloned.1.call-start = ((), (), s32[]{:S(2)}) async-start(), calls=%async_computation.1 | async-start | bytes 1572864 | tf_op jit(solution)/shard_map/psum | solution.py:71
  96.3 409.9 %all-reduce.8.cloned.1.call-start = ((), (), s32[]{:S(2)}) async-start(), calls=%async_computation.2 | async-start | bytes 1572864 | tf_op jit(solution)/shard_map/psum | solution.py:26
  430.9 12.1 %copy-start = (f32[2,48,2048]{2,1,0:T(8,128)}, f32[2,48,2048]{2,1,0:T(8,128)S(1)}, u32[]{:S(2)}) copy-start(f32[2,48,2048]{2,1,0:T(8,128)S(1)} %fusion.46) | copy-start | bytes 2359300
Sparse Core Ops, SparseCore 0:
  21.2 42.9 all-reduce.3
  96.4 331.6 all-reduce.5
  443.2 62.9 all-reduce.7
where the time goes:
time: 540 us
  waiting for transfers between devices  416 us (77%)
  matrix products  87.5 us (16%)
  other arithmetic  17.9 us (3%)
  between operations  14 us (3%)
    psum x1, waiting for transfers between devices, body(): moments = lax.psum(partial_moments, 'runs')  315 us
    psum x2, waiting for transfers between devices, project(): basis = lax.psum(partial_basis, 'chan')  101 us
    dot_general x2, matrix products, project(): jnp.einsum('nrj,nij->nri', rows_low, slices, preferred_element_type=jnp.f...  23.9 us
    dot_general x2, matrix products, project(): jnp.einsum('nsi,nij->nsj', rotated, slices, preferred_element_type=jnp.fl...  20.3 us
  transfers between devices with their start and end apart: 3, of which 3 were waited for; matrix products, arithmetic and copies ran while one was open for 4% of the time, Pallas kernels for 0%

commit v1 on v0

v1 whole, which is shorter than its diff:
```python
import jax
import jax.numpy as jnp
from jax import lax
from jax.sharding import PartitionSpec as P

NS_STEPS = 10


def polar_scale(gram):
    eye_rank = jnp.eye(gram.shape[-1], dtype=jnp.float32)
    traces = jnp.trace(gram, axis1=1, axis2=2)
    start = eye_rank[None] / jnp.sqrt(traces + 1e-06)[:, None, None]

    def advance(step, factor):
        left = jnp.einsum("nrs,nrt->nst", factor, gram, precision=lax.Precision.HIGHEST)
        inner = jnp.einsum("nst,ntu->nsu", left, factor, precision=lax.Precision.HIGHEST)
        return 0.5 * jnp.einsum(
            "nrs,nsu->nru", factor, 3.0 * eye_rank[None] - inner, precision=lax.Precision.HIGHEST
        )

    return lax.fori_loop(0, NS_STEPS, advance, start)


def step_bits(size, order):
    bits = [b for b in order if b < size]
    if sorted(bits) != [1 << i for i in range(size.bit_length() - 1)]:
        bits = [1 << i for i in range(size.bit_length() - 1)]
    return bits


def xor_pairs(size, bit):
    return [(i, i ^ bit) for i in range(size)]


def halving_scatter(x, axis, size, bits, dim):
    idx = lax.axis_index(axis)
    for bit in bits:
        hi = (idx & bit) != 0
        half = x.shape[dim] // 2
        low = lax.slice_in_dim(x, 0, half, axis=dim)
        high = lax.slice_in_dim(x, half, 2 * half, axis=dim)
        send = jnp.where(hi, low, high)
        keep = jnp.where(hi, high, low)
        x = keep + lax.ppermute(send, axis, xor_pairs(size, bit))
    return x


def doubling_gather(x, axis, size, bits, dim):
    idx = lax.axis_index(axis)
    for bit in reversed(bits):
        hi = (idx & bit) != 0
        got = lax.ppermute(x, axis, xor_pairs(size, bit))
        x = jnp.where(hi, jnp.concatenate([got, x], dim), jnp.concatenate([x, got], dim))
    return x


def block_index(axis, bits):
    idx = lax.axis_index(axis)
    block = jnp.int32(0)
    for bit in bits:
        block = block * 2 + ((idx & bit) != 0).astype(jnp.int32)
    return block


def project(slices, rows_low, mixed, chan_size, chan_bits):
    run_count = slices.shape[0]
    partial_basis = jnp.einsum("nrj,nij->nri", rows_low, slices, preferred_element_type=jnp.float32)
    basis = halving_scatter(partial_basis, "chan", chan_size, chan_bits, 0)
    part = basis.shape[0]
    first = block_index("chan", chan_bits) * part
    mixed_part = lax.dynamic_slice_in_dim(mixed, first, part, axis=0)
    scaled = jnp.einsum("nrs,nsi->nri", mixed_part, basis, precision=lax.Precision.HIGHEST)
    gram = jnp.einsum("nri,nsi->nrs", scaled, scaled, precision=lax.Precision.HIGHEST)
    factor = polar_scale(gram)
    rotated = jnp.einsum("nrs,nri->nsi", factor, scaled, precision=lax.Precision.HIGHEST).astype(
        jnp.bfloat16
    )
    rotated = doubling_gather(rotated, "chan", chan_size, chan_bits, 0)
    del run_count
    return jnp.einsum("nsi,nij->nsj", rotated, slices, preferred_element_type=jnp.float32)


def solve_one(lower, target):
    return jax.scipy.linalg.cho_solve((lower, True), target)


def make_body(runs_size, chan_size):
    runs_bits = step_bits(runs_size, (8, 2, 1, 16, 4))
    chan_bits = step_bits(chan_size, (1, 2))

    def body(slices, spectra, loadings, mixing, halves, partner):
        run_count = slices.shape[0]
        total_runs = loadings.shape[0]
        first_run = lax.axis_index("runs") * run_count
        mine = first_run + jnp.arange(run_count, dtype=jnp.int32)
        all_runs = jnp.arange(total_runs, dtype=jnp.int32)
        matches = all_runs[None, :] == mine[:, None]
        my_halves = jnp.sum(jnp.where(matches, halves[None, :], 0), axis=1)
        my_mates = jnp.sum(jnp.where(matches, partner[None, :], 0), axis=1)
        my_loads = jnp.dot(matches.astype(jnp.float32), loadings, precision=lax.Precision.HIGHEST)
        mate_match = (all_runs[None, :] == my_mates[:, None]).astype(jnp.float32)
        mate_loads = jnp.dot(mate_match, loadings, precision=lax.Precision.HIGHEST)
        first_half = (my_halves == 0)[:, None, None]
        own_rows = jnp.where(first_half, spectra[0][None], spectra[1][None])
        own_mix = jnp.where(first_half, mixing[0][None], mixing[1][None]) * my_loads[:, None, :]
        projected = project(slices, own_rows, own_mix, chan_size, chan_bits)
        terms = jnp.einsum("nsr,nsj->nrj", own_mix, projected, precision=lax.Precision.HIGHEST)
        mine_member = (my_halves[:, None] == jnp.arange(2, dtype=jnp.int32)[None, :]).astype(
            jnp.float32
        )
        partial_moments = jnp.einsum(
            "nh,nrj->hrj", mine_member, terms, precision=lax.Precision.HIGHEST
        )
        member = (halves[:, None] == jnp.arange(2, dtype=jnp.int32)[None, :]).astype(jnp.float32)
        cross = jnp.einsum("kh,kr,ks->hrs", member, loadings, loadings, precision=lax.Precision.HIGHEST)
        inner_mix = jnp.einsum("hsr,hst->hrt", mixing, mixing, precision=lax.Precision.HIGHEST)
        system = inner_mix * cross
        lower = jnp.linalg.cholesky(system)
        moments_part = halving_scatter(partial_moments, "runs", runs_size, runs_bits, 2)
        spectra_part = jax.vmap(solve_one)(lower, moments_part)
        new_spectra = doubling_gather(spectra_part, "runs", runs_size, runs_bits, 2)
        held_rows = jnp.where(first_half, new_spectra[1][None], new_spectra[0][None])
        held_mix = jnp.where(first_half, mixing[1][None], mixing[0][None]) * mate_loads[:, None, :]
        held_projected = project(
            slices, held_rows.astype(jnp.bfloat16), held_mix, chan_size, chan_bits
        )
        model_part = jnp.einsum(
            "nrs,nsj->nrj", held_mix, held_rows, precision=lax.Precision.HIGHEST
        )
        return (new_spectra, held_projected - model_part)

    return body


def solution(mesh):
    placed = (P("runs", None, "chan"), P(None, None, "chan"), P(), P(), P(), P())
    return jax.shard_map(
        make_body(mesh.shape["runs"], mesh.shape["chan"]),
        mesh=mesh,
        in_specs=placed,
        out_specs=(P(None, None, "chan"), P("runs", None, "chan")),
        check_vma=False,
    )
```

time: 540 us -> 182 us (0.34)
  waiting for transfers between devices: 416 us -> 51.5 us
  starting transfers between devices: 0.12 us -> 42.1 us
  matrix products: 87.5 us -> 65 us
  between operations: 14 us -> 1.06 us
    psum x3 -> x0, waiting for transfers between devices: 416 us -> none  [the longest x1 315 us: body(): moments = lax.psum(partial_moments, 'runs')]
    ppermute x0 -> x18, waiting for transfers between devices: none -> 51.5 us  [the longest x9 27.9 us: halving_scatter(): x = keep + lax.ppermute(send, axis, xor_pairs(size, bit))]
    ppermute x0 -> x18, starting transfers between devices: none -> 42.1 us  [the longest x9 26.3 us: halving_scatter(): x = keep + lax.ppermute(send, axis, xor_pairs(size, bit))]
  transfers between devices with their start and end apart: 3 -> 18, of which waited for: 3 -> 15; matrix products, arithmetic and copies ran while one was open for 4% -> 11% of each run, Pallas kernels for 0% -> 0%
where the time goes in v1:
time: 182 us
  matrix products  65 us (36%)
  waiting for transfers between devices  51.5 us (28%)
  starting transfers between devices  42.1 us (23%)
  other arithmetic  19.6 us (11%)
    ppermute x9, waiting for transfers between devices, halving_scatter(): x = keep + lax.ppermute(send, axis, xor_pairs(size, bit))  27.9 us
    ppermute x9, starting transfers between devices, halving_scatter(): x = keep + lax.ppermute(send, axis, xor_pairs(size, bit))  26.3 us
    ppermute x9, waiting for transfers between devices, doubling_gather(): got = lax.ppermute(x, axis, xor_pairs(size, bit))  23.6 us
    dot_general x2, matrix products, project(): jnp.einsum('nrj,nij->nri', rows_low, slices, preferred_element_type=jnp.f...  22.1 us
    dot_general x2, matrix products, project(): jnp.einsum('nsi,nij->nsj', rotated, slices, preferred_element_type=jnp.fl...  19.2 us
    ppermute x9, starting transfers between devices, doubling_gather(): got = lax.ppermute(x, axis, xor_pairs(size, bit))  15.8 us
    another operation x3, other arithmetic, body(): lower = jnp.linalg.cholesky(system)  8.93 us
    another operation x3, other arithmetic, solve_one(): return jax.scipy.linalg.cho_solve((lower, True), target)  7.46 us
  transfers between devices with their start and end apart: 18, of which 15 were waited for; matrix products, arithmetic and copies ran while one was open for 11% of the time, Pallas kernels for 0%

profile of v1, /device:TPU:1, one launch (start us, length us, event | category | flops | bytes accessed | tf_op | source)
XLA Modules:
  0.0 181.7 jit_solution(17409069655896785064)
XLA Ops:
  0.6 0.9 select_reduce_fusion.3
  1.6 1.1 slice_bitcast_fusion.3
  2.7 11.0 %fusion.17 = f32[8,48,512]{2,1,0:T(8,128)S(1)} fusion(bf16[8,512,2048]{2,1,0:T(8,128)(2,1)} %param.10, pred[8]{0:T(512)(128)(4,1)S(1)} %broadcast_compare_fusion, bf16[48,2048]{1,0:T(8,128)(2,1)S(1)} %get-tuple-element.83, bf16[48,2048]{1,0:T(8,128)(2,1)S(1)} %get-tuple-element.82), kind=kOutput, calls=%fused_computation.23 | convolution fusion | flops 806092800 | bytes 17956872 | tf_op jit(solution)/shard_map/nrj,nij->nri/dot_general | solution.py:67
  13.7 1.5 collective-permute-start
  16.3 8.8 %custom-call.11 = f32[2,48,48]{2,1,0:T(8,128)S(1)} custom-call(f32[2,48,48]{2,1,0:T(8,128)S(1)} %fusion.57), custom_call_target="Cholesky" | custom-call | tf_op jit(solution)/shard_map/jit(cholesky)/cholesky | solution.py:118
  25.4 1.5 collective-permute-start.1
  27.0 4.9 %collective-permute-done.1 = f32[2,48,512]{2,1,0:T(8,128)S(1)} collective-permute-done((f32[2,48,512]{2,1,0:T(8,128)S(1)}, f32[2,48,512]{2,1,0:T(8,128)S(1)}, u32[]{:S(2)}, u32[]{:S(2)}) %collective-permute-start.1) | collective-permute-done | bytes 196640 | tf_op jit(solution)/shard_map/ppermute | solution.py:44
  32.2 0.4 select_reduce_fusion.1
  32.7 6.2 %while.22 = (s32[]{:T(128)}, f32[2,48,48]{1,2,0:T(8,128)S(1)}, f32[2,48,48]{2,1,0:T(8,128)S(1)}, s32[]{:T(128)}) while((s32[]{:T(128)}, f32[2,48,48]{1,2,0:T(8,128)S(1)}, f32[2,48,48]{2,1,0:T(8,128)S(1)}, s32[]{:T(128)}) %tuple.49), condition=%wide.region_5.6_spmd.clone, body=%wide.region_4.5_spmd.clone.sunk | while | flops 7976450 | bytes 221237 | solution.py:21
  39.2 1.5 collective-permute-start.2
  40.7 2.1 %collective-permute-done.2 = bf16[2,48,512]{2,1,0:T(8,128)(2,1)S(1)} collective-permute-done((bf16[2,48,512]{2,1,0:T(8,128)(2,1)S(1)}, bf16[2,48,512]{2,1,0:T(8,128)(2,1)S(1)}, u32[]{:S(2)}, u32[]{:S(2)}) %collective-permute-start.2) | collective-permute-done | bytes 98336 | tf_op jit(solution)/shard_map/ppermute | solution.py:52
  42.8 2.3 %collective-permute-start.3 = (bf16[4,48,512]{2,1,0:T(8,128)(2,1)S(1)}, bf16[4,48,512]{2,1,0:T(8,128)(2,1)S(1)}, u32[]{:S(2)}, u32[]{:S(2)}) collective-permute-start(bf16[4,48,512]{2,1,0:T(8,128)(2,1)S(1)} %maximum_select_fusion.6), channel_id=1, source_target_pairs={{0,1},{1,0},{2,3},{3,2},{4,5},{5,4},{6,7},{7,6},{8,9},{9,8},{10,11... | collective-permute-start | bytes 589832 | tf_op jit(solution)/shard_map/ppermute | solution.py:52
  45.0 1.1 collective-permute-done.3
  46.1 8.8 %fusion.24 = f32[8,48,2048]{2,1,0:T(8,128)S(1)} fusion(bf16[8,512,2048]{2,1,0:T(8,128)(2,1)} %param.10, bf16[4,48,512]{2,1,0:T(8,128)(2,1)S(1)} %maximum_select_fusion.6, bf16[4,48,512]{2,1,0:T(8,128)(2,1)S(1)} %collective-permute-done.3, pred[]{:T(512)S(6)} %ne.19), kind=kOutput, calls=%fused_computation.36 | convolution fusion | flops 805896192 | bytes 20316160 | tf_op jit(solution)/shard_map/nsi,nij->nsj/dot_general | solution.py:80
  54.9 3.1 %fusion.64 = f32[8,48,2048]{2,1,0:T(8,128)S(1)} fusion(f32[8,48,2048]{2,1,0:T(8,128)S(1)} %fusion.24, f32[8,48]{1,0:T(8,128)S(1)} %fusion.65, f32[48,48]{1,0:T(8,128)S(1)} %get-tuple-element.87, f32[48,48]{1,0:T(8,128)S(1)} %get-tuple-element.86, pred[8]{0:T(512)(128)(4,1)S(1)} %broadcast_compare_fusion), kind=kOutput, calls=%fused_computation.115 | convolution fusion | flops 453021696 | bytes 6311432 | tf_op jit(solution)/shard_map/nsr,nsj->nrj/dot_general | solution.py:107
  58.0 3.3 %fusion.10 = f32[2,48,2048]{2,0,1:T(2,128)S(1)} fusion(f32[8,48,2048]{2,1,0:T(8,128)S(1)} %fusion.64, s32[8]{0:T(128)S(1)} %get-tuple-element.67), kind=kOutput, calls=%fused_computation.15 | convolution fusion | flops 18874384 | bytes 3932192 | tf_op jit(solution)/shard_map/nh,nrj->hrj/dot_general | solution.py:111
  61.5 1.4 collective-permute-start.4
  62.9 9.0 %collective-permute-done.4 = f32[2,48,1024]{2,0,1:T(2,128)S(1)} collective-permute-done((f32[2,48,1024]{2,0,1:T(2,128)S(1)}, f32[2,48,1024]{2,0,1:T(2,128)S(1)}, u32[]{:S(2)}, u32[]{:S(2)}) %collective-permute-start.4) | collective-permute-done | bytes 393248 | tf_op jit(solution)/shard_map/ppermute | solution.py:44
  72.3 1.8 %collective-permute-start.5 = (f32[2,48,512]{2,0,1:T(2,128)S(1)}, f32[2,48,512]{2,0,1:T(2,128)S(1)}, u32[]{:S(2)}, u32[]{:S(2)}) collective-permute-start(f32[2,48,512]{2,0,1:T(2,128)S(1)} %broadcast_select_fusion.1), channel_id=1, source_target_pairs={{0,8},{4,12},{8,0},{12,4},{16,24},{20,28},{24,16},{28,20},{32,40},... | collective-permute-start | bytes 589832 | tf_op jit(solution)/shard_map/ppermute | solution.py:44
  74.1 4.1 %collective-permute-done.5 = f32[2,48,512]{2,0,1:T(2,128)S(1)} collective-permute-done((f32[2,48,512]{2,0,1:T(2,128)S(1)}, f32[2,48,512]{2,0,1:T(2,128)S(1)}, u32[]{:S(2)}, u32[]{:S(2)}) %collective-permute-start.5) | collective-permute-done | bytes 196640 | tf_op jit(solution)/shard_map/ppermute | solution.py:44
  78.4 2.9 %collective-permute-start.6 = (f32[2,48,256]{2,0,1:T(2,128)S(1)}, f32[2,48,256]{2,0,1:T(2,128)S(1)}, u32[]{:S(2)}, u32[]{:S(2)}) collective-permute-start(f32[2,48,256]{2,0,1:T(2,128)S(1)} %broadcast_select_fusion.2), channel_id=1, source_target_pairs={{0,4},{4,0},{8,12},{12,8},{16,20},{20,16},{24,28},{28,24},{32,36},... | collective-permute-start | bytes 294920 | tf_op jit(solution)/shard_map/ppermute | solution.py:44
  81.3 2.1 %collective-permute-done.6 = f32[2,48,256]{2,0,1:T(2,128)S(1)} collective-permute-done((f32[2,48,256]{2,0,1:T(2,128)S(1)}, f32[2,48,256]{2,0,1:T(2,128)S(1)}, u32[]{:S(2)}, u32[]{:S(2)}) %collective-permute-start.6) | collective-permute-done | bytes 98336 | tf_op jit(solution)/shard_map/ppermute | solution.py:44
  83.5 2.7 %collective-permute-start.7 = (f32[2,48,128]{2,0,1:T(2,128)S(1)}, f32[2,48,128]{2,0,1:T(2,128)S(1)}, u32[]{:S(2)}, u32[]{:S(2)}) collective-permute-start(f32[2,48,128]{2,0,1:T(2,128)S(1)} %broadcast_select_fusion.3), channel_id=1, source_target_pairs={{0,64},{4,68},{8,72},{12,76},{16,80},{20,84},{24,88},{28,92},{32,9... | collective-permute-start | bytes 147464 | tf_op jit(solution)/shard_map/ppermute | solution.py:44
  86.4 1.7 collective-permute-done.7
  88.2 3.2 %collective-permute-start.8 = (f32[2,48,64]{2,0,1:T(2,128)S(1)}, f32[2,48,64]{2,0,1:T(2,128)S(1)}, u32[]{:S(2)}, u32[]{:S(2)}) collective-permute-start(f32[2,48,64]{2,0,1:T(2,128)S(1)} %broadcast_select_fusion.4), channel_id=1, source_target_pairs={{0,16},{4,20},{8,24},{12,28},{16,0},{20,4},{24,8},{28,12},{32,48},... | collective-permute-start | bytes 73736 | tf_op jit(solution)/shard_map/ppermute | solution.py:44
  91.5 7.4 %custom-call.12 = f32[2,1,48,48]{2,3,1,0:T(8,128)S(1)} custom-call(f32[2,1,48,48]{3,2,1,0:T(8,128)S(1)} %select_bitcast_fusion), custom_call_target="InvertDiagBlocksLowerTriangular" | custom-call | tf_op jit(solution)/shard_map/vmap(jit(_cho_solve))/triangular_solve | solution.py:84
  99.8 4.4 %collective-permute-done.9 = f32[2,48,64]{2,1,0:T(8,128)S(1)} collective-permute-done((f32[2,48,64]{2,1,0:T(8,128)S(1)}, f32[2,48,64]{2,1,0:T(8,128)S(1)}, u32[]{:S(2)}, u32[]{:S(2)}) %collective-permute-start.9) | collective-permute-done | bytes 24608 | tf_op jit(solution)/shard_map/ppermute | solution.py:52
  104.3 2.8 %collective-permute-start.10 = (f32[2,48,128]{2,1,0:T(8,128)S(1)}, f32[2,48,128]{2,1,0:T(8,128)S(1)}, u32[]{:S(2)}, u32[]{:S(2)}) collective-permute-start(f32[2,48,128]{2,1,0:T(8,128)S(1)} %maximum_select_fusion.10), channel_id=1, source_target_pairs={{0,64},{4,68},{8,72},{12,76},{16,80},{20,84},{24,88},{28,92},{32,9... | collective-permute-start | bytes 147464 | tf_op jit(solution)/shard_map/ppermute | solution.py:52
  107.2 2.0 %collective-permute-done.10 = f32[2,48,128]{2,1,0:T(8,128)S(1)} collective-permute-done((f32[2,48,128]{2,1,0:T(8,128)S(1)}, f32[2,48,128]{2,1,0:T(8,128)S(1)}, u32[]{:S(2)}, u32[]{:S(2)}) %collective-permute-start.10) | collective-permute-done | bytes 49184 | tf_op jit(solution)/shard_map/ppermute | solution.py:52
  109.2 3.0 %collective-permute-start.11 = (f32[2,48,256]{2,1,0:T(8,128)S(1)}, f32[2,48,256]{2,1,0:T(8,128)S(1)}, u32[]{:S(2)}, u32[]{:S(2)}) collective-permute-start(f32[2,48,256]{2,1,0:T(8,128)S(1)} %maximum_select_fusion.9), channel_id=1, source_target_pairs={{0,4},{4,0},{8,12},{12,8},{16,20},{20,16},{24,28},{28,24},{32,36},... | collective-permute-start | bytes 294920 | tf_op jit(solution)/shard_map/ppermute | solution.py:52
  112.2 2.1 %collective-permute-done.11 = f32[2,48,256]{2,1,0:T(8,128)S(1)} collective-permute-done((f32[2,48,256]{2,1,0:T(8,128)S(1)}, f32[2,48,256]{2,1,0:T(8,128)S(1)}, u32[]{:S(2)}, u32[]{:S(2)}) %collective-permute-start.11) | collective-permute-done | bytes 98336 | tf_op jit(solution)/shard_map/ppermute | solution.py:52
  114.2 0.5 collective-permute-start.12
  114.8 4.1 %collective-permute-done.12 = f32[2,48,512]{2,1,0:T(8,128)S(1)} collective-permute-done((f32[2,48,512]{2,1,0:T(8,128)S(1)}, f32[2,48,512]{2,1,0:T(8,128)S(1)}, u32[]{:S(2)}, u32[]{:S(2)}) %collective-permute-start.12) | collective-permute-done | bytes 196640 | tf_op jit(solution)/shard_map/ppermute | solution.py:52
  118.9 1.3 collective-permute-start.13
  120.2 5.7 %collective-permute-done.13 = f32[2,48,1024]{2,1,0:T(8,128)S(1)} collective-permute-done((f32[2,48,1024]{2,1,0:T(8,128)S(1)}, f32[2,48,1024]{2,1,0:T(8,128)S(1)}, u32[]{:S(2)}, u32[]{:S(2)}) %collective-permute-start.13) | collective-permute-done | bytes 393248 | tf_op jit(solution)/shard_map/ppermute | solution.py:52
  126.0 11.2 %fusion.12 = f32[8,48,512]{2,1,0:T(8,128)S(1)} fusion(bf16[8,512,2048]{2,1,0:T(8,128)(2,1)} %param.10, f32[48,2048]{1,0:T(8,128)S(1)} %get-tuple-element.81, f32[48,2048]{1,0:T(8,128)S(1)} %get-tuple-element.80, pred[8]{0:T(512)(128)(4,1)S(1)} %broadcast_compare_fusion), kind=kOutput, calls=%fused_computation.18 | convolution fusion | flops 806092800 | bytes 18350088 | tf_op jit(solution)/shard_map/nrj,nij->nri/dot_general | solution.py:67
  137.3 9.9 %collective-permute-start.14 = (f32[4,48,512]{2,1,0:T(8,128)S(1)}, f32[4,48,512]{2,1,0:T(8,128)S(1)}, u32[]{:S(2)}, u32[]{:S(2)}) collective-permute-start(f32[4,48,512]{2,1,0:T(8,128)S(1)} %slice_select_fusion), channel_id=1, source_target_pairs={{0,1},{1,0},{2,3},{3,2},{4,5},{5,4},{6,7},{7,6},{8,9},{9,8},{10,11... | collective-permute-start | bytes 1179656 | tf_op jit(solution)/shard_map/ppermute | solution.py:44
  147.2 1.3 collective-permute-done.14
  148.7 1.4 collective-permute-start.15
  150.0 4.8 %collective-permute-done.15 = f32[2,48,512]{2,1,0:T(8,128)S(1)} collective-permute-done((f32[2,48,512]{2,1,0:T(8,128)S(1)}, f32[2,48,512]{2,1,0:T(8,128)S(1)}, u32[]{:S(2)}, u32[]{:S(2)}) %collective-permute-start.15) | collective-permute-done | bytes 196640 | tf_op jit(solution)/shard_map/ppermute | solution.py:44
  154.8 0.3 fusion.37
  155.2 0.4 select_reduce_fusion
  155.6 6.2 %while.23 = (s32[]{:T(128)}, f32[2,48,48]{1,2,0:T(8,128)S(1)}, f32[2,48,48]{2,1,0:T(8,128)S(1)}, s32[]{:T(128)}) while((s32[]{:T(128)}, f32[2,48,48]{1,2,0:T(8,128)S(1)}, f32[2,48,48]{2,1,0:T(8,128)S(1)}, s32[]{:T(128)}) %tuple.52), condition=%wide.region_9.10_spmd.clone, body=%wide.region_8.9_spmd.clone.sunk | while | flops 7976450 | bytes 221237 | solution.py:21
  162.1 1.4 collective-permute-start.16
  163.5 2.2 %collective-permute-done.16 = bf16[2,48,512]{2,1,0:T(8,128)(2,1)S(1)} collective-permute-done((bf16[2,48,512]{2,1,0:T(8,128)(2,1)S(1)}, bf16[2,48,512]{2,1,0:T(8,128)(2,1)S(1)}, u32[]{:S(2)}, u32[]{:S(2)}) %collective-permute-start.16) | collective-permute-done | bytes 98336 | tf_op jit(solution)/shard_map/ppermute | solution.py:52
  165.7 2.7 %collective-permute-start.17 = (bf16[4,48,512]{2,1,0:T(8,128)(2,1)S(1)}, bf16[4,48,512]{2,1,0:T(8,128)(2,1)S(1)}, u32[]{:S(2)}, u32[]{:S(2)}) collective-permute-start(bf16[4,48,512]{2,1,0:T(8,128)(2,1)S(1)} %maximum_select_fusion.8), channel_id=1, source_target_pairs={{0,1},{1,0},{2,3},{3,2},{4,5},{5,4},{6,7},{7,6},{8,9},{9,8},{10,11... | collective-permute-start | bytes 589832 | tf_op jit(solution)/shard_map/ppermute | solution.py:52
  168.4 2.8 %fusion.8 = f32[8,48,2048]{2,1,0:T(8,128)S(1)} fusion(f32[48,2048]{1,0:T(8,128)S(1)} %get-tuple-element.81, f32[48,2048]{1,0:T(8,128)S(1)} %get-tuple-element.80, pred[8]{0:T(512)(128)(4,1)S(1)} %broadcast_compare_fusion, f32[8,48]{1,0:T(8,128)S(1)} %fusion.66, f32[48,48]{1,0:T(8,128)S(1)} %get-tuple-element.87, f32[48,48]{1,0:T(8,128)S(1)} %get-tuple-element.86), kind=kOutput, calls=%fused_computation.12 | convolution fusion | flops 453808128 | bytes 3952136 | tf_op jit(solution)/shard_map/nrs,nsj->nrj/dot_general | solution.py:127
  171.2 10.5 %convolution_subtract_fusion.2 = f32[8,48,2048]{2,1,0:T(8,128)} fusion(f32[8,48,2048]{2,1,0:T(8,128)S(1)} %fusion.8, bf16[8,512,2048]{2,1,0:T(8,128)(2,1)} %param.10, bf16[4,48,512]{2,1,0:T(8,128)(2,1)S(1)} %maximum_select_fusion.8, bf16[4,48,512]{2,1,0:T(8,128)(2,1)S(1)} %collective-permute-done.17, pred[]{:T(512)S(6)} %ne.19), kind=kOutput, calls=%fused_computation.17 | convolution fusion | flops 806682624 | bytes 23461888 | tf_op jit(solution)/shard_map/nsi,nij->nsj/dot_general | solution.py:80
  (163 shorter events, 16.6 us)
Async XLA Ops:
  2.6 12.5 %copy-start.3 = (s32[256]{0:T(256)S(1)}, s32[256]{0:T(256)}, u32[]{:S(2)}) copy-start(s32[256]{0:T(256)} %param.14) | copy-start | bytes 3076
  2.6 12.5 %copy-start.2 = (f32[256,48]{0,1:T(8,128)S(1)}, f32[256,48]{0,1:T(8,128)}, u32[]{:S(2)}) copy-start(f32[256,48]{0,1:T(8,128)} %param.12) | copy-start | bytes 147460
  2.6 13.2 %copy-start.1 = (f32[2,48,48]{2,1,0:T(8,128)S(1)}, f32[2,48,48]{2,1,0:T(8,128)}, u32[]{:S(2)}) copy-start(f32[2,48,48]{2,1,0:T(8,128)} %param.13) | copy-start | bytes 55300
  13.7 11.5 %collective-permute-start = (f32[4,48,512]{2,1,0:T(8,128)S(1)}, f32[4,48,512]{2,1,0:T(8,128)S(1)}, u32[]{:S(2)}, u32[]{:S(2)}) collective-permute-start(f32[4,48,512]{2,1,0:T(8,128)S(1)} %slice_select_fusion.1), channel_id=1, source_target_pairs={{0,1},{1,0},{2,3},{3,2},{4,5},{5,4},{6,7},{7,6},{8,9},{9,8},{10,11... | collective-permute-start | bytes 1179656 | tf_op jit(solution)/shard_map/ppermute | solution.py:44
  25.4 6.5 %collective-permute-start.1 = (f32[2,48,512]{2,1,0:T(8,128)S(1)}, f32[2,48,512]{2,1,0:T(8,128)S(1)}, u32[]{:S(2)}, u32[]{:S(2)}) collective-permute-start(f32[2,48,512]{2,1,0:T(8,128)S(1)} %slice_select_fusion.3), channel_id=1, source_target_pairs={{0,2},{1,3},{2,0},{3,1},{4,6},{5,7},{6,4},{7,5},{8,10},{9,11},{10,... | collective-permute-start | bytes 589832 | tf_op jit(solution)/shard_map/ppermute | solution.py:44
  39.2 3.5 %collective-permute-start.2 = (bf16[2,48,512]{2,1,0:T(8,128)(2,1)S(1)}, bf16[2,48,512]{2,1,0:T(8,128)(2,1)S(1)}, u32[]{:S(2)}, u32[]{:S(2)}) collective-permute-start(bf16[2,48,512]{2,1,0:T(8,128)(2,1)S(1)} %convolution_convert_fusion.1), channel_id=1, source_target_pairs={{0,2},{1,3},{2,0},{3,1},{4,6},{5,7},{6,4},{7,5},{8,10},{9,11},{10,... | collective-permute-start | bytes 294920 | tf_op jit(solution)/shard_map/ppermute | solution.py:52
  42.8 3.4 %collective-permute-start.3 = (bf16[4,48,512]{2,1,0:T(8,128)(2,1)S(1)}, bf16[4,48,512]{2,1,0:T(8,128)(2,1)S(1)}, u32[]{:S(2)}, u32[]{:S(2)}) collective-permute-start(bf16[4,48,512]{2,1,0:T(8,128)(2,1)S(1)} %maximum_select_fusion.6), channel_id=1, source_target_pairs={{0,1},{1,0},{2,3},{3,2},{4,5},{5,4},{6,7},{7,6},{8,9},{9,8},{10,11... | collective-permute-start | bytes 589832 | tf_op jit(solution)/shard_map/ppermute | solution.py:52
  61.5 10.4 %collective-permute-start.4 = (f32[2,48,1024]{2,0,1:T(2,128)S(1)}, f32[2,48,1024]{2,0,1:T(2,128)S(1)}, u32[]{:S(2)}, u32[]{:S(2)}) collective-permute-start(f32[2,48,1024]{2,0,1:T(2,128)S(1)} %broadcast_select_fusion), channel_id=1, source_target_pairs={{0,32},{4,36},{8,40},{12,44},{16,48},{20,52},{24,56},{28,60},{32,0... | collective-permute-start | bytes 1179656 | tf_op jit(solution)/shard_map/ppermute | solution.py:44
  72.3 5.9 %collective-permute-start.5 = (f32[2,48,512]{2,0,1:T(2,128)S(1)}, f32[2,48,512]{2,0,1:T(2,128)S(1)}, u32[]{:S(2)}, u32[]{:S(2)}) collective-permute-start(f32[2,48,512]{2,0,1:T(2,128)S(1)} %broadcast_select_fusion.1), channel_id=1, source_target_pairs={{0,8},{4,12},{8,0},{12,4},{16,24},{20,28},{24,16},{28,20},{32,40},... | collective-permute-start | bytes 589832 | tf_op jit(solution)/shard_map/ppermute | solution.py:44
  78.4 5.1 %collective-permute-start.6 = (f32[2,48,256]{2,0,1:T(2,128)S(1)}, f32[2,48,256]{2,0,1:T(2,128)S(1)}, u32[]{:S(2)}, u32[]{:S(2)}) collective-permute-start(f32[2,48,256]{2,0,1:T(2,128)S(1)} %broadcast_select_fusion.2), channel_id=1, source_target_pairs={{0,4},{4,0},{8,12},{12,8},{16,20},{20,16},{24,28},{28,24},{32,36},... | collective-permute-start | bytes 294920 | tf_op jit(solution)/shard_map/ppermute | solution.py:44
  83.5 4.5 %collective-permute-start.7 = (f32[2,48,128]{2,0,1:T(2,128)S(1)}, f32[2,48,128]{2,0,1:T(2,128)S(1)}, u32[]{:S(2)}, u32[]{:S(2)}) collective-permute-start(f32[2,48,128]{2,0,1:T(2,128)S(1)} %broadcast_select_fusion.3), channel_id=1, source_target_pairs={{0,64},{4,68},{8,72},{12,76},{16,80},{20,84},{24,88},{28,92},{32,9... | collective-permute-start | bytes 147464 | tf_op jit(solution)/shard_map/ppermute | solution.py:44
  88.2 10.7 %collective-permute-start.8 = (f32[2,48,64]{2,0,1:T(2,128)S(1)}, f32[2,48,64]{2,0,1:T(2,128)S(1)}, u32[]{:S(2)}, u32[]{:S(2)}) collective-permute-start(f32[2,48,64]{2,0,1:T(2,128)S(1)} %broadcast_select_fusion.4), channel_id=1, source_target_pairs={{0,16},{4,20},{8,24},{12,28},{16,0},{20,4},{24,8},{28,12},{32,48},... | collective-permute-start | bytes 73736 | tf_op jit(solution)/shard_map/ppermute | solution.py:44
  99.5 4.7 %collective-permute-start.9 = (f32[2,48,64]{2,1,0:T(8,128)S(1)}, f32[2,48,64]{2,1,0:T(8,128)S(1)}, u32[]{:S(2)}, u32[]{:S(2)}) collective-permute-start(f32[2,48,64]{2,1,0:T(8,128)S(1)} %fusion.52), channel_id=1, source_target_pairs={{0,16},{4,20},{8,24},{12,28},{16,0},{20,4},{24,8},{28,12},{32,48},... | collective-permute-start | bytes 73736 | tf_op jit(solution)/shard_map/ppermute | solution.py:52
  104.3 4.8 %collective-permute-start.10 = (f32[2,48,128]{2,1,0:T(8,128)S(1)}, f32[2,48,128]{2,1,0:T(8,128)S(1)}, u32[]{:S(2)}, u32[]{:S(2)}) collective-permute-start(f32[2,48,128]{2,1,0:T(8,128)S(1)} %maximum_select_fusion.10), channel_id=1, source_target_pairs={{0,64},{4,68},{8,72},{12,76},{16,80},{20,84},{24,88},{28,92},{32,9... | collective-permute-start | bytes 147464 | tf_op jit(solution)/shard_map/ppermute | solution.py:52
  109.2 5.1 %collective-permute-start.11 = (f32[2,48,256]{2,1,0:T(8,128)S(1)}, f32[2,48,256]{2,1,0:T(8,128)S(1)}, u32[]{:S(2)}, u32[]{:S(2)}) collective-permute-start(f32[2,48,256]{2,1,0:T(8,128)S(1)} %maximum_select_fusion.9), channel_id=1, source_target_pairs={{0,4},{4,0},{8,12},{12,8},{16,20},{20,16},{24,28},{28,24},{32,36},... | collective-permute-start | bytes 294920 | tf_op jit(solution)/shard_map/ppermute | solution.py:52
  114.2 4.6 %collective-permute-start.12 = (f32[2,48,512]{2,1,0:T(8,128)S(1)}, f32[2,48,512]{2,1,0:T(8,128)S(1)}, u32[]{:S(2)}, u32[]{:S(2)}) collective-permute-start(f32[2,48,512]{2,1,0:T(8,128)S(1)} %maximum_select_fusion.7), channel_id=1, source_target_pairs={{0,8},{4,12},{8,0},{12,4},{16,24},{20,28},{24,16},{28,20},{32,40},... | collective-permute-start | bytes 589832 | tf_op jit(solution)/shard_map/ppermute | solution.py:52
  118.9 7.0 %collective-permute-start.13 = (f32[2,48,1024]{2,1,0:T(8,128)S(1)}, f32[2,48,1024]{2,1,0:T(8,128)S(1)}, u32[]{:S(2)}, u32[]{:S(2)}) collective-permute-start(f32[2,48,1024]{2,1,0:T(8,128)S(1)} %maximum_select_fusion.3), channel_id=1, source_target_pairs={{0,32},{4,36},{8,40},{12,44},{16,48},{20,52},{24,56},{28,60},{32,0... | collective-permute-start | bytes 1179656 | tf_op jit(solution)/shard_map/ppermute | solution.py:52
  126.0 11.2 %copy-start = (f32[2,48,2048]{2,1,0:T(8,128)}, f32[2,48,2048]{2,1,0:T(8,128)S(1)}, u32[]{:S(2)}) copy-start(f32[2,48,2048]{2,1,0:T(8,128)S(1)} %maximum_select_fusion) | copy-start | bytes 2359300
  137.3 11.2 %collective-permute-start.14 = (f32[4,48,512]{2,1,0:T(8,128)S(1)}, f32[4,48,512]{2,1,0:T(8,128)S(1)}, u32[]{:S(2)}, u32[]{:S(2)}) collective-permute-start(f32[4,48,512]{2,1,0:T(8,128)S(1)} %slice_select_fusion), channel_id=1, source_target_pairs={{0,1},{1,0},{2,3},{3,2},{4,5},{5,4},{6,7},{7,6},{8,9},{9,8},{10,11... | collective-permute-start | bytes 1179656 | tf_op jit(solution)/shard_map/ppermute | solution.py:44
  148.7 6.2 %collective-permute-start.15 = (f32[2,48,512]{2,1,0:T(8,128)S(1)}, f32[2,48,512]{2,1,0:T(8,128)S(1)}, u32[]{:S(2)}, u32[]{:S(2)}) collective-permute-start(f32[2,48,512]{2,1,0:T(8,128)S(1)} %slice_select_fusion.2), channel_id=1, source_target_pairs={{0,2},{1,3},{2,0},{3,1},{4,6},{5,7},{6,4},{7,5},{8,10},{9,11},{10,... | collective-permute-start | bytes 589832 | tf_op jit(solution)/shard_map/ppermute | solution.py:44
  162.1 3.5 %collective-permute-start.16 = (bf16[2,48,512]{2,1,0:T(8,128)(2,1)S(1)}, bf16[2,48,512]{2,1,0:T(8,128)(2,1)S(1)}, u32[]{:S(2)}, u32[]{:S(2)}) collective-permute-start(bf16[2,48,512]{2,1,0:T(8,128)(2,1)S(1)} %convolution_convert_fusion), channel_id=1, source_target_pairs={{0,2},{1,3},{2,0},{3,1},{4,6},{5,7},{6,4},{7,5},{8,10},{9,11},{10,... | collective-permute-start | bytes 294920 | tf_op jit(solution)/shard_map/ppermute | solution.py:52
  165.7 5.5 %collective-permute-start.17 = (bf16[4,48,512]{2,1,0:T(8,128)(2,1)S(1)}, bf16[4,48,512]{2,1,0:T(8,128)(2,1)S(1)}, u32[]{:S(2)}, u32[]{:S(2)}) collective-permute-start(bf16[4,48,512]{2,1,0:T(8,128)(2,1)S(1)} %maximum_select_fusion.8), channel_id=1, source_target_pairs={{0,1},{1,0},{2,3},{3,2},{4,5},{5,4},{6,7},{7,6},{8,9},{9,8},{10,11... | collective-permute-start | bytes 589832 | tf_op jit(solution)/shard_map/ppermute | solution.py:52

commit v2 on v1

--- a/solution.py
+++ b/solution.py
@@ -80,8 +80,15 @@
     return jnp.einsum("nsi,nij->nsj", rotated, slices, preferred_element_type=jnp.float32)
 
 
-def solve_one(lower, target):
-    return jax.scipy.linalg.cho_solve((lower, True), target)
+def lower_inverse(system):
+    lower = jnp.linalg.cholesky(system)
+    eye_rank = jnp.broadcast_to(jnp.eye(system.shape[-1], dtype=system.dtype), system.shape)
+    return lax.linalg.triangular_solve(lower, eye_rank, left_side=True, lower=True)
+
+
+def apply_inverse(inverse, target):
+    inner = jnp.einsum("hrs,hsj->hrj", inverse, target, precision=lax.Precision.HIGHEST)
+    return jnp.einsum("hsr,hsj->hrj", inverse, inner, precision=lax.Precision.HIGHEST)
 
 
 def make_body(runs_size, chan_size):
@@ -115,9 +122,9 @@
         cross = jnp.einsum("kh,kr,ks->hrs", member, loadings, loadings, precision=lax.Precision.HIGHEST)
         inner_mix = jnp.einsum("hsr,hst->hrt", mixing, mixing, precision=lax.Precision.HIGHEST)
         system = inner_mix * cross
-        lower = jnp.linalg.cholesky(system)
+        inverse = lower_inverse(system)
         moments_part = halving_scatter(partial_moments, "runs", runs_size, runs_bits, 2)
-        spectra_part = jax.vmap(solve_one)(lower, moments_part)
+        spectra_part = apply_inverse(inverse, moments_part)
         new_spectra = doubling_gather(spectra_part, "runs", runs_size, runs_bits, 2)
         held_rows = jnp.where(first_half, new_spectra[1][None], new_spectra[0][None])
         held_mix = jnp.where(first_half, mixing[1][None], mixing[0][None]) * mate_loads[:, None, :]

time: 182 us -> 181 us (level)
  no operation moved by 1% of the time
where the time goes in v2:
time: 181 us
  matrix products  65.2 us (36%)
  waiting for transfers between devices  51.1 us (28%)
  starting transfers between devices  41.8 us (23%)
  other arithmetic  19.6 us (11%)
    ppermute x9, waiting for transfers between devices, halving_scatter(): x = keep + lax.ppermute(send, axis, xor_pairs(size, bit))  27.3 us
    ppermute x9, starting transfers between devices, halving_scatter(): x = keep + lax.ppermute(send, axis, xor_pairs(size, bit))  26.1 us
    ppermute x9, waiting for transfers between devices, doubling_gather(): got = lax.ppermute(x, axis, xor_pairs(size, bit))  23.8 us
    dot_general x2, matrix products, project(): jnp.einsum('nrj,nij->nri', rows_low, slices, preferred_element_type=jnp.f...  22.1 us
    dot_general x2, matrix products, project(): jnp.einsum('nsi,nij->nsj', rotated, slices, preferred_element_type=jnp.fl...  19.2 us
    ppermute x9, starting transfers between devices, doubling_gather(): got = lax.ppermute(x, axis, xor_pairs(size, bit))  15.6 us
    another operation x3, other arithmetic, lower_inverse(): lower = jnp.linalg.cholesky(system)  8.93 us
    another operation x3, other arithmetic, lower_inverse(): lax.linalg.triangular_solve(lower, eye_rank, left_side=True, lower=True)  7.46 us
  transfers between devices with their start and end apart: 18, of which 15 were waited for; matrix products, arithmetic and copies ran while one was open for 11% of the time, Pallas kernels for 0%

profile of v2, /device:TPU:1, one launch (start us, length us, event | category | flops | bytes accessed | tf_op | source)
XLA Modules:
  0.0 181.2 jit_solution(13029707256461114378)
XLA Ops:
  0.6 0.9 select_reduce_fusion.3
  1.6 1.1 slice_bitcast_fusion.3
  2.7 11.0 %fusion.17 = f32[8,48,512]{2,1,0:T(8,128)S(1)} fusion(bf16[8,512,2048]{2,1,0:T(8,128)(2,1)} %param.10, pred[8]{0:T(512)(128)(4,1)S(1)} %broadcast_compare_fusion, bf16[48,2048]{1,0:T(8,128)(2,1)S(1)} %get-tuple-element.83, bf16[48,2048]{1,0:T(8,128)(2,1)S(1)} %get-tuple-element.82), kind=kOutput, calls=%fused_computation.23 | convolution fusion | flops 806092800 | bytes 17956872 | tf_op jit(solution)/shard_map/nrj,nij->nri/dot_general | solution.py:67
  13.7 1.5 collective-permute-start
  16.3 8.8 %custom-call.7 = f32[2,48,48]{2,1,0:T(8,128)S(1)} custom-call(f32[2,48,48]{2,1,0:T(8,128)S(1)} %fusion.55), custom_call_target="Cholesky" | custom-call | tf_op jit(solution)/shard_map/jit(cholesky)/cholesky | solution.py:84
  25.4 1.5 collective-permute-start.1
  27.0 4.9 %collective-permute-done.1 = f32[2,48,512]{2,1,0:T(8,128)S(1)} collective-permute-done((f32[2,48,512]{2,1,0:T(8,128)S(1)}, f32[2,48,512]{2,1,0:T(8,128)S(1)}, u32[]{:S(2)}, u32[]{:S(2)}) %collective-permute-start.1) | collective-permute-done | bytes 196640 | tf_op jit(solution)/shard_map/ppermute | solution.py:44
  31.9 0.3 fusion.40
  32.2 0.4 select_reduce_fusion.1
  32.7 6.2 %while.22 = (s32[]{:T(128)}, f32[2,48,48]{1,2,0:T(8,128)S(1)}, f32[2,48,48]{2,1,0:T(8,128)S(1)}, s32[]{:T(128)}) while((s32[]{:T(128)}, f32[2,48,48]{1,2,0:T(8,128)S(1)}, f32[2,48,48]{2,1,0:T(8,128)S(1)}, s32[]{:T(128)}) %tuple.49), condition=%wide.region_5.6_spmd.clone, body=%wide.region_4.5_spmd.clone.sunk | while | flops 7976450 | bytes 221237 | solution.py:21
  39.2 1.5 collective-permute-start.2
  40.7 2.1 %collective-permute-done.2 = bf16[2,48,512]{2,1,0:T(8,128)(2,1)S(1)} collective-permute-done((bf16[2,48,512]{2,1,0:T(8,128)(2,1)S(1)}, bf16[2,48,512]{2,1,0:T(8,128)(2,1)S(1)}, u32[]{:S(2)}, u32[]{:S(2)}) %collective-permute-start.2) | collective-permute-done | bytes 98336 | tf_op jit(solution)/shard_map/ppermute | solution.py:52
  42.8 2.3 %collective-permute-start.3 = (bf16[4,48,512]{2,1,0:T(8,128)(2,1)S(1)}, bf16[4,48,512]{2,1,0:T(8,128)(2,1)S(1)}, u32[]{:S(2)}, u32[]{:S(2)}) collective-permute-start(bf16[4,48,512]{2,1,0:T(8,128)(2,1)S(1)} %maximum_select_fusion.6), channel_id=1, source_target_pairs={{0,1},{1,0},{2,3},{3,2},{4,5},{5,4},{6,7},{7,6},{8,9},{9,8},{10,11... | collective-permute-start | bytes 589832 | tf_op jit(solution)/shard_map/ppermute | solution.py:52
  45.0 1.1 collective-permute-done.3
  46.1 8.8 %fusion.24 = f32[8,48,2048]{2,1,0:T(8,128)S(1)} fusion(bf16[8,512,2048]{2,1,0:T(8,128)(2,1)} %param.10, bf16[4,48,512]{2,1,0:T(8,128)(2,1)S(1)} %maximum_select_fusion.6, bf16[4,48,512]{2,1,0:T(8,128)(2,1)S(1)} %collective-permute-done.3, pred[]{:T(512)S(6)} %ne.19), kind=kOutput, calls=%fused_computation.36 | convolution fusion | flops 805896192 | bytes 20316160 | tf_op jit(solution)/shard_map/nsi,nij->nsj/dot_general | solution.py:80
  54.9 3.1 %fusion.64 = f32[8,48,2048]{2,1,0:T(8,128)S(1)} fusion(f32[8,48,2048]{2,1,0:T(8,128)S(1)} %fusion.24, f32[8,48]{1,0:T(8,128)S(1)} %fusion.65, f32[48,48]{1,0:T(8,128)S(1)} %get-tuple-element.87, f32[48,48]{1,0:T(8,128)S(1)} %get-tuple-element.86, pred[8]{0:T(512)(128)(4,1)S(1)} %broadcast_compare_fusion), kind=kOutput, calls=%fused_computation.115 | convolution fusion | flops 453021696 | bytes 6311432 | tf_op jit(solution)/shard_map/nsr,nsj->nrj/dot_general | solution.py:114
  58.0 3.3 %fusion.10 = f32[2,48,2048]{2,0,1:T(2,128)S(1)} fusion(f32[8,48,2048]{2,1,0:T(8,128)S(1)} %fusion.64, s32[8]{0:T(128)S(1)} %get-tuple-element.67), kind=kOutput, calls=%fused_computation.15 | convolution fusion | flops 18874384 | bytes 3932192 | tf_op jit(solution)/shard_map/nh,nrj->hrj/dot_general | solution.py:118
  61.5 1.4 collective-permute-start.4
  62.9 9.0 %collective-permute-done.4 = f32[2,48,1024]{2,0,1:T(2,128)S(1)} collective-permute-done((f32[2,48,1024]{2,0,1:T(2,128)S(1)}, f32[2,48,1024]{2,0,1:T(2,128)S(1)}, u32[]{:S(2)}, u32[]{:S(2)}) %collective-permute-start.4) | collective-permute-done | bytes 393248 | tf_op jit(solution)/shard_map/ppermute | solution.py:44
  72.3 1.8 %collective-permute-start.5 = (f32[2,48,512]{2,0,1:T(2,128)S(1)}, f32[2,48,512]{2,0,1:T(2,128)S(1)}, u32[]{:S(2)}, u32[]{:S(2)}) collective-permute-start(f32[2,48,512]{2,0,1:T(2,128)S(1)} %broadcast_select_fusion.1), channel_id=1, source_target_pairs={{0,8},{4,12},{8,0},{12,4},{16,24},{20,28},{24,16},{28,20},{32,40},... | collective-permute-start | bytes 589832 | tf_op jit(solution)/shard_map/ppermute | solution.py:44
  74.1 4.0 %collective-permute-done.5 = f32[2,48,512]{2,0,1:T(2,128)S(1)} collective-permute-done((f32[2,48,512]{2,0,1:T(2,128)S(1)}, f32[2,48,512]{2,0,1:T(2,128)S(1)}, u32[]{:S(2)}, u32[]{:S(2)}) %collective-permute-start.5) | collective-permute-done | bytes 196640 | tf_op jit(solution)/shard_map/ppermute | solution.py:44
  78.4 2.9 %collective-permute-start.6 = (f32[2,48,256]{2,0,1:T(2,128)S(1)}, f32[2,48,256]{2,0,1:T(2,128)S(1)}, u32[]{:S(2)}, u32[]{:S(2)}) collective-permute-start(f32[2,48,256]{2,0,1:T(2,128)S(1)} %broadcast_select_fusion.2), channel_id=1, source_target_pairs={{0,4},{4,0},{8,12},{12,8},{16,20},{20,16},{24,28},{28,24},{32,36},... | collective-permute-start | bytes 294920 | tf_op jit(solution)/shard_map/ppermute | solution.py:44
  81.4 2.0 %collective-permute-done.6 = f32[2,48,256]{2,0,1:T(2,128)S(1)} collective-permute-done((f32[2,48,256]{2,0,1:T(2,128)S(1)}, f32[2,48,256]{2,0,1:T(2,128)S(1)}, u32[]{:S(2)}, u32[]{:S(2)}) %collective-permute-start.6) | collective-permute-done | bytes 98336 | tf_op jit(solution)/shard_map/ppermute | solution.py:44
  83.5 2.7 %collective-permute-start.7 = (f32[2,48,128]{2,0,1:T(2,128)S(1)}, f32[2,48,128]{2,0,1:T(2,128)S(1)}, u32[]{:S(2)}, u32[]{:S(2)}) collective-permute-start(f32[2,48,128]{2,0,1:T(2,128)S(1)} %broadcast_select_fusion.3), channel_id=1, source_target_pairs={{0,64},{4,68},{8,72},{12,76},{16,80},{20,84},{24,88},{28,92},{32,9... | collective-permute-start | bytes 147464 | tf_op jit(solution)/shard_map/ppermute | solution.py:44
  86.3 7.4 %custom-call.8 = f32[2,1,48,48]{2,3,1,0:T(8,128)S(1)} custom-call(f32[2,1,48,48]{3,2,1,0:T(8,128)S(1)} %select_bitcast_fusion), custom_call_target="InvertDiagBlocksLowerTriangular" | custom-call | tf_op jit(solution)/shard_map/triangular_solve | solution.py:86
  93.9 3.3 %collective-permute-start.8 = (f32[2,48,64]{2,0,1:T(2,128)S(1)}, f32[2,48,64]{2,0,1:T(2,128)S(1)}, u32[]{:S(2)}, u32[]{:S(2)}) collective-permute-start(f32[2,48,64]{2,0,1:T(2,128)S(1)} %broadcast_select_fusion.4), channel_id=1, source_target_pairs={{0,16},{4,20},{8,24},{12,28},{16,0},{20,4},{24,8},{28,12},{32,48},... | collective-permute-start | bytes 73736 | tf_op jit(solution)/shard_map/ppermute | solution.py:44
  97.5 1.2 collective-permute-done.8
  99.3 3.3 %collective-permute-start.9 = (f32[2,48,64]{2,1,0:T(8,128)S(1)}, f32[2,48,64]{2,1,0:T(8,128)S(1)}, u32[]{:S(2)}, u32[]{:S(2)}) collective-permute-start(f32[2,48,64]{2,1,0:T(8,128)S(1)} %fusion.81), channel_id=1, source_target_pairs={{0,16},{4,20},{8,24},{12,28},{16,0},{20,4},{24,8},{28,12},{32,48},... | collective-permute-start | bytes 73736 | tf_op jit(solution)/shard_map/ppermute | solution.py:52
  102.5 1.5 collective-permute-done.9
  104.4 4.5 %collective-permute-done.10 = f32[2,48,128]{2,1,0:T(8,128)S(1)} collective-permute-done((f32[2,48,128]{2,1,0:T(8,128)S(1)}, f32[2,48,128]{2,1,0:T(8,128)S(1)}, u32[]{:S(2)}, u32[]{:S(2)}) %collective-permute-start.10) | collective-permute-done | bytes 49184 | tf_op jit(solution)/shard_map/ppermute | solution.py:52
  108.9 3.0 %collective-permute-start.11 = (f32[2,48,256]{2,1,0:T(8,128)S(1)}, f32[2,48,256]{2,1,0:T(8,128)S(1)}, u32[]{:S(2)}, u32[]{:S(2)}) collective-permute-start(f32[2,48,256]{2,1,0:T(8,128)S(1)} %maximum_select_fusion.9), channel_id=1, source_target_pairs={{0,4},{4,0},{8,12},{12,8},{16,20},{20,16},{24,28},{28,24},{32,36},... | collective-permute-start | bytes 294920 | tf_op jit(solution)/shard_map/ppermute | solution.py:52
  111.9 2.1 %collective-permute-done.11 = f32[2,48,256]{2,1,0:T(8,128)S(1)} collective-permute-done((f32[2,48,256]{2,1,0:T(8,128)S(1)}, f32[2,48,256]{2,1,0:T(8,128)S(1)}, u32[]{:S(2)}, u32[]{:S(2)}) %collective-permute-start.11) | collective-permute-done | bytes 98336 | tf_op jit(solution)/shard_map/ppermute | solution.py:52
  114.0 0.8 collective-permute-start.12
  114.8 3.8 %collective-permute-done.12 = f32[2,48,512]{2,1,0:T(8,128)S(1)} collective-permute-done((f32[2,48,512]{2,1,0:T(8,128)S(1)}, f32[2,48,512]{2,1,0:T(8,128)S(1)}, u32[]{:S(2)}, u32[]{:S(2)}) %collective-permute-start.12) | collective-permute-done | bytes 196640 | tf_op jit(solution)/shard_map/ppermute | solution.py:52
  118.6 0.4 collective-permute-start.13
  119.0 6.6 %collective-permute-done.13 = f32[2,48,1024]{2,1,0:T(8,128)S(1)} collective-permute-done((f32[2,48,1024]{2,1,0:T(8,128)S(1)}, f32[2,48,1024]{2,1,0:T(8,128)S(1)}, u32[]{:S(2)}, u32[]{:S(2)}) %collective-permute-start.13) | collective-permute-done | bytes 393248 | tf_op jit(solution)/shard_map/ppermute | solution.py:52
  125.8 11.2 %fusion.12 = f32[8,48,512]{2,1,0:T(8,128)S(1)} fusion(bf16[8,512,2048]{2,1,0:T(8,128)(2,1)} %param.10, f32[48,2048]{1,0:T(8,128)S(1)} %get-tuple-element.81, f32[48,2048]{1,0:T(8,128)S(1)} %get-tuple-element.80, pred[8]{0:T(512)(128)(4,1)S(1)} %broadcast_compare_fusion), kind=kOutput, calls=%fused_computation.18 | convolution fusion | flops 806092800 | bytes 18350088 | tf_op jit(solution)/shard_map/nrj,nij->nri/dot_general | solution.py:67
  137.0 9.6 %collective-permute-start.14 = (f32[4,48,512]{2,1,0:T(8,128)S(1)}, f32[4,48,512]{2,1,0:T(8,128)S(1)}, u32[]{:S(2)}, u32[]{:S(2)}) collective-permute-start(f32[4,48,512]{2,1,0:T(8,128)S(1)} %slice_select_fusion), channel_id=1, source_target_pairs={{0,1},{1,0},{2,3},{3,2},{4,5},{5,4},{6,7},{7,6},{8,9},{9,8},{10,11... | collective-permute-start | bytes 1179656 | tf_op jit(solution)/shard_map/ppermute | solution.py:44
  146.6 1.3 collective-permute-done.14
  148.1 1.4 collective-permute-start.15
  149.5 4.8 %collective-permute-done.15 = f32[2,48,512]{2,1,0:T(8,128)S(1)} collective-permute-done((f32[2,48,512]{2,1,0:T(8,128)S(1)}, f32[2,48,512]{2,1,0:T(8,128)S(1)}, u32[]{:S(2)}, u32[]{:S(2)}) %collective-permute-start.15) | collective-permute-done | bytes 196640 | tf_op jit(solution)/shard_map/ppermute | solution.py:44
  154.6 0.4 select_reduce_fusion
  155.1 6.2 %while.23 = (s32[]{:T(128)}, f32[2,48,48]{1,2,0:T(8,128)S(1)}, f32[2,48,48]{2,1,0:T(8,128)S(1)}, s32[]{:T(128)}) while((s32[]{:T(128)}, f32[2,48,48]{1,2,0:T(8,128)S(1)}, f32[2,48,48]{2,1,0:T(8,128)S(1)}, s32[]{:T(128)}) %tuple.52), condition=%wide.region_9.10_spmd.clone, body=%wide.region_8.9_spmd.clone.sunk | while | flops 7976450 | bytes 221237 | solution.py:21
  161.6 1.4 collective-permute-start.16
  163.0 2.2 %collective-permute-done.16 = bf16[2,48,512]{2,1,0:T(8,128)(2,1)S(1)} collective-permute-done((bf16[2,48,512]{2,1,0:T(8,128)(2,1)S(1)}, bf16[2,48,512]{2,1,0:T(8,128)(2,1)S(1)}, u32[]{:S(2)}, u32[]{:S(2)}) %collective-permute-start.16) | collective-permute-done | bytes 98336 | tf_op jit(solution)/shard_map/ppermute | solution.py:52
  165.2 2.7 %collective-permute-start.17 = (bf16[4,48,512]{2,1,0:T(8,128)(2,1)S(1)}, bf16[4,48,512]{2,1,0:T(8,128)(2,1)S(1)}, u32[]{:S(2)}, u32[]{:S(2)}) collective-permute-start(bf16[4,48,512]{2,1,0:T(8,128)(2,1)S(1)} %maximum_select_fusion.8), channel_id=1, source_target_pairs={{0,1},{1,0},{2,3},{3,2},{4,5},{5,4},{6,7},{7,6},{8,9},{9,8},{10,11... | collective-permute-start | bytes 589832 | tf_op jit(solution)/shard_map/ppermute | solution.py:52
  167.9 2.8 %fusion.8 = f32[8,48,2048]{2,1,0:T(8,128)S(1)} fusion(f32[48,2048]{1,0:T(8,128)S(1)} %get-tuple-element.81, f32[48,2048]{1,0:T(8,128)S(1)} %get-tuple-element.80, pred[8]{0:T(512)(128)(4,1)S(1)} %broadcast_compare_fusion, f32[8,48]{1,0:T(8,128)S(1)} %fusion.66, f32[48,48]{1,0:T(8,128)S(1)} %get-tuple-element.87, f32[48,48]{1,0:T(8,128)S(1)} %get-tuple-element.86), kind=kOutput, calls=%fused_computation.12 | convolution fusion | flops 453808128 | bytes 3952136 | tf_op jit(solution)/shard_map/nrs,nsj->nrj/dot_general | solution.py:134
  170.7 10.5 %convolution_subtract_fusion.2 = f32[8,48,2048]{2,1,0:T(8,128)} fusion(f32[8,48,2048]{2,1,0:T(8,128)S(1)} %fusion.8, bf16[8,512,2048]{2,1,0:T(8,128)(2,1)} %param.10, bf16[4,48,512]{2,1,0:T(8,128)(2,1)S(1)} %maximum_select_fusion.8, bf16[4,48,512]{2,1,0:T(8,128)(2,1)S(1)} %collective-permute-done.17, pred[]{:T(512)S(6)} %ne.19), kind=kOutput, calls=%fused_computation.17 | convolution fusion | flops 806682624 | bytes 23461888 | tf_op jit(solution)/shard_map/nsi,nij->nsj/dot_general | solution.py:80
  (164 shorter events, 16.8 us)
Async XLA Ops:
  2.6 12.5 %copy-start.3 = (s32[256]{0:T(256)S(1)}, s32[256]{0:T(256)}, u32[]{:S(2)}) copy-start(s32[256]{0:T(256)} %param.14) | copy-start | bytes 3076
  2.6 12.5 %copy-start.2 = (f32[256,48]{0,1:T(8,128)S(1)}, f32[256,48]{0,1:T(8,128)}, u32[]{:S(2)}) copy-start(f32[256,48]{0,1:T(8,128)} %param.12) | copy-start | bytes 147460
  2.6 13.2 %copy-start.1 = (f32[2,48,48]{2,1,0:T(8,128)S(1)}, f32[2,48,48]{2,1,0:T(8,128)}, u32[]{:S(2)}) copy-start(f32[2,48,48]{2,1,0:T(8,128)} %param.13) | copy-start | bytes 55300
  13.7 11.5 %collective-permute-start = (f32[4,48,512]{2,1,0:T(8,128)S(1)}, f32[4,48,512]{2,1,0:T(8,128)S(1)}, u32[]{:S(2)}, u32[]{:S(2)}) collective-permute-start(f32[4,48,512]{2,1,0:T(8,128)S(1)} %slice_select_fusion.1), channel_id=1, source_target_pairs={{0,1},{1,0},{2,3},{3,2},{4,5},{5,4},{6,7},{7,6},{8,9},{9,8},{10,11... | collective-permute-start | bytes 1179656 | tf_op jit(solution)/shard_map/ppermute | solution.py:44
  25.4 6.5 %collective-permute-start.1 = (f32[2,48,512]{2,1,0:T(8,128)S(1)}, f32[2,48,512]{2,1,0:T(8,128)S(1)}, u32[]{:S(2)}, u32[]{:S(2)}) collective-permute-start(f32[2,48,512]{2,1,0:T(8,128)S(1)} %slice_select_fusion.3), channel_id=1, source_target_pairs={{0,2},{1,3},{2,0},{3,1},{4,6},{5,7},{6,4},{7,5},{8,10},{9,11},{10,... | collective-permute-start | bytes 589832 | tf_op jit(solution)/shard_map/ppermute | solution.py:44
  39.2 3.5 %collective-permute-start.2 = (bf16[2,48,512]{2,1,0:T(8,128)(2,1)S(1)}, bf16[2,48,512]{2,1,0:T(8,128)(2,1)S(1)}, u32[]{:S(2)}, u32[]{:S(2)}) collective-permute-start(bf16[2,48,512]{2,1,0:T(8,128)(2,1)S(1)} %convolution_convert_fusion.1), channel_id=1, source_target_pairs={{0,2},{1,3},{2,0},{3,1},{4,6},{5,7},{6,4},{7,5},{8,10},{9,11},{10,... | collective-permute-start | bytes 294920 | tf_op jit(solution)/shard_map/ppermute | solution.py:52
  42.8 3.4 %collective-permute-start.3 = (bf16[4,48,512]{2,1,0:T(8,128)(2,1)S(1)}, bf16[4,48,512]{2,1,0:T(8,128)(2,1)S(1)}, u32[]{:S(2)}, u32[]{:S(2)}) collective-permute-start(bf16[4,48,512]{2,1,0:T(8,128)(2,1)S(1)} %maximum_select_fusion.6), channel_id=1, source_target_pairs={{0,1},{1,0},{2,3},{3,2},{4,5},{5,4},{6,7},{7,6},{8,9},{9,8},{10,11... | collective-permute-start | bytes 589832 | tf_op jit(solution)/shard_map/ppermute | solution.py:52
  61.5 10.4 %collective-permute-start.4 = (f32[2,48,1024]{2,0,1:T(2,128)S(1)}, f32[2,48,1024]{2,0,1:T(2,128)S(1)}, u32[]{:S(2)}, u32[]{:S(2)}) collective-permute-start(f32[2,48,1024]{2,0,1:T(2,128)S(1)} %broadcast_select_fusion), channel_id=1, source_target_pairs={{0,32},{4,36},{8,40},{12,44},{16,48},{20,52},{24,56},{28,60},{32,0... | collective-permute-start | bytes 1179656 | tf_op jit(solution)/shard_map/ppermute | solution.py:44
  72.3 5.9 %collective-permute-start.5 = (f32[2,48,512]{2,0,1:T(2,128)S(1)}, f32[2,48,512]{2,0,1:T(2,128)S(1)}, u32[]{:S(2)}, u32[]{:S(2)}) collective-permute-start(f32[2,48,512]{2,0,1:T(2,128)S(1)} %broadcast_select_fusion.1), channel_id=1, source_target_pairs={{0,8},{4,12},{8,0},{12,4},{16,24},{20,28},{24,16},{28,20},{32,40},... | collective-permute-start | bytes 589832 | tf_op jit(solution)/shard_map/ppermute | solution.py:44
  78.4 5.1 %collective-permute-start.6 = (f32[2,48,256]{2,0,1:T(2,128)S(1)}, f32[2,48,256]{2,0,1:T(2,128)S(1)}, u32[]{:S(2)}, u32[]{:S(2)}) collective-permute-start(f32[2,48,256]{2,0,1:T(2,128)S(1)} %broadcast_select_fusion.2), channel_id=1, source_target_pairs={{0,4},{4,0},{8,12},{12,8},{16,20},{20,16},{24,28},{28,24},{32,36},... | collective-permute-start | bytes 294920 | tf_op jit(solution)/shard_map/ppermute | solution.py:44
  83.5 10.2 %collective-permute-start.7 = (f32[2,48,128]{2,0,1:T(2,128)S(1)}, f32[2,48,128]{2,0,1:T(2,128)S(1)}, u32[]{:S(2)}, u32[]{:S(2)}) collective-permute-start(f32[2,48,128]{2,0,1:T(2,128)S(1)} %broadcast_select_fusion.3), channel_id=1, source_target_pairs={{0,64},{4,68},{8,72},{12,76},{16,80},{20,84},{24,88},{28,92},{32,9... | collective-permute-start | bytes 147464 | tf_op jit(solution)/shard_map/ppermute | solution.py:44
  93.9 4.8 %collective-permute-start.8 = (f32[2,48,64]{2,0,1:T(2,128)S(1)}, f32[2,48,64]{2,0,1:T(2,128)S(1)}, u32[]{:S(2)}, u32[]{:S(2)}) collective-permute-start(f32[2,48,64]{2,0,1:T(2,128)S(1)} %broadcast_select_fusion.4), channel_id=1, source_target_pairs={{0,16},{4,20},{8,24},{12,28},{16,0},{20,4},{24,8},{28,12},{32,48},... | collective-permute-start | bytes 73736 | tf_op jit(solution)/shard_map/ppermute | solution.py:44
  99.3 4.7 %collective-permute-start.9 = (f32[2,48,64]{2,1,0:T(8,128)S(1)}, f32[2,48,64]{2,1,0:T(8,128)S(1)}, u32[]{:S(2)}, u32[]{:S(2)}) collective-permute-start(f32[2,48,64]{2,1,0:T(8,128)S(1)} %fusion.81), channel_id=1, source_target_pairs={{0,16},{4,20},{8,24},{12,28},{16,0},{20,4},{24,8},{28,12},{32,48},... | collective-permute-start | bytes 73736 | tf_op jit(solution)/shard_map/ppermute | solution.py:52
  104.1 4.8 %collective-permute-start.10 = (f32[2,48,128]{2,1,0:T(8,128)S(1)}, f32[2,48,128]{2,1,0:T(8,128)S(1)}, u32[]{:S(2)}, u32[]{:S(2)}) collective-permute-start(f32[2,48,128]{2,1,0:T(8,128)S(1)} %maximum_select_fusion.10), channel_id=1, source_target_pairs={{0,64},{4,68},{8,72},{12,76},{16,80},{20,84},{24,88},{28,92},{32,9... | collective-permute-start | bytes 147464 | tf_op jit(solution)/shard_map/ppermute | solution.py:52
  108.9 5.1 %collective-permute-start.11 = (f32[2,48,256]{2,1,0:T(8,128)S(1)}, f32[2,48,256]{2,1,0:T(8,128)S(1)}, u32[]{:S(2)}, u32[]{:S(2)}) collective-permute-start(f32[2,48,256]{2,1,0:T(8,128)S(1)} %maximum_select_fusion.9), channel_id=1, source_target_pairs={{0,4},{4,0},{8,12},{12,8},{16,20},{20,16},{24,28},{28,24},{32,36},... | collective-permute-start | bytes 294920 | tf_op jit(solution)/shard_map/ppermute | solution.py:52
  114.0 4.6 %collective-permute-start.12 = (f32[2,48,512]{2,1,0:T(8,128)S(1)}, f32[2,48,512]{2,1,0:T(8,128)S(1)}, u32[]{:S(2)}, u32[]{:S(2)}) collective-permute-start(f32[2,48,512]{2,1,0:T(8,128)S(1)} %maximum_select_fusion.7), channel_id=1, source_target_pairs={{0,8},{4,12},{8,0},{12,4},{16,24},{20,28},{24,16},{28,20},{32,40},... | collective-permute-start | bytes 589832 | tf_op jit(solution)/shard_map/ppermute | solution.py:52
  118.6 7.0 %collective-permute-start.13 = (f32[2,48,1024]{2,1,0:T(8,128)S(1)}, f32[2,48,1024]{2,1,0:T(8,128)S(1)}, u32[]{:S(2)}, u32[]{:S(2)}) collective-permute-start(f32[2,48,1024]{2,1,0:T(8,128)S(1)} %maximum_select_fusion.3), channel_id=1, source_target_pairs={{0,32},{4,36},{8,40},{12,44},{16,48},{20,52},{24,56},{28,60},{32,0... | collective-permute-start | bytes 1179656 | tf_op jit(solution)/shard_map/ppermute | solution.py:52
  125.7 11.2 %copy-start = (f32[2,48,2048]{2,1,0:T(8,128)}, f32[2,48,2048]{2,1,0:T(8,128)S(1)}, u32[]{:S(2)}) copy-start(f32[2,48,2048]{2,1,0:T(8,128)S(1)} %maximum_select_fusion) | copy-start | bytes 2359300
  137.0 11.0 %collective-permute-start.14 = (f32[4,48,512]{2,1,0:T(8,128)S(1)}, f32[4,48,512]{2,1,0:T(8,128)S(1)}, u32[]{:S(2)}, u32[]{:S(2)}) collective-permute-start(f32[4,48,512]{2,1,0:T(8,128)S(1)} %slice_select_fusion), channel_id=1, source_target_pairs={{0,1},{1,0},{2,3},{3,2},{4,5},{5,4},{6,7},{7,6},{8,9},{9,8},{10,11... | collective-permute-start | bytes 1179656 | tf_op jit(solution)/shard_map/ppermute | solution.py:44
  148.1 6.2 %collective-permute-start.15 = (f32[2,48,512]{2,1,0:T(8,128)S(1)}, f32[2,48,512]{2,1,0:T(8,128)S(1)}, u32[]{:S(2)}, u32[]{:S(2)}) collective-permute-start(f32[2,48,512]{2,1,0:T(8,128)S(1)} %slice_select_fusion.2), channel_id=1, source_target_pairs={{0,2},{1,3},{2,0},{3,1},{4,6},{5,7},{6,4},{7,5},{8,10},{9,11},{10,... | collective-permute-start | bytes 589832 | tf_op jit(solution)/shard_map/ppermute | solution.py:44
  161.6 3.5 %collective-permute-start.16 = (bf16[2,48,512]{2,1,0:T(8,128)(2,1)S(1)}, bf16[2,48,512]{2,1,0:T(8,128)(2,1)S(1)}, u32[]{:S(2)}, u32[]{:S(2)}) collective-permute-start(bf16[2,48,512]{2,1,0:T(8,128)(2,1)S(1)} %convolution_convert_fusion), channel_id=1, source_target_pairs={{0,2},{1,3},{2,0},{3,1},{4,6},{5,7},{6,4},{7,5},{8,10},{9,11},{10,... | collective-permute-start | bytes 294920 | tf_op jit(solution)/shard_map/ppermute | solution.py:52
  165.2 5.5 %collective-permute-start.17 = (bf16[4,48,512]{2,1,0:T(8,128)(2,1)S(1)}, bf16[4,48,512]{2,1,0:T(8,128)(2,1)S(1)}, u32[]{:S(2)}, u32[]{:S(2)}) collective-permute-start(bf16[4,48,512]{2,1,0:T(8,128)(2,1)S(1)} %maximum_select_fusion.8), channel_id=1, source_target_pairs={{0,1},{1,0},{2,3},{3,2},{4,5},{5,4},{6,7},{7,6},{8,9},{9,8},{10,11... | collective-permute-start | bytes 589832 | tf_op jit(solution)/shard_map/ppermute | solution.py:52

commit v3 on v2

--- a/solution.py
+++ b/solution.py
@@ -52,6 +52,56 @@
         got = lax.ppermute(x, axis, xor_pairs(size, bit))
         x = jnp.where(hi, jnp.concatenate([got, x], dim), jnp.concatenate([x, got], dim))
     return x
+
+
+def digit(idx, bits):
+    value = jnp.int32(0)
+    for j, bit in enumerate(bits):
+        value = value + ((idx & bit) != 0).astype(jnp.int32) * (1 << j)
+    return value
+
+
+def partner_mask(bits, offset):
+    return sum(bit for j, bit in enumerate(bits) if (offset >> j) & 1)
+
+
+def radix_scatter(x, axis, size, groups, dim):
+    idx = lax.axis_index(axis)
+    for bits in groups:
+        radix = 1 << len(bits)
+        width = x.shape[dim] // radix
+        mine = digit(idx, bits)
+        acc = lax.dynamic_slice_in_dim(x, mine * width, width, axis=dim)
+        for offset in range(1, radix):
+            mask = partner_mask(bits, offset)
+            send = lax.dynamic_slice_in_dim(x, (mine ^ offset) * width, width, axis=dim)
+            acc = acc + lax.ppermute(send, axis, xor_pairs(size, mask))
+        x = acc
+    return x
+
+
+def radix_gather(x, axis, size, groups, dim):
+    idx = lax.axis_index(axis)
+    for bits in reversed(groups):
+        radix = 1 << len(bits)
+        width = x.shape[dim]
+        mine = digit(idx, bits)
+        shape = list(x.shape)
+        shape[dim] = width * radix
+        out = lax.dynamic_update_slice_in_dim(jnp.zeros(shape, x.dtype), x, mine * width, axis=dim)
+        for offset in range(1, radix):
+            mask = partner_mask(bits, offset)
+            got = lax.ppermute(x, axis, xor_pairs(size, mask))
+            out = lax.dynamic_update_slice_in_dim(out, got, (mine ^ offset) * width, axis=dim)
+        x = out
+    return x
+
+
+def radix_groups(size, groups):
+    flat = sorted(bit for bits in groups for bit in bits)
+    if flat != [1 << i for i in range(size.bit_length() - 1)]:
+        return [(1 << i,) for i in range(size.bit_length() - 1)]
+    return groups
 
 
 def block_index(axis, bits):
@@ -92,7 +142,7 @@
 
 
 def make_body(runs_size, chan_size):
-    runs_bits = step_bits(runs_size, (8, 2, 1, 16, 4))
+    runs_groups = radix_groups(runs_size, [(8, 16), (2, 4), (1,)])
     chan_bits = step_bits(chan_size, (1, 2))
 
     def body(slices, spectra, loadings, mixing, halves, partner):
@@ -123,9 +173,9 @@
         inner_mix = jnp.einsum("hsr,hst->hrt", mixing, mixing, precision=lax.Precision.HIGHEST)
         system = inner_mix * cross
         inverse = lower_inverse(system)
-        moments_part = halving_scatter(partial_moments, "runs", runs_size, runs_bits, 2)
+        moments_part = radix_scatter(partial_moments, "runs", runs_size, runs_groups, 2)
         spectra_part = apply_inverse(inverse, moments_part)
-        new_spectra = doubling_gather(spectra_part, "runs", runs_size, runs_bits, 2)
+        new_spectra = radix_gather(spectra_part, "runs", runs_size, runs_groups, 2)
         held_rows = jnp.where(first_half, new_spectra[1][None], new_spectra[0][None])
         held_mix = jnp.where(first_half, mixing[1][None], mixing[0][None]) * mate_loads[:, None, :]
         held_projected = project(

time: 181 us -> 170 us (0.939)
  waiting for transfers between devices: 51.1 us -> 38.7 us
    ppermute x0 -> x14, starting transfers between devices: none -> 22.9 us  [the longest x7 12.2 us: radix_scatter(): acc = acc + lax.ppermute(send, axis, xor_pairs(size, mask))]
    ppermute x0 -> x14, waiting for transfers between devices: none -> 22.4 us  [the longest x7 12.4 us: radix_scatter(): acc = acc + lax.ppermute(send, axis, xor_pairs(size, mask))]
    ppermute x9 -> x4, waiting for transfers between devices: 23.8 us -> 5.3 us  [doubling_gather(): got = lax.ppermute(x, axis, xor_pairs(size, bit))]
    ppermute x9 -> x4, waiting for transfers between devices: 27.3 us -> 11.1 us  [halving_scatter(): x = keep + lax.ppermute(send, axis, xor_pairs(size, bit))]
    ppermute x9 -> x4, starting transfers between devices: 26.1 us -> 11.8 us  [halving_scatter(): x = keep + lax.ppermute(send, axis, xor_pairs(size, bit))]
    ppermute x9 -> x4, starting transfers between devices: 15.6 us -> 7.88 us  [doubling_gather(): got = lax.ppermute(x, axis, xor_pairs(size, bit))]
  transfers between devices with their start and end apart: 18 -> 22, of which waited for: 15 -> 16; matrix products, arithmetic and copies ran while one was open for 11% -> 12% of each run, Pallas kernels for 0% -> 0%
where the time goes in v3:
time: 170 us
  matrix products  65.2 us (38%)
  starting transfers between devices  42.7 us (25%)
  waiting for transfers between devices  38.7 us (23%)
  other arithmetic  18.6 us (11%)
  local copies, waits for them, and re-layouts  2.85 us (2%)
    dot_general x2, matrix products, project(): jnp.einsum('nrj,nij->nri', rows_low, slices, preferred_element_type=jnp.f...  22.1 us
    dot_general x2, matrix products, project(): jnp.einsum('nsi,nij->nsj', rotated, slices, preferred_element_type=jnp.fl...  19.2 us
    ppermute x7, waiting for transfers between devices, radix_scatter(): acc = acc + lax.ppermute(send, axis, xor_pairs(size, mask))  12.4 us
    ppermute x7, starting transfers between devices, radix_scatter(): acc = acc + lax.ppermute(send, axis, xor_pairs(size, mask))  12.2 us
    ppermute x4, starting transfers between devices, halving_scatter(): x = keep + lax.ppermute(send, axis, xor_pairs(size, bit))  11.8 us
    ppermute x4, waiting for transfers between devices, halving_scatter(): x = keep + lax.ppermute(send, axis, xor_pairs(size, bit))  11.1 us
    ppermute x7, starting transfers between devices, radix_gather(): got = lax.ppermute(x, axis, xor_pairs(size, mask))  10.8 us
    ppermute x7, waiting for transfers between devices, radix_gather(): got = lax.ppermute(x, axis, xor_pairs(size, mask))  10 us
  transfers between devices with their start and end apart: 22, of which 16 were waited for; matrix products, arithmetic and copies ran while one was open for 12% of the time, Pallas kernels for 0%

profile of v3, /device:TPU:1, one launch (start us, length us, event | category | flops | bytes accessed | tf_op | source)
XLA Modules:
  0.0 170.2 jit_solution(16624991712133040800)
XLA Ops:
  0.6 0.9 select_reduce_fusion.3
  1.6 1.1 slice_bitcast_fusion.3
  2.7 11.0 %fusion.17 = f32[8,48,512]{2,1,0:T(8,128)S(1)} fusion(bf16[8,512,2048]{2,1,0:T(8,128)(2,1)} %param.10, pred[8]{0:T(512)(128)(4,1)S(1)} %broadcast_compare_fusion, bf16[48,2048]{1,0:T(8,128)(2,1)S(1)} %get-tuple-element.86, bf16[48,2048]{1,0:T(8,128)(2,1)S(1)} %get-tuple-element.85), kind=kOutput, calls=%fused_computation.23 | convolution fusion | flops 806092800 | bytes 17956872 | tf_op jit(solution)/shard_map/nrj,nij->nri/dot_general | solution.py:117
  13.7 1.5 collective-permute-start
  16.3 8.8 %custom-call.7 = f32[2,48,48]{2,1,0:T(8,128)S(1)} custom-call(f32[2,48,48]{2,1,0:T(8,128)S(1)} %fusion.55), custom_call_target="Cholesky" | custom-call | tf_op jit(solution)/shard_map/jit(cholesky)/cholesky | solution.py:134
  25.4 1.5 collective-permute-start.1
  27.0 4.9 %collective-permute-done.1 = f32[2,48,512]{2,1,0:T(8,128)S(1)} collective-permute-done((f32[2,48,512]{2,1,0:T(8,128)S(1)}, f32[2,48,512]{2,1,0:T(8,128)S(1)}, u32[]{:S(2)}, u32[]{:S(2)}) %collective-permute-start.1) | collective-permute-done | bytes 196640 | tf_op jit(solution)/shard_map/ppermute | solution.py:44
  32.7 6.2 %while.22 = (s32[]{:T(128)}, f32[2,48,48]{1,2,0:T(8,128)S(1)}, f32[2,48,48]{2,1,0:T(8,128)S(1)}, s32[]{:T(128)}) while((s32[]{:T(128)}, f32[2,48,48]{1,2,0:T(8,128)S(1)}, f32[2,48,48]{2,1,0:T(8,128)S(1)}, s32[]{:T(128)}) %tuple.53), condition=%wide.region_5.6_spmd.clone, body=%wide.region_4.5_spmd.clone.sunk | while | flops 7976450 | bytes 221237 | solution.py:21
  39.2 1.5 collective-permute-start.2
  40.7 2.1 %collective-permute-done.2 = bf16[2,48,512]{2,1,0:T(8,128)(2,1)S(1)} collective-permute-done((bf16[2,48,512]{2,1,0:T(8,128)(2,1)S(1)}, bf16[2,48,512]{2,1,0:T(8,128)(2,1)S(1)}, u32[]{:S(2)}, u32[]{:S(2)}) %collective-permute-start.2) | collective-permute-done | bytes 98336 | tf_op jit(solution)/shard_map/ppermute | solution.py:52
  42.8 2.3 %collective-permute-start.3 = (bf16[4,48,512]{2,1,0:T(8,128)(2,1)S(1)}, bf16[4,48,512]{2,1,0:T(8,128)(2,1)S(1)}, u32[]{:S(2)}, u32[]{:S(2)}) collective-permute-start(bf16[4,48,512]{2,1,0:T(8,128)(2,1)S(1)} %maximum_select_fusion.4), channel_id=1, source_target_pairs={{0,1},{1,0},{2,3},{3,2},{4,5},{5,4},{6,7},{7,6},{8,9},{9,8},{10,11... | collective-permute-start | bytes 589832 | tf_op jit(solution)/shard_map/ppermute | solution.py:52
  45.0 1.1 collective-permute-done.3
  46.1 8.8 %fusion.24 = f32[8,48,2048]{2,1,0:T(8,128)S(1)} fusion(bf16[8,512,2048]{2,1,0:T(8,128)(2,1)} %param.10, bf16[4,48,512]{2,1,0:T(8,128)(2,1)S(1)} %maximum_select_fusion.4, bf16[4,48,512]{2,1,0:T(8,128)(2,1)S(1)} %collective-permute-done.3, pred[]{:T(512)S(6)} %ne.14), kind=kOutput, calls=%fused_computation.35 | convolution fusion | flops 805896192 | bytes 20316160 | tf_op jit(solution)/shard_map/nsi,nij->nsj/dot_general | solution.py:130
  54.9 3.1 %fusion.64 = f32[8,48,2048]{2,1,0:T(8,128)S(1)} fusion(f32[8,48,2048]{2,1,0:T(8,128)S(1)} %fusion.24, f32[8,48]{1,0:T(8,128)S(1)} %fusion.65, f32[48,48]{1,0:T(8,128)S(1)} %get-tuple-element.93, f32[48,48]{1,0:T(8,128)S(1)} %get-tuple-element.92, pred[8]{0:T(512)(128)(4,1)S(1)} %broadcast_compare_fusion), kind=kOutput, calls=%fused_computation.103 | convolution fusion | flops 453021696 | bytes 6311432 | tf_op jit(solution)/shard_map/nsr,nsj->nrj/dot_general | solution.py:164
  58.0 3.3 %fusion.10 = f32[2,48,2048]{2,0,1:T(2,128)S(1)} fusion(f32[8,48,2048]{2,1,0:T(8,128)S(1)} %fusion.64, s32[8]{0:T(128)S(1)} %get-tuple-element.67), kind=kOutput, calls=%fused_computation.15 | convolution fusion | flops 18874384 | bytes 3932192 | tf_op jit(solution)/shard_map/nh,nrj->hrj/dot_general | solution.py:168
  61.5 1.4 collective-permute-start.4
  63.0 2.4 %collective-permute-start.5 = (f32[2,48,512]{2,0,1:T(2,128)S(1)}, f32[2,48,512]{2,0,1:T(2,128)S(1)}, u32[]{:S(2)}, u32[]{:S(2)}) collective-permute-start(f32[2,48,512]{2,0,1:T(2,128)S(1)} %get-tuple-element.84), channel_id=1, source_target_pairs={{0,64},{4,68},{8,72},{12,76},{16,80},{20,84},{24,88},{28,92},{32,9... | collective-permute-start | bytes 589832 | tf_op jit(solution)/shard_map/ppermute | solution.py:78
  65.6 2.1 %collective-permute-done.4 = f32[2,48,512]{2,0,1:T(2,128)S(1)} collective-permute-done((f32[2,48,512]{2,0,1:T(2,128)S(1)}, f32[2,48,512]{2,0,1:T(2,128)S(1)}, u32[]{:S(2)}, u32[]{:S(2)}) %collective-permute-start.4) | collective-permute-done | bytes 196640 | tf_op jit(solution)/shard_map/ppermute | solution.py:78
  67.7 6.6 %collective-permute-done.5 = f32[2,48,512]{2,0,1:T(2,128)S(1)} collective-permute-done((f32[2,48,512]{2,0,1:T(2,128)S(1)}, f32[2,48,512]{2,0,1:T(2,128)S(1)}, u32[]{:S(2)}, u32[]{:S(2)}) %collective-permute-start.5) | collective-permute-done | bytes 196640 | tf_op jit(solution)/shard_map/ppermute | solution.py:78
  74.3 2.4 %collective-permute-done.6 = f32[2,48,512]{2,0,1:T(2,128)S(1)} collective-permute-done((f32[2,48,512]{2,0,1:T(2,128)S(1)}, f32[2,48,512]{2,0,1:T(2,128)S(1)}, u32[]{:S(2)}, u32[]{:S(2)}) %collective-permute-start.6) | collective-permute-done | bytes 196640 | tf_op jit(solution)/shard_map/ppermute | solution.py:78
  77.0 1.7 %collective-permute-start.7 = (f32[2,48,128]{2,0,1:T(2,128)S(1)}, f32[2,48,128]{2,0,1:T(2,128)S(1)}, u32[]{:S(2)}, u32[]{:S(2)}) collective-permute-start(f32[2,48,128]{2,0,1:T(2,128)S(1)} %get-tuple-element.87), channel_id=1, source_target_pairs={{0,8},{4,12},{8,0},{12,4},{16,24},{20,28},{24,16},{28,20},{32,40},... | collective-permute-start | bytes 147464 | tf_op jit(solution)/shard_map/ppermute | solution.py:78
  78.7 3.3 %collective-permute-start.8 = (f32[2,48,128]{2,0,1:T(2,128)S(1)}, f32[2,48,128]{2,0,1:T(2,128)S(1)}, u32[]{:S(2)}, u32[]{:S(2)}) collective-permute-start(f32[2,48,128]{2,0,1:T(2,128)S(1)} %get-tuple-element.89), channel_id=1, source_target_pairs={{0,16},{4,20},{8,24},{12,28},{16,0},{20,4},{24,8},{28,12},{32,48},... | collective-permute-start | bytes 147464 | tf_op jit(solution)/shard_map/ppermute | solution.py:78
  82.1 7.4 %custom-call.8 = f32[2,1,48,48]{2,3,1,0:T(8,128)S(1)} custom-call(f32[2,1,48,48]{3,2,1,0:T(8,128)S(1)} %select_bitcast_fusion), custom_call_target="InvertDiagBlocksLowerTriangular" | custom-call | tf_op jit(solution)/shard_map/triangular_solve | solution.py:136
  89.7 3.2 %collective-permute-start.10 = (f32[2,48,64]{2,0,1:T(2,128)S(1)}, f32[2,48,64]{2,0,1:T(2,128)S(1)}, u32[]{:S(2)}, u32[]{:S(2)}) collective-permute-start(f32[2,48,64]{2,0,1:T(2,128)S(1)} %constant_dynamic-slice_fusion), channel_id=1, source_target_pairs={{0,4},{4,0},{8,12},{12,8},{16,20},{20,16},{24,28},{28,24},{32,36},... | collective-permute-start | bytes 73736 | tf_op jit(solution)/shard_map/ppermute | solution.py:78
  93.2 1.3 collective-permute-done.10
  95.0 3.0 %collective-permute-start.11 = (f32[2,48,64]{2,1,0:T(8,128)S(1)}, f32[2,48,64]{2,1,0:T(8,128)S(1)}, u32[]{:S(2)}, u32[]{:S(2)}) collective-permute-start(f32[2,48,64]{2,1,0:T(8,128)S(1)} %fusion.81), channel_id=1, source_target_pairs={{0,4},{4,0},{8,12},{12,8},{16,20},{20,16},{24,28},{28,24},{32,36},... | collective-permute-start | bytes 73736 | tf_op jit(solution)/shard_map/ppermute | solution.py:94
  98.2 1.3 collective-permute-done.11
  99.5 0.5 dynamic_update_slice.31
  100.1 3.8 %collective-permute-start.13 = (f32[2,48,128]{2,1,0:T(8,128)S(1)}, f32[2,48,128]{2,1,0:T(8,128)S(1)}, u32[]{:S(2)}, u32[]{:S(2)}) collective-permute-start(f32[2,48,128]{2,1,0:T(8,128)S(1)} %dynamic_update_slice.31), channel_id=1, source_target_pairs={{0,16},{4,20},{8,24},{12,28},{16,0},{20,4},{24,8},{28,12},{32,48},... | collective-permute-start | bytes 147464 | tf_op jit(solution)/shard_map/ppermute | solution.py:94
  104.0 1.9 %collective-permute-done.13 = f32[2,48,128]{2,1,0:T(8,128)S(1)} collective-permute-done((f32[2,48,128]{2,1,0:T(8,128)S(1)}, f32[2,48,128]{2,1,0:T(8,128)S(1)}, u32[]{:S(2)}, u32[]{:S(2)}) %collective-permute-start.13) | collective-permute-done | bytes 49184 | tf_op jit(solution)/shard_map/ppermute | solution.py:94
  106.0 2.1 %collective-permute-done.14 = f32[2,48,128]{2,1,0:T(8,128)S(1)} collective-permute-done((f32[2,48,128]{2,1,0:T(8,128)S(1)}, f32[2,48,128]{2,1,0:T(8,128)S(1)}, u32[]{:S(2)}, u32[]{:S(2)}) %collective-permute-start.14) | collective-permute-done | bytes 49184 | tf_op jit(solution)/shard_map/ppermute | solution.py:94
  108.1 1.4 collective-permute-start.16
  109.5 2.5 %collective-permute-start.17 = (f32[2,48,512]{2,1,0:T(8,128)S(1)}, f32[2,48,512]{2,1,0:T(8,128)S(1)}, u32[]{:S(2)}, u32[]{:S(2)}) collective-permute-start(f32[2,48,512]{2,1,0:T(8,128)S(1)} %constant_dynamic-update-slice_fusion.4), channel_id=1, source_target_pairs={{0,96},{4,100},{8,104},{12,108},{16,112},{20,116},{24,120},{28,124... | collective-permute-start | bytes 589832 | tf_op jit(solution)/shard_map/ppermute | solution.py:94
  112.1 0.6 collective-permute-done.15
  112.7 2.1 %collective-permute-done.16 = f32[2,48,512]{2,1,0:T(8,128)S(1)} collective-permute-done((f32[2,48,512]{2,1,0:T(8,128)S(1)}, f32[2,48,512]{2,1,0:T(8,128)S(1)}, u32[]{:S(2)}, u32[]{:S(2)}) %collective-permute-start.16) | collective-permute-done | bytes 196640 | tf_op jit(solution)/shard_map/ppermute | solution.py:94
  114.8 2.0 %collective-permute-done.17 = f32[2,48,512]{2,1,0:T(8,128)S(1)} collective-permute-done((f32[2,48,512]{2,1,0:T(8,128)S(1)}, f32[2,48,512]{2,1,0:T(8,128)S(1)}, u32[]{:S(2)}, u32[]{:S(2)}) %collective-permute-start.17) | collective-permute-done | bytes 196640 | tf_op jit(solution)/shard_map/ppermute | solution.py:94
  116.9 11.2 %fusion.12 = f32[8,48,512]{2,1,0:T(8,128)S(1)} fusion(bf16[8,512,2048]{2,1,0:T(8,128)(2,1)} %param.10, f32[48,2048]{1,0:T(8,128)S(1)} %get-tuple-element.81, f32[48,2048]{1,0:T(8,128)S(1)} %get-tuple-element.80, pred[8]{0:T(512)(128)(4,1)S(1)} %broadcast_compare_fusion), kind=kOutput, calls=%fused_computation.18 | convolution fusion | flops 806092800 | bytes 18350088 | tf_op jit(solution)/shard_map/nrj,nij->nri/dot_general | solution.py:117
  128.1 7.5 %collective-permute-start.18 = (f32[4,48,512]{2,1,0:T(8,128)S(1)}, f32[4,48,512]{2,1,0:T(8,128)S(1)}, u32[]{:S(2)}, u32[]{:S(2)}) collective-permute-start(f32[4,48,512]{2,1,0:T(8,128)S(1)} %slice_select_fusion), channel_id=1, source_target_pairs={{0,1},{1,0},{2,3},{3,2},{4,5},{5,4},{6,7},{7,6},{8,9},{9,8},{10,11... | collective-permute-start | bytes 1179656 | tf_op jit(solution)/shard_map/ppermute | solution.py:44
  135.6 1.3 collective-permute-done.18
  137.1 1.4 collective-permute-start.19
  138.5 4.8 %collective-permute-done.19 = f32[2,48,512]{2,1,0:T(8,128)S(1)} collective-permute-done((f32[2,48,512]{2,1,0:T(8,128)S(1)}, f32[2,48,512]{2,1,0:T(8,128)S(1)}, u32[]{:S(2)}, u32[]{:S(2)}) %collective-permute-start.19) | collective-permute-done | bytes 196640 | tf_op jit(solution)/shard_map/ppermute | solution.py:44
  143.6 0.4 select_reduce_fusion
  144.1 6.2 %while.23 = (s32[]{:T(128)}, f32[2,48,48]{1,2,0:T(8,128)S(1)}, f32[2,48,48]{2,1,0:T(8,128)S(1)}, s32[]{:T(128)}) while((s32[]{:T(128)}, f32[2,48,48]{1,2,0:T(8,128)S(1)}, f32[2,48,48]{2,1,0:T(8,128)S(1)}, s32[]{:T(128)}) %tuple.56), condition=%wide.region_9.10_spmd.clone, body=%wide.region_8.9_spmd.clone.sunk | while | flops 7976450 | bytes 221237 | solution.py:21
  150.6 1.4 collective-permute-start.20
  152.0 2.2 %collective-permute-done.20 = bf16[2,48,512]{2,1,0:T(8,128)(2,1)S(1)} collective-permute-done((bf16[2,48,512]{2,1,0:T(8,128)(2,1)S(1)}, bf16[2,48,512]{2,1,0:T(8,128)(2,1)S(1)}, u32[]{:S(2)}, u32[]{:S(2)}) %collective-permute-start.20) | collective-permute-done | bytes 98336 | tf_op jit(solution)/shard_map/ppermute | solution.py:52
  154.2 2.7 %collective-permute-start.21 = (bf16[4,48,512]{2,1,0:T(8,128)(2,1)S(1)}, bf16[4,48,512]{2,1,0:T(8,128)(2,1)S(1)}, u32[]{:S(2)}, u32[]{:S(2)}) collective-permute-start(bf16[4,48,512]{2,1,0:T(8,128)(2,1)S(1)} %maximum_select_fusion.5), channel_id=1, source_target_pairs={{0,1},{1,0},{2,3},{3,2},{4,5},{5,4},{6,7},{7,6},{8,9},{9,8},{10,11... | collective-permute-start | bytes 589832 | tf_op jit(solution)/shard_map/ppermute | solution.py:52
  156.9 2.8 %fusion.8 = f32[8,48,2048]{2,1,0:T(8,128)S(1)} fusion(f32[48,2048]{1,0:T(8,128)S(1)} %get-tuple-element.81, f32[48,2048]{1,0:T(8,128)S(1)} %get-tuple-element.80, pred[8]{0:T(512)(128)(4,1)S(1)} %broadcast_compare_fusion, f32[8,48]{1,0:T(8,128)S(1)} %fusion.66, f32[48,48]{1,0:T(8,128)S(1)} %get-tuple-element.93, f32[48,48]{1,0:T(8,128)S(1)} %get-tuple-element.92), kind=kOutput, calls=%fused_computation.12 | convolution fusion | flops 453808128 | bytes 3952136 | tf_op jit(solution)/shard_map/nrs,nsj->nrj/dot_general | solution.py:184
  159.7 10.5 %convolution_subtract_fusion.2 = f32[8,48,2048]{2,1,0:T(8,128)} fusion(f32[8,48,2048]{2,1,0:T(8,128)S(1)} %fusion.8, bf16[8,512,2048]{2,1,0:T(8,128)(2,1)} %param.10, bf16[4,48,512]{2,1,0:T(8,128)(2,1)S(1)} %maximum_select_fusion.5, bf16[4,48,512]{2,1,0:T(8,128)(2,1)S(1)} %collective-permute-done.21, pred[]{:T(512)S(6)} %ne.14), kind=kOutput, calls=%fused_computation.17 | convolution fusion | flops 806682624 | bytes 23461888 | tf_op jit(solution)/shard_map/nsi,nij->nsj/dot_general | solution.py:130
  (176 shorter events, 17.3 us)
Async XLA Ops:
  2.6 12.5 %copy-start.3 = (s32[256]{0:T(256)S(1)}, s32[256]{0:T(256)}, u32[]{:S(2)}) copy-start(s32[256]{0:T(256)} %param.14) | copy-start | bytes 3076
  2.6 12.5 %copy-start.2 = (f32[256,48]{0,1:T(8,128)S(1)}, f32[256,48]{0,1:T(8,128)}, u32[]{:S(2)}) copy-start(f32[256,48]{0,1:T(8,128)} %param.12) | copy-start | bytes 147460
  2.6 13.2 %copy-start.1 = (f32[2,48,48]{2,1,0:T(8,128)S(1)}, f32[2,48,48]{2,1,0:T(8,128)}, u32[]{:S(2)}) copy-start(f32[2,48,48]{2,1,0:T(8,128)} %param.13) | copy-start | bytes 55300
  13.7 11.5 %collective-permute-start = (f32[4,48,512]{2,1,0:T(8,128)S(1)}, f32[4,48,512]{2,1,0:T(8,128)S(1)}, u32[]{:S(2)}, u32[]{:S(2)}) collective-permute-start(f32[4,48,512]{2,1,0:T(8,128)S(1)} %slice_select_fusion.1), channel_id=1, source_target_pairs={{0,1},{1,0},{2,3},{3,2},{4,5},{5,4},{6,7},{7,6},{8,9},{9,8},{10,11... | collective-permute-start | bytes 1179656 | tf_op jit(solution)/shard_map/ppermute | solution.py:44
  25.4 6.5 %collective-permute-start.1 = (f32[2,48,512]{2,1,0:T(8,128)S(1)}, f32[2,48,512]{2,1,0:T(8,128)S(1)}, u32[]{:S(2)}, u32[]{:S(2)}) collective-permute-start(f32[2,48,512]{2,1,0:T(8,128)S(1)} %slice_select_fusion.3), channel_id=1, source_target_pairs={{0,2},{1,3},{2,0},{3,1},{4,6},{5,7},{6,4},{7,5},{8,10},{9,11},{10,... | collective-permute-start | bytes 589832 | tf_op jit(solution)/shard_map/ppermute | solution.py:44
  39.2 3.5 %collective-permute-start.2 = (bf16[2,48,512]{2,1,0:T(8,128)(2,1)S(1)}, bf16[2,48,512]{2,1,0:T(8,128)(2,1)S(1)}, u32[]{:S(2)}, u32[]{:S(2)}) collective-permute-start(bf16[2,48,512]{2,1,0:T(8,128)(2,1)S(1)} %convolution_convert_fusion.1), channel_id=1, source_target_pairs={{0,2},{1,3},{2,0},{3,1},{4,6},{5,7},{6,4},{7,5},{8,10},{9,11},{10,... | collective-permute-start | bytes 294920 | tf_op jit(solution)/shard_map/ppermute | solution.py:52
  42.8 3.4 %collective-permute-start.3 = (bf16[4,48,512]{2,1,0:T(8,128)(2,1)S(1)}, bf16[4,48,512]{2,1,0:T(8,128)(2,1)S(1)}, u32[]{:S(2)}, u32[]{:S(2)}) collective-permute-start(bf16[4,48,512]{2,1,0:T(8,128)(2,1)S(1)} %maximum_select_fusion.4), channel_id=1, source_target_pairs={{0,1},{1,0},{2,3},{3,2},{4,5},{5,4},{6,7},{7,6},{8,9},{9,8},{10,11... | collective-permute-start | bytes 589832 | tf_op jit(solution)/shard_map/ppermute | solution.py:52
  61.5 6.2 %collective-permute-start.4 = (f32[2,48,512]{2,0,1:T(2,128)S(1)}, f32[2,48,512]{2,0,1:T(2,128)S(1)}, u32[]{:S(2)}, u32[]{:S(2)}) collective-permute-start(f32[2,48,512]{2,0,1:T(2,128)S(1)} %get-tuple-element.82), channel_id=1, source_target_pairs={{0,32},{4,36},{8,40},{12,44},{16,48},{20,52},{24,56},{28,60},{32,0... | collective-permute-start | bytes 589832 | tf_op jit(solution)/shard_map/ppermute | solution.py:78
  63.0 11.3 %collective-permute-start.5 = (f32[2,48,512]{2,0,1:T(2,128)S(1)}, f32[2,48,512]{2,0,1:T(2,128)S(1)}, u32[]{:S(2)}, u32[]{:S(2)}) collective-permute-start(f32[2,48,512]{2,0,1:T(2,128)S(1)} %get-tuple-element.84), channel_id=1, source_target_pairs={{0,64},{4,68},{8,72},{12,76},{16,80},{20,84},{24,88},{28,92},{32,9... | collective-permute-start | bytes 589832 | tf_op jit(solution)/shard_map/ppermute | solution.py:78
  65.4 11.3 %collective-permute-start.6 = (f32[2,48,512]{2,0,1:T(2,128)S(1)}, f32[2,48,512]{2,0,1:T(2,128)S(1)}, u32[]{:S(2)}, u32[]{:S(2)}) collective-permute-start(f32[2,48,512]{2,0,1:T(2,128)S(1)} %get-tuple-element.83), channel_id=1, source_target_pairs={{0,96},{4,100},{8,104},{12,108},{16,112},{20,116},{24,120},{28,124... | collective-permute-start | bytes 589832 | tf_op jit(solution)/shard_map/ppermute | solution.py:78
  77.0 12.5 %collective-permute-start.7 = (f32[2,48,128]{2,0,1:T(2,128)S(1)}, f32[2,48,128]{2,0,1:T(2,128)S(1)}, u32[]{:S(2)}, u32[]{:S(2)}) collective-permute-start(f32[2,48,128]{2,0,1:T(2,128)S(1)} %get-tuple-element.87), channel_id=1, source_target_pairs={{0,8},{4,12},{8,0},{12,4},{16,24},{20,28},{24,16},{28,20},{32,40},... | collective-permute-start | bytes 147464 | tf_op jit(solution)/shard_map/ppermute | solution.py:78
  78.7 10.8 %collective-permute-start.8 = (f32[2,48,128]{2,0,1:T(2,128)S(1)}, f32[2,48,128]{2,0,1:T(2,128)S(1)}, u32[]{:S(2)}, u32[]{:S(2)}) collective-permute-start(f32[2,48,128]{2,0,1:T(2,128)S(1)} %get-tuple-element.89), channel_id=1, source_target_pairs={{0,16},{4,20},{8,24},{12,28},{16,0},{20,4},{24,8},{28,12},{32,48},... | collective-permute-start | bytes 147464 | tf_op jit(solution)/shard_map/ppermute | solution.py:78
  82.0 7.5 %collective-permute-start.9 = (f32[2,48,128]{2,0,1:T(2,128)S(1)}, f32[2,48,128]{2,0,1:T(2,128)S(1)}, u32[]{:S(2)}, u32[]{:S(2)}) collective-permute-start(f32[2,48,128]{2,0,1:T(2,128)S(1)} %get-tuple-element.88), channel_id=1, source_target_pairs={{0,24},{4,28},{8,16},{12,20},{16,8},{20,12},{24,0},{28,4},{32,56},... | collective-permute-start | bytes 147464 | tf_op jit(solution)/shard_map/ppermute | solution.py:78
  89.7 4.7 %collective-permute-start.10 = (f32[2,48,64]{2,0,1:T(2,128)S(1)}, f32[2,48,64]{2,0,1:T(2,128)S(1)}, u32[]{:S(2)}, u32[]{:S(2)}) collective-permute-start(f32[2,48,64]{2,0,1:T(2,128)S(1)} %constant_dynamic-slice_fusion), channel_id=1, source_target_pairs={{0,4},{4,0},{8,12},{12,8},{16,20},{20,16},{24,28},{28,24},{32,36},... | collective-permute-start | bytes 73736 | tf_op jit(solution)/shard_map/ppermute | solution.py:78
  95.0 4.5 %collective-permute-start.11 = (f32[2,48,64]{2,1,0:T(8,128)S(1)}, f32[2,48,64]{2,1,0:T(8,128)S(1)}, u32[]{:S(2)}, u32[]{:S(2)}) collective-permute-start(f32[2,48,64]{2,1,0:T(8,128)S(1)} %fusion.81), channel_id=1, source_target_pairs={{0,4},{4,0},{8,12},{12,8},{16,20},{20,16},{24,28},{28,24},{32,36},... | collective-permute-start | bytes 73736 | tf_op jit(solution)/shard_map/ppermute | solution.py:94
  100.0 4.0 %collective-permute-start.12 = (f32[2,48,128]{2,1,0:T(8,128)S(1)}, f32[2,48,128]{2,1,0:T(8,128)S(1)}, u32[]{:S(2)}, u32[]{:S(2)}) collective-permute-start(f32[2,48,128]{2,1,0:T(8,128)S(1)} %dynamic_update_slice.31), channel_id=1, source_target_pairs={{0,8},{4,12},{8,0},{12,4},{16,24},{20,28},{24,16},{28,20},{32,40},... | collective-permute-start | bytes 147464 | tf_op jit(solution)/shard_map/ppermute | solution.py:94
  100.1 5.8 %collective-permute-start.13 = (f32[2,48,128]{2,1,0:T(8,128)S(1)}, f32[2,48,128]{2,1,0:T(8,128)S(1)}, u32[]{:S(2)}, u32[]{:S(2)}) collective-permute-start(f32[2,48,128]{2,1,0:T(8,128)S(1)} %dynamic_update_slice.31), channel_id=1, source_target_pairs={{0,16},{4,20},{8,24},{12,28},{16,0},{20,4},{24,8},{28,12},{32,48},... | collective-permute-start | bytes 147464 | tf_op jit(solution)/shard_map/ppermute | solution.py:94
  104.0 4.2 %collective-permute-start.14 = (f32[2,48,128]{2,1,0:T(8,128)S(1)}, f32[2,48,128]{2,1,0:T(8,128)S(1)}, u32[]{:S(2)}, u32[]{:S(2)}) collective-permute-start(f32[2,48,128]{2,1,0:T(8,128)S(1)} %dynamic_update_slice.31), channel_id=1, source_target_pairs={{0,24},{4,28},{8,16},{12,20},{16,8},{20,12},{24,0},{28,4},{32,56},... | collective-permute-start | bytes 147464 | tf_op jit(solution)/shard_map/ppermute | solution.py:94
  108.1 4.5 %collective-permute-start.15 = (f32[2,48,512]{2,1,0:T(8,128)S(1)}, f32[2,48,512]{2,1,0:T(8,128)S(1)}, u32[]{:S(2)}, u32[]{:S(2)}) collective-permute-start(f32[2,48,512]{2,1,0:T(8,128)S(1)} %constant_dynamic-update-slice_fusion.4), channel_id=1, source_target_pairs={{0,32},{4,36},{8,40},{12,44},{16,48},{20,52},{24,56},{28,60},{32,0... | collective-permute-start | bytes 589832 | tf_op jit(solution)/shard_map/ppermute | solution.py:94
  108.1 6.6 %collective-permute-start.16 = (f32[2,48,512]{2,1,0:T(8,128)S(1)}, f32[2,48,512]{2,1,0:T(8,128)S(1)}, u32[]{:S(2)}, u32[]{:S(2)}) collective-permute-start(f32[2,48,512]{2,1,0:T(8,128)S(1)} %constant_dynamic-update-slice_fusion.4), channel_id=1, source_target_pairs={{0,64},{4,68},{8,72},{12,76},{16,80},{20,84},{24,88},{28,92},{32,9... | collective-permute-start | bytes 589832 | tf_op jit(solution)/shard_map/ppermute | solution.py:94
  109.5 7.3 %collective-permute-start.17 = (f32[2,48,512]{2,1,0:T(8,128)S(1)}, f32[2,48,512]{2,1,0:T(8,128)S(1)}, u32[]{:S(2)}, u32[]{:S(2)}) collective-permute-start(f32[2,48,512]{2,1,0:T(8,128)S(1)} %constant_dynamic-update-slice_fusion.4), channel_id=1, source_target_pairs={{0,96},{4,100},{8,104},{12,108},{16,112},{20,116},{24,120},{28,124... | collective-permute-start | bytes 589832 | tf_op jit(solution)/shard_map/ppermute | solution.py:94
  116.8 11.2 %copy-start = (f32[2,48,2048]{2,1,0:T(8,128)}, f32[2,48,2048]{2,1,0:T(8,128)S(1)}, u32[]{:S(2)}) copy-start(f32[2,48,2048]{2,1,0:T(8,128)S(1)} %constant_dynamic-update-slice_fusion) | copy-start | bytes 2359300
  128.1 8.9 %collective-permute-start.18 = (f32[4,48,512]{2,1,0:T(8,128)S(1)}, f32[4,48,512]{2,1,0:T(8,128)S(1)}, u32[]{:S(2)}, u32[]{:S(2)}) collective-permute-start(f32[4,48,512]{2,1,0:T(8,128)S(1)} %slice_select_fusion), channel_id=1, source_target_pairs={{0,1},{1,0},{2,3},{3,2},{4,5},{5,4},{6,7},{7,6},{8,9},{9,8},{10,11... | collective-permute-start | bytes 1179656 | tf_op jit(solution)/shard_map/ppermute | solution.py:44
  137.1 6.2 %collective-permute-start.19 = (f32[2,48,512]{2,1,0:T(8,128)S(1)}, f32[2,48,512]{2,1,0:T(8,128)S(1)}, u32[]{:S(2)}, u32[]{:S(2)}) collective-permute-start(f32[2,48,512]{2,1,0:T(8,128)S(1)} %slice_select_fusion.2), channel_id=1, source_target_pairs={{0,2},{1,3},{2,0},{3,1},{4,6},{5,7},{6,4},{7,5},{8,10},{9,11},{10,... | collective-permute-start | bytes 589832 | tf_op jit(solution)/shard_map/ppermute | solution.py:44
  150.6 3.5 %collective-permute-start.20 = (bf16[2,48,512]{2,1,0:T(8,128)(2,1)S(1)}, bf16[2,48,512]{2,1,0:T(8,128)(2,1)S(1)}, u32[]{:S(2)}, u32[]{:S(2)}) collective-permute-start(bf16[2,48,512]{2,1,0:T(8,128)(2,1)S(1)} %convolution_convert_fusion), channel_id=1, source_target_pairs={{0,2},{1,3},{2,0},{3,1},{4,6},{5,7},{6,4},{7,5},{8,10},{9,11},{10,... | collective-permute-start | bytes 294920 | tf_op jit(solution)/shard_map/ppermute | solution.py:52
  154.2 5.5 %collective-permute-start.21 = (bf16[4,48,512]{2,1,0:T(8,128)(2,1)S(1)}, bf16[4,48,512]{2,1,0:T(8,128)(2,1)S(1)}, u32[]{:S(2)}, u32[]{:S(2)}) collective-permute-start(bf16[4,48,512]{2,1,0:T(8,128)(2,1)S(1)} %maximum_select_fusion.5), channel_id=1, source_target_pairs={{0,1},{1,0},{2,3},{3,2},{4,5},{5,4},{6,7},{7,6},{8,9},{9,8},{10,11... | collective-permute-start | bytes 589832 | tf_op jit(solution)/shard_map/ppermute | solution.py:52

commit v4 on v3

--- a/solution.py
+++ b/solution.py
@@ -41,7 +41,8 @@
         high = lax.slice_in_dim(x, half, 2 * half, axis=dim)
         send = jnp.where(hi, low, high)
         keep = jnp.where(hi, high, low)
-        x = keep + lax.ppermute(send, axis, xor_pairs(size, bit))
+        got = lax.ppermute(send, axis, xor_pairs(size, bit))
+        x = keep + got
     return x
 
 
@@ -75,7 +76,8 @@
         for offset in range(1, radix):
             mask = partner_mask(bits, offset)
             send = lax.dynamic_slice_in_dim(x, (mine ^ offset) * width, width, axis=dim)
-            acc = acc + lax.ppermute(send, axis, xor_pairs(size, mask))
+            got = lax.ppermute(send, axis, xor_pairs(size, mask))
+            acc = acc + got
         x = acc
     return x
 
@@ -112,7 +114,7 @@
     return block
 
 
-def project(slices, rows_low, mixed, chan_size, chan_bits):
+def project_body(slices, rows_low, mixed, chan_size, chan_bits):
     run_count = slices.shape[0]
     partial_basis = jnp.einsum("nrj,nij->nri", rows_low, slices, preferred_element_type=jnp.float32)
     basis = halving_scatter(partial_basis, "chan", chan_size, chan_bits, 0)
@@ -145,7 +147,7 @@
     runs_groups = radix_groups(runs_size, [(8, 16), (2, 4), (1,)])
     chan_bits = step_bits(chan_size, (1, 2))
 
-    def body(slices, spectra, loadings, mixing, halves, partner):
+    def layer(slices, spectra, loadings, mixing, halves, partner):
         run_count = slices.shape[0]
         total_runs = loadings.shape[0]
         first_run = lax.axis_index("runs") * run_count
@@ -160,7 +162,7 @@
         first_half = (my_halves == 0)[:, None, None]
         own_rows = jnp.where(first_half, spectra[0][None], spectra[1][None])
         own_mix = jnp.where(first_half, mixing[0][None], mixing[1][None]) * my_loads[:, None, :]
-        projected = project(slices, own_rows, own_mix, chan_size, chan_bits)
+        projected = project_body(slices, own_rows, own_mix, chan_size, chan_bits)
         terms = jnp.einsum("nsr,nsj->nrj", own_mix, projected, precision=lax.Precision.HIGHEST)
         mine_member = (my_halves[:, None] == jnp.arange(2, dtype=jnp.int32)[None, :]).astype(
             jnp.float32
@@ -172,13 +174,14 @@
         cross = jnp.einsum("kh,kr,ks->hrs", member, loadings, loadings, precision=lax.Precision.HIGHEST)
         inner_mix = jnp.einsum("hsr,hst->hrt", mixing, mixing, precision=lax.Precision.HIGHEST)
         system = inner_mix * cross
+        system, partial_moments = lax.optimization_barrier((system, partial_moments))
         inverse = lower_inverse(system)
         moments_part = radix_scatter(partial_moments, "runs", runs_size, runs_groups, 2)
         spectra_part = apply_inverse(inverse, moments_part)
         new_spectra = radix_gather(spectra_part, "runs", runs_size, runs_groups, 2)
         held_rows = jnp.where(first_half, new_spectra[1][None], new_spectra[0][None])
         held_mix = jnp.where(first_half, mixing[1][None], mixing[0][None]) * mate_loads[:, None, :]
-        held_projected = project(
+        held_projected = project_body(
             slices, held_rows.astype(jnp.bfloat16), held_mix, chan_size, chan_bits
         )
         model_part = jnp.einsum(
@@ -186,7 +189,7 @@
         )
         return (new_spectra, held_projected - model_part)
 
-    return body
+    return layer
 
 
 def solution(mesh):

time: 170 us -> 162 us (0.953)
  waiting for transfers between devices: 38.7 us -> 30 us
    ppermute x11, waiting for transfers between devices: 23.4 us -> 14.7 us  [the longest x4 11.3 us: halving_scatter(): got = lax.ppermute(send, axis, xor_pairs(size, bit))]
    another operation x3 -> x4, other arithmetic: 8.93 us -> 8.96 us  [lower_inverse(): lower = jnp.linalg.cholesky(system)]
  transfers between devices with their start and end apart: 22 -> 22, of which waited for: 16 -> 15; matrix products, arithmetic and copies ran while one was open for 12% -> 13% of each run, Pallas kernels for 0% -> 0%
where the time goes in v4:
time: 162 us; the launch traced here: 161 us
  matrix products  65.2 us (40%)
  starting transfers between devices  42.6 us (26%)
  waiting for transfers between devices  30 us (19%)
  other arithmetic  18.5 us (11%)
  local copies, waits for them, and re-layouts  2.77 us (2%)
    dot_general x2, matrix products, project_body(): jnp.einsum('nrj,nij->nri', rows_low, slices, preferred_element_type=jnp.f...  22.1 us
    dot_general x2, matrix products, project_body(): jnp.einsum('nsi,nij->nsj', rotated, slices, preferred_element_type=jnp.fl...  19.3 us
    ppermute x7, starting transfers between devices, radix_scatter(): got = lax.ppermute(send, axis, xor_pairs(size, mask))  12 us
    ppermute x4, starting transfers between devices, halving_scatter(): got = lax.ppermute(send, axis, xor_pairs(size, bit))  11.6 us
    ppermute x4, waiting for transfers between devices, halving_scatter(): got = lax.ppermute(send, axis, xor_pairs(size, bit))  11.3 us
    ppermute x7, starting transfers between devices, radix_gather(): got = lax.ppermute(x, axis, xor_pairs(size, mask))  10.8 us
    ppermute x7, waiting for transfers between devices, radix_gather(): got = lax.ppermute(x, axis, xor_pairs(size, mask))  10.3 us
    another operation x4, other arithmetic, lower_inverse(): lower = jnp.linalg.cholesky(system)  8.96 us
  transfers between devices with their start and end apart: 22, of which 15 were waited for; matrix products, arithmetic and copies ran while one was open for 13% of the time, Pallas kernels for 0%

profile of v4, /device:TPU:1, one launch (start us, length us, event | category | flops | bytes accessed | tf_op | source)
XLA Modules:
  0.0 161.3 jit_solution(5742097605188182151)
XLA Ops:
  0.6 0.9 select_reduce_fusion.3
  1.6 1.1 slice_bitcast_fusion.3
  2.6 11.0 %fusion.17 = f32[8,48,512]{2,1,0:T(8,128)S(1)} fusion(bf16[8,512,2048]{2,1,0:T(8,128)(2,1)} %param.10, pred[8]{0:T(512)(128)(4,1)S(1)} %broadcast_compare_fusion, bf16[48,2048]{1,0:T(8,128)(2,1)S(1)} %get-tuple-element.88, bf16[48,2048]{1,0:T(8,128)(2,1)S(1)} %get-tuple-element.87), kind=kOutput, calls=%fused_computation.23 | convolution fusion | flops 806092800 | bytes 17956872 | tf_op jit(solution)/shard_map/nrj,nij->nri/dot_general | solution.py:119
  13.7 1.5 collective-permute-start
  16.1 0.4 collective-permute-done
  16.6 1.5 collective-permute-start.1
  18.1 4.7 %collective-permute-done.1 = f32[2,48,512]{2,1,0:T(8,128)S(1)} collective-permute-done((f32[2,48,512]{2,1,0:T(8,128)S(1)}, f32[2,48,512]{2,1,0:T(8,128)S(1)}, u32[]{:S(2)}, u32[]{:S(2)}) %collective-permute-start.1) | collective-permute-done | bytes 196640 | tf_op jit(solution)/shard_map/ppermute | solution.py:44
  23.1 0.4 select_reduce_fusion.2
  23.6 6.2 %while.22 = (s32[]{:T(128)}, f32[2,48,48]{1,2,0:T(8,128)S(1)}, f32[2,48,48]{2,1,0:T(8,128)S(1)}, s32[]{:T(128)}) while((s32[]{:T(128)}, f32[2,48,48]{1,2,0:T(8,128)S(1)}, f32[2,48,48]{2,1,0:T(8,128)S(1)}, s32[]{:T(128)}) %tuple.54), condition=%wide.region_3.4_spmd.clone, body=%wide.region_2.3_spmd.clone.sunk | while | flops 7976450 | bytes 221237 | solution.py:21
  30.1 1.5 collective-permute-start.2
  31.6 2.0 %collective-permute-done.2 = bf16[2,48,512]{2,1,0:T(8,128)(2,1)S(1)} collective-permute-done((bf16[2,48,512]{2,1,0:T(8,128)(2,1)S(1)}, bf16[2,48,512]{2,1,0:T(8,128)(2,1)S(1)}, u32[]{:S(2)}, u32[]{:S(2)}) %collective-permute-start.2) | collective-permute-done | bytes 98336 | tf_op jit(solution)/shard_map/ppermute | solution.py:53
  33.7 2.6 %collective-permute-start.3 = (bf16[4,48,512]{2,1,0:T(8,128)(2,1)S(1)}, bf16[4,48,512]{2,1,0:T(8,128)(2,1)S(1)}, u32[]{:S(2)}, u32[]{:S(2)}) collective-permute-start(bf16[4,48,512]{2,1,0:T(8,128)(2,1)S(1)} %maximum_select_fusion.4), channel_id=1, source_target_pairs={{0,1},{1,0},{2,3},{3,2},{4,5},{5,4},{6,7},{7,6},{8,9},{9,8},{10,11... | collective-permute-start | bytes 589832 | tf_op jit(solution)/shard_map/ppermute | solution.py:53
  36.6 0.8 collective-permute-done.3
  37.4 8.8 %fusion.25 = f32[8,48,2048]{2,1,0:T(8,128)S(1)} fusion(bf16[8,512,2048]{2,1,0:T(8,128)(2,1)} %param.10, bf16[4,48,512]{2,1,0:T(8,128)(2,1)S(1)} %maximum_select_fusion.4, bf16[4,48,512]{2,1,0:T(8,128)(2,1)S(1)} %collective-permute-done.3, pred[]{:T(512)S(6)} %ne.14), kind=kOutput, calls=%fused_computation.37 | convolution fusion | flops 805896192 | bytes 20316160 | tf_op jit(solution)/shard_map/nsi,nij->nsj/dot_general | solution.py:132
  46.2 3.1 %fusion.63 = f32[8,48,2048]{2,1,0:T(8,128)S(1)} fusion(f32[8,48,2048]{2,1,0:T(8,128)S(1)} %fusion.25, f32[8,48]{1,0:T(8,128)S(1)} %fusion.64, f32[48,48]{1,0:T(8,128)S(1)} %get-tuple-element.95, f32[48,48]{1,0:T(8,128)S(1)} %get-tuple-element.94, pred[8]{0:T(512)(128)(4,1)S(1)} %broadcast_compare_fusion), kind=kOutput, calls=%fused_computation.102 | convolution fusion | flops 453021696 | bytes 6311432 | tf_op jit(solution)/shard_map/nsr,nsj->nrj/dot_general | solution.py:166
  49.3 3.3 %fusion.10 = f32[2,48,2048]{2,0,1:T(2,128)S(1)} fusion(f32[8,48,2048]{2,1,0:T(8,128)S(1)} %fusion.63, s32[8]{0:T(128)S(1)} %get-tuple-element.69), kind=kOutput, calls=%fused_computation.15 | convolution fusion | flops 18874384 | bytes 3932192 | tf_op jit(solution)/shard_map/nh,nrj->hrj/dot_general | solution.py:170
  52.8 1.4 collective-permute-start.4
  54.3 2.4 %collective-permute-start.5 = (f32[2,48,512]{2,0,1:T(2,128)S(1)}, f32[2,48,512]{2,0,1:T(2,128)S(1)}, u32[]{:S(2)}, u32[]{:S(2)}) collective-permute-start(f32[2,48,512]{2,0,1:T(2,128)S(1)} %get-tuple-element.86), channel_id=1, source_target_pairs={{0,64},{4,68},{8,72},{12,76},{16,80},{20,84},{24,88},{28,92},{32,9... | collective-permute-start | bytes 589832 | tf_op jit(solution)/shard_map/ppermute | solution.py:79
  56.9 8.8 %custom-call.7 = f32[2,48,48]{2,1,0:T(8,128)S(1)} custom-call(f32[2,48,48]{2,1,0:T(8,128)S(1)} %fusion.54), custom_call_target="Cholesky" | custom-call | tf_op jit(solution)/shard_map/jit(cholesky)/cholesky | solution.py:136
  65.8 2.1 %collective-permute-done.6 = f32[2,48,512]{2,0,1:T(2,128)S(1)} collective-permute-done((f32[2,48,512]{2,0,1:T(2,128)S(1)}, f32[2,48,512]{2,0,1:T(2,128)S(1)}, u32[]{:S(2)}, u32[]{:S(2)}) %collective-permute-start.6) | collective-permute-done | bytes 196640 | tf_op jit(solution)/shard_map/ppermute | solution.py:79
  68.2 1.7 %collective-permute-start.7 = (f32[2,48,128]{2,0,1:T(2,128)S(1)}, f32[2,48,128]{2,0,1:T(2,128)S(1)}, u32[]{:S(2)}, u32[]{:S(2)}) collective-permute-start(f32[2,48,128]{2,0,1:T(2,128)S(1)} %get-tuple-element.89), channel_id=1, source_target_pairs={{0,8},{4,12},{8,0},{12,4},{16,24},{20,28},{24,16},{28,20},{32,40},... | collective-permute-start | bytes 147464 | tf_op jit(solution)/shard_map/ppermute | solution.py:79
  70.0 3.3 %collective-permute-start.8 = (f32[2,48,128]{2,0,1:T(2,128)S(1)}, f32[2,48,128]{2,0,1:T(2,128)S(1)}, u32[]{:S(2)}, u32[]{:S(2)}) collective-permute-start(f32[2,48,128]{2,0,1:T(2,128)S(1)} %get-tuple-element.91), channel_id=1, source_target_pairs={{0,16},{4,20},{8,24},{12,28},{16,0},{20,4},{24,8},{28,12},{32,48},... | collective-permute-start | bytes 147464 | tf_op jit(solution)/shard_map/ppermute | solution.py:79
  73.3 7.4 %custom-call.8 = f32[2,1,48,48]{2,3,1,0:T(8,128)S(1)} custom-call(f32[2,1,48,48]{3,2,1,0:T(8,128)S(1)} %select_bitcast_fusion), custom_call_target="InvertDiagBlocksLowerTriangular" | custom-call | tf_op jit(solution)/shard_map/triangular_solve | solution.py:138
  80.9 3.0 %collective-permute-start.10 = (f32[2,48,64]{2,0,1:T(2,128)S(1)}, f32[2,48,64]{2,0,1:T(2,128)S(1)}, u32[]{:S(2)}, u32[]{:S(2)}) collective-permute-start(f32[2,48,64]{2,0,1:T(2,128)S(1)} %constant_dynamic-slice_fusion), channel_id=1, source_target_pairs={{0,4},{4,0},{8,12},{12,8},{16,20},{20,16},{24,28},{28,24},{32,36},... | collective-permute-start | bytes 73736 | tf_op jit(solution)/shard_map/ppermute | solution.py:79
  84.2 1.3 collective-permute-done.10
  86.0 3.0 %collective-permute-start.11 = (f32[2,48,64]{2,1,0:T(8,128)S(1)}, f32[2,48,64]{2,1,0:T(8,128)S(1)}, u32[]{:S(2)}, u32[]{:S(2)}) collective-permute-start(f32[2,48,64]{2,1,0:T(8,128)S(1)} %fusion.80), channel_id=1, source_target_pairs={{0,4},{4,0},{8,12},{12,8},{16,20},{20,16},{24,28},{28,24},{32,36},... | collective-permute-start | bytes 73736 | tf_op jit(solution)/shard_map/ppermute | solution.py:96
  89.3 1.3 collective-permute-done.11
  90.6 0.5 dynamic_update_slice.31
  91.2 3.8 %collective-permute-start.13 = (f32[2,48,128]{2,1,0:T(8,128)S(1)}, f32[2,48,128]{2,1,0:T(8,128)S(1)}, u32[]{:S(2)}, u32[]{:S(2)}) collective-permute-start(f32[2,48,128]{2,1,0:T(8,128)S(1)} %dynamic_update_slice.31), channel_id=1, source_target_pairs={{0,16},{4,20},{8,24},{12,28},{16,0},{20,4},{24,8},{28,12},{32,48},... | collective-permute-start | bytes 147464 | tf_op jit(solution)/shard_map/ppermute | solution.py:96
  95.1 1.9 %collective-permute-done.13 = f32[2,48,128]{2,1,0:T(8,128)S(1)} collective-permute-done((f32[2,48,128]{2,1,0:T(8,128)S(1)}, f32[2,48,128]{2,1,0:T(8,128)S(1)}, u32[]{:S(2)}, u32[]{:S(2)}) %collective-permute-start.13) | collective-permute-done | bytes 49184 | tf_op jit(solution)/shard_map/ppermute | solution.py:96
  97.0 2.1 %collective-permute-done.14 = f32[2,48,128]{2,1,0:T(8,128)S(1)} collective-permute-done((f32[2,48,128]{2,1,0:T(8,128)S(1)}, f32[2,48,128]{2,1,0:T(8,128)S(1)}, u32[]{:S(2)}, u32[]{:S(2)}) %collective-permute-start.14) | collective-permute-done | bytes 49184 | tf_op jit(solution)/shard_map/ppermute | solution.py:96
  99.2 1.7 %collective-permute-start.16 = (f32[2,48,512]{2,1,0:T(8,128)S(1)}, f32[2,48,512]{2,1,0:T(8,128)S(1)}, u32[]{:S(2)}, u32[]{:S(2)}) collective-permute-start(f32[2,48,512]{2,1,0:T(8,128)S(1)} %constant_dynamic-update-slice_fusion.4), channel_id=1, source_target_pairs={{0,64},{4,68},{8,72},{12,76},{16,80},{20,84},{24,88},{28,92},{32,9... | collective-permute-start | bytes 589832 | tf_op jit(solution)/shard_map/ppermute | solution.py:96
  100.8 2.2 %collective-permute-start.17 = (f32[2,48,512]{2,1,0:T(8,128)S(1)}, f32[2,48,512]{2,1,0:T(8,128)S(1)}, u32[]{:S(2)}, u32[]{:S(2)}) collective-permute-start(f32[2,48,512]{2,1,0:T(8,128)S(1)} %constant_dynamic-update-slice_fusion.4), channel_id=1, source_target_pairs={{0,96},{4,100},{8,104},{12,108},{16,112},{20,116},{24,120},{28,124... | collective-permute-start | bytes 589832 | tf_op jit(solution)/shard_map/ppermute | solution.py:96
  103.1 0.6 collective-permute-done.15
  103.7 2.4 %collective-permute-done.16 = f32[2,48,512]{2,1,0:T(8,128)S(1)} collective-permute-done((f32[2,48,512]{2,1,0:T(8,128)S(1)}, f32[2,48,512]{2,1,0:T(8,128)S(1)}, u32[]{:S(2)}, u32[]{:S(2)}) %collective-permute-start.16) | collective-permute-done | bytes 196640 | tf_op jit(solution)/shard_map/ppermute | solution.py:96
  106.1 2.0 %collective-permute-done.17 = f32[2,48,512]{2,1,0:T(8,128)S(1)} collective-permute-done((f32[2,48,512]{2,1,0:T(8,128)S(1)}, f32[2,48,512]{2,1,0:T(8,128)S(1)}, u32[]{:S(2)}, u32[]{:S(2)}) %collective-permute-start.17) | collective-permute-done | bytes 196640 | tf_op jit(solution)/shard_map/ppermute | solution.py:96
  108.2 11.2 %fusion.12 = f32[8,48,512]{2,1,0:T(8,128)S(1)} fusion(bf16[8,512,2048]{2,1,0:T(8,128)(2,1)} %param.10, f32[48,2048]{1,0:T(8,128)S(1)} %get-tuple-element.83, f32[48,2048]{1,0:T(8,128)S(1)} %get-tuple-element.82, pred[8]{0:T(512)(128)(4,1)S(1)} %broadcast_compare_fusion), kind=kOutput, calls=%fused_computation.18 | convolution fusion | flops 806092800 | bytes 18350088 | tf_op jit(solution)/shard_map/nrj,nij->nri/dot_general | solution.py:119
  119.4 7.3 %collective-permute-start.18 = (f32[4,48,512]{2,1,0:T(8,128)S(1)}, f32[4,48,512]{2,1,0:T(8,128)S(1)}, u32[]{:S(2)}, u32[]{:S(2)}) collective-permute-start(f32[4,48,512]{2,1,0:T(8,128)S(1)} %slice_select_fusion), channel_id=1, source_target_pairs={{0,1},{1,0},{2,3},{3,2},{4,5},{5,4},{6,7},{7,6},{8,9},{9,8},{10,11... | collective-permute-start | bytes 1179656 | tf_op jit(solution)/shard_map/ppermute | solution.py:44
  126.7 1.3 collective-permute-done.18
  128.2 1.4 collective-permute-start.19
  129.6 4.8 %collective-permute-done.19 = f32[2,48,512]{2,1,0:T(8,128)S(1)} collective-permute-done((f32[2,48,512]{2,1,0:T(8,128)S(1)}, f32[2,48,512]{2,1,0:T(8,128)S(1)}, u32[]{:S(2)}, u32[]{:S(2)}) %collective-permute-start.19) | collective-permute-done | bytes 196640 | tf_op jit(solution)/shard_map/ppermute | solution.py:44
  134.7 0.4 select_reduce_fusion
  135.2 6.2 %while.23 = (s32[]{:T(128)}, f32[2,48,48]{1,2,0:T(8,128)S(1)}, f32[2,48,48]{2,1,0:T(8,128)S(1)}, s32[]{:T(128)}) while((s32[]{:T(128)}, f32[2,48,48]{1,2,0:T(8,128)S(1)}, f32[2,48,48]{2,1,0:T(8,128)S(1)}, s32[]{:T(128)}) %tuple.57), condition=%wide.region_9.10_spmd.clone, body=%wide.region_8.9_spmd.clone.sunk | while | flops 7976450 | bytes 221237 | solution.py:21
  141.7 1.4 collective-permute-start.20
  143.1 2.2 %collective-permute-done.20 = bf16[2,48,512]{2,1,0:T(8,128)(2,1)S(1)} collective-permute-done((bf16[2,48,512]{2,1,0:T(8,128)(2,1)S(1)}, bf16[2,48,512]{2,1,0:T(8,128)(2,1)S(1)}, u32[]{:S(2)}, u32[]{:S(2)}) %collective-permute-start.20) | collective-permute-done | bytes 98336 | tf_op jit(solution)/shard_map/ppermute | solution.py:53
  145.3 2.7 %collective-permute-start.21 = (bf16[4,48,512]{2,1,0:T(8,128)(2,1)S(1)}, bf16[4,48,512]{2,1,0:T(8,128)(2,1)S(1)}, u32[]{:S(2)}, u32[]{:S(2)}) collective-permute-start(bf16[4,48,512]{2,1,0:T(8,128)(2,1)S(1)} %maximum_select_fusion.5), channel_id=1, source_target_pairs={{0,1},{1,0},{2,3},{3,2},{4,5},{5,4},{6,7},{7,6},{8,9},{9,8},{10,11... | collective-permute-start | bytes 589832 | tf_op jit(solution)/shard_map/ppermute | solution.py:53
  148.0 2.8 %fusion.8 = f32[8,48,2048]{2,1,0:T(8,128)S(1)} fusion(f32[48,2048]{1,0:T(8,128)S(1)} %get-tuple-element.83, f32[48,2048]{1,0:T(8,128)S(1)} %get-tuple-element.82, pred[8]{0:T(512)(128)(4,1)S(1)} %broadcast_compare_fusion, f32[8,48]{1,0:T(8,128)S(1)} %fusion.65, f32[48,48]{1,0:T(8,128)S(1)} %get-tuple-element.95, f32[48,48]{1,0:T(8,128)S(1)} %get-tuple-element.94), kind=kOutput, calls=%fused_computation.12 | convolution fusion | flops 453808128 | bytes 3952136 | tf_op jit(solution)/shard_map/nrs,nsj->nrj/dot_general | solution.py:187
  150.8 10.5 %convolution_subtract_fusion.2 = f32[8,48,2048]{2,1,0:T(8,128)} fusion(f32[8,48,2048]{2,1,0:T(8,128)S(1)} %fusion.8, bf16[8,512,2048]{2,1,0:T(8,128)(2,1)} %param.10, bf16[4,48,512]{2,1,0:T(8,128)(2,1)S(1)} %maximum_select_fusion.5, bf16[4,48,512]{2,1,0:T(8,128)(2,1)S(1)} %collective-permute-done.21, pred[]{:T(512)S(6)} %ne.14), kind=kOutput, calls=%fused_computation.17 | convolution fusion | flops 806682624 | bytes 23461888 | tf_op jit(solution)/shard_map/nsi,nij->nsj/dot_general | solution.py:132
  (176 shorter events, 16.8 us)
Async XLA Ops:
  2.6 12.5 %copy-start.1 = (f32[2,48,48]{2,1,0:T(8,128)S(1)}, f32[2,48,48]{2,1,0:T(8,128)}, u32[]{:S(2)}) copy-start(f32[2,48,48]{2,1,0:T(8,128)} %param.13) | copy-start | bytes 55300
  2.6 12.8 %copy-start.2 = (f32[256,48]{0,1:T(8,128)S(1)}, f32[256,48]{0,1:T(8,128)}, u32[]{:S(2)}) copy-start(f32[256,48]{0,1:T(8,128)} %param.12) | copy-start | bytes 147460
  13.6 4.5 %copy-start.3 = (s32[256]{0:T(256)S(1)}, s32[256]{0:T(256)}, u32[]{:S(2)}) copy-start(s32[256]{0:T(256)} %param.14) | copy-start | bytes 3076
  13.7 2.8 %collective-permute-start = (f32[4,48,512]{2,1,0:T(8,128)S(1)}, f32[4,48,512]{2,1,0:T(8,128)S(1)}, u32[]{:S(2)}, u32[]{:S(2)}) collective-permute-start(f32[4,48,512]{2,1,0:T(8,128)S(1)} %slice_select_fusion.1), channel_id=1, source_target_pairs={{0,1},{1,0},{2,3},{3,2},{4,5},{5,4},{6,7},{7,6},{8,9},{9,8},{10,11... | collective-permute-start | bytes 1179656 | tf_op jit(solution)/shard_map/ppermute | solution.py:44
  16.6 6.2 %collective-permute-start.1 = (f32[2,48,512]{2,1,0:T(8,128)S(1)}, f32[2,48,512]{2,1,0:T(8,128)S(1)}, u32[]{:S(2)}, u32[]{:S(2)}) collective-permute-start(f32[2,48,512]{2,1,0:T(8,128)S(1)} %slice_select_fusion.3), channel_id=1, source_target_pairs={{0,2},{1,3},{2,0},{3,1},{4,6},{5,7},{6,4},{7,5},{8,10},{9,11},{10,... | collective-permute-start | bytes 589832 | tf_op jit(solution)/shard_map/ppermute | solution.py:44
  30.1 3.5 %collective-permute-start.2 = (bf16[2,48,512]{2,1,0:T(8,128)(2,1)S(1)}, bf16[2,48,512]{2,1,0:T(8,128)(2,1)S(1)}, u32[]{:S(2)}, u32[]{:S(2)}) collective-permute-start(bf16[2,48,512]{2,1,0:T(8,128)(2,1)S(1)} %convolution_convert_fusion.1), channel_id=1, source_target_pairs={{0,2},{1,3},{2,0},{3,1},{4,6},{5,7},{6,4},{7,5},{8,10},{9,11},{10,... | collective-permute-start | bytes 294920 | tf_op jit(solution)/shard_map/ppermute | solution.py:53
  33.7 3.7 %collective-permute-start.3 = (bf16[4,48,512]{2,1,0:T(8,128)(2,1)S(1)}, bf16[4,48,512]{2,1,0:T(8,128)(2,1)S(1)}, u32[]{:S(2)}, u32[]{:S(2)}) collective-permute-start(bf16[4,48,512]{2,1,0:T(8,128)(2,1)S(1)} %maximum_select_fusion.4), channel_id=1, source_target_pairs={{0,1},{1,0},{2,3},{3,2},{4,5},{5,4},{6,7},{7,6},{8,9},{9,8},{10,11... | collective-permute-start | bytes 589832 | tf_op jit(solution)/shard_map/ppermute | solution.py:53
  52.8 13.0 %collective-permute-start.4 = (f32[2,48,512]{2,0,1:T(2,128)S(1)}, f32[2,48,512]{2,0,1:T(2,128)S(1)}, u32[]{:S(2)}, u32[]{:S(2)}) collective-permute-start(f32[2,48,512]{2,0,1:T(2,128)S(1)} %get-tuple-element.84), channel_id=1, source_target_pairs={{0,32},{4,36},{8,40},{12,44},{16,48},{20,52},{24,56},{28,60},{32,0... | collective-permute-start | bytes 589832 | tf_op jit(solution)/shard_map/ppermute | solution.py:79
  54.3 11.6 %collective-permute-start.5 = (f32[2,48,512]{2,0,1:T(2,128)S(1)}, f32[2,48,512]{2,0,1:T(2,128)S(1)}, u32[]{:S(2)}, u32[]{:S(2)}) collective-permute-start(f32[2,48,512]{2,0,1:T(2,128)S(1)} %get-tuple-element.86), channel_id=1, source_target_pairs={{0,64},{4,68},{8,72},{12,76},{16,80},{20,84},{24,88},{28,92},{32,9... | collective-permute-start | bytes 589832 | tf_op jit(solution)/shard_map/ppermute | solution.py:79
  56.7 11.3 %collective-permute-start.6 = (f32[2,48,512]{2,0,1:T(2,128)S(1)}, f32[2,48,512]{2,0,1:T(2,128)S(1)}, u32[]{:S(2)}, u32[]{:S(2)}) collective-permute-start(f32[2,48,512]{2,0,1:T(2,128)S(1)} %get-tuple-element.85), channel_id=1, source_target_pairs={{0,96},{4,100},{8,104},{12,108},{16,112},{20,116},{24,120},{28,124... | collective-permute-start | bytes 589832 | tf_op jit(solution)/shard_map/ppermute | solution.py:79
  68.2 12.5 %collective-permute-start.7 = (f32[2,48,128]{2,0,1:T(2,128)S(1)}, f32[2,48,128]{2,0,1:T(2,128)S(1)}, u32[]{:S(2)}, u32[]{:S(2)}) collective-permute-start(f32[2,48,128]{2,0,1:T(2,128)S(1)} %get-tuple-element.89), channel_id=1, source_target_pairs={{0,8},{4,12},{8,0},{12,4},{16,24},{20,28},{24,16},{28,20},{32,40},... | collective-permute-start | bytes 147464 | tf_op jit(solution)/shard_map/ppermute | solution.py:79
  70.0 10.8 %collective-permute-start.8 = (f32[2,48,128]{2,0,1:T(2,128)S(1)}, f32[2,48,128]{2,0,1:T(2,128)S(1)}, u32[]{:S(2)}, u32[]{:S(2)}) collective-permute-start(f32[2,48,128]{2,0,1:T(2,128)S(1)} %get-tuple-element.91), channel_id=1, source_target_pairs={{0,16},{4,20},{8,24},{12,28},{16,0},{20,4},{24,8},{28,12},{32,48},... | collective-permute-start | bytes 147464 | tf_op jit(solution)/shard_map/ppermute | solution.py:79
  73.3 7.5 %collective-permute-start.9 = (f32[2,48,128]{2,0,1:T(2,128)S(1)}, f32[2,48,128]{2,0,1:T(2,128)S(1)}, u32[]{:S(2)}, u32[]{:S(2)}) collective-permute-start(f32[2,48,128]{2,0,1:T(2,128)S(1)} %get-tuple-element.90), channel_id=1, source_target_pairs={{0,24},{4,28},{8,16},{12,20},{16,8},{20,12},{24,0},{28,4},{32,56},... | collective-permute-start | bytes 147464 | tf_op jit(solution)/shard_map/ppermute | solution.py:79
  80.9 4.5 %collective-permute-start.10 = (f32[2,48,64]{2,0,1:T(2,128)S(1)}, f32[2,48,64]{2,0,1:T(2,128)S(1)}, u32[]{:S(2)}, u32[]{:S(2)}) collective-permute-start(f32[2,48,64]{2,0,1:T(2,128)S(1)} %constant_dynamic-slice_fusion), channel_id=1, source_target_pairs={{0,4},{4,0},{8,12},{12,8},{16,20},{20,16},{24,28},{28,24},{32,36},... | collective-permute-start | bytes 73736 | tf_op jit(solution)/shard_map/ppermute | solution.py:79
  86.0 4.5 %collective-permute-start.11 = (f32[2,48,64]{2,1,0:T(8,128)S(1)}, f32[2,48,64]{2,1,0:T(8,128)S(1)}, u32[]{:S(2)}, u32[]{:S(2)}) collective-permute-start(f32[2,48,64]{2,1,0:T(8,128)S(1)} %fusion.80), channel_id=1, source_target_pairs={{0,4},{4,0},{8,12},{12,8},{16,20},{20,16},{24,28},{28,24},{32,36},... | collective-permute-start | bytes 73736 | tf_op jit(solution)/shard_map/ppermute | solution.py:96
  91.1 4.0 %collective-permute-start.12 = (f32[2,48,128]{2,1,0:T(8,128)S(1)}, f32[2,48,128]{2,1,0:T(8,128)S(1)}, u32[]{:S(2)}, u32[]{:S(2)}) collective-permute-start(f32[2,48,128]{2,1,0:T(8,128)S(1)} %dynamic_update_slice.31), channel_id=1, source_target_pairs={{0,8},{4,12},{8,0},{12,4},{16,24},{20,28},{24,16},{28,20},{32,40},... | collective-permute-start | bytes 147464 | tf_op jit(solution)/shard_map/ppermute | solution.py:96
  91.2 5.8 %collective-permute-start.13 = (f32[2,48,128]{2,1,0:T(8,128)S(1)}, f32[2,48,128]{2,1,0:T(8,128)S(1)}, u32[]{:S(2)}, u32[]{:S(2)}) collective-permute-start(f32[2,48,128]{2,1,0:T(8,128)S(1)} %dynamic_update_slice.31), channel_id=1, source_target_pairs={{0,16},{4,20},{8,24},{12,28},{16,0},{20,4},{24,8},{28,12},{32,48},... | collective-permute-start | bytes 147464 | tf_op jit(solution)/shard_map/ppermute | solution.py:96
  95.0 4.2 %collective-permute-start.14 = (f32[2,48,128]{2,1,0:T(8,128)S(1)}, f32[2,48,128]{2,1,0:T(8,128)S(1)}, u32[]{:S(2)}, u32[]{:S(2)}) collective-permute-start(f32[2,48,128]{2,1,0:T(8,128)S(1)} %dynamic_update_slice.31), channel_id=1, source_target_pairs={{0,24},{4,28},{8,16},{12,20},{16,8},{20,12},{24,0},{28,4},{32,56},... | collective-permute-start | bytes 147464 | tf_op jit(solution)/shard_map/ppermute | solution.py:96
  99.2 4.5 %collective-permute-start.15 = (f32[2,48,512]{2,1,0:T(8,128)S(1)}, f32[2,48,512]{2,1,0:T(8,128)S(1)}, u32[]{:S(2)}, u32[]{:S(2)}) collective-permute-start(f32[2,48,512]{2,1,0:T(8,128)S(1)} %constant_dynamic-update-slice_fusion.4), channel_id=1, source_target_pairs={{0,32},{4,36},{8,40},{12,44},{16,48},{20,52},{24,56},{28,60},{32,0... | collective-permute-start | bytes 589832 | tf_op jit(solution)/shard_map/ppermute | solution.py:96
  99.2 6.9 %collective-permute-start.16 = (f32[2,48,512]{2,1,0:T(8,128)S(1)}, f32[2,48,512]{2,1,0:T(8,128)S(1)}, u32[]{:S(2)}, u32[]{:S(2)}) collective-permute-start(f32[2,48,512]{2,1,0:T(8,128)S(1)} %constant_dynamic-update-slice_fusion.4), channel_id=1, source_target_pairs={{0,64},{4,68},{8,72},{12,76},{16,80},{20,84},{24,88},{28,92},{32,9... | collective-permute-start | bytes 589832 | tf_op jit(solution)/shard_map/ppermute | solution.py:96
  100.8 7.3 %collective-permute-start.17 = (f32[2,48,512]{2,1,0:T(8,128)S(1)}, f32[2,48,512]{2,1,0:T(8,128)S(1)}, u32[]{:S(2)}, u32[]{:S(2)}) collective-permute-start(f32[2,48,512]{2,1,0:T(8,128)S(1)} %constant_dynamic-update-slice_fusion.4), channel_id=1, source_target_pairs={{0,96},{4,100},{8,104},{12,108},{16,112},{20,116},{24,120},{28,124... | collective-permute-start | bytes 589832 | tf_op jit(solution)/shard_map/ppermute | solution.py:96
  108.1 11.2 %copy-start = (f32[2,48,2048]{2,1,0:T(8,128)}, f32[2,48,2048]{2,1,0:T(8,128)S(1)}, u32[]{:S(2)}) copy-start(f32[2,48,2048]{2,1,0:T(8,128)S(1)} %constant_dynamic-update-slice_fusion) | copy-start | bytes 2359300
  119.4 8.6 %collective-permute-start.18 = (f32[4,48,512]{2,1,0:T(8,128)S(1)}, f32[4,48,512]{2,1,0:T(8,128)S(1)}, u32[]{:S(2)}, u32[]{:S(2)}) collective-permute-start(f32[4,48,512]{2,1,0:T(8,128)S(1)} %slice_select_fusion), channel_id=1, source_target_pairs={{0,1},{1,0},{2,3},{3,2},{4,5},{5,4},{6,7},{7,6},{8,9},{9,8},{10,11... | collective-permute-start | bytes 1179656 | tf_op jit(solution)/shard_map/ppermute | solution.py:44
  128.2 6.2 %collective-permute-start.19 = (f32[2,48,512]{2,1,0:T(8,128)S(1)}, f32[2,48,512]{2,1,0:T(8,128)S(1)}, u32[]{:S(2)}, u32[]{:S(2)}) collective-permute-start(f32[2,48,512]{2,1,0:T(8,128)S(1)} %slice_select_fusion.2), channel_id=1, source_target_pairs={{0,2},{1,3},{2,0},{3,1},{4,6},{5,7},{6,4},{7,5},{8,10},{9,11},{10,... | collective-permute-start | bytes 589832 | tf_op jit(solution)/shard_map/ppermute | solution.py:44
  141.7 3.5 %collective-permute-start.20 = (bf16[2,48,512]{2,1,0:T(8,128)(2,1)S(1)}, bf16[2,48,512]{2,1,0:T(8,128)(2,1)S(1)}, u32[]{:S(2)}, u32[]{:S(2)}) collective-permute-start(bf16[2,48,512]{2,1,0:T(8,128)(2,1)S(1)} %convolution_convert_fusion), channel_id=1, source_target_pairs={{0,2},{1,3},{2,0},{3,1},{4,6},{5,7},{6,4},{7,5},{8,10},{9,11},{10,... | collective-permute-start | bytes 294920 | tf_op jit(solution)/shard_map/ppermute | solution.py:53
  145.3 5.5 %collective-permute-start.21 = (bf16[4,48,512]{2,1,0:T(8,128)(2,1)S(1)}, bf16[4,48,512]{2,1,0:T(8,128)(2,1)S(1)}, u32[]{:S(2)}, u32[]{:S(2)}) collective-permute-start(bf16[4,48,512]{2,1,0:T(8,128)(2,1)S(1)} %maximum_select_fusion.5), channel_id=1, source_target_pairs={{0,1},{1,0},{2,3},{3,2},{4,5},{5,4},{6,7},{7,6},{8,9},{9,8},{10,11... | collective-permute-start | bytes 589832 | tf_op jit(solution)/shard_map/ppermute | solution.py:53

commit v5 on v4

--- a/solution.py
+++ b/solution.py
@@ -12,10 +12,10 @@
     start = eye_rank[None] / jnp.sqrt(traces + 1e-06)[:, None, None]
 
     def advance(step, factor):
-        left = jnp.einsum("nrs,nrt->nst", factor, gram, precision=lax.Precision.HIGHEST)
-        inner = jnp.einsum("nst,ntu->nsu", left, factor, precision=lax.Precision.HIGHEST)
+        left = jnp.einsum("nrs,nrt->nst", factor, gram, precision=lax.Precision.HIGH)
+        inner = jnp.einsum("nst,ntu->nsu", left, factor, precision=lax.Precision.HIGH)
         return 0.5 * jnp.einsum(
-            "nrs,nsu->nru", factor, 3.0 * eye_rank[None] - inner, precision=lax.Precision.HIGHEST
+            "nrs,nsu->nru", factor, 3.0 * eye_rank[None] - inner, precision=lax.Precision.HIGH
         )
 
     return lax.fori_loop(0, NS_STEPS, advance, start)
@@ -116,10 +116,14 @@
 
 def project_body(slices, rows_low, mixed, chan_size, chan_bits):
     run_count = slices.shape[0]
+    scatter_bits, reduce_bits = chan_bits
     partial_basis = jnp.einsum("nrj,nij->nri", rows_low, slices, preferred_element_type=jnp.float32)
-    basis = halving_scatter(partial_basis, "chan", chan_size, chan_bits, 0)
+    basis = halving_scatter(partial_basis, "chan", chan_size, scatter_bits, 0)
+    for bit in reduce_bits:
+        got = lax.ppermute(basis, "chan", xor_pairs(chan_size, bit))
+        basis = basis + got
     part = basis.shape[0]
-    first = block_index("chan", chan_bits) * part
+    first = block_index("chan", scatter_bits) * part
     mixed_part = lax.dynamic_slice_in_dim(mixed, first, part, axis=0)
     scaled = jnp.einsum("nrs,nsi->nri", mixed_part, basis, precision=lax.Precision.HIGHEST)
     gram = jnp.einsum("nri,nsi->nrs", scaled, scaled, precision=lax.Precision.HIGHEST)
@@ -127,7 +131,7 @@
     rotated = jnp.einsum("nrs,nri->nsi", factor, scaled, precision=lax.Precision.HIGHEST).astype(
         jnp.bfloat16
     )
-    rotated = doubling_gather(rotated, "chan", chan_size, chan_bits, 0)
+    rotated = doubling_gather(rotated, "chan", chan_size, scatter_bits, 0)
     del run_count
     return jnp.einsum("nsi,nij->nsj", rotated, slices, preferred_element_type=jnp.float32)
 
@@ -145,7 +149,8 @@
 
 def make_body(runs_size, chan_size):
     runs_groups = radix_groups(runs_size, [(8, 16), (2, 4), (1,)])
-    chan_bits = step_bits(chan_size, (1, 2))
+    chan_all = step_bits(chan_size, (1, 2))
+    chan_bits = (chan_all[:1], chan_all[1:])
 
     def layer(slices, spectra, loadings, mixing, halves, partner):
         run_count = slices.shape[0]
@@ -163,12 +168,12 @@
         own_rows = jnp.where(first_half, spectra[0][None], spectra[1][None])
         own_mix = jnp.where(first_half, mixing[0][None], mixing[1][None]) * my_loads[:, None, :]
         projected = project_body(slices, own_rows, own_mix, chan_size, chan_bits)
-        terms = jnp.einsum("nsr,nsj->nrj", own_mix, projected, precision=lax.Precision.HIGHEST)
         mine_member = (my_halves[:, None] == jnp.arange(2, dtype=jnp.int32)[None, :]).astype(
             jnp.float32
         )
+        weights = mine_member[:, :, None, None] * own_mix[:, None, :, :]
         partial_moments = jnp.einsum(
-            "nh,nrj->hrj", mine_member, terms, precision=lax.Precision.HIGHEST
+            "nhsr,nsj->hrj", weights, projected, precision=lax.Precision.HIGHEST
         )
         member = (halves[:, None] == jnp.arange(2, dtype=jnp.int32)[None, :]).astype(jnp.float32)
         cross = jnp.einsum("kh,kr,ks->hrs", member, loadings, loadings, precision=lax.Precision.HIGHEST)

time: 162 us -> 156 us (0.963)
  starting transfers between devices: 42.6 us -> 37.1 us
  waiting for transfers between devices: 30 us -> 33.9 us
  matrix products: 65.2 us -> 62.3 us
    ppermute x0 -> x2, waiting for transfers between devices: none -> 17.3 us  [project_body(): got = lax.ppermute(basis, 'chan', xor_pairs(chan_size, bit))]
    ppermute x4 -> x2, waiting for transfers between devices: 11.3 us -> 1.9 us  [halving_scatter(): got = lax.ppermute(send, axis, xor_pairs(size, bit))]
    ppermute x4 -> x2, starting transfers between devices: 8.22 us -> 2.83 us  [doubling_gather(): got = lax.ppermute(x, axis, xor_pairs(size, bit))]
    ppermute x4 -> x2, waiting for transfers between devices: 4.99 us -> 1.07 us  [doubling_gather(): got = lax.ppermute(x, axis, xor_pairs(size, bit))]
    dot_general x42 -> x41, matrix products: 13.8 us -> 9.9 us  [the longest x20 3.98 us: advance(): jnp.einsum('nst,ntu->nsu', left, factor, precision=lax.Precision.HIGH)]
    ppermute x4 -> x2, starting transfers between devices: 11.6 us -> 8.75 us  [halving_scatter(): got = lax.ppermute(send, axis, xor_pairs(size, bit))]
    ppermute x0 -> x2, starting transfers between devices: none -> 2.86 us  [project_body(): got = lax.ppermute(basis, 'chan', xor_pairs(chan_size, bit))]
  transfers between devices with their start and end apart: 22 -> 20, of which waited for: 15 -> 13; matrix products, arithmetic and copies ran while one was open for 13% -> 14% of each run, Pallas kernels for 0% -> 0%
where the time goes in v5:
time: 156 us
  matrix products  62.3 us (40%)
  starting transfers between devices  37.1 us (24%)
  waiting for transfers between devices  33.9 us (22%)
  other arithmetic  18.2 us (12%)
  local copies, waits for them, and re-layouts  2.65 us (2%)
    dot_general x2, matrix products, project_body(): jnp.einsum('nrj,nij->nri', rows_low, slices, preferred_element_type=jnp.f...  22.1 us
    dot_general x2, matrix products, project_body(): jnp.einsum('nsi,nij->nsj', rotated, slices, preferred_element_type=jnp.fl...  19.2 us
    ppermute x2, waiting for transfers between devices, project_body(): got = lax.ppermute(basis, 'chan', xor_pairs(chan_size, bit))  17.3 us
    ppermute x7, starting transfers between devices, radix_scatter(): got = lax.ppermute(send, axis, xor_pairs(size, mask))  11.9 us
    ppermute x7, starting transfers between devices, radix_gather(): got = lax.ppermute(x, axis, xor_pairs(size, mask))  10.8 us
    ppermute x7, waiting for transfers between devices, radix_gather(): got = lax.ppermute(x, axis, xor_pairs(size, mask))  10.3 us
    another operation x4, other arithmetic, lower_inverse(): lower = jnp.linalg.cholesky(system)  8.96 us
    ppermute x2, starting transfers between devices, halving_scatter(): got = lax.ppermute(send, axis, xor_pairs(size, bit))  8.75 us
  transfers between devices with their start and end apart: 20, of which 13 were waited for; matrix products, arithmetic and copies ran while one was open for 14% of the time, Pallas kernels for 0%

profile of v5, /device:TPU:1, one launch (start us, length us, event | category | flops | bytes accessed | tf_op | source)
XLA Modules:
  0.0 156.2 jit_solution(3289015331377756509)
XLA Ops:
  0.6 0.9 select_reduce_fusion.3
  1.6 1.1 slice_bitcast_fusion.3
  2.7 11.0 %fusion.20 = f32[8,48,512]{2,1,0:T(8,128)S(1)} fusion(bf16[8,512,2048]{2,1,0:T(8,128)(2,1)} %param.10, pred[8]{0:T(512)(128)(4,1)S(1)} %broadcast_compare_fusion, bf16[48,2048]{1,0:T(8,128)(2,1)S(1)} %get-tuple-element.88, bf16[48,2048]{1,0:T(8,128)(2,1)S(1)} %get-tuple-element.87), kind=kOutput, calls=%fused_computation.24 | convolution fusion | flops 806092800 | bytes 17956872 | tf_op jit(solution)/shard_map/nrj,nij->nri/dot_general | solution.py:120
  13.7 1.5 collective-permute-start
  16.0 0.5 collective-permute-done
  16.6 1.5 collective-permute-start.1
  18.4 0.3 fusion.25
  18.7 8.3 %collective-permute-done.1 = f32[4,48,512]{2,1,0:T(8,128)S(1)} collective-permute-done((f32[4,48,512]{2,1,0:T(8,128)S(1)}, f32[4,48,512]{2,1,0:T(8,128)S(1)}, u32[]{:S(2)}, u32[]{:S(2)}) %collective-permute-start.1) | collective-permute-done | bytes 393248 | tf_op jit(solution)/shard_map/ppermute | solution.py:123
  27.0 0.5 fusion.41
  27.5 0.6 select_reduce_fusion.1
  28.1 6.1 %while.22 = (s32[]{:T(128)}, f32[4,48,48]{1,2,0:T(8,128)S(1)}, f32[4,48,48]{2,1,0:T(8,128)S(1)}, s32[]{:T(128)}) while((s32[]{:T(128)}, f32[4,48,48]{1,2,0:T(8,128)S(1)}, f32[4,48,48]{2,1,0:T(8,128)S(1)}, s32[]{:T(128)}) %tuple.54), condition=%wide.region_3.4_spmd.clone, body=%wide.region_2.3_spmd.clone.sunk | while | flops 7985666 | bytes 423989 | solution.py:21
  34.3 0.5 convolution_convert_fusion.1
  34.7 1.3 collective-permute-start.2
  36.0 1.1 collective-permute-done.2
  37.1 8.8 %fusion.28 = f32[8,48,2048]{2,1,0:T(8,128)S(1)} fusion(bf16[8,512,2048]{2,1,0:T(8,128)(2,1)} %param.10, bf16[4,48,512]{2,1,0:T(8,128)(2,1)S(1)} %convolution_convert_fusion.1, bf16[4,48,512]{2,1,0:T(8,128)(2,1)S(1)} %collective-permute-done.2, pred[]{:T(512)S(6)} %ne.12), kind=kOutput, calls=%fused_computation.38 | convolution fusion | flops 805896192 | bytes 20316160 | tf_op jit(solution)/shard_map/nsi,nij->nsj/dot_general | solution.py:136
  45.9 2.3 %fusion.12 = f32[2,48,2048]{2,1,0:T(8,128)S(1)} fusion(f32[8,48,2048]{2,1,0:T(8,128)S(1)} %fusion.28, f32[8,48,48]{1,2,0:T(8,128)S(1)} %copy.23, f32[8,2]{0,1:T(2,128)S(1)} %compare_convert_fusion.1), kind=kOutput, calls=%fused_computation.18 | convolution fusion | flops 906006528 | bytes 4005952 | tf_op jit(solution)/shard_map/nhsr,nsj->hrj/dot_general | solution.py:175
  48.3 1.4 collective-permute-start.3
  49.7 2.5 %collective-permute-start.4 = (f32[2,48,512]{2,1,0:T(8,128)S(1)}, f32[2,48,512]{2,1,0:T(8,128)S(1)}, u32[]{:S(2)}, u32[]{:S(2)}) collective-permute-start(f32[2,48,512]{2,1,0:T(8,128)S(1)} %get-tuple-element.86), channel_id=1, source_target_pairs={{0,64},{4,68},{8,72},{12,76},{16,80},{20,84},{24,88},{28,92},{32,9... | collective-permute-start | bytes 589832 | tf_op jit(solution)/shard_map/ppermute | solution.py:79
  52.3 8.8 %custom-call.7 = f32[2,48,48]{2,1,0:T(8,128)S(1)} custom-call(f32[2,48,48]{2,1,0:T(8,128)S(1)} %fusion.54), custom_call_target="Cholesky" | custom-call | tf_op jit(solution)/shard_map/jit(cholesky)/cholesky | solution.py:140
  61.3 2.1 %collective-permute-done.5 = f32[2,48,512]{2,1,0:T(8,128)S(1)} collective-permute-done((f32[2,48,512]{2,1,0:T(8,128)S(1)}, f32[2,48,512]{2,1,0:T(8,128)S(1)}, u32[]{:S(2)}, u32[]{:S(2)}) %collective-permute-start.5) | collective-permute-done | bytes 196640 | tf_op jit(solution)/shard_map/ppermute | solution.py:79
  63.5 1.7 %collective-permute-start.6 = (f32[2,48,128]{2,1,0:T(8,128)S(1)}, f32[2,48,128]{2,1,0:T(8,128)S(1)}, u32[]{:S(2)}, u32[]{:S(2)}) collective-permute-start(f32[2,48,128]{2,1,0:T(8,128)S(1)} %get-tuple-element.89), channel_id=1, source_target_pairs={{0,8},{4,12},{8,0},{12,4},{16,24},{20,28},{24,16},{28,20},{32,40},... | collective-permute-start | bytes 147464 | tf_op jit(solution)/shard_map/ppermute | solution.py:79
  65.3 3.3 %collective-permute-start.7 = (f32[2,48,128]{2,1,0:T(8,128)S(1)}, f32[2,48,128]{2,1,0:T(8,128)S(1)}, u32[]{:S(2)}, u32[]{:S(2)}) collective-permute-start(f32[2,48,128]{2,1,0:T(8,128)S(1)} %get-tuple-element.91), channel_id=1, source_target_pairs={{0,16},{4,20},{8,24},{12,28},{16,0},{20,4},{24,8},{28,12},{32,48},... | collective-permute-start | bytes 147464 | tf_op jit(solution)/shard_map/ppermute | solution.py:79
  68.6 7.4 %custom-call.8 = f32[2,1,48,48]{2,3,1,0:T(8,128)S(1)} custom-call(f32[2,1,48,48]{3,2,1,0:T(8,128)S(1)} %select_bitcast_fusion), custom_call_target="InvertDiagBlocksLowerTriangular" | custom-call | tf_op jit(solution)/shard_map/triangular_solve | solution.py:142
  76.2 2.9 %collective-permute-start.9 = (f32[2,48,64]{2,1,0:T(8,128)S(1)}, f32[2,48,64]{2,1,0:T(8,128)S(1)}, u32[]{:S(2)}, u32[]{:S(2)}) collective-permute-start(f32[2,48,64]{2,1,0:T(8,128)S(1)} %constant_dynamic-slice_fusion), channel_id=1, source_target_pairs={{0,4},{4,0},{8,12},{12,8},{16,20},{20,16},{24,28},{28,24},{32,36},... | collective-permute-start | bytes 73736 | tf_op jit(solution)/shard_map/ppermute | solution.py:79
  79.4 1.3 collective-permute-done.9
  81.2 3.0 %collective-permute-start.10 = (f32[2,48,64]{2,1,0:T(8,128)S(1)}, f32[2,48,64]{2,1,0:T(8,128)S(1)}, u32[]{:S(2)}, u32[]{:S(2)}) collective-permute-start(f32[2,48,64]{2,1,0:T(8,128)S(1)} %fusion.75), channel_id=1, source_target_pairs={{0,4},{4,0},{8,12},{12,8},{16,20},{20,16},{24,28},{28,24},{32,36},... | collective-permute-start | bytes 73736 | tf_op jit(solution)/shard_map/ppermute | solution.py:96
  84.4 1.3 collective-permute-done.10
  85.7 0.5 dynamic_update_slice.31
  86.3 3.8 %collective-permute-start.12 = (f32[2,48,128]{2,1,0:T(8,128)S(1)}, f32[2,48,128]{2,1,0:T(8,128)S(1)}, u32[]{:S(2)}, u32[]{:S(2)}) collective-permute-start(f32[2,48,128]{2,1,0:T(8,128)S(1)} %dynamic_update_slice.31), channel_id=1, source_target_pairs={{0,16},{4,20},{8,24},{12,28},{16,0},{20,4},{24,8},{28,12},{32,48},... | collective-permute-start | bytes 147464 | tf_op jit(solution)/shard_map/ppermute | solution.py:96
  90.2 1.9 %collective-permute-done.12 = f32[2,48,128]{2,1,0:T(8,128)S(1)} collective-permute-done((f32[2,48,128]{2,1,0:T(8,128)S(1)}, f32[2,48,128]{2,1,0:T(8,128)S(1)}, u32[]{:S(2)}, u32[]{:S(2)}) %collective-permute-start.12) | collective-permute-done | bytes 49184 | tf_op jit(solution)/shard_map/ppermute | solution.py:96
  92.1 2.1 %collective-permute-done.13 = f32[2,48,128]{2,1,0:T(8,128)S(1)} collective-permute-done((f32[2,48,128]{2,1,0:T(8,128)S(1)}, f32[2,48,128]{2,1,0:T(8,128)S(1)}, u32[]{:S(2)}, u32[]{:S(2)}) %collective-permute-start.13) | collective-permute-done | bytes 49184 | tf_op jit(solution)/shard_map/ppermute | solution.py:96
  94.3 1.6 %collective-permute-start.15 = (f32[2,48,512]{2,1,0:T(8,128)S(1)}, f32[2,48,512]{2,1,0:T(8,128)S(1)}, u32[]{:S(2)}, u32[]{:S(2)}) collective-permute-start(f32[2,48,512]{2,1,0:T(8,128)S(1)} %constant_dynamic-update-slice_fusion.4), channel_id=1, source_target_pairs={{0,64},{4,68},{8,72},{12,76},{16,80},{20,84},{24,88},{28,92},{32,9... | collective-permute-start | bytes 589832 | tf_op jit(solution)/shard_map/ppermute | solution.py:96
  95.9 2.2 %collective-permute-start.16 = (f32[2,48,512]{2,1,0:T(8,128)S(1)}, f32[2,48,512]{2,1,0:T(8,128)S(1)}, u32[]{:S(2)}, u32[]{:S(2)}) collective-permute-start(f32[2,48,512]{2,1,0:T(8,128)S(1)} %constant_dynamic-update-slice_fusion.4), channel_id=1, source_target_pairs={{0,96},{4,100},{8,104},{12,108},{16,112},{20,116},{24,120},{28,124... | collective-permute-start | bytes 589832 | tf_op jit(solution)/shard_map/ppermute | solution.py:96
  98.2 0.6 collective-permute-done.14
  98.8 2.4 %collective-permute-done.15 = f32[2,48,512]{2,1,0:T(8,128)S(1)} collective-permute-done((f32[2,48,512]{2,1,0:T(8,128)S(1)}, f32[2,48,512]{2,1,0:T(8,128)S(1)}, u32[]{:S(2)}, u32[]{:S(2)}) %collective-permute-start.15) | collective-permute-done | bytes 196640 | tf_op jit(solution)/shard_map/ppermute | solution.py:96
  101.2 2.0 %collective-permute-done.16 = f32[2,48,512]{2,1,0:T(8,128)S(1)} collective-permute-done((f32[2,48,512]{2,1,0:T(8,128)S(1)}, f32[2,48,512]{2,1,0:T(8,128)S(1)}, u32[]{:S(2)}, u32[]{:S(2)}) %collective-permute-start.16) | collective-permute-done | bytes 196640 | tf_op jit(solution)/shard_map/ppermute | solution.py:96
  103.3 11.2 %fusion.15 = f32[8,48,512]{2,1,0:T(8,128)S(1)} fusion(bf16[8,512,2048]{2,1,0:T(8,128)(2,1)} %param.10, f32[48,2048]{1,0:T(8,128)S(1)} %get-tuple-element.83, f32[48,2048]{1,0:T(8,128)S(1)} %get-tuple-element.82, pred[8]{0:T(512)(128)(4,1)S(1)} %broadcast_compare_fusion), kind=kOutput, calls=%fused_computation.19 | convolution fusion | flops 806092800 | bytes 18350088 | tf_op jit(solution)/shard_map/nrj,nij->nri/dot_general | solution.py:120
  114.5 7.3 %collective-permute-start.17 = (f32[4,48,512]{2,1,0:T(8,128)S(1)}, f32[4,48,512]{2,1,0:T(8,128)S(1)}, u32[]{:S(2)}, u32[]{:S(2)}) collective-permute-start(f32[4,48,512]{2,1,0:T(8,128)S(1)} %slice_select_fusion), channel_id=1, source_target_pairs={{0,1},{1,0},{2,3},{3,2},{4,5},{5,4},{6,7},{7,6},{8,9},{9,8},{10,11... | collective-permute-start | bytes 1179656 | tf_op jit(solution)/shard_map/ppermute | solution.py:44
  121.8 1.3 collective-permute-done.17
  123.3 1.4 collective-permute-start.18
  124.6 9.0 %collective-permute-done.18 = f32[4,48,512]{2,1,0:T(8,128)S(1)} collective-permute-done((f32[4,48,512]{2,1,0:T(8,128)S(1)}, f32[4,48,512]{2,1,0:T(8,128)S(1)}, u32[]{:S(2)}, u32[]{:S(2)}) %collective-permute-start.18) | collective-permute-done | bytes 393248 | tf_op jit(solution)/shard_map/ppermute | solution.py:123
  133.6 0.5 fusion.39
  134.1 0.6 select_reduce_fusion
  134.8 6.1 %while.23 = (s32[]{:T(128)}, f32[4,48,48]{1,2,0:T(8,128)S(1)}, f32[4,48,48]{2,1,0:T(8,128)S(1)}, s32[]{:T(128)}) while((s32[]{:T(128)}, f32[4,48,48]{1,2,0:T(8,128)S(1)}, f32[4,48,48]{2,1,0:T(8,128)S(1)}, s32[]{:T(128)}) %tuple.57), condition=%wide.region_9.10_spmd.clone, body=%wide.region_8.9_spmd.clone.sunk | while | flops 7985666 | bytes 423989 | solution.py:21
  140.9 0.5 convolution_convert_fusion
  141.4 1.5 collective-permute-start.19
  142.9 2.8 %fusion.8 = f32[8,48,2048]{2,1,0:T(8,128)S(1)} fusion(f32[48,2048]{1,0:T(8,128)S(1)} %get-tuple-element.83, f32[48,2048]{1,0:T(8,128)S(1)} %get-tuple-element.82, pred[8]{0:T(512)(128)(4,1)S(1)} %broadcast_compare_fusion, f32[8,48]{1,0:T(8,128)S(1)} %fusion.63, f32[48,48]{1,0:T(8,128)S(1)} %get-tuple-element.95, f32[48,48]{1,0:T(8,128)S(1)} %get-tuple-element.94), kind=kOutput, calls=%fused_computation.12 | convolution fusion | flops 453808128 | bytes 3952136 | tf_op jit(solution)/shard_map/nrs,nsj->nrj/dot_general | solution.py:192
  145.7 10.5 %convolution_subtract_fusion.2 = f32[8,48,2048]{2,1,0:T(8,128)} fusion(f32[8,48,2048]{2,1,0:T(8,128)S(1)} %fusion.8, bf16[8,512,2048]{2,1,0:T(8,128)(2,1)} %param.10, bf16[4,48,512]{2,1,0:T(8,128)(2,1)S(1)} %convolution_convert_fusion, bf16[4,48,512]{2,1,0:T(8,128)(2,1)S(1)} %collective-permute-done.19, pred[]{:T(512)S(6)} %ne.12), kind=kOutput, calls=%fused_computation.17 | convolution fusion | flops 806682624 | bytes 23461888 | tf_op jit(solution)/shard_map/nsi,nij->nsj/dot_general | solution.py:136
  (168 shorter events, 15.0 us)
Async XLA Ops:
  2.6 12.5 %copy-start.1 = (f32[2,48,48]{2,1,0:T(8,128)S(1)}, f32[2,48,48]{2,1,0:T(8,128)}, u32[]{:S(2)}) copy-start(f32[2,48,48]{2,1,0:T(8,128)} %param.13) | copy-start | bytes 55300
  2.6 12.8 %copy-start.2 = (f32[256,48]{0,1:T(8,128)S(1)}, f32[256,48]{0,1:T(8,128)}, u32[]{:S(2)}) copy-start(f32[256,48]{0,1:T(8,128)} %param.12) | copy-start | bytes 147460
  2.6 13.2 %copy-start.3 = (s32[256]{0:T(256)S(1)}, s32[256]{0:T(256)}, u32[]{:S(2)}) copy-start(s32[256]{0:T(256)} %param.14) | copy-start | bytes 3076
  13.7 2.8 %collective-permute-start = (f32[4,48,512]{2,1,0:T(8,128)S(1)}, f32[4,48,512]{2,1,0:T(8,128)S(1)}, u32[]{:S(2)}, u32[]{:S(2)}) collective-permute-start(f32[4,48,512]{2,1,0:T(8,128)S(1)} %slice_select_fusion.1), channel_id=1, source_target_pairs={{0,1},{1,0},{2,3},{3,2},{4,5},{5,4},{6,7},{7,6},{8,9},{9,8},{10,11... | collective-permute-start | bytes 1179656 | tf_op jit(solution)/shard_map/ppermute | solution.py:44
  16.6 10.4 %collective-permute-start.1 = (f32[4,48,512]{2,1,0:T(8,128)S(1)}, f32[4,48,512]{2,1,0:T(8,128)S(1)}, u32[]{:S(2)}, u32[]{:S(2)}) collective-permute-start(f32[4,48,512]{2,1,0:T(8,128)S(1)} %select_add_fusion.1), channel_id=1, source_target_pairs={{0,2},{1,3},{2,0},{3,1},{4,6},{5,7},{6,4},{7,5},{8,10},{9,11},{10,... | collective-permute-start | bytes 1179656 | tf_op jit(solution)/shard_map/ppermute | solution.py:123
  34.7 2.4 %collective-permute-start.2 = (bf16[4,48,512]{2,1,0:T(8,128)(2,1)S(1)}, bf16[4,48,512]{2,1,0:T(8,128)(2,1)S(1)}, u32[]{:S(2)}, u32[]{:S(2)}) collective-permute-start(bf16[4,48,512]{2,1,0:T(8,128)(2,1)S(1)} %convolution_convert_fusion.1), channel_id=1, source_target_pairs={{0,1},{1,0},{2,3},{3,2},{4,5},{5,4},{6,7},{7,6},{8,9},{9,8},{10,11... | collective-permute-start | bytes 589832 | tf_op jit(solution)/shard_map/ppermute | solution.py:53
  48.3 13.0 %collective-permute-start.3 = (f32[2,48,512]{2,1,0:T(8,128)S(1)}, f32[2,48,512]{2,1,0:T(8,128)S(1)}, u32[]{:S(2)}, u32[]{:S(2)}) collective-permute-start(f32[2,48,512]{2,1,0:T(8,128)S(1)} %get-tuple-element.84), channel_id=1, source_target_pairs={{0,32},{4,36},{8,40},{12,44},{16,48},{20,52},{24,56},{28,60},{32,0... | collective-permute-start | bytes 589832 | tf_op jit(solution)/shard_map/ppermute | solution.py:79
  49.7 11.6 %collective-permute-start.4 = (f32[2,48,512]{2,1,0:T(8,128)S(1)}, f32[2,48,512]{2,1,0:T(8,128)S(1)}, u32[]{:S(2)}, u32[]{:S(2)}) collective-permute-start(f32[2,48,512]{2,1,0:T(8,128)S(1)} %get-tuple-element.86), channel_id=1, source_target_pairs={{0,64},{4,68},{8,72},{12,76},{16,80},{20,84},{24,88},{28,92},{32,9... | collective-permute-start | bytes 589832 | tf_op jit(solution)/shard_map/ppermute | solution.py:79
  52.1 11.3 %collective-permute-start.5 = (f32[2,48,512]{2,1,0:T(8,128)S(1)}, f32[2,48,512]{2,1,0:T(8,128)S(1)}, u32[]{:S(2)}, u32[]{:S(2)}) collective-permute-start(f32[2,48,512]{2,1,0:T(8,128)S(1)} %get-tuple-element.85), channel_id=1, source_target_pairs={{0,96},{4,100},{8,104},{12,108},{16,112},{20,116},{24,120},{28,124... | collective-permute-start | bytes 589832 | tf_op jit(solution)/shard_map/ppermute | solution.py:79
  63.5 12.5 %collective-permute-start.6 = (f32[2,48,128]{2,1,0:T(8,128)S(1)}, f32[2,48,128]{2,1,0:T(8,128)S(1)}, u32[]{:S(2)}, u32[]{:S(2)}) collective-permute-start(f32[2,48,128]{2,1,0:T(8,128)S(1)} %get-tuple-element.89), channel_id=1, source_target_pairs={{0,8},{4,12},{8,0},{12,4},{16,24},{20,28},{24,16},{28,20},{32,40},... | collective-permute-start | bytes 147464 | tf_op jit(solution)/shard_map/ppermute | solution.py:79
  65.3 10.8 %collective-permute-start.7 = (f32[2,48,128]{2,1,0:T(8,128)S(1)}, f32[2,48,128]{2,1,0:T(8,128)S(1)}, u32[]{:S(2)}, u32[]{:S(2)}) collective-permute-start(f32[2,48,128]{2,1,0:T(8,128)S(1)} %get-tuple-element.91), channel_id=1, source_target_pairs={{0,16},{4,20},{8,24},{12,28},{16,0},{20,4},{24,8},{28,12},{32,48},... | collective-permute-start | bytes 147464 | tf_op jit(solution)/shard_map/ppermute | solution.py:79
  68.6 7.5 %collective-permute-start.8 = (f32[2,48,128]{2,1,0:T(8,128)S(1)}, f32[2,48,128]{2,1,0:T(8,128)S(1)}, u32[]{:S(2)}, u32[]{:S(2)}) collective-permute-start(f32[2,48,128]{2,1,0:T(8,128)S(1)} %get-tuple-element.90), channel_id=1, source_target_pairs={{0,24},{4,28},{8,16},{12,20},{16,8},{20,12},{24,0},{28,4},{32,56},... | collective-permute-start | bytes 147464 | tf_op jit(solution)/shard_map/ppermute | solution.py:79
  76.2 4.5 %collective-permute-start.9 = (f32[2,48,64]{2,1,0:T(8,128)S(1)}, f32[2,48,64]{2,1,0:T(8,128)S(1)}, u32[]{:S(2)}, u32[]{:S(2)}) collective-permute-start(f32[2,48,64]{2,1,0:T(8,128)S(1)} %constant_dynamic-slice_fusion), channel_id=1, source_target_pairs={{0,4},{4,0},{8,12},{12,8},{16,20},{20,16},{24,28},{28,24},{32,36},... | collective-permute-start | bytes 73736 | tf_op jit(solution)/shard_map/ppermute | solution.py:79
  81.2 4.5 %collective-permute-start.10 = (f32[2,48,64]{2,1,0:T(8,128)S(1)}, f32[2,48,64]{2,1,0:T(8,128)S(1)}, u32[]{:S(2)}, u32[]{:S(2)}) collective-permute-start(f32[2,48,64]{2,1,0:T(8,128)S(1)} %fusion.75), channel_id=1, source_target_pairs={{0,4},{4,0},{8,12},{12,8},{16,20},{20,16},{24,28},{28,24},{32,36},... | collective-permute-start | bytes 73736 | tf_op jit(solution)/shard_map/ppermute | solution.py:96
  86.2 4.0 %collective-permute-start.11 = (f32[2,48,128]{2,1,0:T(8,128)S(1)}, f32[2,48,128]{2,1,0:T(8,128)S(1)}, u32[]{:S(2)}, u32[]{:S(2)}) collective-permute-start(f32[2,48,128]{2,1,0:T(8,128)S(1)} %dynamic_update_slice.31), channel_id=1, source_target_pairs={{0,8},{4,12},{8,0},{12,4},{16,24},{20,28},{24,16},{28,20},{32,40},... | collective-permute-start | bytes 147464 | tf_op jit(solution)/shard_map/ppermute | solution.py:96
  86.3 5.8 %collective-permute-start.12 = (f32[2,48,128]{2,1,0:T(8,128)S(1)}, f32[2,48,128]{2,1,0:T(8,128)S(1)}, u32[]{:S(2)}, u32[]{:S(2)}) collective-permute-start(f32[2,48,128]{2,1,0:T(8,128)S(1)} %dynamic_update_slice.31), channel_id=1, source_target_pairs={{0,16},{4,20},{8,24},{12,28},{16,0},{20,4},{24,8},{28,12},{32,48},... | collective-permute-start | bytes 147464 | tf_op jit(solution)/shard_map/ppermute | solution.py:96
  90.1 4.2 %collective-permute-start.13 = (f32[2,48,128]{2,1,0:T(8,128)S(1)}, f32[2,48,128]{2,1,0:T(8,128)S(1)}, u32[]{:S(2)}, u32[]{:S(2)}) collective-permute-start(f32[2,48,128]{2,1,0:T(8,128)S(1)} %dynamic_update_slice.31), channel_id=1, source_target_pairs={{0,24},{4,28},{8,16},{12,20},{16,8},{20,12},{24,0},{28,4},{32,56},... | collective-permute-start | bytes 147464 | tf_op jit(solution)/shard_map/ppermute | solution.py:96
  94.3 4.5 %collective-permute-start.14 = (f32[2,48,512]{2,1,0:T(8,128)S(1)}, f32[2,48,512]{2,1,0:T(8,128)S(1)}, u32[]{:S(2)}, u32[]{:S(2)}) collective-permute-start(f32[2,48,512]{2,1,0:T(8,128)S(1)} %constant_dynamic-update-slice_fusion.4), channel_id=1, source_target_pairs={{0,32},{4,36},{8,40},{12,44},{16,48},{20,52},{24,56},{28,60},{32,0... | collective-permute-start | bytes 589832 | tf_op jit(solution)/shard_map/ppermute | solution.py:96
  94.3 6.9 %collective-permute-start.15 = (f32[2,48,512]{2,1,0:T(8,128)S(1)}, f32[2,48,512]{2,1,0:T(8,128)S(1)}, u32[]{:S(2)}, u32[]{:S(2)}) collective-permute-start(f32[2,48,512]{2,1,0:T(8,128)S(1)} %constant_dynamic-update-slice_fusion.4), channel_id=1, source_target_pairs={{0,64},{4,68},{8,72},{12,76},{16,80},{20,84},{24,88},{28,92},{32,9... | collective-permute-start | bytes 589832 | tf_op jit(solution)/shard_map/ppermute | solution.py:96
  95.9 7.3 %collective-permute-start.16 = (f32[2,48,512]{2,1,0:T(8,128)S(1)}, f32[2,48,512]{2,1,0:T(8,128)S(1)}, u32[]{:S(2)}, u32[]{:S(2)}) collective-permute-start(f32[2,48,512]{2,1,0:T(8,128)S(1)} %constant_dynamic-update-slice_fusion.4), channel_id=1, source_target_pairs={{0,96},{4,100},{8,104},{12,108},{16,112},{20,116},{24,120},{28,124... | collective-permute-start | bytes 589832 | tf_op jit(solution)/shard_map/ppermute | solution.py:96
  103.2 11.2 %copy-start = (f32[2,48,2048]{2,1,0:T(8,128)}, f32[2,48,2048]{2,1,0:T(8,128)S(1)}, u32[]{:S(2)}) copy-start(f32[2,48,2048]{2,1,0:T(8,128)S(1)} %constant_dynamic-update-slice_fusion) | copy-start | bytes 2359300
  114.5 8.6 %collective-permute-start.17 = (f32[4,48,512]{2,1,0:T(8,128)S(1)}, f32[4,48,512]{2,1,0:T(8,128)S(1)}, u32[]{:S(2)}, u32[]{:S(2)}) collective-permute-start(f32[4,48,512]{2,1,0:T(8,128)S(1)} %slice_select_fusion), channel_id=1, source_target_pairs={{0,1},{1,0},{2,3},{3,2},{4,5},{5,4},{6,7},{7,6},{8,9},{9,8},{10,11... | collective-permute-start | bytes 1179656 | tf_op jit(solution)/shard_map/ppermute | solution.py:44
  123.3 10.4 %collective-permute-start.18 = (f32[4,48,512]{2,1,0:T(8,128)S(1)}, f32[4,48,512]{2,1,0:T(8,128)S(1)}, u32[]{:S(2)}, u32[]{:S(2)}) collective-permute-start(f32[4,48,512]{2,1,0:T(8,128)S(1)} %select_add_fusion), channel_id=1, source_target_pairs={{0,2},{1,3},{2,0},{3,1},{4,6},{5,7},{6,4},{7,5},{8,10},{9,11},{10,... | collective-permute-start | bytes 1179656 | tf_op jit(solution)/shard_map/ppermute | solution.py:123
  141.4 4.3 %collective-permute-start.19 = (bf16[4,48,512]{2,1,0:T(8,128)(2,1)S(1)}, bf16[4,48,512]{2,1,0:T(8,128)(2,1)S(1)}, u32[]{:S(2)}, u32[]{:S(2)}) collective-permute-start(bf16[4,48,512]{2,1,0:T(8,128)(2,1)S(1)} %convolution_convert_fusion), channel_id=1, source_target_pairs={{0,1},{1,0},{2,3},{3,2},{4,5},{5,4},{6,7},{7,6},{8,9},{9,8},{10,11... | collective-permute-start | bytes 589832 | tf_op jit(solution)/shard_map/ppermute | solution.py:53

commit v6 on v4

--- a/solution.py
+++ b/solution.py
@@ -12,10 +12,10 @@
     start = eye_rank[None] / jnp.sqrt(traces + 1e-06)[:, None, None]
 
     def advance(step, factor):
-        left = jnp.einsum("nrs,nrt->nst", factor, gram, precision=lax.Precision.HIGHEST)
-        inner = jnp.einsum("nst,ntu->nsu", left, factor, precision=lax.Precision.HIGHEST)
+        left = jnp.einsum("nrs,nrt->nst", factor, gram, precision=lax.Precision.HIGH)
+        inner = jnp.einsum("nst,ntu->nsu", left, factor, precision=lax.Precision.HIGH)
         return 0.5 * jnp.einsum(
-            "nrs,nsu->nru", factor, 3.0 * eye_rank[None] - inner, precision=lax.Precision.HIGHEST
+            "nrs,nsu->nru", factor, 3.0 * eye_rank[None] - inner, precision=lax.Precision.HIGH
         )
 
     return lax.fori_loop(0, NS_STEPS, advance, start)
@@ -163,12 +163,12 @@
         own_rows = jnp.where(first_half, spectra[0][None], spectra[1][None])
         own_mix = jnp.where(first_half, mixing[0][None], mixing[1][None]) * my_loads[:, None, :]
         projected = project_body(slices, own_rows, own_mix, chan_size, chan_bits)
-        terms = jnp.einsum("nsr,nsj->nrj", own_mix, projected, precision=lax.Precision.HIGHEST)
         mine_member = (my_halves[:, None] == jnp.arange(2, dtype=jnp.int32)[None, :]).astype(
             jnp.float32
         )
+        weights = mine_member[:, :, None, None] * own_mix[:, None, :, :]
         partial_moments = jnp.einsum(
-            "nh,nrj->hrj", mine_member, terms, precision=lax.Precision.HIGHEST
+            "nhsr,nsj->hrj", weights, projected, precision=lax.Precision.HIGHEST
         )
         member = (halves[:, None] == jnp.arange(2, dtype=jnp.int32)[None, :]).astype(jnp.float32)
         cross = jnp.einsum("kh,kr,ks->hrs", member, loadings, loadings, precision=lax.Precision.HIGHEST)

time: 162 us -> 155 us (0.957)
  matrix products: 65.2 us -> 59.1 us
    dot_general x42 -> x41, matrix products: 13.8 us -> 8.27 us  [the longest x20 3.09 us: advance(): jnp.einsum('nst,ntu->nsu', left, factor, precision=lax.Precision.HIGH)]
  transfers between devices with their start and end apart: 22 -> 22, of which waited for: 15 -> 15; matrix products, arithmetic and copies ran while one was open for 13% -> 14% of each run, Pallas kernels for 0% -> 0%
where the time goes in v6:
time: 155 us; the launch traced here: 154 us
  matrix products  59.1 us (38%)
  starting transfers between devices  42.3 us (27%)
  waiting for transfers between devices  29.7 us (19%)
  other arithmetic  18.3 us (12%)
  local copies, waits for them, and re-layouts  2.63 us (2%)
    dot_general x2, matrix products, project_body(): jnp.einsum('nrj,nij->nri', rows_low, slices, preferred_element_type=jnp.f...  22.1 us
    dot_general x2, matrix products, project_body(): jnp.einsum('nsi,nij->nsj', rotated, slices, preferred_element_type=jnp.fl...  19.3 us
    ppermute x7, starting transfers between devices, radix_scatter(): got = lax.ppermute(send, axis, xor_pairs(size, mask))  11.9 us
    ppermute x4, starting transfers between devices, halving_scatter(): got = lax.ppermute(send, axis, xor_pairs(size, bit))  11.6 us
    ppermute x7, starting transfers between devices, radix_gather(): got = lax.ppermute(x, axis, xor_pairs(size, mask))  10.8 us
    ppermute x4, waiting for transfers between devices, halving_scatter(): got = lax.ppermute(send, axis, xor_pairs(size, bit))  10.8 us
    ppermute x7, waiting for transfers between devices, radix_gather(): got = lax.ppermute(x, axis, xor_pairs(size, mask))  10.3 us
    another operation x4, other arithmetic, lower_inverse(): lower = jnp.linalg.cholesky(system)  8.96 us
  transfers between devices with their start and end apart: 22, of which 15 were waited for; matrix products, arithmetic and copies ran while one was open for 14% of the time, Pallas kernels for 0%

profile of v6, /device:TPU:1, one launch (start us, length us, event | category | flops | bytes accessed | tf_op | source)
XLA Modules:
  0.0 154.2 jit_solution(3843489359794842143)
XLA Ops:
  0.6 0.9 select_reduce_fusion.3
  1.6 1.1 slice_bitcast_fusion.3
  2.7 11.0 %fusion.20 = f32[8,48,512]{2,1,0:T(8,128)S(1)} fusion(bf16[8,512,2048]{2,1,0:T(8,128)(2,1)} %param.10, pred[8]{0:T(512)(128)(4,1)S(1)} %broadcast_compare_fusion, bf16[48,2048]{1,0:T(8,128)(2,1)S(1)} %get-tuple-element.88, bf16[48,2048]{1,0:T(8,128)(2,1)S(1)} %get-tuple-element.87), kind=kOutput, calls=%fused_computation.24 | convolution fusion | flops 806092800 | bytes 17956872 | tf_op jit(solution)/shard_map/nrj,nij->nri/dot_general | solution.py:119
  13.7 1.5 collective-permute-start
  16.6 1.5 collective-permute-start.1
  18.4 4.4 %collective-permute-done.1 = f32[2,48,512]{2,1,0:T(8,128)S(1)} collective-permute-done((f32[2,48,512]{2,1,0:T(8,128)S(1)}, f32[2,48,512]{2,1,0:T(8,128)S(1)}, u32[]{:S(2)}, u32[]{:S(2)}) %collective-permute-start.1) | collective-permute-done | bytes 196640 | tf_op jit(solution)/shard_map/ppermute | solution.py:44
  22.8 0.3 fusion.45
  23.1 0.4 select_reduce_fusion.2
  23.6 5.1 %while.22 = (s32[]{:T(128)}, f32[2,48,48]{1,2,0:T(8,128)S(1)}, f32[2,48,48]{2,1,0:T(8,128)S(1)}, s32[]{:T(128)}) while((s32[]{:T(128)}, f32[2,48,48]{1,2,0:T(8,128)S(1)}, f32[2,48,48]{2,1,0:T(8,128)S(1)}, s32[]{:T(128)}) %tuple.54), condition=%wide.region_3.4_spmd.clone, body=%wide.region_2.3_spmd.clone.sunk | while | flops 3995138 | bytes 221237 | solution.py:21
  29.0 1.5 collective-permute-start.2
  30.5 2.0 %collective-permute-done.2 = bf16[2,48,512]{2,1,0:T(8,128)(2,1)S(1)} collective-permute-done((bf16[2,48,512]{2,1,0:T(8,128)(2,1)S(1)}, bf16[2,48,512]{2,1,0:T(8,128)(2,1)S(1)}, u32[]{:S(2)}, u32[]{:S(2)}) %collective-permute-start.2) | collective-permute-done | bytes 98336 | tf_op jit(solution)/shard_map/ppermute | solution.py:53
  32.6 2.5 %collective-permute-start.3 = (bf16[4,48,512]{2,1,0:T(8,128)(2,1)S(1)}, bf16[4,48,512]{2,1,0:T(8,128)(2,1)S(1)}, u32[]{:S(2)}, u32[]{:S(2)}) collective-permute-start(bf16[4,48,512]{2,1,0:T(8,128)(2,1)S(1)} %maximum_select_fusion.4), channel_id=1, source_target_pairs={{0,1},{1,0},{2,3},{3,2},{4,5},{5,4},{6,7},{7,6},{8,9},{9,8},{10,11... | collective-permute-start | bytes 589832 | tf_op jit(solution)/shard_map/ppermute | solution.py:53
  35.0 1.1 collective-permute-done.3
  36.1 8.8 %fusion.28 = f32[8,48,2048]{2,1,0:T(8,128)S(1)} fusion(bf16[8,512,2048]{2,1,0:T(8,128)(2,1)} %param.10, bf16[4,48,512]{2,1,0:T(8,128)(2,1)S(1)} %maximum_select_fusion.4, bf16[4,48,512]{2,1,0:T(8,128)(2,1)S(1)} %collective-permute-done.3, pred[]{:T(512)S(6)} %ne.14), kind=kOutput, calls=%fused_computation.38 | convolution fusion | flops 805896192 | bytes 20316160 | tf_op jit(solution)/shard_map/nsi,nij->nsj/dot_general | solution.py:132
  44.9 2.3 %fusion.12 = f32[2,48,2048]{2,1,0:T(8,128)S(1)} fusion(f32[8,48,2048]{2,1,0:T(8,128)S(1)} %fusion.28, f32[8,48,48]{1,2,0:T(8,128)S(1)} %copy.24, f32[8,2]{0,1:T(2,128)S(1)} %compare_convert_fusion.1), kind=kOutput, calls=%fused_computation.18 | convolution fusion | flops 906006528 | bytes 4005952 | tf_op jit(solution)/shard_map/nhsr,nsj->hrj/dot_general | solution.py:170
  47.3 1.4 collective-permute-start.4
  48.7 2.5 %collective-permute-start.5 = (f32[2,48,512]{2,1,0:T(8,128)S(1)}, f32[2,48,512]{2,1,0:T(8,128)S(1)}, u32[]{:S(2)}, u32[]{:S(2)}) collective-permute-start(f32[2,48,512]{2,1,0:T(8,128)S(1)} %get-tuple-element.86), channel_id=1, source_target_pairs={{0,64},{4,68},{8,72},{12,76},{16,80},{20,84},{24,88},{28,92},{32,9... | collective-permute-start | bytes 589832 | tf_op jit(solution)/shard_map/ppermute | solution.py:79
  51.3 8.8 %custom-call.7 = f32[2,48,48]{2,1,0:T(8,128)S(1)} custom-call(f32[2,48,48]{2,1,0:T(8,128)S(1)} %fusion.60), custom_call_target="Cholesky" | custom-call | tf_op jit(solution)/shard_map/jit(cholesky)/cholesky | solution.py:136
  60.3 2.1 %collective-permute-done.6 = f32[2,48,512]{2,1,0:T(8,128)S(1)} collective-permute-done((f32[2,48,512]{2,1,0:T(8,128)S(1)}, f32[2,48,512]{2,1,0:T(8,128)S(1)}, u32[]{:S(2)}, u32[]{:S(2)}) %collective-permute-start.6) | collective-permute-done | bytes 196640 | tf_op jit(solution)/shard_map/ppermute | solution.py:79
  62.6 1.7 %collective-permute-start.7 = (f32[2,48,128]{2,1,0:T(8,128)S(1)}, f32[2,48,128]{2,1,0:T(8,128)S(1)}, u32[]{:S(2)}, u32[]{:S(2)}) collective-permute-start(f32[2,48,128]{2,1,0:T(8,128)S(1)} %get-tuple-element.89), channel_id=1, source_target_pairs={{0,8},{4,12},{8,0},{12,4},{16,24},{20,28},{24,16},{28,20},{32,40},... | collective-permute-start | bytes 147464 | tf_op jit(solution)/shard_map/ppermute | solution.py:79
  64.3 3.3 %collective-permute-start.8 = (f32[2,48,128]{2,1,0:T(8,128)S(1)}, f32[2,48,128]{2,1,0:T(8,128)S(1)}, u32[]{:S(2)}, u32[]{:S(2)}) collective-permute-start(f32[2,48,128]{2,1,0:T(8,128)S(1)} %get-tuple-element.91), channel_id=1, source_target_pairs={{0,16},{4,20},{8,24},{12,28},{16,0},{20,4},{24,8},{28,12},{32,48},... | collective-permute-start | bytes 147464 | tf_op jit(solution)/shard_map/ppermute | solution.py:79
  67.7 7.4 %custom-call.8 = f32[2,1,48,48]{2,3,1,0:T(8,128)S(1)} custom-call(f32[2,1,48,48]{3,2,1,0:T(8,128)S(1)} %select_bitcast_fusion), custom_call_target="InvertDiagBlocksLowerTriangular" | custom-call | tf_op jit(solution)/shard_map/triangular_solve | solution.py:138
  75.2 2.9 %collective-permute-start.10 = (f32[2,48,64]{2,1,0:T(8,128)S(1)}, f32[2,48,64]{2,1,0:T(8,128)S(1)}, u32[]{:S(2)}, u32[]{:S(2)}) collective-permute-start(f32[2,48,64]{2,1,0:T(8,128)S(1)} %constant_dynamic-slice_fusion), channel_id=1, source_target_pairs={{0,4},{4,0},{8,12},{12,8},{16,20},{20,16},{24,28},{28,24},{32,36},... | collective-permute-start | bytes 73736 | tf_op jit(solution)/shard_map/ppermute | solution.py:79
  78.4 1.3 collective-permute-done.10
  80.2 3.0 %collective-permute-start.11 = (f32[2,48,64]{2,1,0:T(8,128)S(1)}, f32[2,48,64]{2,1,0:T(8,128)S(1)}, u32[]{:S(2)}, u32[]{:S(2)}) collective-permute-start(f32[2,48,64]{2,1,0:T(8,128)S(1)} %fusion.83), channel_id=1, source_target_pairs={{0,4},{4,0},{8,12},{12,8},{16,20},{20,16},{24,28},{28,24},{32,36},... | collective-permute-start | bytes 73736 | tf_op jit(solution)/shard_map/ppermute | solution.py:96
  83.4 1.3 collective-permute-done.11
  84.7 0.5 dynamic_update_slice.31
  85.3 3.8 %collective-permute-start.13 = (f32[2,48,128]{2,1,0:T(8,128)S(1)}, f32[2,48,128]{2,1,0:T(8,128)S(1)}, u32[]{:S(2)}, u32[]{:S(2)}) collective-permute-start(f32[2,48,128]{2,1,0:T(8,128)S(1)} %dynamic_update_slice.31), channel_id=1, source_target_pairs={{0,16},{4,20},{8,24},{12,28},{16,0},{20,4},{24,8},{28,12},{32,48},... | collective-permute-start | bytes 147464 | tf_op jit(solution)/shard_map/ppermute | solution.py:96
  89.2 1.9 %collective-permute-done.13 = f32[2,48,128]{2,1,0:T(8,128)S(1)} collective-permute-done((f32[2,48,128]{2,1,0:T(8,128)S(1)}, f32[2,48,128]{2,1,0:T(8,128)S(1)}, u32[]{:S(2)}, u32[]{:S(2)}) %collective-permute-start.13) | collective-permute-done | bytes 49184 | tf_op jit(solution)/shard_map/ppermute | solution.py:96
  91.2 2.1 %collective-permute-done.14 = f32[2,48,128]{2,1,0:T(8,128)S(1)} collective-permute-done((f32[2,48,128]{2,1,0:T(8,128)S(1)}, f32[2,48,128]{2,1,0:T(8,128)S(1)}, u32[]{:S(2)}, u32[]{:S(2)}) %collective-permute-start.14) | collective-permute-done | bytes 49184 | tf_op jit(solution)/shard_map/ppermute | solution.py:96
  93.3 1.6 %collective-permute-start.16 = (f32[2,48,512]{2,1,0:T(8,128)S(1)}, f32[2,48,512]{2,1,0:T(8,128)S(1)}, u32[]{:S(2)}, u32[]{:S(2)}) collective-permute-start(f32[2,48,512]{2,1,0:T(8,128)S(1)} %constant_dynamic-update-slice_fusion.4), channel_id=1, source_target_pairs={{0,64},{4,68},{8,72},{12,76},{16,80},{20,84},{24,88},{28,92},{32,9... | collective-permute-start | bytes 589832 | tf_op jit(solution)/shard_map/ppermute | solution.py:96
  95.0 2.2 %collective-permute-start.17 = (f32[2,48,512]{2,1,0:T(8,128)S(1)}, f32[2,48,512]{2,1,0:T(8,128)S(1)}, u32[]{:S(2)}, u32[]{:S(2)}) collective-permute-start(f32[2,48,512]{2,1,0:T(8,128)S(1)} %constant_dynamic-update-slice_fusion.4), channel_id=1, source_target_pairs={{0,96},{4,100},{8,104},{12,108},{16,112},{20,116},{24,120},{28,124... | collective-permute-start | bytes 589832 | tf_op jit(solution)/shard_map/ppermute | solution.py:96
  97.3 0.6 collective-permute-done.15
  97.8 2.4 %collective-permute-done.16 = f32[2,48,512]{2,1,0:T(8,128)S(1)} collective-permute-done((f32[2,48,512]{2,1,0:T(8,128)S(1)}, f32[2,48,512]{2,1,0:T(8,128)S(1)}, u32[]{:S(2)}, u32[]{:S(2)}) %collective-permute-start.16) | collective-permute-done | bytes 196640 | tf_op jit(solution)/shard_map/ppermute | solution.py:96
  100.2 2.0 %collective-permute-done.17 = f32[2,48,512]{2,1,0:T(8,128)S(1)} collective-permute-done((f32[2,48,512]{2,1,0:T(8,128)S(1)}, f32[2,48,512]{2,1,0:T(8,128)S(1)}, u32[]{:S(2)}, u32[]{:S(2)}) %collective-permute-start.17) | collective-permute-done | bytes 196640 | tf_op jit(solution)/shard_map/ppermute | solution.py:96
  102.3 11.2 %fusion.15 = f32[8,48,512]{2,1,0:T(8,128)S(1)} fusion(bf16[8,512,2048]{2,1,0:T(8,128)(2,1)} %param.10, f32[48,2048]{1,0:T(8,128)S(1)} %get-tuple-element.83, f32[48,2048]{1,0:T(8,128)S(1)} %get-tuple-element.82, pred[8]{0:T(512)(128)(4,1)S(1)} %broadcast_compare_fusion), kind=kOutput, calls=%fused_computation.19 | convolution fusion | flops 806092800 | bytes 18350088 | tf_op jit(solution)/shard_map/nrj,nij->nri/dot_general | solution.py:119
  113.5 7.3 %collective-permute-start.18 = (f32[4,48,512]{2,1,0:T(8,128)S(1)}, f32[4,48,512]{2,1,0:T(8,128)S(1)}, u32[]{:S(2)}, u32[]{:S(2)}) collective-permute-start(f32[4,48,512]{2,1,0:T(8,128)S(1)} %slice_select_fusion), channel_id=1, source_target_pairs={{0,1},{1,0},{2,3},{3,2},{4,5},{5,4},{6,7},{7,6},{8,9},{9,8},{10,11... | collective-permute-start | bytes 1179656 | tf_op jit(solution)/shard_map/ppermute | solution.py:44
  120.8 1.3 collective-permute-done.18
  122.3 1.4 collective-permute-start.19
  123.7 4.8 %collective-permute-done.19 = f32[2,48,512]{2,1,0:T(8,128)S(1)} collective-permute-done((f32[2,48,512]{2,1,0:T(8,128)S(1)}, f32[2,48,512]{2,1,0:T(8,128)S(1)}, u32[]{:S(2)}, u32[]{:S(2)}) %collective-permute-start.19) | collective-permute-done | bytes 196640 | tf_op jit(solution)/shard_map/ppermute | solution.py:44
  128.5 0.3 fusion.42
  128.8 0.4 select_reduce_fusion
  129.3 5.1 %while.23 = (s32[]{:T(128)}, f32[2,48,48]{1,2,0:T(8,128)S(1)}, f32[2,48,48]{2,1,0:T(8,128)S(1)}, s32[]{:T(128)}) while((s32[]{:T(128)}, f32[2,48,48]{1,2,0:T(8,128)S(1)}, f32[2,48,48]{2,1,0:T(8,128)S(1)}, s32[]{:T(128)}) %tuple.57), condition=%wide.region_9.10_spmd.clone, body=%wide.region_8.9_spmd.clone.sunk | while | flops 3995138 | bytes 221237 | solution.py:21
  134.7 1.4 collective-permute-start.20
  136.1 2.2 %collective-permute-done.20 = bf16[2,48,512]{2,1,0:T(8,128)(2,1)S(1)} collective-permute-done((bf16[2,48,512]{2,1,0:T(8,128)(2,1)S(1)}, bf16[2,48,512]{2,1,0:T(8,128)(2,1)S(1)}, u32[]{:S(2)}, u32[]{:S(2)}) %collective-permute-start.20) | collective-permute-done | bytes 98336 | tf_op jit(solution)/shard_map/ppermute | solution.py:53
  138.3 2.7 %collective-permute-start.21 = (bf16[4,48,512]{2,1,0:T(8,128)(2,1)S(1)}, bf16[4,48,512]{2,1,0:T(8,128)(2,1)S(1)}, u32[]{:S(2)}, u32[]{:S(2)}) collective-permute-start(bf16[4,48,512]{2,1,0:T(8,128)(2,1)S(1)} %maximum_select_fusion.5), channel_id=1, source_target_pairs={{0,1},{1,0},{2,3},{3,2},{4,5},{5,4},{6,7},{7,6},{8,9},{9,8},{10,11... | collective-permute-start | bytes 589832 | tf_op jit(solution)/shard_map/ppermute | solution.py:53
  141.0 2.8 %fusion.8 = f32[8,48,2048]{2,1,0:T(8,128)S(1)} fusion(f32[48,2048]{1,0:T(8,128)S(1)} %get-tuple-element.83, f32[48,2048]{1,0:T(8,128)S(1)} %get-tuple-element.82, pred[8]{0:T(512)(128)(4,1)S(1)} %broadcast_compare_fusion, f32[8,48]{1,0:T(8,128)S(1)} %fusion.71, f32[48,48]{1,0:T(8,128)S(1)} %get-tuple-element.95, f32[48,48]{1,0:T(8,128)S(1)} %get-tuple-element.94), kind=kOutput, calls=%fused_computation.12 | convolution fusion | flops 453808128 | bytes 3952136 | tf_op jit(solution)/shard_map/nrs,nsj->nrj/dot_general | solution.py:187
  143.8 10.5 %convolution_subtract_fusion.2 = f32[8,48,2048]{2,1,0:T(8,128)} fusion(f32[8,48,2048]{2,1,0:T(8,128)S(1)} %fusion.8, bf16[8,512,2048]{2,1,0:T(8,128)(2,1)} %param.10, bf16[4,48,512]{2,1,0:T(8,128)(2,1)S(1)} %maximum_select_fusion.5, bf16[4,48,512]{2,1,0:T(8,128)(2,1)S(1)} %collective-permute-done.21, pred[]{:T(512)S(6)} %ne.14), kind=kOutput, calls=%fused_computation.17 | convolution fusion | flops 806682624 | bytes 23461888 | tf_op jit(solution)/shard_map/nsi,nij->nsj/dot_general | solution.py:132
  (176 shorter events, 13.9 us)
Async XLA Ops:
  2.6 12.5 %copy-start.3 = (s32[256]{0:T(256)S(1)}, s32[256]{0:T(256)}, u32[]{:S(2)}) copy-start(s32[256]{0:T(256)} %param.14) | copy-start | bytes 3076
  2.6 12.5 %copy-start.2 = (f32[256,48]{0,1:T(8,128)S(1)}, f32[256,48]{0,1:T(8,128)}, u32[]{:S(2)}) copy-start(f32[256,48]{0,1:T(8,128)} %param.12) | copy-start | bytes 147460
  2.6 12.9 %copy-start.1 = (f32[2,48,48]{2,1,0:T(8,128)S(1)}, f32[2,48,48]{2,1,0:T(8,128)}, u32[]{:S(2)}) copy-start(f32[2,48,48]{2,1,0:T(8,128)} %param.13) | copy-start | bytes 55300
  13.7 2.8 %collective-permute-start = (f32[4,48,512]{2,1,0:T(8,128)S(1)}, f32[4,48,512]{2,1,0:T(8,128)S(1)}, u32[]{:S(2)}, u32[]{:S(2)}) collective-permute-start(f32[4,48,512]{2,1,0:T(8,128)S(1)} %slice_select_fusion.1), channel_id=1, source_target_pairs={{0,1},{1,0},{2,3},{3,2},{4,5},{5,4},{6,7},{7,6},{8,9},{9,8},{10,11... | collective-permute-start | bytes 1179656 | tf_op jit(solution)/shard_map/ppermute | solution.py:44
  16.6 6.2 %collective-permute-start.1 = (f32[2,48,512]{2,1,0:T(8,128)S(1)}, f32[2,48,512]{2,1,0:T(8,128)S(1)}, u32[]{:S(2)}, u32[]{:S(2)}) collective-permute-start(f32[2,48,512]{2,1,0:T(8,128)S(1)} %slice_select_fusion.3), channel_id=1, source_target_pairs={{0,2},{1,3},{2,0},{3,1},{4,6},{5,7},{6,4},{7,5},{8,10},{9,11},{10,... | collective-permute-start | bytes 589832 | tf_op jit(solution)/shard_map/ppermute | solution.py:44
  29.0 3.5 %collective-permute-start.2 = (bf16[2,48,512]{2,1,0:T(8,128)(2,1)S(1)}, bf16[2,48,512]{2,1,0:T(8,128)(2,1)S(1)}, u32[]{:S(2)}, u32[]{:S(2)}) collective-permute-start(bf16[2,48,512]{2,1,0:T(8,128)(2,1)S(1)} %convolution_convert_fusion.1), channel_id=1, source_target_pairs={{0,2},{1,3},{2,0},{3,1},{4,6},{5,7},{6,4},{7,5},{8,10},{9,11},{10,... | collective-permute-start | bytes 294920 | tf_op jit(solution)/shard_map/ppermute | solution.py:53
  32.6 3.5 %collective-permute-start.3 = (bf16[4,48,512]{2,1,0:T(8,128)(2,1)S(1)}, bf16[4,48,512]{2,1,0:T(8,128)(2,1)S(1)}, u32[]{:S(2)}, u32[]{:S(2)}) collective-permute-start(bf16[4,48,512]{2,1,0:T(8,128)(2,1)S(1)} %maximum_select_fusion.4), channel_id=1, source_target_pairs={{0,1},{1,0},{2,3},{3,2},{4,5},{5,4},{6,7},{7,6},{8,9},{9,8},{10,11... | collective-permute-start | bytes 589832 | tf_op jit(solution)/shard_map/ppermute | solution.py:53
  47.3 13.0 %collective-permute-start.4 = (f32[2,48,512]{2,1,0:T(8,128)S(1)}, f32[2,48,512]{2,1,0:T(8,128)S(1)}, u32[]{:S(2)}, u32[]{:S(2)}) collective-permute-start(f32[2,48,512]{2,1,0:T(8,128)S(1)} %get-tuple-element.84), channel_id=1, source_target_pairs={{0,32},{4,36},{8,40},{12,44},{16,48},{20,52},{24,56},{28,60},{32,0... | collective-permute-start | bytes 589832 | tf_op jit(solution)/shard_map/ppermute | solution.py:79
  48.7 11.6 %collective-permute-start.5 = (f32[2,48,512]{2,1,0:T(8,128)S(1)}, f32[2,48,512]{2,1,0:T(8,128)S(1)}, u32[]{:S(2)}, u32[]{:S(2)}) collective-permute-start(f32[2,48,512]{2,1,0:T(8,128)S(1)} %get-tuple-element.86), channel_id=1, source_target_pairs={{0,64},{4,68},{8,72},{12,76},{16,80},{20,84},{24,88},{28,92},{32,9... | collective-permute-start | bytes 589832 | tf_op jit(solution)/shard_map/ppermute | solution.py:79
  51.2 11.3 %collective-permute-start.6 = (f32[2,48,512]{2,1,0:T(8,128)S(1)}, f32[2,48,512]{2,1,0:T(8,128)S(1)}, u32[]{:S(2)}, u32[]{:S(2)}) collective-permute-start(f32[2,48,512]{2,1,0:T(8,128)S(1)} %get-tuple-element.85), channel_id=1, source_target_pairs={{0,96},{4,100},{8,104},{12,108},{16,112},{20,116},{24,120},{28,124... | collective-permute-start | bytes 589832 | tf_op jit(solution)/shard_map/ppermute | solution.py:79
  62.6 12.5 %collective-permute-start.7 = (f32[2,48,128]{2,1,0:T(8,128)S(1)}, f32[2,48,128]{2,1,0:T(8,128)S(1)}, u32[]{:S(2)}, u32[]{:S(2)}) collective-permute-start(f32[2,48,128]{2,1,0:T(8,128)S(1)} %get-tuple-element.89), channel_id=1, source_target_pairs={{0,8},{4,12},{8,0},{12,4},{16,24},{20,28},{24,16},{28,20},{32,40},... | collective-permute-start | bytes 147464 | tf_op jit(solution)/shard_map/ppermute | solution.py:79
  64.3 10.8 %collective-permute-start.8 = (f32[2,48,128]{2,1,0:T(8,128)S(1)}, f32[2,48,128]{2,1,0:T(8,128)S(1)}, u32[]{:S(2)}, u32[]{:S(2)}) collective-permute-start(f32[2,48,128]{2,1,0:T(8,128)S(1)} %get-tuple-element.91), channel_id=1, source_target_pairs={{0,16},{4,20},{8,24},{12,28},{16,0},{20,4},{24,8},{28,12},{32,48},... | collective-permute-start | bytes 147464 | tf_op jit(solution)/shard_map/ppermute | solution.py:79
  67.6 7.5 %collective-permute-start.9 = (f32[2,48,128]{2,1,0:T(8,128)S(1)}, f32[2,48,128]{2,1,0:T(8,128)S(1)}, u32[]{:S(2)}, u32[]{:S(2)}) collective-permute-start(f32[2,48,128]{2,1,0:T(8,128)S(1)} %get-tuple-element.90), channel_id=1, source_target_pairs={{0,24},{4,28},{8,16},{12,20},{16,8},{20,12},{24,0},{28,4},{32,56},... | collective-permute-start | bytes 147464 | tf_op jit(solution)/shard_map/ppermute | solution.py:79
  75.2 4.5 %collective-permute-start.10 = (f32[2,48,64]{2,1,0:T(8,128)S(1)}, f32[2,48,64]{2,1,0:T(8,128)S(1)}, u32[]{:S(2)}, u32[]{:S(2)}) collective-permute-start(f32[2,48,64]{2,1,0:T(8,128)S(1)} %constant_dynamic-slice_fusion), channel_id=1, source_target_pairs={{0,4},{4,0},{8,12},{12,8},{16,20},{20,16},{24,28},{28,24},{32,36},... | collective-permute-start | bytes 73736 | tf_op jit(solution)/shard_map/ppermute | solution.py:79
  80.2 4.5 %collective-permute-start.11 = (f32[2,48,64]{2,1,0:T(8,128)S(1)}, f32[2,48,64]{2,1,0:T(8,128)S(1)}, u32[]{:S(2)}, u32[]{:S(2)}) collective-permute-start(f32[2,48,64]{2,1,0:T(8,128)S(1)} %fusion.83), channel_id=1, source_target_pairs={{0,4},{4,0},{8,12},{12,8},{16,20},{20,16},{24,28},{28,24},{32,36},... | collective-permute-start | bytes 73736 | tf_op jit(solution)/shard_map/ppermute | solution.py:96
  85.2 4.0 %collective-permute-start.12 = (f32[2,48,128]{2,1,0:T(8,128)S(1)}, f32[2,48,128]{2,1,0:T(8,128)S(1)}, u32[]{:S(2)}, u32[]{:S(2)}) collective-permute-start(f32[2,48,128]{2,1,0:T(8,128)S(1)} %dynamic_update_slice.31), channel_id=1, source_target_pairs={{0,8},{4,12},{8,0},{12,4},{16,24},{20,28},{24,16},{28,20},{32,40},... | collective-permute-start | bytes 147464 | tf_op jit(solution)/shard_map/ppermute | solution.py:96
  85.3 5.8 %collective-permute-start.13 = (f32[2,48,128]{2,1,0:T(8,128)S(1)}, f32[2,48,128]{2,1,0:T(8,128)S(1)}, u32[]{:S(2)}, u32[]{:S(2)}) collective-permute-start(f32[2,48,128]{2,1,0:T(8,128)S(1)} %dynamic_update_slice.31), channel_id=1, source_target_pairs={{0,16},{4,20},{8,24},{12,28},{16,0},{20,4},{24,8},{28,12},{32,48},... | collective-permute-start | bytes 147464 | tf_op jit(solution)/shard_map/ppermute | solution.py:96
  89.1 4.2 %collective-permute-start.14 = (f32[2,48,128]{2,1,0:T(8,128)S(1)}, f32[2,48,128]{2,1,0:T(8,128)S(1)}, u32[]{:S(2)}, u32[]{:S(2)}) collective-permute-start(f32[2,48,128]{2,1,0:T(8,128)S(1)} %dynamic_update_slice.31), channel_id=1, source_target_pairs={{0,24},{4,28},{8,16},{12,20},{16,8},{20,12},{24,0},{28,4},{32,56},... | collective-permute-start | bytes 147464 | tf_op jit(solution)/shard_map/ppermute | solution.py:96
  93.3 4.5 %collective-permute-start.15 = (f32[2,48,512]{2,1,0:T(8,128)S(1)}, f32[2,48,512]{2,1,0:T(8,128)S(1)}, u32[]{:S(2)}, u32[]{:S(2)}) collective-permute-start(f32[2,48,512]{2,1,0:T(8,128)S(1)} %constant_dynamic-update-slice_fusion.4), channel_id=1, source_target_pairs={{0,32},{4,36},{8,40},{12,44},{16,48},{20,52},{24,56},{28,60},{32,0... | collective-permute-start | bytes 589832 | tf_op jit(solution)/shard_map/ppermute | solution.py:96
  93.3 6.9 %collective-permute-start.16 = (f32[2,48,512]{2,1,0:T(8,128)S(1)}, f32[2,48,512]{2,1,0:T(8,128)S(1)}, u32[]{:S(2)}, u32[]{:S(2)}) collective-permute-start(f32[2,48,512]{2,1,0:T(8,128)S(1)} %constant_dynamic-update-slice_fusion.4), channel_id=1, source_target_pairs={{0,64},{4,68},{8,72},{12,76},{16,80},{20,84},{24,88},{28,92},{32,9... | collective-permute-start | bytes 589832 | tf_op jit(solution)/shard_map/ppermute | solution.py:96
  95.0 7.3 %collective-permute-start.17 = (f32[2,48,512]{2,1,0:T(8,128)S(1)}, f32[2,48,512]{2,1,0:T(8,128)S(1)}, u32[]{:S(2)}, u32[]{:S(2)}) collective-permute-start(f32[2,48,512]{2,1,0:T(8,128)S(1)} %constant_dynamic-update-slice_fusion.4), channel_id=1, source_target_pairs={{0,96},{4,100},{8,104},{12,108},{16,112},{20,116},{24,120},{28,124... | collective-permute-start | bytes 589832 | tf_op jit(solution)/shard_map/ppermute | solution.py:96
  102.2 11.2 %copy-start = (f32[2,48,2048]{2,1,0:T(8,128)}, f32[2,48,2048]{2,1,0:T(8,128)S(1)}, u32[]{:S(2)}) copy-start(f32[2,48,2048]{2,1,0:T(8,128)S(1)} %constant_dynamic-update-slice_fusion) | copy-start | bytes 2359300
  113.5 8.6 %collective-permute-start.18 = (f32[4,48,512]{2,1,0:T(8,128)S(1)}, f32[4,48,512]{2,1,0:T(8,128)S(1)}, u32[]{:S(2)}, u32[]{:S(2)}) collective-permute-start(f32[4,48,512]{2,1,0:T(8,128)S(1)} %slice_select_fusion), channel_id=1, source_target_pairs={{0,1},{1,0},{2,3},{3,2},{4,5},{5,4},{6,7},{7,6},{8,9},{9,8},{10,11... | collective-permute-start | bytes 1179656 | tf_op jit(solution)/shard_map/ppermute | solution.py:44
  122.3 6.2 %collective-permute-start.19 = (f32[2,48,512]{2,1,0:T(8,128)S(1)}, f32[2,48,512]{2,1,0:T(8,128)S(1)}, u32[]{:S(2)}, u32[]{:S(2)}) collective-permute-start(f32[2,48,512]{2,1,0:T(8,128)S(1)} %slice_select_fusion.2), channel_id=1, source_target_pairs={{0,2},{1,3},{2,0},{3,1},{4,6},{5,7},{6,4},{7,5},{8,10},{9,11},{10,... | collective-permute-start | bytes 589832 | tf_op jit(solution)/shard_map/ppermute | solution.py:44
  134.7 3.5 %collective-permute-start.20 = (bf16[2,48,512]{2,1,0:T(8,128)(2,1)S(1)}, bf16[2,48,512]{2,1,0:T(8,128)(2,1)S(1)}, u32[]{:S(2)}, u32[]{:S(2)}) collective-permute-start(bf16[2,48,512]{2,1,0:T(8,128)(2,1)S(1)} %convolution_convert_fusion), channel_id=1, source_target_pairs={{0,2},{1,3},{2,0},{3,1},{4,6},{5,7},{6,4},{7,5},{8,10},{9,11},{10,... | collective-permute-start | bytes 294920 | tf_op jit(solution)/shard_map/ppermute | solution.py:53
  138.3 5.5 %collective-permute-start.21 = (bf16[4,48,512]{2,1,0:T(8,128)(2,1)S(1)}, bf16[4,48,512]{2,1,0:T(8,128)(2,1)S(1)}, u32[]{:S(2)}, u32[]{:S(2)}) collective-permute-start(bf16[4,48,512]{2,1,0:T(8,128)(2,1)S(1)} %maximum_select_fusion.5), channel_id=1, source_target_pairs={{0,1},{1,0},{2,3},{3,2},{4,5},{5,4},{6,7},{7,6},{8,9},{9,8},{10,11... | collective-permute-start | bytes 589832 | tf_op jit(solution)/shard_map/ppermute | solution.py:53

commit v7 on v6

--- a/solution.py
+++ b/solution.py
@@ -7,18 +7,23 @@
 
 
 def polar_scale(gram):
+    count = gram.shape[0]
     eye_rank = jnp.eye(gram.shape[-1], dtype=jnp.float32)
     traces = jnp.trace(gram, axis1=1, axis2=2)
-    start = eye_rank[None] / jnp.sqrt(traces + 1e-06)[:, None, None]
-
-    def advance(step, factor):
-        left = jnp.einsum("nrs,nrt->nst", factor, gram, precision=lax.Precision.HIGH)
-        inner = jnp.einsum("nst,ntu->nsu", left, factor, precision=lax.Precision.HIGH)
-        return 0.5 * jnp.einsum(
-            "nrs,nsu->nru", factor, 3.0 * eye_rank[None] - inner, precision=lax.Precision.HIGH
-        )
-
-    return lax.fori_loop(0, NS_STEPS, advance, start)
+    scale = 1.0 / jnp.sqrt(traces + 1e-06)
+    factor = eye_rank[None] * scale[:, None, None]
+    inner = gram * (scale * scale)[:, None, None]
+    for step in range(NS_STEPS):
+        half = 0.5 * (3.0 * eye_rank[None] - inner)
+        both = jnp.concatenate([factor, inner], axis=0)
+        moved = jnp.einsum(
+            "nrs,nsu->nru", both, jnp.concatenate([half, half], axis=0),
+            precision=lax.Precision.HIGH,
+        )
+        factor = moved[:count]
+        if step + 1 < NS_STEPS:
+            inner = jnp.einsum("nrs,nsu->nru", moved[count:], half, precision=lax.Precision.HIGH)
+    return factor
 
 
 def step_bits(size, order):

time: 155 us -> 151 us (0.974)
  matrix products: 59.1 us -> 56.5 us
    dot_general x60 -> x36, matrix products: 8.85 us -> 5.78 us  [the longest x18 3.19 us: polar_scale(): jnp.einsum('nrs,nsu->nru', both, jnp.concatenate([half, half], axis=0), p...]
where the time goes in v7:
time: 151 us
  matrix products  56.5 us (37%)
  starting transfers between devices  42.5 us (28%)
  waiting for transfers between devices  29.8 us (20%)
  other arithmetic  18.2 us (12%)
  local copies, waits for them, and re-layouts  2.54 us (2%)
  between operations  1.55 us (1%)
    dot_general x2, matrix products, project_body(): jnp.einsum('nrj,nij->nri', rows_low, slices, preferred_element_type=jnp.f...  22.1 us
    dot_general x2, matrix products, project_body(): jnp.einsum('nsi,nij->nsj', rotated, slices, preferred_element_type=jnp.fl...  19.3 us
    ppermute x7, starting transfers between devices, radix_scatter(): got = lax.ppermute(send, axis, xor_pairs(size, mask))  11.9 us
    ppermute x4, starting transfers between devices, halving_scatter(): got = lax.ppermute(send, axis, xor_pairs(size, bit))  11.6 us
    ppermute x4, waiting for transfers between devices, halving_scatter(): got = lax.ppermute(send, axis, xor_pairs(size, bit))  10.8 us
    ppermute x7, starting transfers between devices, radix_gather(): got = lax.ppermute(x, axis, xor_pairs(size, mask))  10.8 us
    ppermute x7, waiting for transfers between devices, radix_gather(): got = lax.ppermute(x, axis, xor_pairs(size, mask))  10.3 us
    another operation x4, other arithmetic, lower_inverse(): lower = jnp.linalg.cholesky(system)  8.96 us
  transfers between devices with their start and end apart: 22, of which 15 were waited for; matrix products, arithmetic and copies ran while one was open for 14% of the time, Pallas kernels for 0%

profile of v7, /device:TPU:1, one launch (start us, length us, event | category | flops | bytes accessed | tf_op | source)
XLA Modules:
  0.0 151.1 jit_solution(6092084097891122552)
XLA Ops:
  0.6 0.9 select_reduce_fusion.3
  1.6 1.1 slice_bitcast_fusion.3
  2.7 11.0 %fusion.12 = f32[8,48,512]{2,1,0:T(8,128)S(1)} fusion(bf16[8,512,2048]{2,1,0:T(8,128)(2,1)} %param.6, pred[8]{0:T(512)(128)(4,1)S(1)} %broadcast_compare_fusion, bf16[48,2048]{1,0:T(8,128)(2,1)S(1)} %get-tuple-element.18, bf16[48,2048]{1,0:T(8,128)(2,1)S(1)} %get-tuple-element.17), kind=kOutput, calls=%fused_computation.12 | convolution fusion | flops 806092800 | bytes 17956872 | tf_op jit(solution)/shard_map/nrj,nij->nri/dot_general | solution.py:124
  13.7 1.5 collective-permute-start
  16.7 1.5 collective-permute-start.1
  18.4 4.4 %collective-permute-done.1 = f32[2,48,512]{2,1,0:T(8,128)S(1)} collective-permute-done((f32[2,48,512]{2,1,0:T(8,128)S(1)}, f32[2,48,512]{2,1,0:T(8,128)S(1)}, u32[]{:S(2)}, u32[]{:S(2)}) %collective-permute-start.1) | collective-permute-done | bytes 196640 | tf_op jit(solution)/shard_map/ppermute | solution.py:49
  22.8 0.3 fusion.37
  23.1 0.4 select_reduce_fusion.2
  27.0 0.3 convolution_convert_fusion.1
  27.3 1.5 collective-permute-start.2
  28.8 2.0 %collective-permute-done.2 = bf16[2,48,512]{2,1,0:T(8,128)(2,1)S(1)} collective-permute-done((bf16[2,48,512]{2,1,0:T(8,128)(2,1)S(1)}, bf16[2,48,512]{2,1,0:T(8,128)(2,1)S(1)}, u32[]{:S(2)}, u32[]{:S(2)}) %collective-permute-start.2) | collective-permute-done | bytes 98336 | tf_op jit(solution)/shard_map/ppermute | solution.py:58
  30.9 2.6 %collective-permute-start.3 = (bf16[4,48,512]{2,1,0:T(8,128)(2,1)S(1)}, bf16[4,48,512]{2,1,0:T(8,128)(2,1)S(1)}, u32[]{:S(2)}, u32[]{:S(2)}) collective-permute-start(bf16[4,48,512]{2,1,0:T(8,128)(2,1)S(1)} %maximum_select_fusion.4), channel_id=1, source_target_pairs={{0,1},{1,0},{2,3},{3,2},{4,5},{5,4},{6,7},{7,6},{8,9},{9,8},{10,11... | collective-permute-start | bytes 589832 | tf_op jit(solution)/shard_map/ppermute | solution.py:58
  33.5 1.1 collective-permute-done.3
  34.6 8.8 %fusion.20 = f32[8,48,2048]{2,1,0:T(8,128)S(1)} fusion(bf16[8,512,2048]{2,1,0:T(8,128)(2,1)} %param.6, bf16[4,48,512]{2,1,0:T(8,128)(2,1)S(1)} %maximum_select_fusion.4, bf16[4,48,512]{2,1,0:T(8,128)(2,1)S(1)} %collective-permute-done.3, pred[]{:T(512)S(6)} %ne.14), kind=kOutput, calls=%fused_computation.26 | convolution fusion | flops 805896192 | bytes 20316160 | tf_op jit(solution)/shard_map/nsi,nij->nsj/dot_general | solution.py:137
  43.4 2.3 %fusion.4 = f32[2,48,2048]{2,1,0:T(8,128)S(1)} fusion(f32[8,48,2048]{2,1,0:T(8,128)S(1)} %fusion.20, f32[8,48,48]{1,2,0:T(8,128)S(1)} %copy.18, f32[8,2]{0,1:T(2,128)S(1)} %compare_convert_fusion.1), kind=kOutput, calls=%fused_computation.6 | convolution fusion | flops 906006528 | bytes 4005952 | tf_op jit(solution)/shard_map/nhsr,nsj->hrj/dot_general | solution.py:175
  45.8 1.4 collective-permute-start.4
  47.2 2.4 %collective-permute-start.5 = (f32[2,48,512]{2,1,0:T(8,128)S(1)}, f32[2,48,512]{2,1,0:T(8,128)S(1)}, u32[]{:S(2)}, u32[]{:S(2)}) collective-permute-start(f32[2,48,512]{2,1,0:T(8,128)S(1)} %get-tuple-element.16), channel_id=1, source_target_pairs={{0,64},{4,68},{8,72},{12,76},{16,80},{20,84},{24,88},{28,92},{32,9... | collective-permute-start | bytes 589832 | tf_op jit(solution)/shard_map/ppermute | solution.py:84
  49.8 8.8 %custom-call.7 = f32[2,48,48]{2,1,0:T(8,128)S(1)} custom-call(f32[2,48,48]{2,1,0:T(8,128)S(1)} %fusion.192), custom_call_target="Cholesky" | custom-call | tf_op jit(solution)/shard_map/jit(cholesky)/cholesky | solution.py:141
  58.8 2.1 %collective-permute-done.6 = f32[2,48,512]{2,1,0:T(8,128)S(1)} collective-permute-done((f32[2,48,512]{2,1,0:T(8,128)S(1)}, f32[2,48,512]{2,1,0:T(8,128)S(1)}, u32[]{:S(2)}, u32[]{:S(2)}) %collective-permute-start.6) | collective-permute-done | bytes 196640 | tf_op jit(solution)/shard_map/ppermute | solution.py:84
  61.0 1.7 %collective-permute-start.7 = (f32[2,48,128]{2,1,0:T(8,128)S(1)}, f32[2,48,128]{2,1,0:T(8,128)S(1)}, u32[]{:S(2)}, u32[]{:S(2)}) collective-permute-start(f32[2,48,128]{2,1,0:T(8,128)S(1)} %get-tuple-element.19), channel_id=1, source_target_pairs={{0,8},{4,12},{8,0},{12,4},{16,24},{20,28},{24,16},{28,20},{32,40},... | collective-permute-start | bytes 147464 | tf_op jit(solution)/shard_map/ppermute | solution.py:84
  62.7 3.3 %collective-permute-start.8 = (f32[2,48,128]{2,1,0:T(8,128)S(1)}, f32[2,48,128]{2,1,0:T(8,128)S(1)}, u32[]{:S(2)}, u32[]{:S(2)}) collective-permute-start(f32[2,48,128]{2,1,0:T(8,128)S(1)} %get-tuple-element.21), channel_id=1, source_target_pairs={{0,16},{4,20},{8,24},{12,28},{16,0},{20,4},{24,8},{28,12},{32,48},... | collective-permute-start | bytes 147464 | tf_op jit(solution)/shard_map/ppermute | solution.py:84
  66.1 7.4 %custom-call.8 = f32[2,1,48,48]{2,3,1,0:T(8,128)S(1)} custom-call(f32[2,1,48,48]{3,2,1,0:T(8,128)S(1)} %select_bitcast_fusion), custom_call_target="InvertDiagBlocksLowerTriangular" | custom-call | tf_op jit(solution)/shard_map/triangular_solve | solution.py:143
  73.6 2.9 %collective-permute-start.10 = (f32[2,48,64]{2,1,0:T(8,128)S(1)}, f32[2,48,64]{2,1,0:T(8,128)S(1)}, u32[]{:S(2)}, u32[]{:S(2)}) collective-permute-start(f32[2,48,64]{2,1,0:T(8,128)S(1)} %constant_dynamic-slice_fusion), channel_id=1, source_target_pairs={{0,4},{4,0},{8,12},{12,8},{16,20},{20,16},{24,28},{28,24},{32,36},... | collective-permute-start | bytes 73736 | tf_op jit(solution)/shard_map/ppermute | solution.py:84
  76.9 1.3 collective-permute-done.10
  78.6 3.0 %collective-permute-start.11 = (f32[2,48,64]{2,1,0:T(8,128)S(1)}, f32[2,48,64]{2,1,0:T(8,128)S(1)}, u32[]{:S(2)}, u32[]{:S(2)}) collective-permute-start(f32[2,48,64]{2,1,0:T(8,128)S(1)} %fusion.236), channel_id=1, source_target_pairs={{0,4},{4,0},{8,12},{12,8},{16,20},{20,16},{24,28},{28,24},{32,36},... | collective-permute-start | bytes 73736 | tf_op jit(solution)/shard_map/ppermute | solution.py:101
  81.9 1.3 collective-permute-done.11
  83.2 0.5 dynamic_update_slice.31
  83.8 3.8 %collective-permute-start.13 = (f32[2,48,128]{2,1,0:T(8,128)S(1)}, f32[2,48,128]{2,1,0:T(8,128)S(1)}, u32[]{:S(2)}, u32[]{:S(2)}) collective-permute-start(f32[2,48,128]{2,1,0:T(8,128)S(1)} %dynamic_update_slice.31), channel_id=1, source_target_pairs={{0,16},{4,20},{8,24},{12,28},{16,0},{20,4},{24,8},{28,12},{32,48},... | collective-permute-start | bytes 147464 | tf_op jit(solution)/shard_map/ppermute | solution.py:101
  87.7 1.9 %collective-permute-done.13 = f32[2,48,128]{2,1,0:T(8,128)S(1)} collective-permute-done((f32[2,48,128]{2,1,0:T(8,128)S(1)}, f32[2,48,128]{2,1,0:T(8,128)S(1)}, u32[]{:S(2)}, u32[]{:S(2)}) %collective-permute-start.13) | collective-permute-done | bytes 49184 | tf_op jit(solution)/shard_map/ppermute | solution.py:101
  89.6 2.1 %collective-permute-done.14 = f32[2,48,128]{2,1,0:T(8,128)S(1)} collective-permute-done((f32[2,48,128]{2,1,0:T(8,128)S(1)}, f32[2,48,128]{2,1,0:T(8,128)S(1)}, u32[]{:S(2)}, u32[]{:S(2)}) %collective-permute-start.14) | collective-permute-done | bytes 49184 | tf_op jit(solution)/shard_map/ppermute | solution.py:101
  91.8 1.6 %collective-permute-start.16 = (f32[2,48,512]{2,1,0:T(8,128)S(1)}, f32[2,48,512]{2,1,0:T(8,128)S(1)}, u32[]{:S(2)}, u32[]{:S(2)}) collective-permute-start(f32[2,48,512]{2,1,0:T(8,128)S(1)} %constant_dynamic-update-slice_fusion.4), channel_id=1, source_target_pairs={{0,64},{4,68},{8,72},{12,76},{16,80},{20,84},{24,88},{28,92},{32,9... | collective-permute-start | bytes 589832 | tf_op jit(solution)/shard_map/ppermute | solution.py:101
  93.4 2.2 %collective-permute-start.17 = (f32[2,48,512]{2,1,0:T(8,128)S(1)}, f32[2,48,512]{2,1,0:T(8,128)S(1)}, u32[]{:S(2)}, u32[]{:S(2)}) collective-permute-start(f32[2,48,512]{2,1,0:T(8,128)S(1)} %constant_dynamic-update-slice_fusion.4), channel_id=1, source_target_pairs={{0,96},{4,100},{8,104},{12,108},{16,112},{20,116},{24,120},{28,124... | collective-permute-start | bytes 589832 | tf_op jit(solution)/shard_map/ppermute | solution.py:101
  95.7 0.6 collective-permute-done.15
  96.3 2.4 %collective-permute-done.16 = f32[2,48,512]{2,1,0:T(8,128)S(1)} collective-permute-done((f32[2,48,512]{2,1,0:T(8,128)S(1)}, f32[2,48,512]{2,1,0:T(8,128)S(1)}, u32[]{:S(2)}, u32[]{:S(2)}) %collective-permute-start.16) | collective-permute-done | bytes 196640 | tf_op jit(solution)/shard_map/ppermute | solution.py:101
  98.7 2.0 %collective-permute-done.17 = f32[2,48,512]{2,1,0:T(8,128)S(1)} collective-permute-done((f32[2,48,512]{2,1,0:T(8,128)S(1)}, f32[2,48,512]{2,1,0:T(8,128)S(1)}, u32[]{:S(2)}, u32[]{:S(2)}) %collective-permute-start.17) | collective-permute-done | bytes 196640 | tf_op jit(solution)/shard_map/ppermute | solution.py:101
  100.8 11.2 %fusion.7 = f32[8,48,512]{2,1,0:T(8,128)S(1)} fusion(bf16[8,512,2048]{2,1,0:T(8,128)(2,1)} %param.6, f32[48,2048]{1,0:T(8,128)S(1)} %get-tuple-element.13, f32[48,2048]{1,0:T(8,128)S(1)} %get-tuple-element.12, pred[8]{0:T(512)(128)(4,1)S(1)} %broadcast_compare_fusion), kind=kOutput, calls=%fused_computation.7 | convolution fusion | flops 806092800 | bytes 18350088 | tf_op jit(solution)/shard_map/nrj,nij->nri/dot_general | solution.py:124
  112.0 7.3 %collective-permute-start.18 = (f32[4,48,512]{2,1,0:T(8,128)S(1)}, f32[4,48,512]{2,1,0:T(8,128)S(1)}, u32[]{:S(2)}, u32[]{:S(2)}) collective-permute-start(f32[4,48,512]{2,1,0:T(8,128)S(1)} %slice_select_fusion), channel_id=1, source_target_pairs={{0,1},{1,0},{2,3},{3,2},{4,5},{5,4},{6,7},{7,6},{8,9},{9,8},{10,11... | collective-permute-start | bytes 1179656 | tf_op jit(solution)/shard_map/ppermute | solution.py:49
  119.3 1.3 collective-permute-done.18
  120.8 1.4 collective-permute-start.19
  122.2 4.8 %collective-permute-done.19 = f32[2,48,512]{2,1,0:T(8,128)S(1)} collective-permute-done((f32[2,48,512]{2,1,0:T(8,128)S(1)}, f32[2,48,512]{2,1,0:T(8,128)S(1)}, u32[]{:S(2)}, u32[]{:S(2)}) %collective-permute-start.19) | collective-permute-done | bytes 196640 | tf_op jit(solution)/shard_map/ppermute | solution.py:49
  127.0 0.3 fusion.34
  127.3 0.4 select_reduce_fusion
  131.2 0.3 convolution_convert_fusion
  131.5 1.4 collective-permute-start.20
  132.9 2.2 %collective-permute-done.20 = bf16[2,48,512]{2,1,0:T(8,128)(2,1)S(1)} collective-permute-done((bf16[2,48,512]{2,1,0:T(8,128)(2,1)S(1)}, bf16[2,48,512]{2,1,0:T(8,128)(2,1)S(1)}, u32[]{:S(2)}, u32[]{:S(2)}) %collective-permute-start.20) | collective-permute-done | bytes 98336 | tf_op jit(solution)/shard_map/ppermute | solution.py:58
  135.1 2.7 %collective-permute-start.21 = (bf16[4,48,512]{2,1,0:T(8,128)(2,1)S(1)}, bf16[4,48,512]{2,1,0:T(8,128)(2,1)S(1)}, u32[]{:S(2)}, u32[]{:S(2)}) collective-permute-start(bf16[4,48,512]{2,1,0:T(8,128)(2,1)S(1)} %maximum_select_fusion.5), channel_id=1, source_target_pairs={{0,1},{1,0},{2,3},{3,2},{4,5},{5,4},{6,7},{7,6},{8,9},{9,8},{10,11... | collective-permute-start | bytes 589832 | tf_op jit(solution)/shard_map/ppermute | solution.py:58
  137.8 2.8 %fusion = f32[8,48,2048]{2,1,0:T(8,128)S(1)} fusion(f32[48,2048]{1,0:T(8,128)S(1)} %get-tuple-element.13, f32[48,2048]{1,0:T(8,128)S(1)} %get-tuple-element.12, pred[8]{0:T(512)(128)(4,1)S(1)} %broadcast_compare_fusion, f32[8,48]{1,0:T(8,128)S(1)} %fusion.205, f32[48,48]{1,0:T(8,128)S(1)} %get-tuple-element.25, f32[48,48]{1,0:T(8,128)S(1)} %get-tuple-element.24), kind=kOutput, calls=%fused_computation | convolution fusion | flops 453808128 | bytes 3952136 | tf_op jit(solution)/shard_map/nrs,nsj->nrj/dot_general | solution.py:192
  140.6 10.5 %convolution_subtract_fusion = f32[8,48,2048]{2,1,0:T(8,128)} fusion(f32[8,48,2048]{2,1,0:T(8,128)S(1)} %fusion, bf16[8,512,2048]{2,1,0:T(8,128)(2,1)} %param.6, bf16[4,48,512]{2,1,0:T(8,128)(2,1)S(1)} %maximum_select_fusion.5, bf16[4,48,512]{2,1,0:T(8,128)(2,1)S(1)} %collective-permute-done.21, pred[]{:T(512)S(6)} %ne.14), kind=kOutput, calls=%fused_computation.5 | convolution fusion | flops 806682624 | bytes 23461888 | tf_op jit(solution)/shard_map/nsi,nij->nsj/dot_general | solution.py:137
  (131 shorter events, 10.6 us)
Async XLA Ops:
  2.6 12.5 %copy-start.3 = (s32[256]{0:T(256)S(1)}, s32[256]{0:T(256)}, u32[]{:S(2)}) copy-start(s32[256]{0:T(256)} %param.10) | copy-start | bytes 3076
  2.6 12.6 %copy-start.2 = (f32[256,48]{0,1:T(8,128)S(1)}, f32[256,48]{0,1:T(8,128)}, u32[]{:S(2)}) copy-start(f32[256,48]{0,1:T(8,128)} %param.8) | copy-start | bytes 147460
  2.7 12.9 %copy-start.1 = (f32[2,48,48]{2,1,0:T(8,128)S(1)}, f32[2,48,48]{2,1,0:T(8,128)}, u32[]{:S(2)}) copy-start(f32[2,48,48]{2,1,0:T(8,128)} %param.9) | copy-start | bytes 55300
  13.7 2.8 %collective-permute-start = (f32[4,48,512]{2,1,0:T(8,128)S(1)}, f32[4,48,512]{2,1,0:T(8,128)S(1)}, u32[]{:S(2)}, u32[]{:S(2)}) collective-permute-start(f32[4,48,512]{2,1,0:T(8,128)S(1)} %slice_select_fusion.1), channel_id=1, source_target_pairs={{0,1},{1,0},{2,3},{3,2},{4,5},{5,4},{6,7},{7,6},{8,9},{9,8},{10,11... | collective-permute-start | bytes 1179656 | tf_op jit(solution)/shard_map/ppermute | solution.py:49
  16.7 6.2 %collective-permute-start.1 = (f32[2,48,512]{2,1,0:T(8,128)S(1)}, f32[2,48,512]{2,1,0:T(8,128)S(1)}, u32[]{:S(2)}, u32[]{:S(2)}) collective-permute-start(f32[2,48,512]{2,1,0:T(8,128)S(1)} %slice_select_fusion.3), channel_id=1, source_target_pairs={{0,2},{1,3},{2,0},{3,1},{4,6},{5,7},{6,4},{7,5},{8,10},{9,11},{10,... | collective-permute-start | bytes 589832 | tf_op jit(solution)/shard_map/ppermute | solution.py:49
  27.3 3.5 %collective-permute-start.2 = (bf16[2,48,512]{2,1,0:T(8,128)(2,1)S(1)}, bf16[2,48,512]{2,1,0:T(8,128)(2,1)S(1)}, u32[]{:S(2)}, u32[]{:S(2)}) collective-permute-start(bf16[2,48,512]{2,1,0:T(8,128)(2,1)S(1)} %convolution_convert_fusion.1), channel_id=1, source_target_pairs={{0,2},{1,3},{2,0},{3,1},{4,6},{5,7},{6,4},{7,5},{8,10},{9,11},{10,... | collective-permute-start | bytes 294920 | tf_op jit(solution)/shard_map/ppermute | solution.py:58
  30.9 3.7 %collective-permute-start.3 = (bf16[4,48,512]{2,1,0:T(8,128)(2,1)S(1)}, bf16[4,48,512]{2,1,0:T(8,128)(2,1)S(1)}, u32[]{:S(2)}, u32[]{:S(2)}) collective-permute-start(bf16[4,48,512]{2,1,0:T(8,128)(2,1)S(1)} %maximum_select_fusion.4), channel_id=1, source_target_pairs={{0,1},{1,0},{2,3},{3,2},{4,5},{5,4},{6,7},{7,6},{8,9},{9,8},{10,11... | collective-permute-start | bytes 589832 | tf_op jit(solution)/shard_map/ppermute | solution.py:58
  45.8 13.0 %collective-permute-start.4 = (f32[2,48,512]{2,1,0:T(8,128)S(1)}, f32[2,48,512]{2,1,0:T(8,128)S(1)}, u32[]{:S(2)}, u32[]{:S(2)}) collective-permute-start(f32[2,48,512]{2,1,0:T(8,128)S(1)} %get-tuple-element.14), channel_id=1, source_target_pairs={{0,32},{4,36},{8,40},{12,44},{16,48},{20,52},{24,56},{28,60},{32,0... | collective-permute-start | bytes 589832 | tf_op jit(solution)/shard_map/ppermute | solution.py:84
  47.2 11.6 %collective-permute-start.5 = (f32[2,48,512]{2,1,0:T(8,128)S(1)}, f32[2,48,512]{2,1,0:T(8,128)S(1)}, u32[]{:S(2)}, u32[]{:S(2)}) collective-permute-start(f32[2,48,512]{2,1,0:T(8,128)S(1)} %get-tuple-element.16), channel_id=1, source_target_pairs={{0,64},{4,68},{8,72},{12,76},{16,80},{20,84},{24,88},{28,92},{32,9... | collective-permute-start | bytes 589832 | tf_op jit(solution)/shard_map/ppermute | solution.py:84
  49.6 11.3 %collective-permute-start.6 = (f32[2,48,512]{2,1,0:T(8,128)S(1)}, f32[2,48,512]{2,1,0:T(8,128)S(1)}, u32[]{:S(2)}, u32[]{:S(2)}) collective-permute-start(f32[2,48,512]{2,1,0:T(8,128)S(1)} %get-tuple-element.15), channel_id=1, source_target_pairs={{0,96},{4,100},{8,104},{12,108},{16,112},{20,116},{24,120},{28,124... | collective-permute-start | bytes 589832 | tf_op jit(solution)/shard_map/ppermute | solution.py:84
  61.0 12.5 %collective-permute-start.7 = (f32[2,48,128]{2,1,0:T(8,128)S(1)}, f32[2,48,128]{2,1,0:T(8,128)S(1)}, u32[]{:S(2)}, u32[]{:S(2)}) collective-permute-start(f32[2,48,128]{2,1,0:T(8,128)S(1)} %get-tuple-element.19), channel_id=1, source_target_pairs={{0,8},{4,12},{8,0},{12,4},{16,24},{20,28},{24,16},{28,20},{32,40},... | collective-permute-start | bytes 147464 | tf_op jit(solution)/shard_map/ppermute | solution.py:84
  62.7 10.8 %collective-permute-start.8 = (f32[2,48,128]{2,1,0:T(8,128)S(1)}, f32[2,48,128]{2,1,0:T(8,128)S(1)}, u32[]{:S(2)}, u32[]{:S(2)}) collective-permute-start(f32[2,48,128]{2,1,0:T(8,128)S(1)} %get-tuple-element.21), channel_id=1, source_target_pairs={{0,16},{4,20},{8,24},{12,28},{16,0},{20,4},{24,8},{28,12},{32,48},... | collective-permute-start | bytes 147464 | tf_op jit(solution)/shard_map/ppermute | solution.py:84
  66.0 7.5 %collective-permute-start.9 = (f32[2,48,128]{2,1,0:T(8,128)S(1)}, f32[2,48,128]{2,1,0:T(8,128)S(1)}, u32[]{:S(2)}, u32[]{:S(2)}) collective-permute-start(f32[2,48,128]{2,1,0:T(8,128)S(1)} %get-tuple-element.20), channel_id=1, source_target_pairs={{0,24},{4,28},{8,16},{12,20},{16,8},{20,12},{24,0},{28,4},{32,56},... | collective-permute-start | bytes 147464 | tf_op jit(solution)/shard_map/ppermute | solution.py:84
  73.6 4.5 %collective-permute-start.10 = (f32[2,48,64]{2,1,0:T(8,128)S(1)}, f32[2,48,64]{2,1,0:T(8,128)S(1)}, u32[]{:S(2)}, u32[]{:S(2)}) collective-permute-start(f32[2,48,64]{2,1,0:T(8,128)S(1)} %constant_dynamic-slice_fusion), channel_id=1, source_target_pairs={{0,4},{4,0},{8,12},{12,8},{16,20},{20,16},{24,28},{28,24},{32,36},... | collective-permute-start | bytes 73736 | tf_op jit(solution)/shard_map/ppermute | solution.py:84
  78.6 4.5 %collective-permute-start.11 = (f32[2,48,64]{2,1,0:T(8,128)S(1)}, f32[2,48,64]{2,1,0:T(8,128)S(1)}, u32[]{:S(2)}, u32[]{:S(2)}) collective-permute-start(f32[2,48,64]{2,1,0:T(8,128)S(1)} %fusion.236), channel_id=1, source_target_pairs={{0,4},{4,0},{8,12},{12,8},{16,20},{20,16},{24,28},{28,24},{32,36},... | collective-permute-start | bytes 73736 | tf_op jit(solution)/shard_map/ppermute | solution.py:101
  83.7 4.0 %collective-permute-start.12 = (f32[2,48,128]{2,1,0:T(8,128)S(1)}, f32[2,48,128]{2,1,0:T(8,128)S(1)}, u32[]{:S(2)}, u32[]{:S(2)}) collective-permute-start(f32[2,48,128]{2,1,0:T(8,128)S(1)} %dynamic_update_slice.31), channel_id=1, source_target_pairs={{0,8},{4,12},{8,0},{12,4},{16,24},{20,28},{24,16},{28,20},{32,40},... | collective-permute-start | bytes 147464 | tf_op jit(solution)/shard_map/ppermute | solution.py:101
  83.8 5.8 %collective-permute-start.13 = (f32[2,48,128]{2,1,0:T(8,128)S(1)}, f32[2,48,128]{2,1,0:T(8,128)S(1)}, u32[]{:S(2)}, u32[]{:S(2)}) collective-permute-start(f32[2,48,128]{2,1,0:T(8,128)S(1)} %dynamic_update_slice.31), channel_id=1, source_target_pairs={{0,16},{4,20},{8,24},{12,28},{16,0},{20,4},{24,8},{28,12},{32,48},... | collective-permute-start | bytes 147464 | tf_op jit(solution)/shard_map/ppermute | solution.py:101
  87.6 4.2 %collective-permute-start.14 = (f32[2,48,128]{2,1,0:T(8,128)S(1)}, f32[2,48,128]{2,1,0:T(8,128)S(1)}, u32[]{:S(2)}, u32[]{:S(2)}) collective-permute-start(f32[2,48,128]{2,1,0:T(8,128)S(1)} %dynamic_update_slice.31), channel_id=1, source_target_pairs={{0,24},{4,28},{8,16},{12,20},{16,8},{20,12},{24,0},{28,4},{32,56},... | collective-permute-start | bytes 147464 | tf_op jit(solution)/shard_map/ppermute | solution.py:101
  91.8 4.5 %collective-permute-start.15 = (f32[2,48,512]{2,1,0:T(8,128)S(1)}, f32[2,48,512]{2,1,0:T(8,128)S(1)}, u32[]{:S(2)}, u32[]{:S(2)}) collective-permute-start(f32[2,48,512]{2,1,0:T(8,128)S(1)} %constant_dynamic-update-slice_fusion.4), channel_id=1, source_target_pairs={{0,32},{4,36},{8,40},{12,44},{16,48},{20,52},{24,56},{28,60},{32,0... | collective-permute-start | bytes 589832 | tf_op jit(solution)/shard_map/ppermute | solution.py:101
  91.8 6.9 %collective-permute-start.16 = (f32[2,48,512]{2,1,0:T(8,128)S(1)}, f32[2,48,512]{2,1,0:T(8,128)S(1)}, u32[]{:S(2)}, u32[]{:S(2)}) collective-permute-start(f32[2,48,512]{2,1,0:T(8,128)S(1)} %constant_dynamic-update-slice_fusion.4), channel_id=1, source_target_pairs={{0,64},{4,68},{8,72},{12,76},{16,80},{20,84},{24,88},{28,92},{32,9... | collective-permute-start | bytes 589832 | tf_op jit(solution)/shard_map/ppermute | solution.py:101
  93.4 7.3 %collective-permute-start.17 = (f32[2,48,512]{2,1,0:T(8,128)S(1)}, f32[2,48,512]{2,1,0:T(8,128)S(1)}, u32[]{:S(2)}, u32[]{:S(2)}) collective-permute-start(f32[2,48,512]{2,1,0:T(8,128)S(1)} %constant_dynamic-update-slice_fusion.4), channel_id=1, source_target_pairs={{0,96},{4,100},{8,104},{12,108},{16,112},{20,116},{24,120},{28,124... | collective-permute-start | bytes 589832 | tf_op jit(solution)/shard_map/ppermute | solution.py:101
  100.7 11.2 %copy-start = (f32[2,48,2048]{2,1,0:T(8,128)}, f32[2,48,2048]{2,1,0:T(8,128)S(1)}, u32[]{:S(2)}) copy-start(f32[2,48,2048]{2,1,0:T(8,128)S(1)} %constant_dynamic-update-slice_fusion) | copy-start | bytes 2359300
  112.0 8.6 %collective-permute-start.18 = (f32[4,48,512]{2,1,0:T(8,128)S(1)}, f32[4,48,512]{2,1,0:T(8,128)S(1)}, u32[]{:S(2)}, u32[]{:S(2)}) collective-permute-start(f32[4,48,512]{2,1,0:T(8,128)S(1)} %slice_select_fusion), channel_id=1, source_target_pairs={{0,1},{1,0},{2,3},{3,2},{4,5},{5,4},{6,7},{7,6},{8,9},{9,8},{10,11... | collective-permute-start | bytes 1179656 | tf_op jit(solution)/shard_map/ppermute | solution.py:49
  120.8 6.2 %collective-permute-start.19 = (f32[2,48,512]{2,1,0:T(8,128)S(1)}, f32[2,48,512]{2,1,0:T(8,128)S(1)}, u32[]{:S(2)}, u32[]{:S(2)}) collective-permute-start(f32[2,48,512]{2,1,0:T(8,128)S(1)} %slice_select_fusion.2), channel_id=1, source_target_pairs={{0,2},{1,3},{2,0},{3,1},{4,6},{5,7},{6,4},{7,5},{8,10},{9,11},{10,... | collective-permute-start | bytes 589832 | tf_op jit(solution)/shard_map/ppermute | solution.py:49
  131.5 3.5 %collective-permute-start.20 = (bf16[2,48,512]{2,1,0:T(8,128)(2,1)S(1)}, bf16[2,48,512]{2,1,0:T(8,128)(2,1)S(1)}, u32[]{:S(2)}, u32[]{:S(2)}) collective-permute-start(bf16[2,48,512]{2,1,0:T(8,128)(2,1)S(1)} %convolution_convert_fusion), channel_id=1, source_target_pairs={{0,2},{1,3},{2,0},{3,1},{4,6},{5,7},{6,4},{7,5},{8,10},{9,11},{10,... | collective-permute-start | bytes 294920 | tf_op jit(solution)/shard_map/ppermute | solution.py:58
  135.1 5.5 %collective-permute-start.21 = (bf16[4,48,512]{2,1,0:T(8,128)(2,1)S(1)}, bf16[4,48,512]{2,1,0:T(8,128)(2,1)S(1)}, u32[]{:S(2)}, u32[]{:S(2)}) collective-permute-start(bf16[4,48,512]{2,1,0:T(8,128)(2,1)S(1)} %maximum_select_fusion.5), channel_id=1, source_target_pairs={{0,1},{1,0},{2,3},{3,2},{4,5},{5,4},{6,7},{7,6},{8,9},{9,8},{10,11... | collective-permute-start | bytes 589832 | tf_op jit(solution)/shard_map/ppermute | solution.py:58

commit v8 on v7

--- a/solution.py
+++ b/solution.py
@@ -119,9 +119,15 @@
     return block
 
 
-def project_body(slices, rows_low, mixed, chan_size, chan_bits):
+def project(slices, rows_low, mixed, chan_size, chan_bits, carried=None):
+    return project_body(slices, rows_low, mixed, chan_size, chan_bits, carried)
+
+
+def project_body(slices, rows_low, mixed, chan_size, chan_bits, carried):
     run_count = slices.shape[0]
     partial_basis = jnp.einsum("nrj,nij->nri", rows_low, slices, preferred_element_type=jnp.float32)
+    if carried is not None:
+        partial_basis, carried = lax.optimization_barrier((partial_basis, carried))
     basis = halving_scatter(partial_basis, "chan", chan_size, chan_bits, 0)
     part = basis.shape[0]
     first = block_index("chan", chan_bits) * part
@@ -134,7 +140,10 @@
     )
     rotated = doubling_gather(rotated, "chan", chan_size, chan_bits, 0)
     del run_count
-    return jnp.einsum("nsi,nij->nsj", rotated, slices, preferred_element_type=jnp.float32)
+    projected = jnp.einsum("nsi,nij->nsj", rotated, slices, preferred_element_type=jnp.float32)
+    if carried is None:
+        return projected
+    return projected, carried
 
 
 def lower_inverse(system):
@@ -167,26 +176,25 @@
         first_half = (my_halves == 0)[:, None, None]
         own_rows = jnp.where(first_half, spectra[0][None], spectra[1][None])
         own_mix = jnp.where(first_half, mixing[0][None], mixing[1][None]) * my_loads[:, None, :]
-        projected = project_body(slices, own_rows, own_mix, chan_size, chan_bits)
-        mine_member = (my_halves[:, None] == jnp.arange(2, dtype=jnp.int32)[None, :]).astype(
-            jnp.float32
-        )
-        weights = mine_member[:, :, None, None] * own_mix[:, None, :, :]
-        partial_moments = jnp.einsum(
-            "nhsr,nsj->hrj", weights, projected, precision=lax.Precision.HIGHEST
-        )
         member = (halves[:, None] == jnp.arange(2, dtype=jnp.int32)[None, :]).astype(jnp.float32)
         cross = jnp.einsum("kh,kr,ks->hrs", member, loadings, loadings, precision=lax.Precision.HIGHEST)
         inner_mix = jnp.einsum("hsr,hst->hrt", mixing, mixing, precision=lax.Precision.HIGHEST)
         system = inner_mix * cross
-        system, partial_moments = lax.optimization_barrier((system, partial_moments))
+        projected, system = project(slices, own_rows, own_mix, chan_size, chan_bits, carried=system)
         inverse = lower_inverse(system)
+        mine_member = (my_halves[:, None] == jnp.arange(2, dtype=jnp.int32)[None, :]).astype(
+            jnp.float32
+        )
+        weights = mine_member[:, :, None, None] * own_mix[:, None, :, :]
+        partial_moments = jnp.einsum(
+            "nhsr,nsj->hrj", weights, projected, precision=lax.Precision.HIGHEST
+        )
         moments_part = radix_scatter(partial_moments, "runs", runs_size, runs_groups, 2)
         spectra_part = apply_inverse(inverse, moments_part)
         new_spectra = radix_gather(spectra_part, "runs", runs_size, runs_groups, 2)
         held_rows = jnp.where(first_half, new_spectra[1][None], new_spectra[0][None])
         held_mix = jnp.where(first_half, mixing[1][None], mixing[0][None]) * mate_loads[:, None, :]
-        held_projected = project_body(
+        held_projected = project(
             slices, held_rows.astype(jnp.bfloat16), held_mix, chan_size, chan_bits
         )
         model_part = jnp.einsum(

time: 151 us -> 163 us (1.079)
  waiting for transfers between devices: 29.8 us -> 38.5 us
  matrix products: 56.5 us -> 58.2 us
    ppermute x7, waiting for transfers between devices: 3.43 us -> 12.4 us  [radix_scatter(): got = lax.ppermute(send, axis, xor_pairs(size, mask))]
    another operation x4 -> x3, other arithmetic: 8.96 us -> 8.93 us  [lower_inverse(): lower = jnp.linalg.cholesky(system)]
  transfers between devices with their start and end apart: 22 -> 22, of which waited for: 15 -> 16; matrix products, arithmetic and copies ran while one was open for 14% -> 13% of each run, Pallas kernels for 0% -> 0%
where the time goes in v8:
time: 163 us; the launch traced here: 162 us
  matrix products  58.2 us (36%)
  starting transfers between devices  42.4 us (26%)
  waiting for transfers between devices  38.5 us (24%)
  other arithmetic  18.9 us (12%)
  local copies, waits for them, and re-layouts  2.51 us (2%)
    dot_general x2, matrix products, project_body(): jnp.einsum('nrj,nij->nri', rows_low, slices, preferred_element_type=jnp.f...  22.1 us
    dot_general x2, matrix products, project_body(): jnp.einsum('nsi,nij->nsj', rotated, slices, preferred_element_type=jnp.fl...  19.3 us
    ppermute x7, waiting for transfers between devices, radix_scatter(): got = lax.ppermute(send, axis, xor_pairs(size, mask))  12.4 us
    ppermute x7, starting transfers between devices, radix_scatter(): got = lax.ppermute(send, axis, xor_pairs(size, mask))  11.9 us
    ppermute x4, starting transfers between devices, halving_scatter(): got = lax.ppermute(send, axis, xor_pairs(size, bit))  11.8 us
    ppermute x4, waiting for transfers between devices, halving_scatter(): got = lax.ppermute(send, axis, xor_pairs(size, bit))  11.1 us
    ppermute x7, starting transfers between devices, radix_gather(): got = lax.ppermute(x, axis, xor_pairs(size, mask))  10.8 us
    ppermute x7, waiting for transfers between devices, radix_gather(): got = lax.ppermute(x, axis, xor_pairs(size, mask))  9.98 us
  transfers between devices with their start and end apart: 22, of which 16 were waited for; matrix products, arithmetic and copies ran while one was open for 13% of the time, Pallas kernels for 0%

profile of v8, /device:TPU:1, one launch (start us, length us, event | category | flops | bytes accessed | tf_op | source)
XLA Modules:
  0.0 162.1 jit_solution(14521831323514006575)
XLA Ops:
  0.6 0.7 compare_convert_fusion
  1.3 0.9 select_reduce_fusion.3
  2.2 1.1 slice_bitcast_fusion.3
  3.3 1.1 fusion.235
  4.4 1.2 fusion.17
  5.6 11.0 %fusion.12 = f32[8,48,512]{2,1,0:T(8,128)S(1)} fusion(bf16[8,512,2048]{2,1,0:T(8,128)(2,1)} %param.6, pred[8]{0:T(512)(128)(4,1)S(1)} %broadcast_compare_fusion, bf16[48,2048]{1,0:T(8,128)(2,1)S(1)} %get-tuple-element.20, bf16[48,2048]{1,0:T(8,128)(2,1)S(1)} %get-tuple-element.19), kind=kOutput, calls=%fused_computation.12 | convolution fusion | flops 806092800 | bytes 17956872 | tf_op jit(solution)/shard_map/nrj,nij->nri/dot_general | solution.py:128
  16.7 1.5 collective-permute-start
  18.7 8.8 %custom-call.7 = f32[2,48,48]{2,1,0:T(8,128)S(1)} custom-call(f32[2,48,48]{2,1,0:T(8,128)S(1)} %fusion.192), custom_call_target="Cholesky" | custom-call | tf_op jit(solution)/shard_map/jit(cholesky)/cholesky | solution.py:150
  27.7 1.5 collective-permute-start.1
  29.3 4.9 %collective-permute-done.1 = f32[2,48,512]{2,1,0:T(8,128)S(1)} collective-permute-done((f32[2,48,512]{2,1,0:T(8,128)S(1)}, f32[2,48,512]{2,1,0:T(8,128)S(1)}, u32[]{:S(2)}, u32[]{:S(2)}) %collective-permute-start.1) | collective-permute-done | bytes 196640 | tf_op jit(solution)/shard_map/ppermute | solution.py:49
  34.5 0.4 select_reduce_fusion.1
  38.7 1.5 collective-permute-start.2
  40.3 1.9 %collective-permute-done.2 = bf16[2,48,512]{2,1,0:T(8,128)(2,1)S(1)} collective-permute-done((bf16[2,48,512]{2,1,0:T(8,128)(2,1)S(1)}, bf16[2,48,512]{2,1,0:T(8,128)(2,1)S(1)}, u32[]{:S(2)}, u32[]{:S(2)}) %collective-permute-start.2) | collective-permute-done | bytes 98336 | tf_op jit(solution)/shard_map/ppermute | solution.py:58
  42.2 2.3 %collective-permute-start.3 = (bf16[4,48,512]{2,1,0:T(8,128)(2,1)S(1)}, bf16[4,48,512]{2,1,0:T(8,128)(2,1)S(1)}, u32[]{:S(2)}, u32[]{:S(2)}) collective-permute-start(bf16[4,48,512]{2,1,0:T(8,128)(2,1)S(1)} %maximum_select_fusion.4), channel_id=1, source_target_pairs={{0,1},{1,0},{2,3},{3,2},{4,5},{5,4},{6,7},{7,6},{8,9},{9,8},{10,11... | collective-permute-start | bytes 589832 | tf_op jit(solution)/shard_map/ppermute | solution.py:58
  44.5 1.1 collective-permute-done.3
  45.6 8.8 %fusion.20 = f32[8,48,2048]{2,1,0:T(8,128)S(1)} fusion(bf16[8,512,2048]{2,1,0:T(8,128)(2,1)} %param.6, bf16[4,48,512]{2,1,0:T(8,128)(2,1)S(1)} %maximum_select_fusion.4, bf16[4,48,512]{2,1,0:T(8,128)(2,1)S(1)} %collective-permute-done.3, pred[]{:T(512)S(6)} %ne.14), kind=kOutput, calls=%fused_computation.26 | convolution fusion | flops 805896192 | bytes 20316160 | tf_op jit(solution)/shard_map/nsi,nij->nsj/dot_general | solution.py:143
  54.4 2.3 %fusion.4 = f32[2,48,2048]{2,1,0:T(8,128)S(1)} fusion(f32[8,48,2048]{2,1,0:T(8,128)S(1)} %fusion.20, f32[8,48,48]{1,2,0:T(8,128)S(1)} %copy.20, f32[8,2]{0,1:T(2,128)S(1)} %compare_convert_fusion.1), kind=kOutput, calls=%fused_computation.6 | convolution fusion | flops 906006528 | bytes 4005952 | tf_op jit(solution)/shard_map/nhsr,nsj->hrj/dot_general | solution.py:189
  56.8 1.4 collective-permute-start.4
  58.2 2.5 %collective-permute-start.5 = (f32[2,48,512]{2,1,0:T(8,128)S(1)}, f32[2,48,512]{2,1,0:T(8,128)S(1)}, u32[]{:S(2)}, u32[]{:S(2)}) collective-permute-start(f32[2,48,512]{2,1,0:T(8,128)S(1)} %get-tuple-element.18), channel_id=1, source_target_pairs={{0,64},{4,68},{8,72},{12,76},{16,80},{20,84},{24,88},{28,92},{32,9... | collective-permute-start | bytes 589832 | tf_op jit(solution)/shard_map/ppermute | solution.py:84
  60.9 2.1 %collective-permute-done.4 = f32[2,48,512]{2,1,0:T(8,128)S(1)} collective-permute-done((f32[2,48,512]{2,1,0:T(8,128)S(1)}, f32[2,48,512]{2,1,0:T(8,128)S(1)}, u32[]{:S(2)}, u32[]{:S(2)}) %collective-permute-start.4) | collective-permute-done | bytes 196640 | tf_op jit(solution)/shard_map/ppermute | solution.py:84
  63.0 6.6 %collective-permute-done.5 = f32[2,48,512]{2,1,0:T(8,128)S(1)} collective-permute-done((f32[2,48,512]{2,1,0:T(8,128)S(1)}, f32[2,48,512]{2,1,0:T(8,128)S(1)}, u32[]{:S(2)}, u32[]{:S(2)}) %collective-permute-start.5) | collective-permute-done | bytes 196640 | tf_op jit(solution)/shard_map/ppermute | solution.py:84
  69.5 2.4 %collective-permute-done.6 = f32[2,48,512]{2,1,0:T(8,128)S(1)} collective-permute-done((f32[2,48,512]{2,1,0:T(8,128)S(1)}, f32[2,48,512]{2,1,0:T(8,128)S(1)}, u32[]{:S(2)}, u32[]{:S(2)}) %collective-permute-start.6) | collective-permute-done | bytes 196640 | tf_op jit(solution)/shard_map/ppermute | solution.py:84
  72.1 1.7 %collective-permute-start.7 = (f32[2,48,128]{2,1,0:T(8,128)S(1)}, f32[2,48,128]{2,1,0:T(8,128)S(1)}, u32[]{:S(2)}, u32[]{:S(2)}) collective-permute-start(f32[2,48,128]{2,1,0:T(8,128)S(1)} %get-tuple-element.21), channel_id=1, source_target_pairs={{0,8},{4,12},{8,0},{12,4},{16,24},{20,28},{24,16},{28,20},{32,40},... | collective-permute-start | bytes 147464 | tf_op jit(solution)/shard_map/ppermute | solution.py:84
  73.8 3.3 %collective-permute-start.8 = (f32[2,48,128]{2,1,0:T(8,128)S(1)}, f32[2,48,128]{2,1,0:T(8,128)S(1)}, u32[]{:S(2)}, u32[]{:S(2)}) collective-permute-start(f32[2,48,128]{2,1,0:T(8,128)S(1)} %get-tuple-element.23), channel_id=1, source_target_pairs={{0,16},{4,20},{8,24},{12,28},{16,0},{20,4},{24,8},{28,12},{32,48},... | collective-permute-start | bytes 147464 | tf_op jit(solution)/shard_map/ppermute | solution.py:84
  77.2 7.4 %custom-call.8 = f32[2,1,48,48]{2,3,1,0:T(8,128)S(1)} custom-call(f32[2,1,48,48]{3,2,1,0:T(8,128)S(1)} %select_bitcast_fusion), custom_call_target="InvertDiagBlocksLowerTriangular" | custom-call | tf_op jit(solution)/shard_map/triangular_solve | solution.py:152
  84.7 3.0 %collective-permute-start.10 = (f32[2,48,64]{2,1,0:T(8,128)S(1)}, f32[2,48,64]{2,1,0:T(8,128)S(1)}, u32[]{:S(2)}, u32[]{:S(2)}) collective-permute-start(f32[2,48,64]{2,1,0:T(8,128)S(1)} %constant_dynamic-slice_fusion), channel_id=1, source_target_pairs={{0,4},{4,0},{8,12},{12,8},{16,20},{20,16},{24,28},{28,24},{32,36},... | collective-permute-start | bytes 73736 | tf_op jit(solution)/shard_map/ppermute | solution.py:84
  87.9 1.3 collective-permute-done.10
  89.7 3.0 %collective-permute-start.11 = (f32[2,48,64]{2,1,0:T(8,128)S(1)}, f32[2,48,64]{2,1,0:T(8,128)S(1)}, u32[]{:S(2)}, u32[]{:S(2)}) collective-permute-start(f32[2,48,64]{2,1,0:T(8,128)S(1)} %fusion.236), channel_id=1, source_target_pairs={{0,4},{4,0},{8,12},{12,8},{16,20},{20,16},{24,28},{28,24},{32,36},... | collective-permute-start | bytes 73736 | tf_op jit(solution)/shard_map/ppermute | solution.py:101
  92.9 1.3 collective-permute-done.11
  94.2 0.5 dynamic_update_slice.31
  94.8 3.8 %collective-permute-start.13 = (f32[2,48,128]{2,1,0:T(8,128)S(1)}, f32[2,48,128]{2,1,0:T(8,128)S(1)}, u32[]{:S(2)}, u32[]{:S(2)}) collective-permute-start(f32[2,48,128]{2,1,0:T(8,128)S(1)} %dynamic_update_slice.31), channel_id=1, source_target_pairs={{0,16},{4,20},{8,24},{12,28},{16,0},{20,4},{24,8},{28,12},{32,48},... | collective-permute-start | bytes 147464 | tf_op jit(solution)/shard_map/ppermute | solution.py:101
  98.7 1.9 %collective-permute-done.13 = f32[2,48,128]{2,1,0:T(8,128)S(1)} collective-permute-done((f32[2,48,128]{2,1,0:T(8,128)S(1)}, f32[2,48,128]{2,1,0:T(8,128)S(1)}, u32[]{:S(2)}, u32[]{:S(2)}) %collective-permute-start.13) | collective-permute-done | bytes 49184 | tf_op jit(solution)/shard_map/ppermute | solution.py:101
  100.6 2.1 %collective-permute-done.14 = f32[2,48,128]{2,1,0:T(8,128)S(1)} collective-permute-done((f32[2,48,128]{2,1,0:T(8,128)S(1)}, f32[2,48,128]{2,1,0:T(8,128)S(1)}, u32[]{:S(2)}, u32[]{:S(2)}) %collective-permute-start.14) | collective-permute-done | bytes 49184 | tf_op jit(solution)/shard_map/ppermute | solution.py:101
  102.8 1.4 collective-permute-start.16
  104.2 2.5 %collective-permute-start.17 = (f32[2,48,512]{2,1,0:T(8,128)S(1)}, f32[2,48,512]{2,1,0:T(8,128)S(1)}, u32[]{:S(2)}, u32[]{:S(2)}) collective-permute-start(f32[2,48,512]{2,1,0:T(8,128)S(1)} %constant_dynamic-update-slice_fusion.4), channel_id=1, source_target_pairs={{0,96},{4,100},{8,104},{12,108},{16,112},{20,116},{24,120},{28,124... | collective-permute-start | bytes 589832 | tf_op jit(solution)/shard_map/ppermute | solution.py:101
  106.8 0.6 collective-permute-done.15
  107.3 2.1 %collective-permute-done.16 = f32[2,48,512]{2,1,0:T(8,128)S(1)} collective-permute-done((f32[2,48,512]{2,1,0:T(8,128)S(1)}, f32[2,48,512]{2,1,0:T(8,128)S(1)}, u32[]{:S(2)}, u32[]{:S(2)}) %collective-permute-start.16) | collective-permute-done | bytes 196640 | tf_op jit(solution)/shard_map/ppermute | solution.py:101
  109.5 2.0 %collective-permute-done.17 = f32[2,48,512]{2,1,0:T(8,128)S(1)} collective-permute-done((f32[2,48,512]{2,1,0:T(8,128)S(1)}, f32[2,48,512]{2,1,0:T(8,128)S(1)}, u32[]{:S(2)}, u32[]{:S(2)}) %collective-permute-start.17) | collective-permute-done | bytes 196640 | tf_op jit(solution)/shard_map/ppermute | solution.py:101
  111.5 11.2 %fusion.7 = f32[8,48,512]{2,1,0:T(8,128)S(1)} fusion(bf16[8,512,2048]{2,1,0:T(8,128)(2,1)} %param.6, f32[48,2048]{1,0:T(8,128)S(1)} %get-tuple-element.15, f32[48,2048]{1,0:T(8,128)S(1)} %get-tuple-element.14, pred[8]{0:T(512)(128)(4,1)S(1)} %broadcast_compare_fusion), kind=kOutput, calls=%fused_computation.7 | convolution fusion | flops 806092800 | bytes 18350088 | tf_op jit(solution)/shard_map/nrj,nij->nri/dot_general | solution.py:128
  122.8 7.5 %collective-permute-start.18 = (f32[4,48,512]{2,1,0:T(8,128)S(1)}, f32[4,48,512]{2,1,0:T(8,128)S(1)}, u32[]{:S(2)}, u32[]{:S(2)}) collective-permute-start(f32[4,48,512]{2,1,0:T(8,128)S(1)} %slice_select_fusion), channel_id=1, source_target_pairs={{0,1},{1,0},{2,3},{3,2},{4,5},{5,4},{6,7},{7,6},{8,9},{9,8},{10,11... | collective-permute-start | bytes 1179656 | tf_op jit(solution)/shard_map/ppermute | solution.py:49
  130.3 1.3 collective-permute-done.18
  131.8 1.4 collective-permute-start.19
  133.2 4.8 %collective-permute-done.19 = f32[2,48,512]{2,1,0:T(8,128)S(1)} collective-permute-done((f32[2,48,512]{2,1,0:T(8,128)S(1)}, f32[2,48,512]{2,1,0:T(8,128)S(1)}, u32[]{:S(2)}, u32[]{:S(2)}) %collective-permute-start.19) | collective-permute-done | bytes 196640 | tf_op jit(solution)/shard_map/ppermute | solution.py:49
  142.5 1.4 collective-permute-start.20
  143.9 2.2 %collective-permute-done.20 = bf16[2,48,512]{2,1,0:T(8,128)(2,1)S(1)} collective-permute-done((bf16[2,48,512]{2,1,0:T(8,128)(2,1)S(1)}, bf16[2,48,512]{2,1,0:T(8,128)(2,1)S(1)}, u32[]{:S(2)}, u32[]{:S(2)}) %collective-permute-start.20) | collective-permute-done | bytes 98336 | tf_op jit(solution)/shard_map/ppermute | solution.py:58
  146.1 2.7 %collective-permute-start.21 = (bf16[4,48,512]{2,1,0:T(8,128)(2,1)S(1)}, bf16[4,48,512]{2,1,0:T(8,128)(2,1)S(1)}, u32[]{:S(2)}, u32[]{:S(2)}) collective-permute-start(bf16[4,48,512]{2,1,0:T(8,128)(2,1)S(1)} %maximum_select_fusion.5), channel_id=1, source_target_pairs={{0,1},{1,0},{2,3},{3,2},{4,5},{5,4},{6,7},{7,6},{8,9},{9,8},{10,11... | collective-permute-start | bytes 589832 | tf_op jit(solution)/shard_map/ppermute | solution.py:58
  148.8 2.8 %fusion = f32[8,48,2048]{2,1,0:T(8,128)S(1)} fusion(f32[48,2048]{1,0:T(8,128)S(1)} %get-tuple-element.15, f32[48,2048]{1,0:T(8,128)S(1)} %get-tuple-element.14, pred[8]{0:T(512)(128)(4,1)S(1)} %broadcast_compare_fusion, f32[8,48]{1,0:T(8,128)S(1)} %fusion.205, f32[48,48]{1,0:T(8,128)S(1)} %get-tuple-element.27, f32[48,48]{1,0:T(8,128)S(1)} %get-tuple-element.26), kind=kOutput, calls=%fused_computation | convolution fusion | flops 453808128 | bytes 3952136 | tf_op jit(solution)/shard_map/nrs,nsj->nrj/dot_general | solution.py:200
  151.6 10.5 %convolution_subtract_fusion = f32[8,48,2048]{2,1,0:T(8,128)} fusion(f32[8,48,2048]{2,1,0:T(8,128)S(1)} %fusion, bf16[8,512,2048]{2,1,0:T(8,128)(2,1)} %param.6, bf16[4,48,512]{2,1,0:T(8,128)(2,1)S(1)} %maximum_select_fusion.5, bf16[4,48,512]{2,1,0:T(8,128)(2,1)S(1)} %collective-permute-done.21, pred[]{:T(512)S(6)} %ne.14), kind=kOutput, calls=%fused_computation.5 | convolution fusion | flops 806682624 | bytes 23461888 | tf_op jit(solution)/shard_map/nsi,nij->nsj/dot_general | solution.py:143
  (128 shorter events, 11.3 us)
Async XLA Ops:
  5.6 12.5 %copy-start.2 = (f32[256,48]{0,1:T(8,128)S(1)}, f32[256,48]{0,1:T(8,128)}, u32[]{:S(2)}) copy-start(f32[256,48]{0,1:T(8,128)} %param.8) | copy-start | bytes 147460
  5.6 21.9 %copy-start.1 = (f32[2,48,48]{2,1,0:T(8,128)S(1)}, f32[2,48,48]{2,1,0:T(8,128)}, u32[]{:S(2)}) copy-start(f32[2,48,48]{2,1,0:T(8,128)} %param.9) | copy-start | bytes 55300
  16.7 10.8 %collective-permute-start = (f32[4,48,512]{2,1,0:T(8,128)S(1)}, f32[4,48,512]{2,1,0:T(8,128)S(1)}, u32[]{:S(2)}, u32[]{:S(2)}) collective-permute-start(f32[4,48,512]{2,1,0:T(8,128)S(1)} %slice_select_fusion.1), channel_id=1, source_target_pairs={{0,1},{1,0},{2,3},{3,2},{4,5},{5,4},{6,7},{7,6},{8,9},{9,8},{10,11... | collective-permute-start | bytes 1179656 | tf_op jit(solution)/shard_map/ppermute | solution.py:49
  27.7 6.5 %collective-permute-start.1 = (f32[2,48,512]{2,1,0:T(8,128)S(1)}, f32[2,48,512]{2,1,0:T(8,128)S(1)}, u32[]{:S(2)}, u32[]{:S(2)}) collective-permute-start(f32[2,48,512]{2,1,0:T(8,128)S(1)} %slice_select_fusion.3), channel_id=1, source_target_pairs={{0,2},{1,3},{2,0},{3,1},{4,6},{5,7},{6,4},{7,5},{8,10},{9,11},{10,... | collective-permute-start | bytes 589832 | tf_op jit(solution)/shard_map/ppermute | solution.py:49
  38.7 3.5 %collective-permute-start.2 = (bf16[2,48,512]{2,1,0:T(8,128)(2,1)S(1)}, bf16[2,48,512]{2,1,0:T(8,128)(2,1)S(1)}, u32[]{:S(2)}, u32[]{:S(2)}) collective-permute-start(bf16[2,48,512]{2,1,0:T(8,128)(2,1)S(1)} %convolution_convert_fusion.1), channel_id=1, source_target_pairs={{0,2},{1,3},{2,0},{3,1},{4,6},{5,7},{6,4},{7,5},{8,10},{9,11},{10,... | collective-permute-start | bytes 294920 | tf_op jit(solution)/shard_map/ppermute | solution.py:58
  42.2 3.4 %collective-permute-start.3 = (bf16[4,48,512]{2,1,0:T(8,128)(2,1)S(1)}, bf16[4,48,512]{2,1,0:T(8,128)(2,1)S(1)}, u32[]{:S(2)}, u32[]{:S(2)}) collective-permute-start(bf16[4,48,512]{2,1,0:T(8,128)(2,1)S(1)} %maximum_select_fusion.4), channel_id=1, source_target_pairs={{0,1},{1,0},{2,3},{3,2},{4,5},{5,4},{6,7},{7,6},{8,9},{9,8},{10,11... | collective-permute-start | bytes 589832 | tf_op jit(solution)/shard_map/ppermute | solution.py:58
  56.8 6.2 %collective-permute-start.4 = (f32[2,48,512]{2,1,0:T(8,128)S(1)}, f32[2,48,512]{2,1,0:T(8,128)S(1)}, u32[]{:S(2)}, u32[]{:S(2)}) collective-permute-start(f32[2,48,512]{2,1,0:T(8,128)S(1)} %get-tuple-element.16), channel_id=1, source_target_pairs={{0,32},{4,36},{8,40},{12,44},{16,48},{20,52},{24,56},{28,60},{32,0... | collective-permute-start | bytes 589832 | tf_op jit(solution)/shard_map/ppermute | solution.py:84
  58.2 11.3 %collective-permute-start.5 = (f32[2,48,512]{2,1,0:T(8,128)S(1)}, f32[2,48,512]{2,1,0:T(8,128)S(1)}, u32[]{:S(2)}, u32[]{:S(2)}) collective-permute-start(f32[2,48,512]{2,1,0:T(8,128)S(1)} %get-tuple-element.18), channel_id=1, source_target_pairs={{0,64},{4,68},{8,72},{12,76},{16,80},{20,84},{24,88},{28,92},{32,9... | collective-permute-start | bytes 589832 | tf_op jit(solution)/shard_map/ppermute | solution.py:84
  60.7 11.3 %collective-permute-start.6 = (f32[2,48,512]{2,1,0:T(8,128)S(1)}, f32[2,48,512]{2,1,0:T(8,128)S(1)}, u32[]{:S(2)}, u32[]{:S(2)}) collective-permute-start(f32[2,48,512]{2,1,0:T(8,128)S(1)} %get-tuple-element.17), channel_id=1, source_target_pairs={{0,96},{4,100},{8,104},{12,108},{16,112},{20,116},{24,120},{28,124... | collective-permute-start | bytes 589832 | tf_op jit(solution)/shard_map/ppermute | solution.py:84
  72.1 12.5 %collective-permute-start.7 = (f32[2,48,128]{2,1,0:T(8,128)S(1)}, f32[2,48,128]{2,1,0:T(8,128)S(1)}, u32[]{:S(2)}, u32[]{:S(2)}) collective-permute-start(f32[2,48,128]{2,1,0:T(8,128)S(1)} %get-tuple-element.21), channel_id=1, source_target_pairs={{0,8},{4,12},{8,0},{12,4},{16,24},{20,28},{24,16},{28,20},{32,40},... | collective-permute-start | bytes 147464 | tf_op jit(solution)/shard_map/ppermute | solution.py:84
  73.8 10.8 %collective-permute-start.8 = (f32[2,48,128]{2,1,0:T(8,128)S(1)}, f32[2,48,128]{2,1,0:T(8,128)S(1)}, u32[]{:S(2)}, u32[]{:S(2)}) collective-permute-start(f32[2,48,128]{2,1,0:T(8,128)S(1)} %get-tuple-element.23), channel_id=1, source_target_pairs={{0,16},{4,20},{8,24},{12,28},{16,0},{20,4},{24,8},{28,12},{32,48},... | collective-permute-start | bytes 147464 | tf_op jit(solution)/shard_map/ppermute | solution.py:84
  77.1 7.5 %collective-permute-start.9 = (f32[2,48,128]{2,1,0:T(8,128)S(1)}, f32[2,48,128]{2,1,0:T(8,128)S(1)}, u32[]{:S(2)}, u32[]{:S(2)}) collective-permute-start(f32[2,48,128]{2,1,0:T(8,128)S(1)} %get-tuple-element.22), channel_id=1, source_target_pairs={{0,24},{4,28},{8,16},{12,20},{16,8},{20,12},{24,0},{28,4},{32,56},... | collective-permute-start | bytes 147464 | tf_op jit(solution)/shard_map/ppermute | solution.py:84
  84.7 4.5 %collective-permute-start.10 = (f32[2,48,64]{2,1,0:T(8,128)S(1)}, f32[2,48,64]{2,1,0:T(8,128)S(1)}, u32[]{:S(2)}, u32[]{:S(2)}) collective-permute-start(f32[2,48,64]{2,1,0:T(8,128)S(1)} %constant_dynamic-slice_fusion), channel_id=1, source_target_pairs={{0,4},{4,0},{8,12},{12,8},{16,20},{20,16},{24,28},{28,24},{32,36},... | collective-permute-start | bytes 73736 | tf_op jit(solution)/shard_map/ppermute | solution.py:84
  89.7 4.5 %collective-permute-start.11 = (f32[2,48,64]{2,1,0:T(8,128)S(1)}, f32[2,48,64]{2,1,0:T(8,128)S(1)}, u32[]{:S(2)}, u32[]{:S(2)}) collective-permute-start(f32[2,48,64]{2,1,0:T(8,128)S(1)} %fusion.236), channel_id=1, source_target_pairs={{0,4},{4,0},{8,12},{12,8},{16,20},{20,16},{24,28},{28,24},{32,36},... | collective-permute-start | bytes 73736 | tf_op jit(solution)/shard_map/ppermute | solution.py:101
  94.7 4.0 %collective-permute-start.12 = (f32[2,48,128]{2,1,0:T(8,128)S(1)}, f32[2,48,128]{2,1,0:T(8,128)S(1)}, u32[]{:S(2)}, u32[]{:S(2)}) collective-permute-start(f32[2,48,128]{2,1,0:T(8,128)S(1)} %dynamic_update_slice.31), channel_id=1, source_target_pairs={{0,8},{4,12},{8,0},{12,4},{16,24},{20,28},{24,16},{28,20},{32,40},... | collective-permute-start | bytes 147464 | tf_op jit(solution)/shard_map/ppermute | solution.py:101
  94.8 5.8 %collective-permute-start.13 = (f32[2,48,128]{2,1,0:T(8,128)S(1)}, f32[2,48,128]{2,1,0:T(8,128)S(1)}, u32[]{:S(2)}, u32[]{:S(2)}) collective-permute-start(f32[2,48,128]{2,1,0:T(8,128)S(1)} %dynamic_update_slice.31), channel_id=1, source_target_pairs={{0,16},{4,20},{8,24},{12,28},{16,0},{20,4},{24,8},{28,12},{32,48},... | collective-permute-start | bytes 147464 | tf_op jit(solution)/shard_map/ppermute | solution.py:101
  98.6 4.2 %collective-permute-start.14 = (f32[2,48,128]{2,1,0:T(8,128)S(1)}, f32[2,48,128]{2,1,0:T(8,128)S(1)}, u32[]{:S(2)}, u32[]{:S(2)}) collective-permute-start(f32[2,48,128]{2,1,0:T(8,128)S(1)} %dynamic_update_slice.31), channel_id=1, source_target_pairs={{0,24},{4,28},{8,16},{12,20},{16,8},{20,12},{24,0},{28,4},{32,56},... | collective-permute-start | bytes 147464 | tf_op jit(solution)/shard_map/ppermute | solution.py:101
  102.8 4.5 %collective-permute-start.15 = (f32[2,48,512]{2,1,0:T(8,128)S(1)}, f32[2,48,512]{2,1,0:T(8,128)S(1)}, u32[]{:S(2)}, u32[]{:S(2)}) collective-permute-start(f32[2,48,512]{2,1,0:T(8,128)S(1)} %constant_dynamic-update-slice_fusion.4), channel_id=1, source_target_pairs={{0,32},{4,36},{8,40},{12,44},{16,48},{20,52},{24,56},{28,60},{32,0... | collective-permute-start | bytes 589832 | tf_op jit(solution)/shard_map/ppermute | solution.py:101
  102.8 6.6 %collective-permute-start.16 = (f32[2,48,512]{2,1,0:T(8,128)S(1)}, f32[2,48,512]{2,1,0:T(8,128)S(1)}, u32[]{:S(2)}, u32[]{:S(2)}) collective-permute-start(f32[2,48,512]{2,1,0:T(8,128)S(1)} %constant_dynamic-update-slice_fusion.4), channel_id=1, source_target_pairs={{0,64},{4,68},{8,72},{12,76},{16,80},{20,84},{24,88},{28,92},{32,9... | collective-permute-start | bytes 589832 | tf_op jit(solution)/shard_map/ppermute | solution.py:101
  104.2 7.3 %collective-permute-start.17 = (f32[2,48,512]{2,1,0:T(8,128)S(1)}, f32[2,48,512]{2,1,0:T(8,128)S(1)}, u32[]{:S(2)}, u32[]{:S(2)}) collective-permute-start(f32[2,48,512]{2,1,0:T(8,128)S(1)} %constant_dynamic-update-slice_fusion.4), channel_id=1, source_target_pairs={{0,96},{4,100},{8,104},{12,108},{16,112},{20,116},{24,120},{28,124... | collective-permute-start | bytes 589832 | tf_op jit(solution)/shard_map/ppermute | solution.py:101
  111.5 11.2 %copy-start = (f32[2,48,2048]{2,1,0:T(8,128)}, f32[2,48,2048]{2,1,0:T(8,128)S(1)}, u32[]{:S(2)}) copy-start(f32[2,48,2048]{2,1,0:T(8,128)S(1)} %constant_dynamic-update-slice_fusion) | copy-start | bytes 2359300
  122.8 8.9 %collective-permute-start.18 = (f32[4,48,512]{2,1,0:T(8,128)S(1)}, f32[4,48,512]{2,1,0:T(8,128)S(1)}, u32[]{:S(2)}, u32[]{:S(2)}) collective-permute-start(f32[4,48,512]{2,1,0:T(8,128)S(1)} %slice_select_fusion), channel_id=1, source_target_pairs={{0,1},{1,0},{2,3},{3,2},{4,5},{5,4},{6,7},{7,6},{8,9},{9,8},{10,11... | collective-permute-start | bytes 1179656 | tf_op jit(solution)/shard_map/ppermute | solution.py:49
  131.8 6.2 %collective-permute-start.19 = (f32[2,48,512]{2,1,0:T(8,128)S(1)}, f32[2,48,512]{2,1,0:T(8,128)S(1)}, u32[]{:S(2)}, u32[]{:S(2)}) collective-permute-start(f32[2,48,512]{2,1,0:T(8,128)S(1)} %slice_select_fusion.2), channel_id=1, source_target_pairs={{0,2},{1,3},{2,0},{3,1},{4,6},{5,7},{6,4},{7,5},{8,10},{9,11},{10,... | collective-permute-start | bytes 589832 | tf_op jit(solution)/shard_map/ppermute | solution.py:49
  142.5 3.5 %collective-permute-start.20 = (bf16[2,48,512]{2,1,0:T(8,128)(2,1)S(1)}, bf16[2,48,512]{2,1,0:T(8,128)(2,1)S(1)}, u32[]{:S(2)}, u32[]{:S(2)}) collective-permute-start(bf16[2,48,512]{2,1,0:T(8,128)(2,1)S(1)} %convolution_convert_fusion), channel_id=1, source_target_pairs={{0,2},{1,3},{2,0},{3,1},{4,6},{5,7},{6,4},{7,5},{8,10},{9,11},{10,... | collective-permute-start | bytes 294920 | tf_op jit(solution)/shard_map/ppermute | solution.py:58
  146.1 5.5 %collective-permute-start.21 = (bf16[4,48,512]{2,1,0:T(8,128)(2,1)S(1)}, bf16[4,48,512]{2,1,0:T(8,128)(2,1)S(1)}, u32[]{:S(2)}, u32[]{:S(2)}) collective-permute-start(bf16[4,48,512]{2,1,0:T(8,128)(2,1)S(1)} %maximum_select_fusion.5), channel_id=1, source_target_pairs={{0,1},{1,0},{2,3},{3,2},{4,5},{5,4},{6,7},{7,6},{8,9},{9,8},{10,11... | collective-permute-start | bytes 589832 | tf_op jit(solution)/shard_map/ppermute | solution.py:58

commit v9 on v8

--- a/solution.py
+++ b/solution.py
@@ -127,7 +127,7 @@
     run_count = slices.shape[0]
     partial_basis = jnp.einsum("nrj,nij->nri", rows_low, slices, preferred_element_type=jnp.float32)
     if carried is not None:
-        partial_basis, carried = lax.optimization_barrier((partial_basis, carried))
+        carried = lax.optimization_barrier((partial_basis, carried))[1]
     basis = halving_scatter(partial_basis, "chan", chan_size, chan_bits, 0)
     part = basis.shape[0]
     first = block_index("chan", chan_bits) * part
@@ -177,8 +177,12 @@
         own_rows = jnp.where(first_half, spectra[0][None], spectra[1][None])
         own_mix = jnp.where(first_half, mixing[0][None], mixing[1][None]) * my_loads[:, None, :]
         member = (halves[:, None] == jnp.arange(2, dtype=jnp.int32)[None, :]).astype(jnp.float32)
-        cross = jnp.einsum("kh,kr,ks->hrs", member, loadings, loadings, precision=lax.Precision.HIGHEST)
-        inner_mix = jnp.einsum("hsr,hst->hrt", mixing, mixing, precision=lax.Precision.HIGHEST)
+        cross = jnp.einsum(
+            "kh,kr,ks->hrs", member, loadings, loadings, precision=lax.Precision.HIGHEST
+        )
+        inner_mix = jnp.einsum(
+            "hsr,hst->hrt", mixing, mixing, precision=lax.Precision.HIGHEST
+        )
         system = inner_mix * cross
         projected, system = project(slices, own_rows, own_mix, chan_size, chan_bits, carried=system)
         inverse = lower_inverse(system)

time: 163 us -> 160 us (0.982)
  matrix products: 58.2 us -> 56.5 us
where the time goes in v9:
time: 160 us
  matrix products  56.5 us (35%)
  starting transfers between devices  42.4 us (26%)
  waiting for transfers between devices  38.5 us (24%)
  other arithmetic  18.2 us (11%)
  local copies, waits for them, and re-layouts  2.52 us (2%)
    dot_general x2, matrix products, project_body(): jnp.einsum('nrj,nij->nri', rows_low, slices, preferred_element_type=jnp.f...  22.1 us
    dot_general x2, matrix products, project_body(): jnp.einsum('nsi,nij->nsj', rotated, slices, preferred_element_type=jnp.fl...  19.3 us
    ppermute x7, waiting for transfers between devices, radix_scatter(): got = lax.ppermute(send, axis, xor_pairs(size, mask))  12.4 us
    ppermute x7, starting transfers between devices, radix_scatter(): got = lax.ppermute(send, axis, xor_pairs(size, mask))  11.9 us
    ppermute x4, starting transfers between devices, halving_scatter(): got = lax.ppermute(send, axis, xor_pairs(size, bit))  11.8 us
    ppermute x4, waiting for transfers between devices, halving_scatter(): got = lax.ppermute(send, axis, xor_pairs(size, bit))  11.1 us
    ppermute x7, starting transfers between devices, radix_gather(): got = lax.ppermute(x, axis, xor_pairs(size, mask))  10.8 us
    ppermute x7, waiting for transfers between devices, radix_gather(): got = lax.ppermute(x, axis, xor_pairs(size, mask))  9.99 us
  transfers between devices with their start and end apart: 22, of which 16 were waited for; matrix products, arithmetic and copies ran while one was open for 13% of the time, Pallas kernels for 0%

profile of v9, /device:TPU:1, one launch (start us, length us, event | category | flops | bytes accessed | tf_op | source)
XLA Modules:
  0.0 159.7 jit_solution(4080563641094200445)
XLA Ops:
  0.6 0.9 select_reduce_fusion.3
  1.6 1.1 slice_bitcast_fusion.3
  2.7 11.0 %fusion.12 = f32[8,48,512]{2,1,0:T(8,128)S(1)} fusion(bf16[8,512,2048]{2,1,0:T(8,128)(2,1)} %param.6, pred[8]{0:T(512)(128)(4,1)S(1)} %broadcast_compare_fusion, bf16[48,2048]{1,0:T(8,128)(2,1)S(1)} %get-tuple-element.18, bf16[48,2048]{1,0:T(8,128)(2,1)S(1)} %get-tuple-element.17), kind=kOutput, calls=%fused_computation.12 | convolution fusion | flops 806092800 | bytes 17956872 | tf_op jit(solution)/shard_map/nrj,nij->nri/dot_general | solution.py:128
  13.7 1.5 collective-permute-start
  16.3 8.8 %custom-call.7 = f32[2,48,48]{2,1,0:T(8,128)S(1)} custom-call(f32[2,48,48]{2,1,0:T(8,128)S(1)} %fusion.192), custom_call_target="Cholesky" | custom-call | tf_op jit(solution)/shard_map/jit(cholesky)/cholesky | solution.py:150
  25.3 1.5 collective-permute-start.1
  26.9 4.9 %collective-permute-done.1 = f32[2,48,512]{2,1,0:T(8,128)S(1)} collective-permute-done((f32[2,48,512]{2,1,0:T(8,128)S(1)}, f32[2,48,512]{2,1,0:T(8,128)S(1)}, u32[]{:S(2)}, u32[]{:S(2)}) %collective-permute-start.1) | collective-permute-done | bytes 196640 | tf_op jit(solution)/shard_map/ppermute | solution.py:49
  31.8 0.3 fusion.37
  32.1 0.4 select_reduce_fusion.1
  36.2 1.5 collective-permute-start.2
  37.9 1.9 %collective-permute-done.2 = bf16[2,48,512]{2,1,0:T(8,128)(2,1)S(1)} collective-permute-done((bf16[2,48,512]{2,1,0:T(8,128)(2,1)S(1)}, bf16[2,48,512]{2,1,0:T(8,128)(2,1)S(1)}, u32[]{:S(2)}, u32[]{:S(2)}) %collective-permute-start.2) | collective-permute-done | bytes 98336 | tf_op jit(solution)/shard_map/ppermute | solution.py:58
  39.8 2.3 %collective-permute-start.3 = (bf16[4,48,512]{2,1,0:T(8,128)(2,1)S(1)}, bf16[4,48,512]{2,1,0:T(8,128)(2,1)S(1)}, u32[]{:S(2)}, u32[]{:S(2)}) collective-permute-start(bf16[4,48,512]{2,1,0:T(8,128)(2,1)S(1)} %maximum_select_fusion.4), channel_id=1, source_target_pairs={{0,1},{1,0},{2,3},{3,2},{4,5},{5,4},{6,7},{7,6},{8,9},{9,8},{10,11... | collective-permute-start | bytes 589832 | tf_op jit(solution)/shard_map/ppermute | solution.py:58
  42.1 1.1 collective-permute-done.3
  43.2 8.8 %fusion.20 = f32[8,48,2048]{2,1,0:T(8,128)S(1)} fusion(bf16[8,512,2048]{2,1,0:T(8,128)(2,1)} %param.6, bf16[4,48,512]{2,1,0:T(8,128)(2,1)S(1)} %maximum_select_fusion.4, bf16[4,48,512]{2,1,0:T(8,128)(2,1)S(1)} %collective-permute-done.3, pred[]{:T(512)S(6)} %ne.14), kind=kOutput, calls=%fused_computation.26 | convolution fusion | flops 805896192 | bytes 20316160 | tf_op jit(solution)/shard_map/nsi,nij->nsj/dot_general | solution.py:143
  52.0 2.3 %fusion.4 = f32[2,48,2048]{2,1,0:T(8,128)S(1)} fusion(f32[8,48,2048]{2,1,0:T(8,128)S(1)} %fusion.20, f32[8,48,48]{1,2,0:T(8,128)S(1)} %copy.20, f32[8,2]{0,1:T(2,128)S(1)} %compare_convert_fusion.1), kind=kOutput, calls=%fused_computation.6 | convolution fusion | flops 906006528 | bytes 4005952 | tf_op jit(solution)/shard_map/nhsr,nsj->hrj/dot_general | solution.py:193
  54.4 1.4 collective-permute-start.4
  55.8 2.5 %collective-permute-start.5 = (f32[2,48,512]{2,1,0:T(8,128)S(1)}, f32[2,48,512]{2,1,0:T(8,128)S(1)}, u32[]{:S(2)}, u32[]{:S(2)}) collective-permute-start(f32[2,48,512]{2,1,0:T(8,128)S(1)} %get-tuple-element.16), channel_id=1, source_target_pairs={{0,64},{4,68},{8,72},{12,76},{16,80},{20,84},{24,88},{28,92},{32,9... | collective-permute-start | bytes 589832 | tf_op jit(solution)/shard_map/ppermute | solution.py:84
  58.5 2.1 %collective-permute-done.4 = f32[2,48,512]{2,1,0:T(8,128)S(1)} collective-permute-done((f32[2,48,512]{2,1,0:T(8,128)S(1)}, f32[2,48,512]{2,1,0:T(8,128)S(1)}, u32[]{:S(2)}, u32[]{:S(2)}) %collective-permute-start.4) | collective-permute-done | bytes 196640 | tf_op jit(solution)/shard_map/ppermute | solution.py:84
  60.6 6.6 %collective-permute-done.5 = f32[2,48,512]{2,1,0:T(8,128)S(1)} collective-permute-done((f32[2,48,512]{2,1,0:T(8,128)S(1)}, f32[2,48,512]{2,1,0:T(8,128)S(1)}, u32[]{:S(2)}, u32[]{:S(2)}) %collective-permute-start.5) | collective-permute-done | bytes 196640 | tf_op jit(solution)/shard_map/ppermute | solution.py:84
  67.1 2.4 %collective-permute-done.6 = f32[2,48,512]{2,1,0:T(8,128)S(1)} collective-permute-done((f32[2,48,512]{2,1,0:T(8,128)S(1)}, f32[2,48,512]{2,1,0:T(8,128)S(1)}, u32[]{:S(2)}, u32[]{:S(2)}) %collective-permute-start.6) | collective-permute-done | bytes 196640 | tf_op jit(solution)/shard_map/ppermute | solution.py:84
  69.7 1.7 %collective-permute-start.7 = (f32[2,48,128]{2,1,0:T(8,128)S(1)}, f32[2,48,128]{2,1,0:T(8,128)S(1)}, u32[]{:S(2)}, u32[]{:S(2)}) collective-permute-start(f32[2,48,128]{2,1,0:T(8,128)S(1)} %get-tuple-element.19), channel_id=1, source_target_pairs={{0,8},{4,12},{8,0},{12,4},{16,24},{20,28},{24,16},{28,20},{32,40},... | collective-permute-start | bytes 147464 | tf_op jit(solution)/shard_map/ppermute | solution.py:84
  71.4 3.3 %collective-permute-start.8 = (f32[2,48,128]{2,1,0:T(8,128)S(1)}, f32[2,48,128]{2,1,0:T(8,128)S(1)}, u32[]{:S(2)}, u32[]{:S(2)}) collective-permute-start(f32[2,48,128]{2,1,0:T(8,128)S(1)} %get-tuple-element.21), channel_id=1, source_target_pairs={{0,16},{4,20},{8,24},{12,28},{16,0},{20,4},{24,8},{28,12},{32,48},... | collective-permute-start | bytes 147464 | tf_op jit(solution)/shard_map/ppermute | solution.py:84
  74.8 7.4 %custom-call.8 = f32[2,1,48,48]{2,3,1,0:T(8,128)S(1)} custom-call(f32[2,1,48,48]{3,2,1,0:T(8,128)S(1)} %select_bitcast_fusion), custom_call_target="InvertDiagBlocksLowerTriangular" | custom-call | tf_op jit(solution)/shard_map/triangular_solve | solution.py:152
  82.3 2.9 %collective-permute-start.10 = (f32[2,48,64]{2,1,0:T(8,128)S(1)}, f32[2,48,64]{2,1,0:T(8,128)S(1)}, u32[]{:S(2)}, u32[]{:S(2)}) collective-permute-start(f32[2,48,64]{2,1,0:T(8,128)S(1)} %constant_dynamic-slice_fusion), channel_id=1, source_target_pairs={{0,4},{4,0},{8,12},{12,8},{16,20},{20,16},{24,28},{28,24},{32,36},... | collective-permute-start | bytes 73736 | tf_op jit(solution)/shard_map/ppermute | solution.py:84
  85.5 1.3 collective-permute-done.10
  87.3 3.0 %collective-permute-start.11 = (f32[2,48,64]{2,1,0:T(8,128)S(1)}, f32[2,48,64]{2,1,0:T(8,128)S(1)}, u32[]{:S(2)}, u32[]{:S(2)}) collective-permute-start(f32[2,48,64]{2,1,0:T(8,128)S(1)} %fusion.236), channel_id=1, source_target_pairs={{0,4},{4,0},{8,12},{12,8},{16,20},{20,16},{24,28},{28,24},{32,36},... | collective-permute-start | bytes 73736 | tf_op jit(solution)/shard_map/ppermute | solution.py:101
  90.5 1.3 collective-permute-done.11
  91.8 0.5 dynamic_update_slice.31
  92.4 3.8 %collective-permute-start.13 = (f32[2,48,128]{2,1,0:T(8,128)S(1)}, f32[2,48,128]{2,1,0:T(8,128)S(1)}, u32[]{:S(2)}, u32[]{:S(2)}) collective-permute-start(f32[2,48,128]{2,1,0:T(8,128)S(1)} %dynamic_update_slice.31), channel_id=1, source_target_pairs={{0,16},{4,20},{8,24},{12,28},{16,0},{20,4},{24,8},{28,12},{32,48},... | collective-permute-start | bytes 147464 | tf_op jit(solution)/shard_map/ppermute | solution.py:101
  96.3 1.9 %collective-permute-done.13 = f32[2,48,128]{2,1,0:T(8,128)S(1)} collective-permute-done((f32[2,48,128]{2,1,0:T(8,128)S(1)}, f32[2,48,128]{2,1,0:T(8,128)S(1)}, u32[]{:S(2)}, u32[]{:S(2)}) %collective-permute-start.13) | collective-permute-done | bytes 49184 | tf_op jit(solution)/shard_map/ppermute | solution.py:101
  98.2 2.1 %collective-permute-done.14 = f32[2,48,128]{2,1,0:T(8,128)S(1)} collective-permute-done((f32[2,48,128]{2,1,0:T(8,128)S(1)}, f32[2,48,128]{2,1,0:T(8,128)S(1)}, u32[]{:S(2)}, u32[]{:S(2)}) %collective-permute-start.14) | collective-permute-done | bytes 49184 | tf_op jit(solution)/shard_map/ppermute | solution.py:101
  100.4 1.4 collective-permute-start.16
  101.8 2.5 %collective-permute-start.17 = (f32[2,48,512]{2,1,0:T(8,128)S(1)}, f32[2,48,512]{2,1,0:T(8,128)S(1)}, u32[]{:S(2)}, u32[]{:S(2)}) collective-permute-start(f32[2,48,512]{2,1,0:T(8,128)S(1)} %constant_dynamic-update-slice_fusion.4), channel_id=1, source_target_pairs={{0,96},{4,100},{8,104},{12,108},{16,112},{20,116},{24,120},{28,124... | collective-permute-start | bytes 589832 | tf_op jit(solution)/shard_map/ppermute | solution.py:101
  104.4 0.6 collective-permute-done.15
  104.9 2.1 %collective-permute-done.16 = f32[2,48,512]{2,1,0:T(8,128)S(1)} collective-permute-done((f32[2,48,512]{2,1,0:T(8,128)S(1)}, f32[2,48,512]{2,1,0:T(8,128)S(1)}, u32[]{:S(2)}, u32[]{:S(2)}) %collective-permute-start.16) | collective-permute-done | bytes 196640 | tf_op jit(solution)/shard_map/ppermute | solution.py:101
  107.1 2.0 %collective-permute-done.17 = f32[2,48,512]{2,1,0:T(8,128)S(1)} collective-permute-done((f32[2,48,512]{2,1,0:T(8,128)S(1)}, f32[2,48,512]{2,1,0:T(8,128)S(1)}, u32[]{:S(2)}, u32[]{:S(2)}) %collective-permute-start.17) | collective-permute-done | bytes 196640 | tf_op jit(solution)/shard_map/ppermute | solution.py:101
  109.1 11.2 %fusion.7 = f32[8,48,512]{2,1,0:T(8,128)S(1)} fusion(bf16[8,512,2048]{2,1,0:T(8,128)(2,1)} %param.6, f32[48,2048]{1,0:T(8,128)S(1)} %get-tuple-element.13, f32[48,2048]{1,0:T(8,128)S(1)} %get-tuple-element.12, pred[8]{0:T(512)(128)(4,1)S(1)} %broadcast_compare_fusion), kind=kOutput, calls=%fused_computation.7 | convolution fusion | flops 806092800 | bytes 18350088 | tf_op jit(solution)/shard_map/nrj,nij->nri/dot_general | solution.py:128
  120.4 7.5 %collective-permute-start.18 = (f32[4,48,512]{2,1,0:T(8,128)S(1)}, f32[4,48,512]{2,1,0:T(8,128)S(1)}, u32[]{:S(2)}, u32[]{:S(2)}) collective-permute-start(f32[4,48,512]{2,1,0:T(8,128)S(1)} %slice_select_fusion), channel_id=1, source_target_pairs={{0,1},{1,0},{2,3},{3,2},{4,5},{5,4},{6,7},{7,6},{8,9},{9,8},{10,11... | collective-permute-start | bytes 1179656 | tf_op jit(solution)/shard_map/ppermute | solution.py:49
  127.9 1.3 collective-permute-done.18
  129.4 1.4 collective-permute-start.19
  130.8 4.8 %collective-permute-done.19 = f32[2,48,512]{2,1,0:T(8,128)S(1)} collective-permute-done((f32[2,48,512]{2,1,0:T(8,128)S(1)}, f32[2,48,512]{2,1,0:T(8,128)S(1)}, u32[]{:S(2)}, u32[]{:S(2)}) %collective-permute-start.19) | collective-permute-done | bytes 196640 | tf_op jit(solution)/shard_map/ppermute | solution.py:49
  135.6 0.3 fusion.34
  135.9 0.4 select_reduce_fusion
  140.1 1.4 collective-permute-start.20
  141.5 2.2 %collective-permute-done.20 = bf16[2,48,512]{2,1,0:T(8,128)(2,1)S(1)} collective-permute-done((bf16[2,48,512]{2,1,0:T(8,128)(2,1)S(1)}, bf16[2,48,512]{2,1,0:T(8,128)(2,1)S(1)}, u32[]{:S(2)}, u32[]{:S(2)}) %collective-permute-start.20) | collective-permute-done | bytes 98336 | tf_op jit(solution)/shard_map/ppermute | solution.py:58
  143.7 2.7 %collective-permute-start.21 = (bf16[4,48,512]{2,1,0:T(8,128)(2,1)S(1)}, bf16[4,48,512]{2,1,0:T(8,128)(2,1)S(1)}, u32[]{:S(2)}, u32[]{:S(2)}) collective-permute-start(bf16[4,48,512]{2,1,0:T(8,128)(2,1)S(1)} %maximum_select_fusion.5), channel_id=1, source_target_pairs={{0,1},{1,0},{2,3},{3,2},{4,5},{5,4},{6,7},{7,6},{8,9},{9,8},{10,11... | collective-permute-start | bytes 589832 | tf_op jit(solution)/shard_map/ppermute | solution.py:58
  146.4 2.8 %fusion = f32[8,48,2048]{2,1,0:T(8,128)S(1)} fusion(f32[48,2048]{1,0:T(8,128)S(1)} %get-tuple-element.13, f32[48,2048]{1,0:T(8,128)S(1)} %get-tuple-element.12, pred[8]{0:T(512)(128)(4,1)S(1)} %broadcast_compare_fusion, f32[8,48]{1,0:T(8,128)S(1)} %fusion.205, f32[48,48]{1,0:T(8,128)S(1)} %get-tuple-element.25, f32[48,48]{1,0:T(8,128)S(1)} %get-tuple-element.24), kind=kOutput, calls=%fused_computation | convolution fusion | flops 453808128 | bytes 3952136 | tf_op jit(solution)/shard_map/nrs,nsj->nrj/dot_general | solution.py:204
  149.2 10.5 %convolution_subtract_fusion = f32[8,48,2048]{2,1,0:T(8,128)} fusion(f32[8,48,2048]{2,1,0:T(8,128)S(1)} %fusion, bf16[8,512,2048]{2,1,0:T(8,128)(2,1)} %param.6, bf16[4,48,512]{2,1,0:T(8,128)(2,1)S(1)} %maximum_select_fusion.5, bf16[4,48,512]{2,1,0:T(8,128)(2,1)S(1)} %collective-permute-done.21, pred[]{:T(512)S(6)} %ne.14), kind=kOutput, calls=%fused_computation.5 | convolution fusion | flops 806682624 | bytes 23461888 | tf_op jit(solution)/shard_map/nsi,nij->nsj/dot_general | solution.py:143
  (130 shorter events, 10.9 us)
Async XLA Ops:
  2.6 12.5 %copy-start.3 = (s32[256]{0:T(256)S(1)}, s32[256]{0:T(256)}, u32[]{:S(2)}) copy-start(s32[256]{0:T(256)} %param.10) | copy-start | bytes 3076
  2.6 12.5 %copy-start.2 = (f32[256,48]{0,1:T(8,128)S(1)}, f32[256,48]{0,1:T(8,128)}, u32[]{:S(2)}) copy-start(f32[256,48]{0,1:T(8,128)} %param.8) | copy-start | bytes 147460
  2.7 12.9 %copy-start.1 = (f32[2,48,48]{2,1,0:T(8,128)S(1)}, f32[2,48,48]{2,1,0:T(8,128)}, u32[]{:S(2)}) copy-start(f32[2,48,48]{2,1,0:T(8,128)} %param.9) | copy-start | bytes 55300
  13.7 11.4 %collective-permute-start = (f32[4,48,512]{2,1,0:T(8,128)S(1)}, f32[4,48,512]{2,1,0:T(8,128)S(1)}, u32[]{:S(2)}, u32[]{:S(2)}) collective-permute-start(f32[4,48,512]{2,1,0:T(8,128)S(1)} %slice_select_fusion.1), channel_id=1, source_target_pairs={{0,1},{1,0},{2,3},{3,2},{4,5},{5,4},{6,7},{7,6},{8,9},{9,8},{10,11... | collective-permute-start | bytes 1179656 | tf_op jit(solution)/shard_map/ppermute | solution.py:49
  25.3 6.5 %collective-permute-start.1 = (f32[2,48,512]{2,1,0:T(8,128)S(1)}, f32[2,48,512]{2,1,0:T(8,128)S(1)}, u32[]{:S(2)}, u32[]{:S(2)}) collective-permute-start(f32[2,48,512]{2,1,0:T(8,128)S(1)} %slice_select_fusion.3), channel_id=1, source_target_pairs={{0,2},{1,3},{2,0},{3,1},{4,6},{5,7},{6,4},{7,5},{8,10},{9,11},{10,... | collective-permute-start | bytes 589832 | tf_op jit(solution)/shard_map/ppermute | solution.py:49
  36.2 3.5 %collective-permute-start.2 = (bf16[2,48,512]{2,1,0:T(8,128)(2,1)S(1)}, bf16[2,48,512]{2,1,0:T(8,128)(2,1)S(1)}, u32[]{:S(2)}, u32[]{:S(2)}) collective-permute-start(bf16[2,48,512]{2,1,0:T(8,128)(2,1)S(1)} %convolution_convert_fusion.1), channel_id=1, source_target_pairs={{0,2},{1,3},{2,0},{3,1},{4,6},{5,7},{6,4},{7,5},{8,10},{9,11},{10,... | collective-permute-start | bytes 294920 | tf_op jit(solution)/shard_map/ppermute | solution.py:58
  39.8 3.4 %collective-permute-start.3 = (bf16[4,48,512]{2,1,0:T(8,128)(2,1)S(1)}, bf16[4,48,512]{2,1,0:T(8,128)(2,1)S(1)}, u32[]{:S(2)}, u32[]{:S(2)}) collective-permute-start(bf16[4,48,512]{2,1,0:T(8,128)(2,1)S(1)} %maximum_select_fusion.4), channel_id=1, source_target_pairs={{0,1},{1,0},{2,3},{3,2},{4,5},{5,4},{6,7},{7,6},{8,9},{9,8},{10,11... | collective-permute-start | bytes 589832 | tf_op jit(solution)/shard_map/ppermute | solution.py:58
  54.4 6.2 %collective-permute-start.4 = (f32[2,48,512]{2,1,0:T(8,128)S(1)}, f32[2,48,512]{2,1,0:T(8,128)S(1)}, u32[]{:S(2)}, u32[]{:S(2)}) collective-permute-start(f32[2,48,512]{2,1,0:T(8,128)S(1)} %get-tuple-element.14), channel_id=1, source_target_pairs={{0,32},{4,36},{8,40},{12,44},{16,48},{20,52},{24,56},{28,60},{32,0... | collective-permute-start | bytes 589832 | tf_op jit(solution)/shard_map/ppermute | solution.py:84
  55.8 11.3 %collective-permute-start.5 = (f32[2,48,512]{2,1,0:T(8,128)S(1)}, f32[2,48,512]{2,1,0:T(8,128)S(1)}, u32[]{:S(2)}, u32[]{:S(2)}) collective-permute-start(f32[2,48,512]{2,1,0:T(8,128)S(1)} %get-tuple-element.16), channel_id=1, source_target_pairs={{0,64},{4,68},{8,72},{12,76},{16,80},{20,84},{24,88},{28,92},{32,9... | collective-permute-start | bytes 589832 | tf_op jit(solution)/shard_map/ppermute | solution.py:84
  58.3 11.3 %collective-permute-start.6 = (f32[2,48,512]{2,1,0:T(8,128)S(1)}, f32[2,48,512]{2,1,0:T(8,128)S(1)}, u32[]{:S(2)}, u32[]{:S(2)}) collective-permute-start(f32[2,48,512]{2,1,0:T(8,128)S(1)} %get-tuple-element.15), channel_id=1, source_target_pairs={{0,96},{4,100},{8,104},{12,108},{16,112},{20,116},{24,120},{28,124... | collective-permute-start | bytes 589832 | tf_op jit(solution)/shard_map/ppermute | solution.py:84
  69.7 12.5 %collective-permute-start.7 = (f32[2,48,128]{2,1,0:T(8,128)S(1)}, f32[2,48,128]{2,1,0:T(8,128)S(1)}, u32[]{:S(2)}, u32[]{:S(2)}) collective-permute-start(f32[2,48,128]{2,1,0:T(8,128)S(1)} %get-tuple-element.19), channel_id=1, source_target_pairs={{0,8},{4,12},{8,0},{12,4},{16,24},{20,28},{24,16},{28,20},{32,40},... | collective-permute-start | bytes 147464 | tf_op jit(solution)/shard_map/ppermute | solution.py:84
  71.4 10.8 %collective-permute-start.8 = (f32[2,48,128]{2,1,0:T(8,128)S(1)}, f32[2,48,128]{2,1,0:T(8,128)S(1)}, u32[]{:S(2)}, u32[]{:S(2)}) collective-permute-start(f32[2,48,128]{2,1,0:T(8,128)S(1)} %get-tuple-element.21), channel_id=1, source_target_pairs={{0,16},{4,20},{8,24},{12,28},{16,0},{20,4},{24,8},{28,12},{32,48},... | collective-permute-start | bytes 147464 | tf_op jit(solution)/shard_map/ppermute | solution.py:84
  74.7 7.5 %collective-permute-start.9 = (f32[2,48,128]{2,1,0:T(8,128)S(1)}, f32[2,48,128]{2,1,0:T(8,128)S(1)}, u32[]{:S(2)}, u32[]{:S(2)}) collective-permute-start(f32[2,48,128]{2,1,0:T(8,128)S(1)} %get-tuple-element.20), channel_id=1, source_target_pairs={{0,24},{4,28},{8,16},{12,20},{16,8},{20,12},{24,0},{28,4},{32,56},... | collective-permute-start | bytes 147464 | tf_op jit(solution)/shard_map/ppermute | solution.py:84
  82.3 4.5 %collective-permute-start.10 = (f32[2,48,64]{2,1,0:T(8,128)S(1)}, f32[2,48,64]{2,1,0:T(8,128)S(1)}, u32[]{:S(2)}, u32[]{:S(2)}) collective-permute-start(f32[2,48,64]{2,1,0:T(8,128)S(1)} %constant_dynamic-slice_fusion), channel_id=1, source_target_pairs={{0,4},{4,0},{8,12},{12,8},{16,20},{20,16},{24,28},{28,24},{32,36},... | collective-permute-start | bytes 73736 | tf_op jit(solution)/shard_map/ppermute | solution.py:84
  87.3 4.5 %collective-permute-start.11 = (f32[2,48,64]{2,1,0:T(8,128)S(1)}, f32[2,48,64]{2,1,0:T(8,128)S(1)}, u32[]{:S(2)}, u32[]{:S(2)}) collective-permute-start(f32[2,48,64]{2,1,0:T(8,128)S(1)} %fusion.236), channel_id=1, source_target_pairs={{0,4},{4,0},{8,12},{12,8},{16,20},{20,16},{24,28},{28,24},{32,36},... | collective-permute-start | bytes 73736 | tf_op jit(solution)/shard_map/ppermute | solution.py:101
  92.3 4.0 %collective-permute-start.12 = (f32[2,48,128]{2,1,0:T(8,128)S(1)}, f32[2,48,128]{2,1,0:T(8,128)S(1)}, u32[]{:S(2)}, u32[]{:S(2)}) collective-permute-start(f32[2,48,128]{2,1,0:T(8,128)S(1)} %dynamic_update_slice.31), channel_id=1, source_target_pairs={{0,8},{4,12},{8,0},{12,4},{16,24},{20,28},{24,16},{28,20},{32,40},... | collective-permute-start | bytes 147464 | tf_op jit(solution)/shard_map/ppermute | solution.py:101
  92.4 5.8 %collective-permute-start.13 = (f32[2,48,128]{2,1,0:T(8,128)S(1)}, f32[2,48,128]{2,1,0:T(8,128)S(1)}, u32[]{:S(2)}, u32[]{:S(2)}) collective-permute-start(f32[2,48,128]{2,1,0:T(8,128)S(1)} %dynamic_update_slice.31), channel_id=1, source_target_pairs={{0,16},{4,20},{8,24},{12,28},{16,0},{20,4},{24,8},{28,12},{32,48},... | collective-permute-start | bytes 147464 | tf_op jit(solution)/shard_map/ppermute | solution.py:101
  96.2 4.2 %collective-permute-start.14 = (f32[2,48,128]{2,1,0:T(8,128)S(1)}, f32[2,48,128]{2,1,0:T(8,128)S(1)}, u32[]{:S(2)}, u32[]{:S(2)}) collective-permute-start(f32[2,48,128]{2,1,0:T(8,128)S(1)} %dynamic_update_slice.31), channel_id=1, source_target_pairs={{0,24},{4,28},{8,16},{12,20},{16,8},{20,12},{24,0},{28,4},{32,56},... | collective-permute-start | bytes 147464 | tf_op jit(solution)/shard_map/ppermute | solution.py:101
  100.4 4.5 %collective-permute-start.15 = (f32[2,48,512]{2,1,0:T(8,128)S(1)}, f32[2,48,512]{2,1,0:T(8,128)S(1)}, u32[]{:S(2)}, u32[]{:S(2)}) collective-permute-start(f32[2,48,512]{2,1,0:T(8,128)S(1)} %constant_dynamic-update-slice_fusion.4), channel_id=1, source_target_pairs={{0,32},{4,36},{8,40},{12,44},{16,48},{20,52},{24,56},{28,60},{32,0... | collective-permute-start | bytes 589832 | tf_op jit(solution)/shard_map/ppermute | solution.py:101
  100.4 6.6 %collective-permute-start.16 = (f32[2,48,512]{2,1,0:T(8,128)S(1)}, f32[2,48,512]{2,1,0:T(8,128)S(1)}, u32[]{:S(2)}, u32[]{:S(2)}) collective-permute-start(f32[2,48,512]{2,1,0:T(8,128)S(1)} %constant_dynamic-update-slice_fusion.4), channel_id=1, source_target_pairs={{0,64},{4,68},{8,72},{12,76},{16,80},{20,84},{24,88},{28,92},{32,9... | collective-permute-start | bytes 589832 | tf_op jit(solution)/shard_map/ppermute | solution.py:101
  101.8 7.3 %collective-permute-start.17 = (f32[2,48,512]{2,1,0:T(8,128)S(1)}, f32[2,48,512]{2,1,0:T(8,128)S(1)}, u32[]{:S(2)}, u32[]{:S(2)}) collective-permute-start(f32[2,48,512]{2,1,0:T(8,128)S(1)} %constant_dynamic-update-slice_fusion.4), channel_id=1, source_target_pairs={{0,96},{4,100},{8,104},{12,108},{16,112},{20,116},{24,120},{28,124... | collective-permute-start | bytes 589832 | tf_op jit(solution)/shard_map/ppermute | solution.py:101
  109.1 11.2 %copy-start = (f32[2,48,2048]{2,1,0:T(8,128)}, f32[2,48,2048]{2,1,0:T(8,128)S(1)}, u32[]{:S(2)}) copy-start(f32[2,48,2048]{2,1,0:T(8,128)S(1)} %constant_dynamic-update-slice_fusion) | copy-start | bytes 2359300
  120.4 8.9 %collective-permute-start.18 = (f32[4,48,512]{2,1,0:T(8,128)S(1)}, f32[4,48,512]{2,1,0:T(8,128)S(1)}, u32[]{:S(2)}, u32[]{:S(2)}) collective-permute-start(f32[4,48,512]{2,1,0:T(8,128)S(1)} %slice_select_fusion), channel_id=1, source_target_pairs={{0,1},{1,0},{2,3},{3,2},{4,5},{5,4},{6,7},{7,6},{8,9},{9,8},{10,11... | collective-permute-start | bytes 1179656 | tf_op jit(solution)/shard_map/ppermute | solution.py:49
  129.4 6.2 %collective-permute-start.19 = (f32[2,48,512]{2,1,0:T(8,128)S(1)}, f32[2,48,512]{2,1,0:T(8,128)S(1)}, u32[]{:S(2)}, u32[]{:S(2)}) collective-permute-start(f32[2,48,512]{2,1,0:T(8,128)S(1)} %slice_select_fusion.2), channel_id=1, source_target_pairs={{0,2},{1,3},{2,0},{3,1},{4,6},{5,7},{6,4},{7,5},{8,10},{9,11},{10,... | collective-permute-start | bytes 589832 | tf_op jit(solution)/shard_map/ppermute | solution.py:49
  140.1 3.5 %collective-permute-start.20 = (bf16[2,48,512]{2,1,0:T(8,128)(2,1)S(1)}, bf16[2,48,512]{2,1,0:T(8,128)(2,1)S(1)}, u32[]{:S(2)}, u32[]{:S(2)}) collective-permute-start(bf16[2,48,512]{2,1,0:T(8,128)(2,1)S(1)} %convolution_convert_fusion), channel_id=1, source_target_pairs={{0,2},{1,3},{2,0},{3,1},{4,6},{5,7},{6,4},{7,5},{8,10},{9,11},{10,... | collective-permute-start | bytes 294920 | tf_op jit(solution)/shard_map/ppermute | solution.py:58
  143.7 5.5 %collective-permute-start.21 = (bf16[4,48,512]{2,1,0:T(8,128)(2,1)S(1)}, bf16[4,48,512]{2,1,0:T(8,128)(2,1)S(1)}, u32[]{:S(2)}, u32[]{:S(2)}) collective-permute-start(bf16[4,48,512]{2,1,0:T(8,128)(2,1)S(1)} %maximum_select_fusion.5), channel_id=1, source_target_pairs={{0,1},{1,0},{2,3},{3,2},{4,5},{5,4},{6,7},{7,6},{8,9},{9,8},{10,11... | collective-permute-start | bytes 589832 | tf_op jit(solution)/shard_map/ppermute | solution.py:58

commit v10 on v9

--- a/solution.py
+++ b/solution.py
@@ -191,7 +191,7 @@
         )
         weights = mine_member[:, :, None, None] * own_mix[:, None, :, :]
         partial_moments = jnp.einsum(
-            "nhsr,nsj->hrj", weights, projected, precision=lax.Precision.HIGHEST
+            "nhsr,nsj->hrj", weights, projected, precision=lax.Precision.HIGH
         )
         moments_part = radix_scatter(partial_moments, "runs", runs_size, runs_groups, 2)
         spectra_part = apply_inverse(inverse, moments_part)
@@ -201,9 +201,7 @@
         held_projected = project(
             slices, held_rows.astype(jnp.bfloat16), held_mix, chan_size, chan_bits
         )
-        model_part = jnp.einsum(
-            "nrs,nsj->nrj", held_mix, held_rows, precision=lax.Precision.HIGHEST
-        )
+        model_part = jnp.einsum("nrs,nsj->nrj", held_mix, held_rows, precision=lax.Precision.HIGH)
         return (new_spectra, held_projected - model_part)
 
     return layer

time: 160 us -> 158 us (0.988)
  matrix products: 56.5 us -> 54.4 us
where the time goes in v10:
time: 158 us
  matrix products  54.4 us (34%)
  starting transfers between devices  42.4 us (27%)
  waiting for transfers between devices  38.5 us (24%)
  other arithmetic  18.2 us (12%)
  local copies, waits for them, and re-layouts  2.52 us (2%)
    dot_general x2, matrix products, project_body(): jnp.einsum('nrj,nij->nri', rows_low, slices, preferred_element_type=jnp.f...  22.1 us
    dot_general x2, matrix products, project_body(): jnp.einsum('nsi,nij->nsj', rotated, slices, preferred_element_type=jnp.fl...  19.3 us
    ppermute x7, waiting for transfers between devices, radix_scatter(): got = lax.ppermute(send, axis, xor_pairs(size, mask))  12.4 us
    ppermute x7, starting transfers between devices, radix_scatter(): got = lax.ppermute(send, axis, xor_pairs(size, mask))  12.1 us
    ppermute x4, starting transfers between devices, halving_scatter(): got = lax.ppermute(send, axis, xor_pairs(size, bit))  11.8 us
    ppermute x4, waiting for transfers between devices, halving_scatter(): got = lax.ppermute(send, axis, xor_pairs(size, bit))  11.1 us
    ppermute x7, starting transfers between devices, radix_gather(): got = lax.ppermute(x, axis, xor_pairs(size, mask))  10.8 us
    ppermute x7, waiting for transfers between devices, radix_gather(): got = lax.ppermute(x, axis, xor_pairs(size, mask))  9.99 us
  transfers between devices with their start and end apart: 22, of which 16 were waited for; matrix products, arithmetic and copies ran while one was open for 13% of the time, Pallas kernels for 0%

profile of v10, /device:TPU:1, one launch (start us, length us, event | category | flops | bytes accessed | tf_op | source)
XLA Modules:
  0.0 157.5 jit_solution(8097728341245581028)
XLA Ops:
  0.6 0.9 select_reduce_fusion.3
  1.6 1.1 slice_bitcast_fusion.3
  2.7 11.0 %fusion.12 = f32[8,48,512]{2,1,0:T(8,128)S(1)} fusion(bf16[8,512,2048]{2,1,0:T(8,128)(2,1)} %param.6, pred[8]{0:T(512)(128)(4,1)S(1)} %broadcast_compare_fusion, bf16[48,2048]{1,0:T(8,128)(2,1)S(1)} %get-tuple-element.18, bf16[48,2048]{1,0:T(8,128)(2,1)S(1)} %get-tuple-element.17), kind=kOutput, calls=%fused_computation.12 | convolution fusion | flops 806092800 | bytes 17956872 | tf_op jit(solution)/shard_map/nrj,nij->nri/dot_general | solution.py:128
  13.7 1.5 collective-permute-start
  16.3 8.8 %custom-call.7 = f32[2,48,48]{2,1,0:T(8,128)S(1)} custom-call(f32[2,48,48]{2,1,0:T(8,128)S(1)} %fusion.192), custom_call_target="Cholesky" | custom-call | tf_op jit(solution)/shard_map/jit(cholesky)/cholesky | solution.py:150
  25.3 1.5 collective-permute-start.1
  26.9 4.9 %collective-permute-done.1 = f32[2,48,512]{2,1,0:T(8,128)S(1)} collective-permute-done((f32[2,48,512]{2,1,0:T(8,128)S(1)}, f32[2,48,512]{2,1,0:T(8,128)S(1)}, u32[]{:S(2)}, u32[]{:S(2)}) %collective-permute-start.1) | collective-permute-done | bytes 196640 | tf_op jit(solution)/shard_map/ppermute | solution.py:49
  31.8 0.3 fusion.37
  32.1 0.4 select_reduce_fusion.1
  36.2 1.5 collective-permute-start.2
  37.9 1.9 %collective-permute-done.2 = bf16[2,48,512]{2,1,0:T(8,128)(2,1)S(1)} collective-permute-done((bf16[2,48,512]{2,1,0:T(8,128)(2,1)S(1)}, bf16[2,48,512]{2,1,0:T(8,128)(2,1)S(1)}, u32[]{:S(2)}, u32[]{:S(2)}) %collective-permute-start.2) | collective-permute-done | bytes 98336 | tf_op jit(solution)/shard_map/ppermute | solution.py:58
  39.8 2.1 %collective-permute-start.3 = (bf16[4,48,512]{2,1,0:T(8,128)(2,1)S(1)}, bf16[4,48,512]{2,1,0:T(8,128)(2,1)S(1)}, u32[]{:S(2)}, u32[]{:S(2)}) collective-permute-start(bf16[4,48,512]{2,1,0:T(8,128)(2,1)S(1)} %maximum_select_fusion.4), channel_id=1, source_target_pairs={{0,1},{1,0},{2,3},{3,2},{4,5},{5,4},{6,7},{7,6},{8,9},{9,8},{10,11... | collective-permute-start | bytes 589832 | tf_op jit(solution)/shard_map/ppermute | solution.py:58
  41.9 1.1 collective-permute-done.3
  43.0 8.8 %fusion.20 = f32[8,48,2048]{2,1,0:T(8,128)S(1)} fusion(bf16[8,512,2048]{2,1,0:T(8,128)(2,1)} %param.6, bf16[4,48,512]{2,1,0:T(8,128)(2,1)S(1)} %maximum_select_fusion.4, bf16[4,48,512]{2,1,0:T(8,128)(2,1)S(1)} %collective-permute-done.3, pred[]{:T(512)S(6)} %ne.14), kind=kOutput, calls=%fused_computation.26 | convolution fusion | flops 805896192 | bytes 20316160 | tf_op jit(solution)/shard_map/nsi,nij->nsj/dot_general | solution.py:143
  51.8 1.4 fusion.4
  53.2 1.6 %collective-permute-start.4 = (f32[2,48,512]{2,1,0:T(8,128)S(1)}, f32[2,48,512]{2,1,0:T(8,128)S(1)}, u32[]{:S(2)}, u32[]{:S(2)}) collective-permute-start(f32[2,48,512]{2,1,0:T(8,128)S(1)} %get-tuple-element.14), channel_id=1, source_target_pairs={{0,32},{4,36},{8,40},{12,44},{16,48},{20,52},{24,56},{28,60},{32,0... | collective-permute-start | bytes 589832 | tf_op jit(solution)/shard_map/ppermute | solution.py:84
  54.8 2.5 %collective-permute-start.5 = (f32[2,48,512]{2,1,0:T(8,128)S(1)}, f32[2,48,512]{2,1,0:T(8,128)S(1)}, u32[]{:S(2)}, u32[]{:S(2)}) collective-permute-start(f32[2,48,512]{2,1,0:T(8,128)S(1)} %get-tuple-element.16), channel_id=1, source_target_pairs={{0,64},{4,68},{8,72},{12,76},{16,80},{20,84},{24,88},{28,92},{32,9... | collective-permute-start | bytes 589832 | tf_op jit(solution)/shard_map/ppermute | solution.py:84
  57.5 2.1 %collective-permute-done.4 = f32[2,48,512]{2,1,0:T(8,128)S(1)} collective-permute-done((f32[2,48,512]{2,1,0:T(8,128)S(1)}, f32[2,48,512]{2,1,0:T(8,128)S(1)}, u32[]{:S(2)}, u32[]{:S(2)}) %collective-permute-start.4) | collective-permute-done | bytes 196640 | tf_op jit(solution)/shard_map/ppermute | solution.py:84
  59.6 6.6 %collective-permute-done.5 = f32[2,48,512]{2,1,0:T(8,128)S(1)} collective-permute-done((f32[2,48,512]{2,1,0:T(8,128)S(1)}, f32[2,48,512]{2,1,0:T(8,128)S(1)}, u32[]{:S(2)}, u32[]{:S(2)}) %collective-permute-start.5) | collective-permute-done | bytes 196640 | tf_op jit(solution)/shard_map/ppermute | solution.py:84
  66.2 2.4 %collective-permute-done.6 = f32[2,48,512]{2,1,0:T(8,128)S(1)} collective-permute-done((f32[2,48,512]{2,1,0:T(8,128)S(1)}, f32[2,48,512]{2,1,0:T(8,128)S(1)}, u32[]{:S(2)}, u32[]{:S(2)}) %collective-permute-start.6) | collective-permute-done | bytes 196640 | tf_op jit(solution)/shard_map/ppermute | solution.py:84
  68.7 1.7 %collective-permute-start.7 = (f32[2,48,128]{2,1,0:T(8,128)S(1)}, f32[2,48,128]{2,1,0:T(8,128)S(1)}, u32[]{:S(2)}, u32[]{:S(2)}) collective-permute-start(f32[2,48,128]{2,1,0:T(8,128)S(1)} %get-tuple-element.19), channel_id=1, source_target_pairs={{0,8},{4,12},{8,0},{12,4},{16,24},{20,28},{24,16},{28,20},{32,40},... | collective-permute-start | bytes 147464 | tf_op jit(solution)/shard_map/ppermute | solution.py:84
  70.4 3.3 %collective-permute-start.8 = (f32[2,48,128]{2,1,0:T(8,128)S(1)}, f32[2,48,128]{2,1,0:T(8,128)S(1)}, u32[]{:S(2)}, u32[]{:S(2)}) collective-permute-start(f32[2,48,128]{2,1,0:T(8,128)S(1)} %get-tuple-element.21), channel_id=1, source_target_pairs={{0,16},{4,20},{8,24},{12,28},{16,0},{20,4},{24,8},{28,12},{32,48},... | collective-permute-start | bytes 147464 | tf_op jit(solution)/shard_map/ppermute | solution.py:84
  73.8 7.4 %custom-call.8 = f32[2,1,48,48]{2,3,1,0:T(8,128)S(1)} custom-call(f32[2,1,48,48]{3,2,1,0:T(8,128)S(1)} %select_bitcast_fusion), custom_call_target="InvertDiagBlocksLowerTriangular" | custom-call | tf_op jit(solution)/shard_map/triangular_solve | solution.py:152
  81.3 2.9 %collective-permute-start.10 = (f32[2,48,64]{2,1,0:T(8,128)S(1)}, f32[2,48,64]{2,1,0:T(8,128)S(1)}, u32[]{:S(2)}, u32[]{:S(2)}) collective-permute-start(f32[2,48,64]{2,1,0:T(8,128)S(1)} %constant_dynamic-slice_fusion), channel_id=1, source_target_pairs={{0,4},{4,0},{8,12},{12,8},{16,20},{20,16},{24,28},{28,24},{32,36},... | collective-permute-start | bytes 73736 | tf_op jit(solution)/shard_map/ppermute | solution.py:84
  84.5 1.3 collective-permute-done.10
  86.3 3.0 %collective-permute-start.11 = (f32[2,48,64]{2,1,0:T(8,128)S(1)}, f32[2,48,64]{2,1,0:T(8,128)S(1)}, u32[]{:S(2)}, u32[]{:S(2)}) collective-permute-start(f32[2,48,64]{2,1,0:T(8,128)S(1)} %fusion.236), channel_id=1, source_target_pairs={{0,4},{4,0},{8,12},{12,8},{16,20},{20,16},{24,28},{28,24},{32,36},... | collective-permute-start | bytes 73736 | tf_op jit(solution)/shard_map/ppermute | solution.py:101
  89.6 1.3 collective-permute-done.11
  90.8 0.5 dynamic_update_slice.31
  91.4 3.8 %collective-permute-start.13 = (f32[2,48,128]{2,1,0:T(8,128)S(1)}, f32[2,48,128]{2,1,0:T(8,128)S(1)}, u32[]{:S(2)}, u32[]{:S(2)}) collective-permute-start(f32[2,48,128]{2,1,0:T(8,128)S(1)} %dynamic_update_slice.31), channel_id=1, source_target_pairs={{0,16},{4,20},{8,24},{12,28},{16,0},{20,4},{24,8},{28,12},{32,48},... | collective-permute-start | bytes 147464 | tf_op jit(solution)/shard_map/ppermute | solution.py:101
  95.3 1.9 %collective-permute-done.13 = f32[2,48,128]{2,1,0:T(8,128)S(1)} collective-permute-done((f32[2,48,128]{2,1,0:T(8,128)S(1)}, f32[2,48,128]{2,1,0:T(8,128)S(1)}, u32[]{:S(2)}, u32[]{:S(2)}) %collective-permute-start.13) | collective-permute-done | bytes 49184 | tf_op jit(solution)/shard_map/ppermute | solution.py:101
  97.3 2.1 %collective-permute-done.14 = f32[2,48,128]{2,1,0:T(8,128)S(1)} collective-permute-done((f32[2,48,128]{2,1,0:T(8,128)S(1)}, f32[2,48,128]{2,1,0:T(8,128)S(1)}, u32[]{:S(2)}, u32[]{:S(2)}) %collective-permute-start.14) | collective-permute-done | bytes 49184 | tf_op jit(solution)/shard_map/ppermute | solution.py:101
  99.4 1.4 collective-permute-start.16
  100.8 2.5 %collective-permute-start.17 = (f32[2,48,512]{2,1,0:T(8,128)S(1)}, f32[2,48,512]{2,1,0:T(8,128)S(1)}, u32[]{:S(2)}, u32[]{:S(2)}) collective-permute-start(f32[2,48,512]{2,1,0:T(8,128)S(1)} %constant_dynamic-update-slice_fusion.4), channel_id=1, source_target_pairs={{0,96},{4,100},{8,104},{12,108},{16,112},{20,116},{24,120},{28,124... | collective-permute-start | bytes 589832 | tf_op jit(solution)/shard_map/ppermute | solution.py:101
  103.4 0.6 collective-permute-done.15
  104.0 2.1 %collective-permute-done.16 = f32[2,48,512]{2,1,0:T(8,128)S(1)} collective-permute-done((f32[2,48,512]{2,1,0:T(8,128)S(1)}, f32[2,48,512]{2,1,0:T(8,128)S(1)}, u32[]{:S(2)}, u32[]{:S(2)}) %collective-permute-start.16) | collective-permute-done | bytes 196640 | tf_op jit(solution)/shard_map/ppermute | solution.py:101
  106.1 2.0 %collective-permute-done.17 = f32[2,48,512]{2,1,0:T(8,128)S(1)} collective-permute-done((f32[2,48,512]{2,1,0:T(8,128)S(1)}, f32[2,48,512]{2,1,0:T(8,128)S(1)}, u32[]{:S(2)}, u32[]{:S(2)}) %collective-permute-start.17) | collective-permute-done | bytes 196640 | tf_op jit(solution)/shard_map/ppermute | solution.py:101
  108.2 11.2 %fusion.7 = f32[8,48,512]{2,1,0:T(8,128)S(1)} fusion(bf16[8,512,2048]{2,1,0:T(8,128)(2,1)} %param.6, f32[48,2048]{1,0:T(8,128)S(1)} %get-tuple-element.13, f32[48,2048]{1,0:T(8,128)S(1)} %get-tuple-element.12, pred[8]{0:T(512)(128)(4,1)S(1)} %broadcast_compare_fusion), kind=kOutput, calls=%fused_computation.7 | convolution fusion | flops 806092800 | bytes 18350088 | tf_op jit(solution)/shard_map/nrj,nij->nri/dot_general | solution.py:128
  119.4 7.5 %collective-permute-start.18 = (f32[4,48,512]{2,1,0:T(8,128)S(1)}, f32[4,48,512]{2,1,0:T(8,128)S(1)}, u32[]{:S(2)}, u32[]{:S(2)}) collective-permute-start(f32[4,48,512]{2,1,0:T(8,128)S(1)} %slice_select_fusion), channel_id=1, source_target_pairs={{0,1},{1,0},{2,3},{3,2},{4,5},{5,4},{6,7},{7,6},{8,9},{9,8},{10,11... | collective-permute-start | bytes 1179656 | tf_op jit(solution)/shard_map/ppermute | solution.py:49
  126.9 1.3 collective-permute-done.18
  128.4 1.4 collective-permute-start.19
  129.8 4.8 %collective-permute-done.19 = f32[2,48,512]{2,1,0:T(8,128)S(1)} collective-permute-done((f32[2,48,512]{2,1,0:T(8,128)S(1)}, f32[2,48,512]{2,1,0:T(8,128)S(1)}, u32[]{:S(2)}, u32[]{:S(2)}) %collective-permute-start.19) | collective-permute-done | bytes 196640 | tf_op jit(solution)/shard_map/ppermute | solution.py:49
  134.6 0.3 fusion.34
  134.9 0.4 select_reduce_fusion
  139.1 1.4 collective-permute-start.20
  140.5 2.2 %collective-permute-done.20 = bf16[2,48,512]{2,1,0:T(8,128)(2,1)S(1)} collective-permute-done((bf16[2,48,512]{2,1,0:T(8,128)(2,1)S(1)}, bf16[2,48,512]{2,1,0:T(8,128)(2,1)S(1)}, u32[]{:S(2)}, u32[]{:S(2)}) %collective-permute-start.20) | collective-permute-done | bytes 98336 | tf_op jit(solution)/shard_map/ppermute | solution.py:58
  142.7 2.7 %collective-permute-start.21 = (bf16[4,48,512]{2,1,0:T(8,128)(2,1)S(1)}, bf16[4,48,512]{2,1,0:T(8,128)(2,1)S(1)}, u32[]{:S(2)}, u32[]{:S(2)}) collective-permute-start(bf16[4,48,512]{2,1,0:T(8,128)(2,1)S(1)} %maximum_select_fusion.5), channel_id=1, source_target_pairs={{0,1},{1,0},{2,3},{3,2},{4,5},{5,4},{6,7},{7,6},{8,9},{9,8},{10,11... | collective-permute-start | bytes 589832 | tf_op jit(solution)/shard_map/ppermute | solution.py:58
  145.4 1.6 %fusion = f32[8,48,2048]{2,1,0:T(8,128)S(1)} fusion(f32[48,2048]{1,0:T(8,128)S(1)} %get-tuple-element.13, f32[48,2048]{1,0:T(8,128)S(1)} %get-tuple-element.12, pred[8]{0:T(512)(128)(4,1)S(1)} %broadcast_compare_fusion, f32[8,48]{1,0:T(8,128)S(1)} %fusion.205, f32[48,48]{1,0:T(8,128)S(1)} %get-tuple-element.25, f32[48,48]{1,0:T(8,128)S(1)} %get-tuple-element.24), kind=kOutput, calls=%fused_computation | convolution fusion | flops 227315712 | bytes 3952136 | tf_op jit(solution)/shard_map/nrs,nsj->nrj/dot_general | solution.py:204
  147.0 10.5 %convolution_subtract_fusion = f32[8,48,2048]{2,1,0:T(8,128)} fusion(f32[8,48,2048]{2,1,0:T(8,128)S(1)} %fusion, bf16[8,512,2048]{2,1,0:T(8,128)(2,1)} %param.6, bf16[4,48,512]{2,1,0:T(8,128)(2,1)S(1)} %maximum_select_fusion.5, bf16[4,48,512]{2,1,0:T(8,128)(2,1)S(1)} %collective-permute-done.21, pred[]{:T(512)S(6)} %ne.14), kind=kOutput, calls=%fused_computation.5 | convolution fusion | flops 806682624 | bytes 23461888 | tf_op jit(solution)/shard_map/nsi,nij->nsj/dot_general | solution.py:143
  (130 shorter events, 10.9 us)
Async XLA Ops:
  2.6 12.5 %copy-start.3 = (s32[256]{0:T(256)S(1)}, s32[256]{0:T(256)}, u32[]{:S(2)}) copy-start(s32[256]{0:T(256)} %param.10) | copy-start | bytes 3076
  2.6 12.5 %copy-start.2 = (f32[256,48]{0,1:T(8,128)S(1)}, f32[256,48]{0,1:T(8,128)}, u32[]{:S(2)}) copy-start(f32[256,48]{0,1:T(8,128)} %param.8) | copy-start | bytes 147460
  2.7 12.9 %copy-start.1 = (f32[2,48,48]{2,1,0:T(8,128)S(1)}, f32[2,48,48]{2,1,0:T(8,128)}, u32[]{:S(2)}) copy-start(f32[2,48,48]{2,1,0:T(8,128)} %param.9) | copy-start | bytes 55300
  13.7 11.4 %collective-permute-start = (f32[4,48,512]{2,1,0:T(8,128)S(1)}, f32[4,48,512]{2,1,0:T(8,128)S(1)}, u32[]{:S(2)}, u32[]{:S(2)}) collective-permute-start(f32[4,48,512]{2,1,0:T(8,128)S(1)} %slice_select_fusion.1), channel_id=1, source_target_pairs={{0,1},{1,0},{2,3},{3,2},{4,5},{5,4},{6,7},{7,6},{8,9},{9,8},{10,11... | collective-permute-start | bytes 1179656 | tf_op jit(solution)/shard_map/ppermute | solution.py:49
  25.3 6.5 %collective-permute-start.1 = (f32[2,48,512]{2,1,0:T(8,128)S(1)}, f32[2,48,512]{2,1,0:T(8,128)S(1)}, u32[]{:S(2)}, u32[]{:S(2)}) collective-permute-start(f32[2,48,512]{2,1,0:T(8,128)S(1)} %slice_select_fusion.3), channel_id=1, source_target_pairs={{0,2},{1,3},{2,0},{3,1},{4,6},{5,7},{6,4},{7,5},{8,10},{9,11},{10,... | collective-permute-start | bytes 589832 | tf_op jit(solution)/shard_map/ppermute | solution.py:49
  36.2 3.5 %collective-permute-start.2 = (bf16[2,48,512]{2,1,0:T(8,128)(2,1)S(1)}, bf16[2,48,512]{2,1,0:T(8,128)(2,1)S(1)}, u32[]{:S(2)}, u32[]{:S(2)}) collective-permute-start(bf16[2,48,512]{2,1,0:T(8,128)(2,1)S(1)} %convolution_convert_fusion.1), channel_id=1, source_target_pairs={{0,2},{1,3},{2,0},{3,1},{4,6},{5,7},{6,4},{7,5},{8,10},{9,11},{10,... | collective-permute-start | bytes 294920 | tf_op jit(solution)/shard_map/ppermute | solution.py:58
  39.8 3.2 %collective-permute-start.3 = (bf16[4,48,512]{2,1,0:T(8,128)(2,1)S(1)}, bf16[4,48,512]{2,1,0:T(8,128)(2,1)S(1)}, u32[]{:S(2)}, u32[]{:S(2)}) collective-permute-start(bf16[4,48,512]{2,1,0:T(8,128)(2,1)S(1)} %maximum_select_fusion.4), channel_id=1, source_target_pairs={{0,1},{1,0},{2,3},{3,2},{4,5},{5,4},{6,7},{7,6},{8,9},{9,8},{10,11... | collective-permute-start | bytes 589832 | tf_op jit(solution)/shard_map/ppermute | solution.py:58
  53.2 6.3 %collective-permute-start.4 = (f32[2,48,512]{2,1,0:T(8,128)S(1)}, f32[2,48,512]{2,1,0:T(8,128)S(1)}, u32[]{:S(2)}, u32[]{:S(2)}) collective-permute-start(f32[2,48,512]{2,1,0:T(8,128)S(1)} %get-tuple-element.14), channel_id=1, source_target_pairs={{0,32},{4,36},{8,40},{12,44},{16,48},{20,52},{24,56},{28,60},{32,0... | collective-permute-start | bytes 589832 | tf_op jit(solution)/shard_map/ppermute | solution.py:84
  54.8 11.3 %collective-permute-start.5 = (f32[2,48,512]{2,1,0:T(8,128)S(1)}, f32[2,48,512]{2,1,0:T(8,128)S(1)}, u32[]{:S(2)}, u32[]{:S(2)}) collective-permute-start(f32[2,48,512]{2,1,0:T(8,128)S(1)} %get-tuple-element.16), channel_id=1, source_target_pairs={{0,64},{4,68},{8,72},{12,76},{16,80},{20,84},{24,88},{28,92},{32,9... | collective-permute-start | bytes 589832 | tf_op jit(solution)/shard_map/ppermute | solution.py:84
  57.3 11.3 %collective-permute-start.6 = (f32[2,48,512]{2,1,0:T(8,128)S(1)}, f32[2,48,512]{2,1,0:T(8,128)S(1)}, u32[]{:S(2)}, u32[]{:S(2)}) collective-permute-start(f32[2,48,512]{2,1,0:T(8,128)S(1)} %get-tuple-element.15), channel_id=1, source_target_pairs={{0,96},{4,100},{8,104},{12,108},{16,112},{20,116},{24,120},{28,124... | collective-permute-start | bytes 589832 | tf_op jit(solution)/shard_map/ppermute | solution.py:84
  68.7 12.5 %collective-permute-start.7 = (f32[2,48,128]{2,1,0:T(8,128)S(1)}, f32[2,48,128]{2,1,0:T(8,128)S(1)}, u32[]{:S(2)}, u32[]{:S(2)}) collective-permute-start(f32[2,48,128]{2,1,0:T(8,128)S(1)} %get-tuple-element.19), channel_id=1, source_target_pairs={{0,8},{4,12},{8,0},{12,4},{16,24},{20,28},{24,16},{28,20},{32,40},... | collective-permute-start | bytes 147464 | tf_op jit(solution)/shard_map/ppermute | solution.py:84
  70.4 10.8 %collective-permute-start.8 = (f32[2,48,128]{2,1,0:T(8,128)S(1)}, f32[2,48,128]{2,1,0:T(8,128)S(1)}, u32[]{:S(2)}, u32[]{:S(2)}) collective-permute-start(f32[2,48,128]{2,1,0:T(8,128)S(1)} %get-tuple-element.21), channel_id=1, source_target_pairs={{0,16},{4,20},{8,24},{12,28},{16,0},{20,4},{24,8},{28,12},{32,48},... | collective-permute-start | bytes 147464 | tf_op jit(solution)/shard_map/ppermute | solution.py:84
  73.7 7.5 %collective-permute-start.9 = (f32[2,48,128]{2,1,0:T(8,128)S(1)}, f32[2,48,128]{2,1,0:T(8,128)S(1)}, u32[]{:S(2)}, u32[]{:S(2)}) collective-permute-start(f32[2,48,128]{2,1,0:T(8,128)S(1)} %get-tuple-element.20), channel_id=1, source_target_pairs={{0,24},{4,28},{8,16},{12,20},{16,8},{20,12},{24,0},{28,4},{32,56},... | collective-permute-start | bytes 147464 | tf_op jit(solution)/shard_map/ppermute | solution.py:84
  81.3 4.5 %collective-permute-start.10 = (f32[2,48,64]{2,1,0:T(8,128)S(1)}, f32[2,48,64]{2,1,0:T(8,128)S(1)}, u32[]{:S(2)}, u32[]{:S(2)}) collective-permute-start(f32[2,48,64]{2,1,0:T(8,128)S(1)} %constant_dynamic-slice_fusion), channel_id=1, source_target_pairs={{0,4},{4,0},{8,12},{12,8},{16,20},{20,16},{24,28},{28,24},{32,36},... | collective-permute-start | bytes 73736 | tf_op jit(solution)/shard_map/ppermute | solution.py:84
  86.3 4.5 %collective-permute-start.11 = (f32[2,48,64]{2,1,0:T(8,128)S(1)}, f32[2,48,64]{2,1,0:T(8,128)S(1)}, u32[]{:S(2)}, u32[]{:S(2)}) collective-permute-start(f32[2,48,64]{2,1,0:T(8,128)S(1)} %fusion.236), channel_id=1, source_target_pairs={{0,4},{4,0},{8,12},{12,8},{16,20},{20,16},{24,28},{28,24},{32,36},... | collective-permute-start | bytes 73736 | tf_op jit(solution)/shard_map/ppermute | solution.py:101
  91.3 4.0 %collective-permute-start.12 = (f32[2,48,128]{2,1,0:T(8,128)S(1)}, f32[2,48,128]{2,1,0:T(8,128)S(1)}, u32[]{:S(2)}, u32[]{:S(2)}) collective-permute-start(f32[2,48,128]{2,1,0:T(8,128)S(1)} %dynamic_update_slice.31), channel_id=1, source_target_pairs={{0,8},{4,12},{8,0},{12,4},{16,24},{20,28},{24,16},{28,20},{32,40},... | collective-permute-start | bytes 147464 | tf_op jit(solution)/shard_map/ppermute | solution.py:101
  91.4 5.8 %collective-permute-start.13 = (f32[2,48,128]{2,1,0:T(8,128)S(1)}, f32[2,48,128]{2,1,0:T(8,128)S(1)}, u32[]{:S(2)}, u32[]{:S(2)}) collective-permute-start(f32[2,48,128]{2,1,0:T(8,128)S(1)} %dynamic_update_slice.31), channel_id=1, source_target_pairs={{0,16},{4,20},{8,24},{12,28},{16,0},{20,4},{24,8},{28,12},{32,48},... | collective-permute-start | bytes 147464 | tf_op jit(solution)/shard_map/ppermute | solution.py:101
  95.3 4.2 %collective-permute-start.14 = (f32[2,48,128]{2,1,0:T(8,128)S(1)}, f32[2,48,128]{2,1,0:T(8,128)S(1)}, u32[]{:S(2)}, u32[]{:S(2)}) collective-permute-start(f32[2,48,128]{2,1,0:T(8,128)S(1)} %dynamic_update_slice.31), channel_id=1, source_target_pairs={{0,24},{4,28},{8,16},{12,20},{16,8},{20,12},{24,0},{28,4},{32,56},... | collective-permute-start | bytes 147464 | tf_op jit(solution)/shard_map/ppermute | solution.py:101
  99.4 4.5 %collective-permute-start.15 = (f32[2,48,512]{2,1,0:T(8,128)S(1)}, f32[2,48,512]{2,1,0:T(8,128)S(1)}, u32[]{:S(2)}, u32[]{:S(2)}) collective-permute-start(f32[2,48,512]{2,1,0:T(8,128)S(1)} %constant_dynamic-update-slice_fusion.4), channel_id=1, source_target_pairs={{0,32},{4,36},{8,40},{12,44},{16,48},{20,52},{24,56},{28,60},{32,0... | collective-permute-start | bytes 589832 | tf_op jit(solution)/shard_map/ppermute | solution.py:101
  99.4 6.6 %collective-permute-start.16 = (f32[2,48,512]{2,1,0:T(8,128)S(1)}, f32[2,48,512]{2,1,0:T(8,128)S(1)}, u32[]{:S(2)}, u32[]{:S(2)}) collective-permute-start(f32[2,48,512]{2,1,0:T(8,128)S(1)} %constant_dynamic-update-slice_fusion.4), channel_id=1, source_target_pairs={{0,64},{4,68},{8,72},{12,76},{16,80},{20,84},{24,88},{28,92},{32,9... | collective-permute-start | bytes 589832 | tf_op jit(solution)/shard_map/ppermute | solution.py:101
  100.8 7.3 %collective-permute-start.17 = (f32[2,48,512]{2,1,0:T(8,128)S(1)}, f32[2,48,512]{2,1,0:T(8,128)S(1)}, u32[]{:S(2)}, u32[]{:S(2)}) collective-permute-start(f32[2,48,512]{2,1,0:T(8,128)S(1)} %constant_dynamic-update-slice_fusion.4), channel_id=1, source_target_pairs={{0,96},{4,100},{8,104},{12,108},{16,112},{20,116},{24,120},{28,124... | collective-permute-start | bytes 589832 | tf_op jit(solution)/shard_map/ppermute | solution.py:101
  108.1 11.2 %copy-start = (f32[2,48,2048]{2,1,0:T(8,128)}, f32[2,48,2048]{2,1,0:T(8,128)S(1)}, u32[]{:S(2)}) copy-start(f32[2,48,2048]{2,1,0:T(8,128)S(1)} %constant_dynamic-update-slice_fusion) | copy-start | bytes 2359300
  119.4 8.9 %collective-permute-start.18 = (f32[4,48,512]{2,1,0:T(8,128)S(1)}, f32[4,48,512]{2,1,0:T(8,128)S(1)}, u32[]{:S(2)}, u32[]{:S(2)}) collective-permute-start(f32[4,48,512]{2,1,0:T(8,128)S(1)} %slice_select_fusion), channel_id=1, source_target_pairs={{0,1},{1,0},{2,3},{3,2},{4,5},{5,4},{6,7},{7,6},{8,9},{9,8},{10,11... | collective-permute-start | bytes 1179656 | tf_op jit(solution)/shard_map/ppermute | solution.py:49
  128.4 6.2 %collective-permute-start.19 = (f32[2,48,512]{2,1,0:T(8,128)S(1)}, f32[2,48,512]{2,1,0:T(8,128)S(1)}, u32[]{:S(2)}, u32[]{:S(2)}) collective-permute-start(f32[2,48,512]{2,1,0:T(8,128)S(1)} %slice_select_fusion.2), channel_id=1, source_target_pairs={{0,2},{1,3},{2,0},{3,1},{4,6},{5,7},{6,4},{7,5},{8,10},{9,11},{10,... | collective-permute-start | bytes 589832 | tf_op jit(solution)/shard_map/ppermute | solution.py:49
  139.1 3.5 %collective-permute-start.20 = (bf16[2,48,512]{2,1,0:T(8,128)(2,1)S(1)}, bf16[2,48,512]{2,1,0:T(8,128)(2,1)S(1)}, u32[]{:S(2)}, u32[]{:S(2)}) collective-permute-start(bf16[2,48,512]{2,1,0:T(8,128)(2,1)S(1)} %convolution_convert_fusion), channel_id=1, source_target_pairs={{0,2},{1,3},{2,0},{3,1},{4,6},{5,7},{6,4},{7,5},{8,10},{9,11},{10,... | collective-permute-start | bytes 294920 | tf_op jit(solution)/shard_map/ppermute | solution.py:58
  142.7 4.3 %collective-permute-start.21 = (bf16[4,48,512]{2,1,0:T(8,128)(2,1)S(1)}, bf16[4,48,512]{2,1,0:T(8,128)(2,1)S(1)}, u32[]{:S(2)}, u32[]{:S(2)}) collective-permute-start(bf16[4,48,512]{2,1,0:T(8,128)(2,1)S(1)} %maximum_select_fusion.5), channel_id=1, source_target_pairs={{0,1},{1,0},{2,3},{3,2},{4,5},{5,4},{6,7},{7,6},{8,9},{9,8},{10,11... | collective-permute-start | bytes 589832 | tf_op jit(solution)/shard_map/ppermute | solution.py:58

commit v11 on v9

--- a/solution.py
+++ b/solution.py
@@ -125,7 +125,11 @@
 
 def project_body(slices, rows_low, mixed, chan_size, chan_bits, carried):
     run_count = slices.shape[0]
-    partial_basis = jnp.einsum("nrj,nij->nri", rows_low, slices, preferred_element_type=jnp.float32)
+    rows_both, pick = rows_low
+    partial_both = jnp.einsum(
+        "hrj,nij->nhri", rows_both, slices, preferred_element_type=jnp.float32
+    )
+    partial_basis = jnp.where((pick == 0)[:, None, None], partial_both[:, 0], partial_both[:, 1])
     if carried is not None:
         carried = lax.optimization_barrier((partial_basis, carried))[1]
     basis = halving_scatter(partial_basis, "chan", chan_size, chan_bits, 0)
@@ -174,7 +178,6 @@
         mate_match = (all_runs[None, :] == my_mates[:, None]).astype(jnp.float32)
         mate_loads = jnp.dot(mate_match, loadings, precision=lax.Precision.HIGHEST)
         first_half = (my_halves == 0)[:, None, None]
-        own_rows = jnp.where(first_half, spectra[0][None], spectra[1][None])
         own_mix = jnp.where(first_half, mixing[0][None], mixing[1][None]) * my_loads[:, None, :]
         member = (halves[:, None] == jnp.arange(2, dtype=jnp.int32)[None, :]).astype(jnp.float32)
         cross = jnp.einsum(
@@ -184,7 +187,9 @@
             "hsr,hst->hrt", mixing, mixing, precision=lax.Precision.HIGHEST
         )
         system = inner_mix * cross
-        projected, system = project(slices, own_rows, own_mix, chan_size, chan_bits, carried=system)
+        projected, system = project(
+            slices, (spectra, my_halves), own_mix, chan_size, chan_bits, carried=system
+        )
         inverse = lower_inverse(system)
         mine_member = (my_halves[:, None] == jnp.arange(2, dtype=jnp.int32)[None, :]).astype(
             jnp.float32
@@ -199,7 +204,8 @@
         held_rows = jnp.where(first_half, new_spectra[1][None], new_spectra[0][None])
         held_mix = jnp.where(first_half, mixing[1][None], mixing[0][None]) * mate_loads[:, None, :]
         held_projected = project(
-            slices, held_rows.astype(jnp.bfloat16), held_mix, chan_size, chan_bits
+            slices, (new_spectra.astype(jnp.bfloat16), 1 - my_halves), held_mix, chan_size,
+            chan_bits,
         )
         model_part = jnp.einsum(
             "nrs,nsj->nrj", held_mix, held_rows, precision=lax.Precision.HIGHEST

time: 160 us -> 160 us (level)
  no operation moved by 1% of the time
where the time goes in v11:
time: 160 us; the launch traced here: 159 us
  matrix products  56.7 us (35%)
  starting transfers between devices  42.8 us (27%)
  waiting for transfers between devices  38.1 us (24%)
  other arithmetic  18.6 us (12%)
    dot_general x2, matrix products, project_body(): jnp.einsum('hrj,nij->nhri', rows_both, slices, preferred_element_type=jnp...  22.3 us
    dot_general x2, matrix products, project_body(): jnp.einsum('nsi,nij->nsj', rotated, slices, preferred_element_type=jnp.fl...  19.3 us
    ppermute x7, waiting for transfers between devices, radix_scatter(): got = lax.ppermute(send, axis, xor_pairs(size, mask))  12.4 us
    ppermute x7, starting transfers between devices, radix_scatter(): got = lax.ppermute(send, axis, xor_pairs(size, mask))  11.9 us
    ppermute x4, starting transfers between devices, halving_scatter(): got = lax.ppermute(send, axis, xor_pairs(size, bit))  11.8 us
    ppermute x7, starting transfers between devices, radix_gather(): got = lax.ppermute(x, axis, xor_pairs(size, mask))  10.8 us
    ppermute x4, waiting for transfers between devices, halving_scatter(): got = lax.ppermute(send, axis, xor_pairs(size, bit))  10.7 us
    ppermute x7, waiting for transfers between devices, radix_gather(): got = lax.ppermute(x, axis, xor_pairs(size, mask))  9.99 us
  transfers between devices with their start and end apart: 22, of which 16 were waited for; matrix products, arithmetic and copies ran while one was open for 13% of the time, Pallas kernels for 0%

profile of v11, /device:TPU:1, one launch (start us, length us, event | category | flops | bytes accessed | tf_op | source)
XLA Modules:
  0.0 159.2 jit_solution(14717179024823793252)
XLA Ops:
  0.7 1.0 select_reduce_fusion.3
  1.7 11.0 %fusion.17 = f32[8,2,48,512]{3,2,1,0:T(8,128)S(1)} fusion(bf16[8,512,2048]{2,1,0:T(8,128)(2,1)} %param.6, bf16[2,48,2048]{2,1,0:T(8,128)(2,1)S(1)} %copy-done), kind=kOutput, calls=%fused_computation.14 | convolution fusion | flops 1610612736 | bytes 18743296 | tf_op jit(solution)/shard_map/hrj,nij->nhri/dot_general | solution.py:129
  13.0 1.5 collective-permute-start
  15.5 8.8 %custom-call.7 = f32[2,48,48]{2,1,0:T(8,128)S(1)} custom-call(f32[2,48,48]{2,1,0:T(8,128)S(1)} %fusion.198), custom_call_target="Cholesky" | custom-call | tf_op jit(solution)/shard_map/jit(cholesky)/cholesky | solution.py:154
  24.5 1.5 collective-permute-start.1
  26.1 4.5 %collective-permute-done.1 = f32[2,48,512]{2,1,0:T(8,128)S(1)} collective-permute-done((f32[2,48,512]{2,1,0:T(8,128)S(1)}, f32[2,48,512]{2,1,0:T(8,128)S(1)}, u32[]{:S(2)}, u32[]{:S(2)}) %collective-permute-start.1) | collective-permute-done | bytes 196640 | tf_op jit(solution)/shard_map/ppermute | solution.py:49
  30.7 0.3 fusion.43
  31.0 0.4 select_reduce_fusion.1
  34.8 0.3 convolution_convert_fusion.1
  35.1 1.5 collective-permute-start.2
  36.8 1.9 %collective-permute-done.2 = bf16[2,48,512]{2,1,0:T(8,128)(2,1)S(1)} collective-permute-done((bf16[2,48,512]{2,1,0:T(8,128)(2,1)S(1)}, bf16[2,48,512]{2,1,0:T(8,128)(2,1)S(1)}, u32[]{:S(2)}, u32[]{:S(2)}) %collective-permute-start.2) | collective-permute-done | bytes 98336 | tf_op jit(solution)/shard_map/ppermute | solution.py:58
  38.7 2.7 %collective-permute-start.3 = (bf16[4,48,512]{2,1,0:T(8,128)(2,1)S(1)}, bf16[4,48,512]{2,1,0:T(8,128)(2,1)S(1)}, u32[]{:S(2)}, u32[]{:S(2)}) collective-permute-start(bf16[4,48,512]{2,1,0:T(8,128)(2,1)S(1)} %maximum_select_fusion.4), channel_id=1, source_target_pairs={{0,1},{1,0},{2,3},{3,2},{4,5},{5,4},{6,7},{7,6},{8,9},{9,8},{10,11... | collective-permute-start | bytes 589832 | tf_op jit(solution)/shard_map/ppermute | solution.py:58
  41.4 1.1 collective-permute-done.3
  42.4 8.8 %fusion.23 = f32[8,48,2048]{2,1,0:T(8,128)S(1)} fusion(bf16[8,512,2048]{2,1,0:T(8,128)(2,1)} %param.6, bf16[4,48,512]{2,1,0:T(8,128)(2,1)S(1)} %maximum_select_fusion.4, bf16[4,48,512]{2,1,0:T(8,128)(2,1)S(1)} %collective-permute-done.3, pred[]{:T(512)S(6)} %ne.14), kind=kOutput, calls=%fused_computation.28 | convolution fusion | flops 805896192 | bytes 20316160 | tf_op jit(solution)/shard_map/nsi,nij->nsj/dot_general | solution.py:147
  51.3 2.3 %fusion.8 = f32[2,48,2048]{2,1,0:T(8,128)S(1)} fusion(f32[8,48,2048]{2,1,0:T(8,128)S(1)} %fusion.23, f32[8,48,48]{1,2,0:T(8,128)S(1)} %copy.22, f32[8,2]{0,1:T(2,128)S(1)} %compare_convert_fusion.1), kind=kOutput, calls=%fused_computation.9 | convolution fusion | flops 906006528 | bytes 4005952 | tf_op jit(solution)/shard_map/nhsr,nsj->hrj/dot_general | solution.py:198
  53.7 1.4 collective-permute-start.4
  55.1 2.5 %collective-permute-start.5 = (f32[2,48,512]{2,1,0:T(8,128)S(1)}, f32[2,48,512]{2,1,0:T(8,128)S(1)}, u32[]{:S(2)}, u32[]{:S(2)}) collective-permute-start(f32[2,48,512]{2,1,0:T(8,128)S(1)} %get-tuple-element.16), channel_id=1, source_target_pairs={{0,64},{4,68},{8,72},{12,76},{16,80},{20,84},{24,88},{28,92},{32,9... | collective-permute-start | bytes 589832 | tf_op jit(solution)/shard_map/ppermute | solution.py:84
  57.7 2.1 %collective-permute-done.4 = f32[2,48,512]{2,1,0:T(8,128)S(1)} collective-permute-done((f32[2,48,512]{2,1,0:T(8,128)S(1)}, f32[2,48,512]{2,1,0:T(8,128)S(1)}, u32[]{:S(2)}, u32[]{:S(2)}) %collective-permute-start.4) | collective-permute-done | bytes 196640 | tf_op jit(solution)/shard_map/ppermute | solution.py:84
  59.8 6.6 %collective-permute-done.5 = f32[2,48,512]{2,1,0:T(8,128)S(1)} collective-permute-done((f32[2,48,512]{2,1,0:T(8,128)S(1)}, f32[2,48,512]{2,1,0:T(8,128)S(1)}, u32[]{:S(2)}, u32[]{:S(2)}) %collective-permute-start.5) | collective-permute-done | bytes 196640 | tf_op jit(solution)/shard_map/ppermute | solution.py:84
  66.4 2.4 %collective-permute-done.6 = f32[2,48,512]{2,1,0:T(8,128)S(1)} collective-permute-done((f32[2,48,512]{2,1,0:T(8,128)S(1)}, f32[2,48,512]{2,1,0:T(8,128)S(1)}, u32[]{:S(2)}, u32[]{:S(2)}) %collective-permute-start.6) | collective-permute-done | bytes 196640 | tf_op jit(solution)/shard_map/ppermute | solution.py:84
  68.9 1.7 %collective-permute-start.7 = (f32[2,48,128]{2,1,0:T(8,128)S(1)}, f32[2,48,128]{2,1,0:T(8,128)S(1)}, u32[]{:S(2)}, u32[]{:S(2)}) collective-permute-start(f32[2,48,128]{2,1,0:T(8,128)S(1)} %get-tuple-element.17), channel_id=1, source_target_pairs={{0,8},{4,12},{8,0},{12,4},{16,24},{20,28},{24,16},{28,20},{32,40},... | collective-permute-start | bytes 147464 | tf_op jit(solution)/shard_map/ppermute | solution.py:84
  70.6 3.3 %collective-permute-start.8 = (f32[2,48,128]{2,1,0:T(8,128)S(1)}, f32[2,48,128]{2,1,0:T(8,128)S(1)}, u32[]{:S(2)}, u32[]{:S(2)}) collective-permute-start(f32[2,48,128]{2,1,0:T(8,128)S(1)} %get-tuple-element.19), channel_id=1, source_target_pairs={{0,16},{4,20},{8,24},{12,28},{16,0},{20,4},{24,8},{28,12},{32,48},... | collective-permute-start | bytes 147464 | tf_op jit(solution)/shard_map/ppermute | solution.py:84
  74.0 7.4 %custom-call.8 = f32[2,1,48,48]{2,3,1,0:T(8,128)S(1)} custom-call(f32[2,1,48,48]{3,2,1,0:T(8,128)S(1)} %select_bitcast_fusion), custom_call_target="InvertDiagBlocksLowerTriangular" | custom-call | tf_op jit(solution)/shard_map/triangular_solve | solution.py:156
  81.5 2.9 %collective-permute-start.10 = (f32[2,48,64]{2,1,0:T(8,128)S(1)}, f32[2,48,64]{2,1,0:T(8,128)S(1)}, u32[]{:S(2)}, u32[]{:S(2)}) collective-permute-start(f32[2,48,64]{2,1,0:T(8,128)S(1)} %constant_dynamic-slice_fusion), channel_id=1, source_target_pairs={{0,4},{4,0},{8,12},{12,8},{16,20},{20,16},{24,28},{28,24},{32,36},... | collective-permute-start | bytes 73736 | tf_op jit(solution)/shard_map/ppermute | solution.py:84
  84.8 1.3 collective-permute-done.10
  86.5 3.0 %collective-permute-start.11 = (f32[2,48,64]{2,1,0:T(8,128)S(1)}, f32[2,48,64]{2,1,0:T(8,128)S(1)}, u32[]{:S(2)}, u32[]{:S(2)}) collective-permute-start(f32[2,48,64]{2,1,0:T(8,128)S(1)} %fusion.242), channel_id=1, source_target_pairs={{0,4},{4,0},{8,12},{12,8},{16,20},{20,16},{24,28},{28,24},{32,36},... | collective-permute-start | bytes 73736 | tf_op jit(solution)/shard_map/ppermute | solution.py:101
  89.8 1.3 collective-permute-done.11
  91.1 0.5 dynamic_update_slice.31
  91.7 3.8 %collective-permute-start.13 = (f32[2,48,128]{2,1,0:T(8,128)S(1)}, f32[2,48,128]{2,1,0:T(8,128)S(1)}, u32[]{:S(2)}, u32[]{:S(2)}) collective-permute-start(f32[2,48,128]{2,1,0:T(8,128)S(1)} %dynamic_update_slice.31), channel_id=1, source_target_pairs={{0,16},{4,20},{8,24},{12,28},{16,0},{20,4},{24,8},{28,12},{32,48},... | collective-permute-start | bytes 147464 | tf_op jit(solution)/shard_map/ppermute | solution.py:101
  95.6 1.9 %collective-permute-done.13 = f32[2,48,128]{2,1,0:T(8,128)S(1)} collective-permute-done((f32[2,48,128]{2,1,0:T(8,128)S(1)}, f32[2,48,128]{2,1,0:T(8,128)S(1)}, u32[]{:S(2)}, u32[]{:S(2)}) %collective-permute-start.13) | collective-permute-done | bytes 49184 | tf_op jit(solution)/shard_map/ppermute | solution.py:101
  97.5 2.1 %collective-permute-done.14 = f32[2,48,128]{2,1,0:T(8,128)S(1)} collective-permute-done((f32[2,48,128]{2,1,0:T(8,128)S(1)}, f32[2,48,128]{2,1,0:T(8,128)S(1)}, u32[]{:S(2)}, u32[]{:S(2)}) %collective-permute-start.14) | collective-permute-done | bytes 49184 | tf_op jit(solution)/shard_map/ppermute | solution.py:101
  99.7 1.4 collective-permute-start.16
  101.0 2.5 %collective-permute-start.17 = (f32[2,48,512]{2,1,0:T(8,128)S(1)}, f32[2,48,512]{2,1,0:T(8,128)S(1)}, u32[]{:S(2)}, u32[]{:S(2)}) collective-permute-start(f32[2,48,512]{2,1,0:T(8,128)S(1)} %constant_dynamic-update-slice_fusion.4), channel_id=1, source_target_pairs={{0,96},{4,100},{8,104},{12,108},{16,112},{20,116},{24,120},{28,124... | collective-permute-start | bytes 589832 | tf_op jit(solution)/shard_map/ppermute | solution.py:101
  103.6 0.6 collective-permute-done.15
  104.2 2.1 %collective-permute-done.16 = f32[2,48,512]{2,1,0:T(8,128)S(1)} collective-permute-done((f32[2,48,512]{2,1,0:T(8,128)S(1)}, f32[2,48,512]{2,1,0:T(8,128)S(1)}, u32[]{:S(2)}, u32[]{:S(2)}) %collective-permute-start.16) | collective-permute-done | bytes 196640 | tf_op jit(solution)/shard_map/ppermute | solution.py:101
  106.3 2.0 %collective-permute-done.17 = f32[2,48,512]{2,1,0:T(8,128)S(1)} collective-permute-done((f32[2,48,512]{2,1,0:T(8,128)S(1)}, f32[2,48,512]{2,1,0:T(8,128)S(1)}, u32[]{:S(2)}, u32[]{:S(2)}) %collective-permute-start.17) | collective-permute-done | bytes 196640 | tf_op jit(solution)/shard_map/ppermute | solution.py:101
  108.4 11.3 %fusion.14 = f32[8,2,48,512]{3,2,0,1:T(8,128)S(1)} fusion(bf16[8,512,2048]{2,1,0:T(8,128)(2,1)} %param.6, f32[2,48,2048]{2,1,0:T(8,128)S(1)} %constant_dynamic-update-slice_fusion), kind=kOutput, calls=%fused_computation.13 | convolution fusion | flops 1610809344 | bytes 19136512 | tf_op jit(solution)/shard_map/hrj,nij->nhri/dot_general | solution.py:129
  119.9 7.5 %collective-permute-start.18 = (f32[4,48,512]{2,1,0:T(8,128)S(1)}, f32[4,48,512]{2,1,0:T(8,128)S(1)}, u32[]{:S(2)}, u32[]{:S(2)}) collective-permute-start(f32[4,48,512]{2,1,0:T(8,128)S(1)} %slice_select_fusion), channel_id=1, source_target_pairs={{0,1},{1,0},{2,3},{3,2},{4,5},{5,4},{6,7},{7,6},{8,9},{9,8},{10,11... | collective-permute-start | bytes 1179656 | tf_op jit(solution)/shard_map/ppermute | solution.py:49
  127.4 1.3 collective-permute-done.18
  128.9 1.4 collective-permute-start.19
  130.3 4.8 %collective-permute-done.19 = f32[2,48,512]{2,1,0:T(8,128)S(1)} collective-permute-done((f32[2,48,512]{2,1,0:T(8,128)S(1)}, f32[2,48,512]{2,1,0:T(8,128)S(1)}, u32[]{:S(2)}, u32[]{:S(2)}) %collective-permute-start.19) | collective-permute-done | bytes 196640 | tf_op jit(solution)/shard_map/ppermute | solution.py:49
  135.1 0.3 fusion.40
  135.4 0.4 select_reduce_fusion
  139.6 1.4 collective-permute-start.20
  141.1 2.1 %collective-permute-done.20 = bf16[2,48,512]{2,1,0:T(8,128)(2,1)S(1)} collective-permute-done((bf16[2,48,512]{2,1,0:T(8,128)(2,1)S(1)}, bf16[2,48,512]{2,1,0:T(8,128)(2,1)S(1)}, u32[]{:S(2)}, u32[]{:S(2)}) %collective-permute-start.20) | collective-permute-done | bytes 98336 | tf_op jit(solution)/shard_map/ppermute | solution.py:58
  143.2 2.7 %collective-permute-start.21 = (bf16[4,48,512]{2,1,0:T(8,128)(2,1)S(1)}, bf16[4,48,512]{2,1,0:T(8,128)(2,1)S(1)}, u32[]{:S(2)}, u32[]{:S(2)}) collective-permute-start(bf16[4,48,512]{2,1,0:T(8,128)(2,1)S(1)} %maximum_select_fusion.5), channel_id=1, source_target_pairs={{0,1},{1,0},{2,3},{3,2},{4,5},{5,4},{6,7},{7,6},{8,9},{9,8},{10,11... | collective-permute-start | bytes 589832 | tf_op jit(solution)/shard_map/ppermute | solution.py:58
  145.9 2.8 %fusion.6 = f32[8,48,2048]{2,1,0:T(8,128)S(1)} fusion(f32[48,2048]{1,0:T(8,128)S(1)} %get-tuple-element.13, f32[48,2048]{1,0:T(8,128)S(1)} %get-tuple-element.12, pred[8]{0:T(512)(128)(4,1)S(1)} %get-tuple-element.27, f32[8,48]{1,0:T(8,128)S(1)} %fusion.211, f32[48,48]{1,0:T(8,128)S(1)} %get-tuple-element.23, f32[48,48]{1,0:T(8,128)S(1)} %get-tuple-element.22), kind=kOutput, calls=%fused_computation.6 | convolution fusion | flops 453808128 | bytes 3952136 | tf_op jit(solution)/shard_map/nrs,nsj->nrj/dot_general | solution.py:210
  148.7 10.5 %convolution_subtract_fusion = f32[8,48,2048]{2,1,0:T(8,128)} fusion(f32[8,48,2048]{2,1,0:T(8,128)S(1)} %fusion.6, bf16[8,512,2048]{2,1,0:T(8,128)(2,1)} %param.6, bf16[4,48,512]{2,1,0:T(8,128)(2,1)S(1)} %maximum_select_fusion.5, bf16[4,48,512]{2,1,0:T(8,128)(2,1)S(1)} %collective-permute-done.21, pred[]{:T(512)S(6)} %ne.14), kind=kOutput, calls=%fused_computation.8 | convolution fusion | flops 806682624 | bytes 23461888 | tf_op jit(solution)/shard_map/nsi,nij->nsj/dot_general | solution.py:147
  (133 shorter events, 11.0 us)
Async XLA Ops:
  0.6 1.0 copy-start
  12.7 1.8 %copy-start.4 = (s32[256]{0:T(256)S(1)}, s32[256]{0:T(256)}, u32[]{:S(2)}) copy-start(s32[256]{0:T(256)} %param.10) | copy-start | bytes 3076
  12.7 1.8 %copy-start.3 = (f32[256,48]{0,1:T(8,128)S(1)}, f32[256,48]{0,1:T(8,128)}, u32[]{:S(2)}) copy-start(f32[256,48]{0,1:T(8,128)} %param.8) | copy-start | bytes 147460
  12.7 2.1 %copy-start.2 = (f32[2,48,48]{2,1,0:T(8,128)S(1)}, f32[2,48,48]{2,1,0:T(8,128)}, u32[]{:S(2)}) copy-start(f32[2,48,48]{2,1,0:T(8,128)} %param.9) | copy-start | bytes 55300
  13.0 11.4 %collective-permute-start = (f32[4,48,512]{2,1,0:T(8,128)S(1)}, f32[4,48,512]{2,1,0:T(8,128)S(1)}, u32[]{:S(2)}, u32[]{:S(2)}) collective-permute-start(f32[4,48,512]{2,1,0:T(8,128)S(1)} %slice_select_fusion.1), channel_id=1, source_target_pairs={{0,1},{1,0},{2,3},{3,2},{4,5},{5,4},{6,7},{7,6},{8,9},{9,8},{10,11... | collective-permute-start | bytes 1179656 | tf_op jit(solution)/shard_map/ppermute | solution.py:49
  24.5 6.1 %collective-permute-start.1 = (f32[2,48,512]{2,1,0:T(8,128)S(1)}, f32[2,48,512]{2,1,0:T(8,128)S(1)}, u32[]{:S(2)}, u32[]{:S(2)}) collective-permute-start(f32[2,48,512]{2,1,0:T(8,128)S(1)} %slice_select_fusion.3), channel_id=1, source_target_pairs={{0,2},{1,3},{2,0},{3,1},{4,6},{5,7},{6,4},{7,5},{8,10},{9,11},{10,... | collective-permute-start | bytes 589832 | tf_op jit(solution)/shard_map/ppermute | solution.py:49
  35.1 3.5 %collective-permute-start.2 = (bf16[2,48,512]{2,1,0:T(8,128)(2,1)S(1)}, bf16[2,48,512]{2,1,0:T(8,128)(2,1)S(1)}, u32[]{:S(2)}, u32[]{:S(2)}) collective-permute-start(bf16[2,48,512]{2,1,0:T(8,128)(2,1)S(1)} %convolution_convert_fusion.1), channel_id=1, source_target_pairs={{0,2},{1,3},{2,0},{3,1},{4,6},{5,7},{6,4},{7,5},{8,10},{9,11},{10,... | collective-permute-start | bytes 294920 | tf_op jit(solution)/shard_map/ppermute | solution.py:58
  38.7 3.8 %collective-permute-start.3 = (bf16[4,48,512]{2,1,0:T(8,128)(2,1)S(1)}, bf16[4,48,512]{2,1,0:T(8,128)(2,1)S(1)}, u32[]{:S(2)}, u32[]{:S(2)}) collective-permute-start(bf16[4,48,512]{2,1,0:T(8,128)(2,1)S(1)} %maximum_select_fusion.4), channel_id=1, source_target_pairs={{0,1},{1,0},{2,3},{3,2},{4,5},{5,4},{6,7},{7,6},{8,9},{9,8},{10,11... | collective-permute-start | bytes 589832 | tf_op jit(solution)/shard_map/ppermute | solution.py:58
  53.7 6.2 %collective-permute-start.4 = (f32[2,48,512]{2,1,0:T(8,128)S(1)}, f32[2,48,512]{2,1,0:T(8,128)S(1)}, u32[]{:S(2)}, u32[]{:S(2)}) collective-permute-start(f32[2,48,512]{2,1,0:T(8,128)S(1)} %get-tuple-element.14), channel_id=1, source_target_pairs={{0,32},{4,36},{8,40},{12,44},{16,48},{20,52},{24,56},{28,60},{32,0... | collective-permute-start | bytes 589832 | tf_op jit(solution)/shard_map/ppermute | solution.py:84
  55.1 11.3 %collective-permute-start.5 = (f32[2,48,512]{2,1,0:T(8,128)S(1)}, f32[2,48,512]{2,1,0:T(8,128)S(1)}, u32[]{:S(2)}, u32[]{:S(2)}) collective-permute-start(f32[2,48,512]{2,1,0:T(8,128)S(1)} %get-tuple-element.16), channel_id=1, source_target_pairs={{0,64},{4,68},{8,72},{12,76},{16,80},{20,84},{24,88},{28,92},{32,9... | collective-permute-start | bytes 589832 | tf_op jit(solution)/shard_map/ppermute | solution.py:84
  57.5 11.3 %collective-permute-start.6 = (f32[2,48,512]{2,1,0:T(8,128)S(1)}, f32[2,48,512]{2,1,0:T(8,128)S(1)}, u32[]{:S(2)}, u32[]{:S(2)}) collective-permute-start(f32[2,48,512]{2,1,0:T(8,128)S(1)} %get-tuple-element.15), channel_id=1, source_target_pairs={{0,96},{4,100},{8,104},{12,108},{16,112},{20,116},{24,120},{28,124... | collective-permute-start | bytes 589832 | tf_op jit(solution)/shard_map/ppermute | solution.py:84
  68.9 12.5 %collective-permute-start.7 = (f32[2,48,128]{2,1,0:T(8,128)S(1)}, f32[2,48,128]{2,1,0:T(8,128)S(1)}, u32[]{:S(2)}, u32[]{:S(2)}) collective-permute-start(f32[2,48,128]{2,1,0:T(8,128)S(1)} %get-tuple-element.17), channel_id=1, source_target_pairs={{0,8},{4,12},{8,0},{12,4},{16,24},{20,28},{24,16},{28,20},{32,40},... | collective-permute-start | bytes 147464 | tf_op jit(solution)/shard_map/ppermute | solution.py:84
  70.6 10.8 %collective-permute-start.8 = (f32[2,48,128]{2,1,0:T(8,128)S(1)}, f32[2,48,128]{2,1,0:T(8,128)S(1)}, u32[]{:S(2)}, u32[]{:S(2)}) collective-permute-start(f32[2,48,128]{2,1,0:T(8,128)S(1)} %get-tuple-element.19), channel_id=1, source_target_pairs={{0,16},{4,20},{8,24},{12,28},{16,0},{20,4},{24,8},{28,12},{32,48},... | collective-permute-start | bytes 147464 | tf_op jit(solution)/shard_map/ppermute | solution.py:84
  73.9 7.5 %collective-permute-start.9 = (f32[2,48,128]{2,1,0:T(8,128)S(1)}, f32[2,48,128]{2,1,0:T(8,128)S(1)}, u32[]{:S(2)}, u32[]{:S(2)}) collective-permute-start(f32[2,48,128]{2,1,0:T(8,128)S(1)} %get-tuple-element.18), channel_id=1, source_target_pairs={{0,24},{4,28},{8,16},{12,20},{16,8},{20,12},{24,0},{28,4},{32,56},... | collective-permute-start | bytes 147464 | tf_op jit(solution)/shard_map/ppermute | solution.py:84
  81.5 4.5 %collective-permute-start.10 = (f32[2,48,64]{2,1,0:T(8,128)S(1)}, f32[2,48,64]{2,1,0:T(8,128)S(1)}, u32[]{:S(2)}, u32[]{:S(2)}) collective-permute-start(f32[2,48,64]{2,1,0:T(8,128)S(1)} %constant_dynamic-slice_fusion), channel_id=1, source_target_pairs={{0,4},{4,0},{8,12},{12,8},{16,20},{20,16},{24,28},{28,24},{32,36},... | collective-permute-start | bytes 73736 | tf_op jit(solution)/shard_map/ppermute | solution.py:84
  86.5 4.5 %collective-permute-start.11 = (f32[2,48,64]{2,1,0:T(8,128)S(1)}, f32[2,48,64]{2,1,0:T(8,128)S(1)}, u32[]{:S(2)}, u32[]{:S(2)}) collective-permute-start(f32[2,48,64]{2,1,0:T(8,128)S(1)} %fusion.242), channel_id=1, source_target_pairs={{0,4},{4,0},{8,12},{12,8},{16,20},{20,16},{24,28},{28,24},{32,36},... | collective-permute-start | bytes 73736 | tf_op jit(solution)/shard_map/ppermute | solution.py:101
  91.6 4.0 %collective-permute-start.12 = (f32[2,48,128]{2,1,0:T(8,128)S(1)}, f32[2,48,128]{2,1,0:T(8,128)S(1)}, u32[]{:S(2)}, u32[]{:S(2)}) collective-permute-start(f32[2,48,128]{2,1,0:T(8,128)S(1)} %dynamic_update_slice.31), channel_id=1, source_target_pairs={{0,8},{4,12},{8,0},{12,4},{16,24},{20,28},{24,16},{28,20},{32,40},... | collective-permute-start | bytes 147464 | tf_op jit(solution)/shard_map/ppermute | solution.py:101
  91.7 5.8 %collective-permute-start.13 = (f32[2,48,128]{2,1,0:T(8,128)S(1)}, f32[2,48,128]{2,1,0:T(8,128)S(1)}, u32[]{:S(2)}, u32[]{:S(2)}) collective-permute-start(f32[2,48,128]{2,1,0:T(8,128)S(1)} %dynamic_update_slice.31), channel_id=1, source_target_pairs={{0,16},{4,20},{8,24},{12,28},{16,0},{20,4},{24,8},{28,12},{32,48},... | collective-permute-start | bytes 147464 | tf_op jit(solution)/shard_map/ppermute | solution.py:101
  95.5 4.2 %collective-permute-start.14 = (f32[2,48,128]{2,1,0:T(8,128)S(1)}, f32[2,48,128]{2,1,0:T(8,128)S(1)}, u32[]{:S(2)}, u32[]{:S(2)}) collective-permute-start(f32[2,48,128]{2,1,0:T(8,128)S(1)} %dynamic_update_slice.31), channel_id=1, source_target_pairs={{0,24},{4,28},{8,16},{12,20},{16,8},{20,12},{24,0},{28,4},{32,56},... | collective-permute-start | bytes 147464 | tf_op jit(solution)/shard_map/ppermute | solution.py:101
  99.7 4.5 %collective-permute-start.15 = (f32[2,48,512]{2,1,0:T(8,128)S(1)}, f32[2,48,512]{2,1,0:T(8,128)S(1)}, u32[]{:S(2)}, u32[]{:S(2)}) collective-permute-start(f32[2,48,512]{2,1,0:T(8,128)S(1)} %constant_dynamic-update-slice_fusion.4), channel_id=1, source_target_pairs={{0,32},{4,36},{8,40},{12,44},{16,48},{20,52},{24,56},{28,60},{32,0... | collective-permute-start | bytes 589832 | tf_op jit(solution)/shard_map/ppermute | solution.py:101
  99.7 6.6 %collective-permute-start.16 = (f32[2,48,512]{2,1,0:T(8,128)S(1)}, f32[2,48,512]{2,1,0:T(8,128)S(1)}, u32[]{:S(2)}, u32[]{:S(2)}) collective-permute-start(f32[2,48,512]{2,1,0:T(8,128)S(1)} %constant_dynamic-update-slice_fusion.4), channel_id=1, source_target_pairs={{0,64},{4,68},{8,72},{12,76},{16,80},{20,84},{24,88},{28,92},{32,9... | collective-permute-start | bytes 589832 | tf_op jit(solution)/shard_map/ppermute | solution.py:101
  101.0 7.3 %collective-permute-start.17 = (f32[2,48,512]{2,1,0:T(8,128)S(1)}, f32[2,48,512]{2,1,0:T(8,128)S(1)}, u32[]{:S(2)}, u32[]{:S(2)}) collective-permute-start(f32[2,48,512]{2,1,0:T(8,128)S(1)} %constant_dynamic-update-slice_fusion.4), channel_id=1, source_target_pairs={{0,96},{4,100},{8,104},{12,108},{16,112},{20,116},{24,120},{28,124... | collective-permute-start | bytes 589832 | tf_op jit(solution)/shard_map/ppermute | solution.py:101
  108.3 32.7 %copy-start.1 = (f32[2,48,2048]{2,1,0:T(8,128)}, f32[2,48,2048]{2,1,0:T(8,128)S(1)}, u32[]{:S(2)}) copy-start(f32[2,48,2048]{2,1,0:T(8,128)S(1)} %constant_dynamic-update-slice_fusion) | copy-start | bytes 2359300
  119.9 8.9 %collective-permute-start.18 = (f32[4,48,512]{2,1,0:T(8,128)S(1)}, f32[4,48,512]{2,1,0:T(8,128)S(1)}, u32[]{:S(2)}, u32[]{:S(2)}) collective-permute-start(f32[4,48,512]{2,1,0:T(8,128)S(1)} %slice_select_fusion), channel_id=1, source_target_pairs={{0,1},{1,0},{2,3},{3,2},{4,5},{5,4},{6,7},{7,6},{8,9},{9,8},{10,11... | collective-permute-start | bytes 1179656 | tf_op jit(solution)/shard_map/ppermute | solution.py:49
  128.9 6.2 %collective-permute-start.19 = (f32[2,48,512]{2,1,0:T(8,128)S(1)}, f32[2,48,512]{2,1,0:T(8,128)S(1)}, u32[]{:S(2)}, u32[]{:S(2)}) collective-permute-start(f32[2,48,512]{2,1,0:T(8,128)S(1)} %slice_select_fusion.2), channel_id=1, source_target_pairs={{0,2},{1,3},{2,0},{3,1},{4,6},{5,7},{6,4},{7,5},{8,10},{9,11},{10,... | collective-permute-start | bytes 589832 | tf_op jit(solution)/shard_map/ppermute | solution.py:49
  139.6 3.5 %collective-permute-start.20 = (bf16[2,48,512]{2,1,0:T(8,128)(2,1)S(1)}, bf16[2,48,512]{2,1,0:T(8,128)(2,1)S(1)}, u32[]{:S(2)}, u32[]{:S(2)}) collective-permute-start(bf16[2,48,512]{2,1,0:T(8,128)(2,1)S(1)} %convolution_convert_fusion), channel_id=1, source_target_pairs={{0,2},{1,3},{2,0},{3,1},{4,6},{5,7},{6,4},{7,5},{8,10},{9,11},{10,... | collective-permute-start | bytes 294920 | tf_op jit(solution)/shard_map/ppermute | solution.py:58
  143.2 5.5 %collective-permute-start.21 = (bf16[4,48,512]{2,1,0:T(8,128)(2,1)S(1)}, bf16[4,48,512]{2,1,0:T(8,128)(2,1)S(1)}, u32[]{:S(2)}, u32[]{:S(2)}) collective-permute-start(bf16[4,48,512]{2,1,0:T(8,128)(2,1)S(1)} %maximum_select_fusion.5), channel_id=1, source_target_pairs={{0,1},{1,0},{2,3},{3,2},{4,5},{5,4},{6,7},{7,6},{8,9},{9,8},{10,11... | collective-permute-start | bytes 589832 | tf_op jit(solution)/shard_map/ppermute | solution.py:58

commit v12 on v11

--- a/solution.py
+++ b/solution.py
@@ -169,14 +169,11 @@
         run_count = slices.shape[0]
         total_runs = loadings.shape[0]
         first_run = lax.axis_index("runs") * run_count
-        mine = first_run + jnp.arange(run_count, dtype=jnp.int32)
-        all_runs = jnp.arange(total_runs, dtype=jnp.int32)
-        matches = all_runs[None, :] == mine[:, None]
-        my_halves = jnp.sum(jnp.where(matches, halves[None, :], 0), axis=1)
-        my_mates = jnp.sum(jnp.where(matches, partner[None, :], 0), axis=1)
-        my_loads = jnp.dot(matches.astype(jnp.float32), loadings, precision=lax.Precision.HIGHEST)
-        mate_match = (all_runs[None, :] == my_mates[:, None]).astype(jnp.float32)
-        mate_loads = jnp.dot(mate_match, loadings, precision=lax.Precision.HIGHEST)
+        del total_runs
+        my_halves = lax.dynamic_slice_in_dim(halves, first_run, run_count)
+        my_mates = lax.dynamic_slice_in_dim(partner, first_run, run_count)
+        my_loads = lax.dynamic_slice_in_dim(loadings, first_run, run_count, axis=0)
+        mate_loads = jnp.take(loadings, my_mates, axis=0, mode="clip")
         first_half = (my_halves == 0)[:, None, None]
         own_mix = jnp.where(first_half, mixing[0][None], mixing[1][None]) * my_loads[:, None, :]
         member = (halves[:, None] == jnp.arange(2, dtype=jnp.int32)[None, :]).astype(jnp.float32)

time: 160 us -> 160 us (level)
  transfers between devices with their start and end apart: 22 -> 22, of which waited for: 16 -> 16; matrix products, arithmetic and copies ran while one was open for 13% -> 14% of each run, Pallas kernels for 0% -> 0%
where the time goes in v12:
time: 160 us
  matrix products  56.3 us (35%)
  starting transfers between devices  42.7 us (27%)
  waiting for transfers between devices  38.2 us (24%)
  other arithmetic  18.5 us (12%)
  local copies, waits for them, and re-layouts  2.54 us (2%)
    dot_general x2, matrix products, project_body(): jnp.einsum('hrj,nij->nhri', rows_both, slices, preferred_element_type=jnp...  22.3 us
    dot_general x2, matrix products, project_body(): jnp.einsum('nsi,nij->nsj', rotated, slices, preferred_element_type=jnp.fl...  19.3 us
    ppermute x7, waiting for transfers between devices, radix_scatter(): got = lax.ppermute(send, axis, xor_pairs(size, mask))  12.4 us
    ppermute x7, starting transfers between devices, radix_scatter(): got = lax.ppermute(send, axis, xor_pairs(size, mask))  11.9 us
    ppermute x4, starting transfers between devices, halving_scatter(): got = lax.ppermute(send, axis, xor_pairs(size, bit))  11.8 us
    ppermute x7, starting transfers between devices, radix_gather(): got = lax.ppermute(x, axis, xor_pairs(size, mask))  10.8 us
    ppermute x4, waiting for transfers between devices, halving_scatter(): got = lax.ppermute(send, axis, xor_pairs(size, bit))  10.8 us
    ppermute x7, waiting for transfers between devices, radix_gather(): got = lax.ppermute(x, axis, xor_pairs(size, mask))  9.99 us
  transfers between devices with their start and end apart: 22, of which 16 were waited for; matrix products, arithmetic and copies ran while one was open for 14% of the time, Pallas kernels for 0%

profile of v12, /device:TPU:1, one launch (start us, length us, event | category | flops | bytes accessed | tf_op | source)
XLA Modules:
  0.0 159.7 jit_solution(10994582965111389466)
XLA Ops:
  0.7 0.8 subtract_compare_fusion
  1.6 11.0 %fusion.17 = f32[8,2,48,512]{3,2,1,0:T(8,128)S(1)} fusion(bf16[8,512,2048]{2,1,0:T(8,128)(2,1)} %param.6, bf16[2,48,2048]{2,1,0:T(8,128)(2,1)S(1)} %copy-done), kind=kOutput, calls=%fused_computation.15 | convolution fusion | flops 1610612736 | bytes 18743296 | tf_op jit(solution)/shard_map/hrj,nij->nhri/dot_general | solution.py:129
  13.0 1.5 collective-permute-start
  15.5 8.8 %custom-call.7 = f32[2,48,48]{2,1,0:T(8,128)S(1)} custom-call(f32[2,48,48]{2,1,0:T(8,128)S(1)} %fusion.198), custom_call_target="Cholesky" | custom-call | tf_op jit(solution)/shard_map/jit(cholesky)/cholesky | solution.py:154
  24.3 0.6 gather_fusion
  25.0 1.5 collective-permute-start.1
  26.6 4.6 %collective-permute-done.1 = f32[2,48,512]{2,1,0:T(8,128)S(1)} collective-permute-done((f32[2,48,512]{2,1,0:T(8,128)S(1)}, f32[2,48,512]{2,1,0:T(8,128)S(1)}, u32[]{:S(2)}, u32[]{:S(2)}) %collective-permute-start.1) | collective-permute-done | bytes 196640 | tf_op jit(solution)/shard_map/ppermute | solution.py:49
  31.2 0.3 fusion.43
  31.6 0.4 select_reduce_fusion.1
  35.7 1.5 collective-permute-start.2
  37.4 1.9 %collective-permute-done.2 = bf16[2,48,512]{2,1,0:T(8,128)(2,1)S(1)} collective-permute-done((bf16[2,48,512]{2,1,0:T(8,128)(2,1)S(1)}, bf16[2,48,512]{2,1,0:T(8,128)(2,1)S(1)}, u32[]{:S(2)}, u32[]{:S(2)}) %collective-permute-start.2) | collective-permute-done | bytes 98336 | tf_op jit(solution)/shard_map/ppermute | solution.py:58
  39.3 2.6 %collective-permute-start.3 = (bf16[4,48,512]{2,1,0:T(8,128)(2,1)S(1)}, bf16[4,48,512]{2,1,0:T(8,128)(2,1)S(1)}, u32[]{:S(2)}, u32[]{:S(2)}) collective-permute-start(bf16[4,48,512]{2,1,0:T(8,128)(2,1)S(1)} %maximum_select_fusion.4), channel_id=1, source_target_pairs={{0,1},{1,0},{2,3},{3,2},{4,5},{5,4},{6,7},{7,6},{8,9},{9,8},{10,11... | collective-permute-start | bytes 589832 | tf_op jit(solution)/shard_map/ppermute | solution.py:58
  41.9 1.1 collective-permute-done.3
  42.9 8.8 %fusion.23 = f32[8,48,2048]{2,1,0:T(8,128)S(1)} fusion(bf16[8,512,2048]{2,1,0:T(8,128)(2,1)} %param.6, bf16[4,48,512]{2,1,0:T(8,128)(2,1)S(1)} %maximum_select_fusion.4, bf16[4,48,512]{2,1,0:T(8,128)(2,1)S(1)} %collective-permute-done.3, pred[]{:T(512)S(6)} %ne.14), kind=kOutput, calls=%fused_computation.29 | convolution fusion | flops 805896192 | bytes 20316160 | tf_op jit(solution)/shard_map/nsi,nij->nsj/dot_general | solution.py:147
  51.8 2.3 %fusion.8 = f32[2,48,2048]{2,1,0:T(8,128)S(1)} fusion(f32[8,48,2048]{2,1,0:T(8,128)S(1)} %fusion.23, f32[8,48,48]{1,2,0:T(8,128)S(1)} %copy.25, f32[8,2]{0,1:T(2,128)S(1)} %compare_convert_fusion.1), kind=kOutput, calls=%fused_computation.10 | convolution fusion | flops 906006528 | bytes 4005952 | tf_op jit(solution)/shard_map/nhsr,nsj->hrj/dot_general | solution.py:195
  54.2 1.4 collective-permute-start.4
  55.5 2.5 %collective-permute-start.5 = (f32[2,48,512]{2,1,0:T(8,128)S(1)}, f32[2,48,512]{2,1,0:T(8,128)S(1)}, u32[]{:S(2)}, u32[]{:S(2)}) collective-permute-start(f32[2,48,512]{2,1,0:T(8,128)S(1)} %get-tuple-element.16), channel_id=1, source_target_pairs={{0,64},{4,68},{8,72},{12,76},{16,80},{20,84},{24,88},{28,92},{32,9... | collective-permute-start | bytes 589832 | tf_op jit(solution)/shard_map/ppermute | solution.py:84
  58.2 2.1 %collective-permute-done.4 = f32[2,48,512]{2,1,0:T(8,128)S(1)} collective-permute-done((f32[2,48,512]{2,1,0:T(8,128)S(1)}, f32[2,48,512]{2,1,0:T(8,128)S(1)}, u32[]{:S(2)}, u32[]{:S(2)}) %collective-permute-start.4) | collective-permute-done | bytes 196640 | tf_op jit(solution)/shard_map/ppermute | solution.py:84
  60.3 6.6 %collective-permute-done.5 = f32[2,48,512]{2,1,0:T(8,128)S(1)} collective-permute-done((f32[2,48,512]{2,1,0:T(8,128)S(1)}, f32[2,48,512]{2,1,0:T(8,128)S(1)}, u32[]{:S(2)}, u32[]{:S(2)}) %collective-permute-start.5) | collective-permute-done | bytes 196640 | tf_op jit(solution)/shard_map/ppermute | solution.py:84
  66.9 2.4 %collective-permute-done.6 = f32[2,48,512]{2,1,0:T(8,128)S(1)} collective-permute-done((f32[2,48,512]{2,1,0:T(8,128)S(1)}, f32[2,48,512]{2,1,0:T(8,128)S(1)}, u32[]{:S(2)}, u32[]{:S(2)}) %collective-permute-start.6) | collective-permute-done | bytes 196640 | tf_op jit(solution)/shard_map/ppermute | solution.py:84
  69.4 1.7 %collective-permute-start.7 = (f32[2,48,128]{2,1,0:T(8,128)S(1)}, f32[2,48,128]{2,1,0:T(8,128)S(1)}, u32[]{:S(2)}, u32[]{:S(2)}) collective-permute-start(f32[2,48,128]{2,1,0:T(8,128)S(1)} %get-tuple-element.17), channel_id=1, source_target_pairs={{0,8},{4,12},{8,0},{12,4},{16,24},{20,28},{24,16},{28,20},{32,40},... | collective-permute-start | bytes 147464 | tf_op jit(solution)/shard_map/ppermute | solution.py:84
  71.1 3.3 %collective-permute-start.8 = (f32[2,48,128]{2,1,0:T(8,128)S(1)}, f32[2,48,128]{2,1,0:T(8,128)S(1)}, u32[]{:S(2)}, u32[]{:S(2)}) collective-permute-start(f32[2,48,128]{2,1,0:T(8,128)S(1)} %get-tuple-element.19), channel_id=1, source_target_pairs={{0,16},{4,20},{8,24},{12,28},{16,0},{20,4},{24,8},{28,12},{32,48},... | collective-permute-start | bytes 147464 | tf_op jit(solution)/shard_map/ppermute | solution.py:84
  74.5 7.4 %custom-call.8 = f32[2,1,48,48]{2,3,1,0:T(8,128)S(1)} custom-call(f32[2,1,48,48]{3,2,1,0:T(8,128)S(1)} %select_bitcast_fusion), custom_call_target="InvertDiagBlocksLowerTriangular" | custom-call | tf_op jit(solution)/shard_map/triangular_solve | solution.py:156
  82.0 2.9 %collective-permute-start.10 = (f32[2,48,64]{2,1,0:T(8,128)S(1)}, f32[2,48,64]{2,1,0:T(8,128)S(1)}, u32[]{:S(2)}, u32[]{:S(2)}) collective-permute-start(f32[2,48,64]{2,1,0:T(8,128)S(1)} %constant_dynamic-slice_fusion), channel_id=1, source_target_pairs={{0,4},{4,0},{8,12},{12,8},{16,20},{20,16},{24,28},{28,24},{32,36},... | collective-permute-start | bytes 73736 | tf_op jit(solution)/shard_map/ppermute | solution.py:84
  85.2 1.3 collective-permute-done.10
  87.0 3.0 %collective-permute-start.11 = (f32[2,48,64]{2,1,0:T(8,128)S(1)}, f32[2,48,64]{2,1,0:T(8,128)S(1)}, u32[]{:S(2)}, u32[]{:S(2)}) collective-permute-start(f32[2,48,64]{2,1,0:T(8,128)S(1)} %fusion.238), channel_id=1, source_target_pairs={{0,4},{4,0},{8,12},{12,8},{16,20},{20,16},{24,28},{28,24},{32,36},... | collective-permute-start | bytes 73736 | tf_op jit(solution)/shard_map/ppermute | solution.py:101
  90.3 1.3 collective-permute-done.11
  91.5 0.5 dynamic_update_slice.31
  92.1 3.8 %collective-permute-start.13 = (f32[2,48,128]{2,1,0:T(8,128)S(1)}, f32[2,48,128]{2,1,0:T(8,128)S(1)}, u32[]{:S(2)}, u32[]{:S(2)}) collective-permute-start(f32[2,48,128]{2,1,0:T(8,128)S(1)} %dynamic_update_slice.31), channel_id=1, source_target_pairs={{0,16},{4,20},{8,24},{12,28},{16,0},{20,4},{24,8},{28,12},{32,48},... | collective-permute-start | bytes 147464 | tf_op jit(solution)/shard_map/ppermute | solution.py:101
  96.1 1.9 %collective-permute-done.13 = f32[2,48,128]{2,1,0:T(8,128)S(1)} collective-permute-done((f32[2,48,128]{2,1,0:T(8,128)S(1)}, f32[2,48,128]{2,1,0:T(8,128)S(1)}, u32[]{:S(2)}, u32[]{:S(2)}) %collective-permute-start.13) | collective-permute-done | bytes 49184 | tf_op jit(solution)/shard_map/ppermute | solution.py:101
  98.0 2.1 %collective-permute-done.14 = f32[2,48,128]{2,1,0:T(8,128)S(1)} collective-permute-done((f32[2,48,128]{2,1,0:T(8,128)S(1)}, f32[2,48,128]{2,1,0:T(8,128)S(1)}, u32[]{:S(2)}, u32[]{:S(2)}) %collective-permute-start.14) | collective-permute-done | bytes 49184 | tf_op jit(solution)/shard_map/ppermute | solution.py:101
  100.2 1.4 collective-permute-start.16
  101.5 2.5 %collective-permute-start.17 = (f32[2,48,512]{2,1,0:T(8,128)S(1)}, f32[2,48,512]{2,1,0:T(8,128)S(1)}, u32[]{:S(2)}, u32[]{:S(2)}) collective-permute-start(f32[2,48,512]{2,1,0:T(8,128)S(1)} %constant_dynamic-update-slice_fusion.4), channel_id=1, source_target_pairs={{0,96},{4,100},{8,104},{12,108},{16,112},{20,116},{24,120},{28,124... | collective-permute-start | bytes 589832 | tf_op jit(solution)/shard_map/ppermute | solution.py:101
  104.1 0.6 collective-permute-done.15
  104.7 2.1 %collective-permute-done.16 = f32[2,48,512]{2,1,0:T(8,128)S(1)} collective-permute-done((f32[2,48,512]{2,1,0:T(8,128)S(1)}, f32[2,48,512]{2,1,0:T(8,128)S(1)}, u32[]{:S(2)}, u32[]{:S(2)}) %collective-permute-start.16) | collective-permute-done | bytes 196640 | tf_op jit(solution)/shard_map/ppermute | solution.py:101
  106.8 2.0 %collective-permute-done.17 = f32[2,48,512]{2,1,0:T(8,128)S(1)} collective-permute-done((f32[2,48,512]{2,1,0:T(8,128)S(1)}, f32[2,48,512]{2,1,0:T(8,128)S(1)}, u32[]{:S(2)}, u32[]{:S(2)}) %collective-permute-start.17) | collective-permute-done | bytes 196640 | tf_op jit(solution)/shard_map/ppermute | solution.py:101
  108.8 11.3 %fusion.14 = f32[8,2,48,512]{3,2,0,1:T(8,128)S(1)} fusion(bf16[8,512,2048]{2,1,0:T(8,128)(2,1)} %param.6, f32[2,48,2048]{2,1,0:T(8,128)S(1)} %constant_dynamic-update-slice_fusion), kind=kOutput, calls=%fused_computation.14 | convolution fusion | flops 1610809344 | bytes 19136512 | tf_op jit(solution)/shard_map/hrj,nij->nhri/dot_general | solution.py:129
  120.4 7.5 %collective-permute-start.18 = (f32[4,48,512]{2,1,0:T(8,128)S(1)}, f32[4,48,512]{2,1,0:T(8,128)S(1)}, u32[]{:S(2)}, u32[]{:S(2)}) collective-permute-start(f32[4,48,512]{2,1,0:T(8,128)S(1)} %slice_select_fusion), channel_id=1, source_target_pairs={{0,1},{1,0},{2,3},{3,2},{4,5},{5,4},{6,7},{7,6},{8,9},{9,8},{10,11... | collective-permute-start | bytes 1179656 | tf_op jit(solution)/shard_map/ppermute | solution.py:49
  127.9 1.3 collective-permute-done.18
  129.4 1.4 collective-permute-start.19
  130.8 4.8 %collective-permute-done.19 = f32[2,48,512]{2,1,0:T(8,128)S(1)} collective-permute-done((f32[2,48,512]{2,1,0:T(8,128)S(1)}, f32[2,48,512]{2,1,0:T(8,128)S(1)}, u32[]{:S(2)}, u32[]{:S(2)}) %collective-permute-start.19) | collective-permute-done | bytes 196640 | tf_op jit(solution)/shard_map/ppermute | solution.py:49
  135.6 0.3 fusion.40
  135.9 0.4 select_reduce_fusion
  140.1 1.4 collective-permute-start.20
  141.5 2.1 %collective-permute-done.20 = bf16[2,48,512]{2,1,0:T(8,128)(2,1)S(1)} collective-permute-done((bf16[2,48,512]{2,1,0:T(8,128)(2,1)S(1)}, bf16[2,48,512]{2,1,0:T(8,128)(2,1)S(1)}, u32[]{:S(2)}, u32[]{:S(2)}) %collective-permute-start.20) | collective-permute-done | bytes 98336 | tf_op jit(solution)/shard_map/ppermute | solution.py:58
  143.7 2.7 %collective-permute-start.21 = (bf16[4,48,512]{2,1,0:T(8,128)(2,1)S(1)}, bf16[4,48,512]{2,1,0:T(8,128)(2,1)S(1)}, u32[]{:S(2)}, u32[]{:S(2)}) collective-permute-start(bf16[4,48,512]{2,1,0:T(8,128)(2,1)S(1)} %maximum_select_fusion.5), channel_id=1, source_target_pairs={{0,1},{1,0},{2,3},{3,2},{4,5},{5,4},{6,7},{7,6},{8,9},{9,8},{10,11... | collective-permute-start | bytes 589832 | tf_op jit(solution)/shard_map/ppermute | solution.py:58
  146.4 2.8 %fusion.6 = f32[8,48,2048]{2,1,0:T(8,128)S(1)} fusion(f32[48,2048]{1,0:T(8,128)S(1)} %get-tuple-element.13, f32[48,2048]{1,0:T(8,128)S(1)} %get-tuple-element.12, pred[8]{0:T(512)(128)(4,1)S(1)} %broadcast_compare_fusion, f32[8,48]{1,0:T(8,128)S(1)} %gather_fusion, f32[48,48]{1,0:T(8,128)S(1)} %get-tuple-element.23, f32[48,48]{1,0:T(8,128)S(1)} %get-tuple-element.22), kind=kOutput, calls=%fused_computation.7 | convolution fusion | flops 453808128 | bytes 3952136 | tf_op jit(solution)/shard_map/nrs,nsj->nrj/dot_general | solution.py:207
  149.2 10.5 %convolution_subtract_fusion = f32[8,48,2048]{2,1,0:T(8,128)} fusion(f32[8,48,2048]{2,1,0:T(8,128)S(1)} %fusion.6, bf16[8,512,2048]{2,1,0:T(8,128)(2,1)} %param.6, bf16[4,48,512]{2,1,0:T(8,128)(2,1)S(1)} %maximum_select_fusion.5, bf16[4,48,512]{2,1,0:T(8,128)(2,1)S(1)} %collective-permute-done.21, pred[]{:T(512)S(6)} %ne.14), kind=kOutput, calls=%fused_computation.9 | convolution fusion | flops 806682624 | bytes 23461888 | tf_op jit(solution)/shard_map/nsi,nij->nsj/dot_general | solution.py:147
  (138 shorter events, 11.3 us)
Async XLA Ops:
  0.6 1.0 copy-start
  12.7 1.8 %copy-start.4 = (s32[256]{0:T(256)S(1)}, s32[256]{0:T(256)}, u32[]{:S(2)}) copy-start(s32[256]{0:T(256)} %param.10) | copy-start | bytes 3076
  12.7 1.8 %copy-start.5 = (s32[256]{0:T(256)S(1)}, s32[256]{0:T(256)}, u32[]{:S(2)}) copy-start(s32[256]{0:T(256)} %param.11) | copy-start | bytes 3076
  12.7 1.9 %copy-start.2 = (f32[256,48]{0,1:T(8,128)S(1)}, f32[256,48]{0,1:T(8,128)}, u32[]{:S(2)}) copy-start(f32[256,48]{0,1:T(8,128)} %param.8) | copy-start | bytes 147460
  12.7 1.9 %copy-start.3 = (f32[2,48,48]{2,1,0:T(8,128)S(1)}, f32[2,48,48]{2,1,0:T(8,128)}, u32[]{:S(2)}) copy-start(f32[2,48,48]{2,1,0:T(8,128)} %param.9) | copy-start | bytes 55300
  13.0 11.9 %collective-permute-start = (f32[4,48,512]{2,1,0:T(8,128)S(1)}, f32[4,48,512]{2,1,0:T(8,128)S(1)}, u32[]{:S(2)}, u32[]{:S(2)}) collective-permute-start(f32[4,48,512]{2,1,0:T(8,128)S(1)} %slice_select_fusion.1), channel_id=1, source_target_pairs={{0,1},{1,0},{2,3},{3,2},{4,5},{5,4},{6,7},{7,6},{8,9},{9,8},{10,11... | collective-permute-start | bytes 1179656 | tf_op jit(solution)/shard_map/ppermute | solution.py:49
  25.0 6.2 %collective-permute-start.1 = (f32[2,48,512]{2,1,0:T(8,128)S(1)}, f32[2,48,512]{2,1,0:T(8,128)S(1)}, u32[]{:S(2)}, u32[]{:S(2)}) collective-permute-start(f32[2,48,512]{2,1,0:T(8,128)S(1)} %slice_select_fusion.3), channel_id=1, source_target_pairs={{0,2},{1,3},{2,0},{3,1},{4,6},{5,7},{6,4},{7,5},{8,10},{9,11},{10,... | collective-permute-start | bytes 589832 | tf_op jit(solution)/shard_map/ppermute | solution.py:49
  35.7 3.5 %collective-permute-start.2 = (bf16[2,48,512]{2,1,0:T(8,128)(2,1)S(1)}, bf16[2,48,512]{2,1,0:T(8,128)(2,1)S(1)}, u32[]{:S(2)}, u32[]{:S(2)}) collective-permute-start(bf16[2,48,512]{2,1,0:T(8,128)(2,1)S(1)} %convolution_convert_fusion.1), channel_id=1, source_target_pairs={{0,2},{1,3},{2,0},{3,1},{4,6},{5,7},{6,4},{7,5},{8,10},{9,11},{10,... | collective-permute-start | bytes 294920 | tf_op jit(solution)/shard_map/ppermute | solution.py:58
  39.3 3.7 %collective-permute-start.3 = (bf16[4,48,512]{2,1,0:T(8,128)(2,1)S(1)}, bf16[4,48,512]{2,1,0:T(8,128)(2,1)S(1)}, u32[]{:S(2)}, u32[]{:S(2)}) collective-permute-start(bf16[4,48,512]{2,1,0:T(8,128)(2,1)S(1)} %maximum_select_fusion.4), channel_id=1, source_target_pairs={{0,1},{1,0},{2,3},{3,2},{4,5},{5,4},{6,7},{7,6},{8,9},{9,8},{10,11... | collective-permute-start | bytes 589832 | tf_op jit(solution)/shard_map/ppermute | solution.py:58
  54.2 6.2 %collective-permute-start.4 = (f32[2,48,512]{2,1,0:T(8,128)S(1)}, f32[2,48,512]{2,1,0:T(8,128)S(1)}, u32[]{:S(2)}, u32[]{:S(2)}) collective-permute-start(f32[2,48,512]{2,1,0:T(8,128)S(1)} %get-tuple-element.14), channel_id=1, source_target_pairs={{0,32},{4,36},{8,40},{12,44},{16,48},{20,52},{24,56},{28,60},{32,0... | collective-permute-start | bytes 589832 | tf_op jit(solution)/shard_map/ppermute | solution.py:84
  55.5 11.3 %collective-permute-start.5 = (f32[2,48,512]{2,1,0:T(8,128)S(1)}, f32[2,48,512]{2,1,0:T(8,128)S(1)}, u32[]{:S(2)}, u32[]{:S(2)}) collective-permute-start(f32[2,48,512]{2,1,0:T(8,128)S(1)} %get-tuple-element.16), channel_id=1, source_target_pairs={{0,64},{4,68},{8,72},{12,76},{16,80},{20,84},{24,88},{28,92},{32,9... | collective-permute-start | bytes 589832 | tf_op jit(solution)/shard_map/ppermute | solution.py:84
  58.0 11.3 %collective-permute-start.6 = (f32[2,48,512]{2,1,0:T(8,128)S(1)}, f32[2,48,512]{2,1,0:T(8,128)S(1)}, u32[]{:S(2)}, u32[]{:S(2)}) collective-permute-start(f32[2,48,512]{2,1,0:T(8,128)S(1)} %get-tuple-element.15), channel_id=1, source_target_pairs={{0,96},{4,100},{8,104},{12,108},{16,112},{20,116},{24,120},{28,124... | collective-permute-start | bytes 589832 | tf_op jit(solution)/shard_map/ppermute | solution.py:84
  69.4 12.5 %collective-permute-start.7 = (f32[2,48,128]{2,1,0:T(8,128)S(1)}, f32[2,48,128]{2,1,0:T(8,128)S(1)}, u32[]{:S(2)}, u32[]{:S(2)}) collective-permute-start(f32[2,48,128]{2,1,0:T(8,128)S(1)} %get-tuple-element.17), channel_id=1, source_target_pairs={{0,8},{4,12},{8,0},{12,4},{16,24},{20,28},{24,16},{28,20},{32,40},... | collective-permute-start | bytes 147464 | tf_op jit(solution)/shard_map/ppermute | solution.py:84
  71.1 10.8 %collective-permute-start.8 = (f32[2,48,128]{2,1,0:T(8,128)S(1)}, f32[2,48,128]{2,1,0:T(8,128)S(1)}, u32[]{:S(2)}, u32[]{:S(2)}) collective-permute-start(f32[2,48,128]{2,1,0:T(8,128)S(1)} %get-tuple-element.19), channel_id=1, source_target_pairs={{0,16},{4,20},{8,24},{12,28},{16,0},{20,4},{24,8},{28,12},{32,48},... | collective-permute-start | bytes 147464 | tf_op jit(solution)/shard_map/ppermute | solution.py:84
  74.4 7.5 %collective-permute-start.9 = (f32[2,48,128]{2,1,0:T(8,128)S(1)}, f32[2,48,128]{2,1,0:T(8,128)S(1)}, u32[]{:S(2)}, u32[]{:S(2)}) collective-permute-start(f32[2,48,128]{2,1,0:T(8,128)S(1)} %get-tuple-element.18), channel_id=1, source_target_pairs={{0,24},{4,28},{8,16},{12,20},{16,8},{20,12},{24,0},{28,4},{32,56},... | collective-permute-start | bytes 147464 | tf_op jit(solution)/shard_map/ppermute | solution.py:84
  82.0 4.5 %collective-permute-start.10 = (f32[2,48,64]{2,1,0:T(8,128)S(1)}, f32[2,48,64]{2,1,0:T(8,128)S(1)}, u32[]{:S(2)}, u32[]{:S(2)}) collective-permute-start(f32[2,48,64]{2,1,0:T(8,128)S(1)} %constant_dynamic-slice_fusion), channel_id=1, source_target_pairs={{0,4},{4,0},{8,12},{12,8},{16,20},{20,16},{24,28},{28,24},{32,36},... | collective-permute-start | bytes 73736 | tf_op jit(solution)/shard_map/ppermute | solution.py:84
  87.0 4.5 %collective-permute-start.11 = (f32[2,48,64]{2,1,0:T(8,128)S(1)}, f32[2,48,64]{2,1,0:T(8,128)S(1)}, u32[]{:S(2)}, u32[]{:S(2)}) collective-permute-start(f32[2,48,64]{2,1,0:T(8,128)S(1)} %fusion.238), channel_id=1, source_target_pairs={{0,4},{4,0},{8,12},{12,8},{16,20},{20,16},{24,28},{28,24},{32,36},... | collective-permute-start | bytes 73736 | tf_op jit(solution)/shard_map/ppermute | solution.py:101
  92.1 4.0 %collective-permute-start.12 = (f32[2,48,128]{2,1,0:T(8,128)S(1)}, f32[2,48,128]{2,1,0:T(8,128)S(1)}, u32[]{:S(2)}, u32[]{:S(2)}) collective-permute-start(f32[2,48,128]{2,1,0:T(8,128)S(1)} %dynamic_update_slice.31), channel_id=1, source_target_pairs={{0,8},{4,12},{8,0},{12,4},{16,24},{20,28},{24,16},{28,20},{32,40},... | collective-permute-start | bytes 147464 | tf_op jit(solution)/shard_map/ppermute | solution.py:101
  92.1 5.8 %collective-permute-start.13 = (f32[2,48,128]{2,1,0:T(8,128)S(1)}, f32[2,48,128]{2,1,0:T(8,128)S(1)}, u32[]{:S(2)}, u32[]{:S(2)}) collective-permute-start(f32[2,48,128]{2,1,0:T(8,128)S(1)} %dynamic_update_slice.31), channel_id=1, source_target_pairs={{0,16},{4,20},{8,24},{12,28},{16,0},{20,4},{24,8},{28,12},{32,48},... | collective-permute-start | bytes 147464 | tf_op jit(solution)/shard_map/ppermute | solution.py:101
  96.0 4.2 %collective-permute-start.14 = (f32[2,48,128]{2,1,0:T(8,128)S(1)}, f32[2,48,128]{2,1,0:T(8,128)S(1)}, u32[]{:S(2)}, u32[]{:S(2)}) collective-permute-start(f32[2,48,128]{2,1,0:T(8,128)S(1)} %dynamic_update_slice.31), channel_id=1, source_target_pairs={{0,24},{4,28},{8,16},{12,20},{16,8},{20,12},{24,0},{28,4},{32,56},... | collective-permute-start | bytes 147464 | tf_op jit(solution)/shard_map/ppermute | solution.py:101
  100.1 4.5 %collective-permute-start.15 = (f32[2,48,512]{2,1,0:T(8,128)S(1)}, f32[2,48,512]{2,1,0:T(8,128)S(1)}, u32[]{:S(2)}, u32[]{:S(2)}) collective-permute-start(f32[2,48,512]{2,1,0:T(8,128)S(1)} %constant_dynamic-update-slice_fusion.4), channel_id=1, source_target_pairs={{0,32},{4,36},{8,40},{12,44},{16,48},{20,52},{24,56},{28,60},{32,0... | collective-permute-start | bytes 589832 | tf_op jit(solution)/shard_map/ppermute | solution.py:101
  100.2 6.6 %collective-permute-start.16 = (f32[2,48,512]{2,1,0:T(8,128)S(1)}, f32[2,48,512]{2,1,0:T(8,128)S(1)}, u32[]{:S(2)}, u32[]{:S(2)}) collective-permute-start(f32[2,48,512]{2,1,0:T(8,128)S(1)} %constant_dynamic-update-slice_fusion.4), channel_id=1, source_target_pairs={{0,64},{4,68},{8,72},{12,76},{16,80},{20,84},{24,88},{28,92},{32,9... | collective-permute-start | bytes 589832 | tf_op jit(solution)/shard_map/ppermute | solution.py:101
  101.5 7.3 %collective-permute-start.17 = (f32[2,48,512]{2,1,0:T(8,128)S(1)}, f32[2,48,512]{2,1,0:T(8,128)S(1)}, u32[]{:S(2)}, u32[]{:S(2)}) collective-permute-start(f32[2,48,512]{2,1,0:T(8,128)S(1)} %constant_dynamic-update-slice_fusion.4), channel_id=1, source_target_pairs={{0,96},{4,100},{8,104},{12,108},{16,112},{20,116},{24,120},{28,124... | collective-permute-start | bytes 589832 | tf_op jit(solution)/shard_map/ppermute | solution.py:101
  108.8 32.7 %copy-start.1 = (f32[2,48,2048]{2,1,0:T(8,128)}, f32[2,48,2048]{2,1,0:T(8,128)S(1)}, u32[]{:S(2)}) copy-start(f32[2,48,2048]{2,1,0:T(8,128)S(1)} %constant_dynamic-update-slice_fusion) | copy-start | bytes 2359300
  120.4 8.9 %collective-permute-start.18 = (f32[4,48,512]{2,1,0:T(8,128)S(1)}, f32[4,48,512]{2,1,0:T(8,128)S(1)}, u32[]{:S(2)}, u32[]{:S(2)}) collective-permute-start(f32[4,48,512]{2,1,0:T(8,128)S(1)} %slice_select_fusion), channel_id=1, source_target_pairs={{0,1},{1,0},{2,3},{3,2},{4,5},{5,4},{6,7},{7,6},{8,9},{9,8},{10,11... | collective-permute-start | bytes 1179656 | tf_op jit(solution)/shard_map/ppermute | solution.py:49
  129.4 6.2 %collective-permute-start.19 = (f32[2,48,512]{2,1,0:T(8,128)S(1)}, f32[2,48,512]{2,1,0:T(8,128)S(1)}, u32[]{:S(2)}, u32[]{:S(2)}) collective-permute-start(f32[2,48,512]{2,1,0:T(8,128)S(1)} %slice_select_fusion.2), channel_id=1, source_target_pairs={{0,2},{1,3},{2,0},{3,1},{4,6},{5,7},{6,4},{7,5},{8,10},{9,11},{10,... | collective-permute-start | bytes 589832 | tf_op jit(solution)/shard_map/ppermute | solution.py:49
  140.1 3.5 %collective-permute-start.20 = (bf16[2,48,512]{2,1,0:T(8,128)(2,1)S(1)}, bf16[2,48,512]{2,1,0:T(8,128)(2,1)S(1)}, u32[]{:S(2)}, u32[]{:S(2)}) collective-permute-start(bf16[2,48,512]{2,1,0:T(8,128)(2,1)S(1)} %convolution_convert_fusion), channel_id=1, source_target_pairs={{0,2},{1,3},{2,0},{3,1},{4,6},{5,7},{6,4},{7,5},{8,10},{9,11},{10,... | collective-permute-start | bytes 294920 | tf_op jit(solution)/shard_map/ppermute | solution.py:58
  143.7 5.5 %collective-permute-start.21 = (bf16[4,48,512]{2,1,0:T(8,128)(2,1)S(1)}, bf16[4,48,512]{2,1,0:T(8,128)(2,1)S(1)}, u32[]{:S(2)}, u32[]{:S(2)}) collective-permute-start(bf16[4,48,512]{2,1,0:T(8,128)(2,1)S(1)} %maximum_select_fusion.5), channel_id=1, source_target_pairs={{0,1},{1,0},{2,3},{3,2},{4,5},{5,4},{6,7},{7,6},{8,9},{9,8},{10,11... | collective-permute-start | bytes 589832 | tf_op jit(solution)/shard_map/ppermute | solution.py:58
